TPU v7x, 32 devices: a whole 2x2x4 slice. The times are simulated.
32 devices in a mesh: groups: 2 (over y), paths: 4 (over z), cols: 2 (over x), depth: 2 (over core).
Axes of the slice: x: 2, y: 2, z: 4, core: 2. Of those that a mesh axis runs over, the one named last changes fastest.
Arguments:
- panels: bfloat16 [96, 64, 1024], P(('groups', 'cols', 'paths'), None, 'depth'), parts along dimension 0, may hold values from -0.0546875 to 0.0546875
- model: bfloat16 [96, 1024], P(('groups', 'cols', 'paths'), 'depth'), parts along dimension 0, may hold values from -6 to 6
- depth_weight: bfloat16 [2048, 1024], P(('groups', 'paths'), 'depth'), parts along dimension 0, may hold values from -6 to 6
- seg_len: bfloat16 [2048, 48], P(('groups', 'paths'), 'cols'), parts along dimension 0, may hold values from 0.29882812 to 3
- path_start: int32 [2048], P(('groups', 'paths')), parts along dimension 0, may hold values from 0 to 47, as said below
- path_end: int32 [2048], P(('groups', 'paths')), parts along dimension 0, may hold values from 1 to 48, as said below
- mode_index: int32 [2048, 4], P(('groups', 'paths')), parts along dimension 0, may hold values from 0 to 63, all different within a row
- observed: float32 [2048, 4], P(('groups', 'paths')), parts along dimension 0, may hold values from -6 to 6
Outputs:
- gradient: float32 [96, 1024], P(('groups', 'cols', 'paths'), 'depth'), parts along dimension 0
- misfit: float32 [2048, 4], P(('groups', 'paths')), parts along dimension 0
There are 2 independent parts, one for each index of `groups`. A program takes and returns all parts, laid end to end along the dimension named above; each array names one. Nothing has to cross between parts.
Inputs may be any that keep to these rules, and one draw needn't show every extreme that they name: `path_start`: each path starts before it ends; path 0 spans all 48 columns. `path_end`: each path ends after it starts. `mode_index`: each path names 4 different modes.
All inputs are finite; a program needn't handle non-finite values.
Results may differ from a plain program's by a relative error of at most 0.011.
Values may be sent and summed in bfloat16 or wider, within the bound.
No kernel may reach another device: no remote copies, remote signals or barrier semaphores. Data moves between devices by JAX's collectives and lax.ppermute only.
A program may use at most 64 MiB of HBM per device.

v0:
```python
import jax
import jax.numpy as jnp
from jax import lax
from jax.sharding import PartitionSpec as P


def finish(partial_value, one_hot, observed):
    combined = lax.psum(partial_value, ("cols", "depth"))
    travel = jnp.einsum("pkm,pm->pk", one_hot, combined)
    misfit = travel - observed
    resid_modes = jnp.einsum("pk,pkm->pm", misfit, one_hot)
    return (misfit, resid_modes)


def shards(panels, model, depth_weight, seg_len, path_start, path_end, mode_index, observed):
    own_cols, modes, depth_half = panels.shape
    path_rows, block_cols = seg_len.shape
    columns = lax.axis_index("cols") * block_cols + lax.iota(jnp.int32, block_cols)
    inside = (columns[None, :] >= path_start[:, None]) & (columns[None, :] < path_end[:, None])
    lengths = jnp.where(inside, seg_len, jnp.zeros_like(seg_len))
    one_hot = (mode_index[:, :, None] == lax.iota(jnp.int32, modes)[None, None, :]).astype(
        jnp.float32
    )
    kernel_piece = lax.all_gather(panels, "paths", axis=0, tiled=True)
    model_piece = lax.all_gather(model, "paths", axis=0, tiled=True)
    row_count = kernel_piece.shape[0]
    scaled = (
        kernel_piece.astype(jnp.float32) * model_piece.astype(jnp.float32)[:, None, :]
    ).astype(jnp.bfloat16)
    scaled = scaled.reshape(row_count * modes, depth_half)
    weighted = lax.dot_general(
        depth_weight, scaled, (((1,), (1,)), ((), ())), preferred_element_type=jnp.float32
    )
    weighted = weighted.reshape(path_rows, row_count, modes)
    row_weights = lengths.astype(jnp.float32)
    partial_value = jnp.einsum("pc,pcm->pm", row_weights, weighted)
    misfit, resid_modes = finish(partial_value, one_hot, observed)
    kernel_piece = lax.all_gather(panels, "paths", axis=0, tiled=True)
    row_count = kernel_piece.shape[0]
    row_weights = lengths.astype(jnp.float32)
    spread = (
        (row_weights[:, :, None] * resid_modes[:, None, :])
        .astype(jnp.bfloat16)
        .reshape(path_rows, row_count * modes)
    )
    summed = lax.dot_general(
        spread, depth_weight, (((0,), (0,)), ((), ())), preferred_element_type=jnp.float32
    )
    summed = summed.reshape(row_count, modes, depth_half)
    block_terms = jnp.sum(summed * kernel_piece.astype(jnp.float32), axis=1)
    gradient = lax.psum_scatter(block_terms, "paths", scatter_dimension=0, tiled=True)
    return (gradient, misfit)


def solution(mesh):
    return jax.shard_map(
        shards,
        mesh=mesh,
        in_specs=(
            P(("groups", "cols", "paths"), None, "depth"),
            P(("groups", "cols", "paths"), "depth"),
            P(("groups", "paths"), "depth"),
            P(("groups", "paths"), "cols"),
            P(("groups", "paths")),
            P(("groups", "paths")),
            P(("groups", "paths"), None),
            P(("groups", "paths"), None),
        ),
        out_specs=(P(("groups", "cols", "paths"), "depth"), P(("groups", "paths"), None)),
        check_vma=False,
    )
```

profile of v0, /device:TPU:0, one launch (start us, length us, event | category | flops | bytes accessed | tf_op | source)
XLA Modules:
  0.0 111.6 jit_solution(14641012471253387348)
XLA Ops:
  7.2 0.0 copy-start
  7.2 0.0 all-gather.3.cloned.1.call-start
  7.2 0.7 all-gather.3.cloned.1.call-update
  7.9 0.0 all-reduce.4.cloned.1.call-start
  8.0 15.0 %all-gather = bf16[4,6,512]{2,1,0:T(8,128)(2,1)S(1)} all-gather(bf16[1,6,512]{2,1,0:T(8,128)(2,1)} %bitcast.28), channel_id=1, replica_groups=mesh['groups'=2,'paths'=4,'cols'=2,'depth'=2] {'paths'}, dimensions={0}, use_global_device_ids=true | all-gather | bytes 30720 | tf_op jit(solution)/shard_map/all_gather | solution.py:25
  23.0 0.8 fusion.10
  23.8 25.6 %all-gather.3.cloned.1.call-done = bf16[24,64,512]{2,1,0:T(8,128)(2,1)} async-done(((bf16[6,64,512]{2,1,0:T(8,128)(2,1)}), bf16[24,64,512]{2,1,0:T(8,128)(2,1)}) %all-gather.3.cloned.1.call-update) | async-done | bytes 1572880 | tf_op jit(solution)/shard_map/all_gather | solution.py:24
  49.4 1.7 %fusion.1 = bf16[24,64,512]{2,1,0:T(8,128)(2,1)S(1)} fusion(bf16[24,64,512]{2,1,0:T(8,128)(2,1)} %all-gather.3.cloned.1.call-done, f32[24,512]{1,0:T(8,128)S(1)} %reshape.31), kind=kLoop, calls=%fused_computation.2 | loop fusion | flops 2359296 | bytes 3194880 | tf_op jit(solution)/shard_map/convert_element_type | solution.py:29
  51.2 0.6 fusion.11
  51.8 0.0 copy-start.3
  51.8 0.1 multiply_reduce_fusion
  51.9 0.0 copy-start.4
  52.0 0.8 copy.17
  52.7 0.0 all-reduce.4.cloned.1.call-update
  52.7 0.1 copy.12
  52.9 30.3 %all-reduce.4.cloned.1.call-done = f32[256,64]{1,0:T(8,128)} async-done(((f32[256,64]{1,0:T(8,128)}), f32[256,64]{1,0:T(8,128)}) %all-reduce.4.cloned.1.call-update) | async-done | bytes 65552 | tf_op jit(solution)/shard_map/psum | solution.py:8
  83.2 1.4 %fusion.7 = f32[256,1,4]{2,1,0:T(1,128)S(1)} fusion(f32[256,64,1]{1,2,0:T(1,128)} %bitcast.29, s32[256,4]{1,0:T(8,128)S(1)} %copy.12), kind=kOutput, calls=%fused_computation.11 | convolution fusion | flops 196608 | bytes 73728 | tf_op jit(solution)/shard_map/pkm,pm->pk/dot_general | solution.py:9
  84.6 0.1 copy.19
  84.7 0.0 copy-start.2
  84.7 0.1 copy.26
  84.8 1.4 %select_reduce_fusion = f32[256,64]{1,0:T(8,128)S(1)} fusion(f32[256,4]{1,0:T(8,128)S(1)} %copy.26, s32[256,4]{1,0:T(8,128)S(1)} %copy.12), kind=kLoop, calls=%fused_computation.9 | loop fusion | flops 180224 | bytes 73728
  86.3 0.1 copy.23
  86.4 0.0 copy-done.1
  86.4 0.0 copy-start.5
  86.4 0.6 fusion.2
  87.0 12.8 %fusion = f32[8,512]{1,0:T(8,128)S(1)} fusion(f32[24,512]{1,0:T(8,128)S(1)} %fusion.2), kind=kCustom, calls=%all-reduce-scatter | all-reduce-scatter fusion | flops 16385 | bytes 66048
  99.8 2.9 %collective-permute-start = (f32[6,512]{1,0:T(8,128)S(1)}, f32[6,512]{1,0:T(8,128)S(1)}, u32[]{:S(2)}, u32[]{:S(2)}) collective-permute-start(f32[6,512]{1,0:T(8,128)S(1)} %slice), channel_id=1, source_target_pairs={{0,4},{4,8},{8,12},{1,5},{5,9},{9,13},{2,6},{6,10},{10,14},{3,7},{... | collective-permute-start | bytes 36872
  102.7 0.0 copy-done.5
  102.7 0.6 dynamic-slice.4
  103.9 0.2 collective-permute-done
  104.1 0.1 concatenate
  104.2 0.6 constant_dynamic-slice_fusion
  (9 shorter events, 0.0 us)
Async XLA Ops:
  7.2 44.0 %copy-start = (bf16[256,512]{1,0:T(8,128)(2,1)S(1)}, bf16[256,512]{1,0:T(8,128)(2,1)}, u32[]{:S(2)}) copy-start(bf16[256,512]{1,0:T(8,128)(2,1)} %param.10) | copy-start | bytes 786436
  7.2 42.2 %all-gather.3.cloned.1.call-start = ((), (), s32[]{:S(2)}) async-start(), calls=%async_computation | async-start | bytes 1966080 | tf_op jit(solution)/shard_map/all_gather | solution.py:24
  7.9 75.2 %all-reduce.4.cloned.1.call-start = ((), (), s32[]{:S(2)}) async-start(), calls=%async_computation.1 | async-start | bytes 262144 | tf_op jit(solution)/shard_map/psum | solution.py:8
  51.8 1.0 copy-start.3
  51.9 32.7 %copy-start.4 = (f32[256,4]{0,1:T(4,128)S(1)}, f32[256,4]{0,1:T(4,128)}, u32[]{:S(2)}) copy-start(f32[256,4]{0,1:T(4,128)} %param.15) | copy-start | bytes 12292
  52.7 33.7 %copy-start.1 = (bf16[24,64,512]{2,1,0:T(8,128)(2,1)S(1)}, bf16[24,64,512]{2,1,0:T(8,128)(2,1)}, u32[]{:S(2)}) copy-start(bf16[24,64,512]{2,1,0:T(8,128)(2,1)} %all-gather.3.cloned.1.call-done) | copy-start | bytes 4718596
  84.7 2.3 %copy-start.2 = (f32[256,4]{0,1:T(4,128)}, f32[256,4]{0,1:T(4,128)S(1)}, u32[]{:S(2)}) copy-start(f32[256,4]{0,1:T(4,128)S(1)} %bitcast_subtract_fusion) | copy-start | bytes 12292
  86.4 16.3 %copy-start.5 = (u32[32]{0:T(128)S(1)}, u32[32]{0:T(128)}, u32[]{:S(2)}) copy-start(u32[32]{0:T(128)} %constant.17) | copy-start | bytes 388
  99.8 4.3 %collective-permute-start = (f32[6,512]{1,0:T(8,128)S(1)}, f32[6,512]{1,0:T(8,128)S(1)}, u32[]{:S(2)}, u32[]{:S(2)}) collective-permute-start(f32[6,512]{1,0:T(8,128)S(1)} %slice), channel_id=1, source_target_pairs={{0,4},{4,8},{8,12},{1,5},{5,9},{9,13},{2,6},{6,10},{10,14},{3,7},{... | collective-permute-start | bytes 36872
Sparse Core Ops, SparseCore 0:
  9.6 39.7 all-gather.2
  52.9 30.2 all-reduce.3
where the time goes:
time: 112 us
  waiting for transfers between devices  56.8 us (51%)
  blocking collectives  27.8 us (25%)
  between operations  14.9 us (13%)
  other arithmetic  4.14 us (4%)
  starting transfers between devices  2.94 us (3%)
  matrix products  2.64 us (2%)
  local copies, waits for them, and re-layouts  2.5 us (2%)
    psum x1, waiting for transfers between devices, finish(): combined = lax.psum(partial_value, ('cols', 'depth'))  30.3 us
    all_gather x1, waiting for transfers between devices, shards(): kernel_piece = lax.all_gather(panels, 'paths', axis=0, tiled=True)  25.6 us
    all_gather x1, blocking collectives, shards(): model_piece = lax.all_gather(model, 'paths', axis=0, tiled=True)  15 us
    unnamed x1, blocking collectives  12.8 us
    unnamed x1, starting transfers between devices  2.87 us
  transfers between devices with their start and end apart: 3, of which 3 were waited for; matrix products, arithmetic and copies ran while one was open for 1% of the time, Pallas kernels for 0%

commit v1 on v0

v1 whole, which is shorter than its diff:
```python
import jax
import jax.numpy as jnp
from jax import lax
from jax.sharding import PartitionSpec as P

GROUP_AXES = ("paths", "cols", "depth")


def shifted_copies(x, axes, count):
    copies = [x]
    for shift in range(1, count):
        perm = [(i, (i + shift) % count) for i in range(count)]
        copies.append(lax.ppermute(x, axes, perm))
    return copies


def exchange_sum(x, axes, count):
    me = lax.axis_index(axes)
    copies = jnp.stack(shifted_copies(x, axes, count))
    copies = jnp.take(copies, (me - lax.iota(jnp.int32, count)) % count, axis=0)
    return jnp.sum(copies, axis=0)


def make_shards(n_paths, n_cols, n_depth):
    group = n_cols * n_paths * n_depth

    def shards(panels, model, depth_weight, seg_len, path_start, path_end, mode_index, observed):
        own_cols, modes, depth_half = panels.shape
        path_rows, block_cols = seg_len.shape
        kept = mode_index.shape[1]
        f32, bf16 = jnp.float32, jnp.bfloat16
        p_idx = lax.axis_index("paths")
        c_idx = lax.axis_index("cols")
        d_idx = lax.axis_index("depth")

        columns = c_idx * block_cols + lax.iota(jnp.int32, block_cols)
        inside = (columns[None, :] >= path_start[:, None]) & (columns[None, :] < path_end[:, None])
        lengths = jnp.where(inside, seg_len, jnp.zeros_like(seg_len))

        n_len = path_rows * block_cols
        n_mi = path_rows * kept
        small = jnp.concatenate([lengths.reshape(-1), mode_index.astype(bf16).reshape(-1)])
        pad = (-small.shape[0]) % depth_half
        small = jnp.pad(small, (0, pad)).reshape(-1, depth_half)
        payload = jnp.concatenate([depth_weight, small], axis=0)
        blocks = shifted_copies(payload, "paths", n_paths)

        scaled = (panels.astype(f32) * model.astype(f32)[:, None, :]).astype(bf16)
        scaled = scaled.reshape(own_cols * modes, depth_half)
        mode_ids = lax.iota(jnp.int32, modes)

        unpacked = []
        parts = []
        for s, blk in enumerate(blocks):
            dw_b = blk[:path_rows]
            sm = blk[path_rows:].reshape(-1)
            len_b = sm[:n_len].reshape(path_rows, block_cols)
            mi_b = sm[n_len:n_len + n_mi].reshape(path_rows, kept).astype(jnp.int32)
            len_own = lax.dynamic_slice_in_dim(len_b, p_idx * own_cols, own_cols, axis=1).astype(f32)
            one_hot = (mi_b[:, :, None] == mode_ids[None, None, :]).astype(f32)
            unpacked.append((dw_b, len_own, one_hot))
            weighted = lax.dot_general(
                dw_b, scaled, (((1,), (1,)), ((), ())), preferred_element_type=f32
            ).reshape(path_rows, own_cols, modes)
            per_mode = jnp.sum(len_own[:, :, None] * weighted, axis=1)
            part = jnp.sum(one_hot * per_mode[:, None, :], axis=2)
            parts.append(part.T)
        first = (c_idx == 0) & (d_idx == 0)
        parts[0] = parts[0] - jnp.where(first, observed.T, jnp.zeros_like(observed.T))
        by_shift = jnp.stack(parts)
        order = (p_idx - lax.iota(jnp.int32, n_paths)) % n_paths
        canon = jnp.take(by_shift, order, axis=0)

        if group <= 16:
            misfit_all = exchange_sum(canon, GROUP_AXES, group)
        else:
            misfit_all = exchange_sum(canon, ("cols", "depth"), n_cols * n_depth)
            misfit_all = exchange_sum(misfit_all, "paths", n_paths)
        misfit = jnp.take(misfit_all, p_idx, axis=0).T

        mis_shift = jnp.take(misfit_all, order, axis=0)
        summed = None
        for s, (dw_b, len_own, one_hot) in enumerate(unpacked):
            resid = jnp.sum(mis_shift[s].T[:, :, None] * one_hot, axis=1)
            spread = (len_own[:, :, None] * resid[:, None, :]).astype(bf16)
            spread = spread.reshape(path_rows, own_cols * modes)
            term = lax.dot_general(
                spread, dw_b, (((0,), (0,)), ((), ())), preferred_element_type=f32
            )
            summed = term if summed is None else summed + term
        summed = summed.reshape(own_cols, modes, depth_half)
        gradient = jnp.sum(summed * panels.astype(f32), axis=1)
        return (gradient, misfit)

    return shards


def solution(mesh):
    shards = make_shards(mesh.shape["paths"], mesh.shape["cols"], mesh.shape["depth"])
    return jax.shard_map(
        shards,
        mesh=mesh,
        in_specs=(
            P(("groups", "cols", "paths"), None, "depth"),
            P(("groups", "cols", "paths"), "depth"),
            P(("groups", "paths"), "depth"),
            P(("groups", "paths"), "cols"),
            P(("groups", "paths")),
            P(("groups", "paths")),
            P(("groups", "paths"), None),
            P(("groups", "paths"), None),
        ),
        out_specs=(P(("groups", "cols", "paths"), "depth"), P(("groups", "paths"), None)),
        check_vma=False,
    )
```

time: 112 us -> 63.4 us (0.57)
  waiting for transfers between devices: 56.8 us -> 22.8 us
  blocking collectives: 27.8 us -> 0 us
  starting transfers between devices: 2.94 us -> 27 us
  between operations: 14.9 us -> 1.15 us
  local copies, waits for them, and re-layouts: 2.5 us -> 7.25 us
  other arithmetic: 4.14 us -> 2.38 us
    psum x1 -> x0, waiting for transfers between devices: 30.3 us -> none  [finish(): combined = lax.psum(partial_value, ('cols', 'depth'))]
    ppermute x0 -> x18, starting transfers between devices: none -> 27 us  [shifted_copies(): copies.append(lax.ppermute(x, axes, perm))]
    all_gather x1 -> x0, waiting for transfers between devices: 25.6 us -> none  [shards(): kernel_piece = lax.all_gather(panels, 'paths', axis=0, tiled=True)]
    ppermute x0 -> x18, waiting for transfers between devices: none -> 22.8 us  [shifted_copies(): copies.append(lax.ppermute(x, axes, perm))]
    all_gather x1 -> x0, blocking collectives: 15 us -> none  [shards(): model_piece = lax.all_gather(model, 'paths', axis=0, tiled=True)]
    unnamed x1 -> x0, blocking collectives: 12.8 us -> none
    unnamed x1 -> x0, starting transfers between devices: 2.87 us -> none
    convert_element_type x2 -> x14, other arithmetic: 2.54 us -> 0.28 us  [the longest x4 0.11 us: shards(): spread = (len_own[:, :, None] * resid[:, None, :]).astype(bf16)]
  transfers between devices with their start and end apart: 3 -> 18, of which waited for: 3 -> 4; matrix products, arithmetic and copies ran while one was open for 1% -> 3% of each run, Pallas kernels for 0% -> 0%
where the time goes in v1:
time: 63.4 us; the launch traced here: 62.9 us
  starting transfers between devices  27 us (43%)
  waiting for transfers between devices  22.8 us (36%)
  local copies, waits for them, and re-layouts  7.25 us (11%)
  other arithmetic  2.38 us (4%)
  matrix products  2.25 us (4%)
  between operations  1.15 us (2%)
    ppermute x18, starting transfers between devices, shifted_copies(): copies.append(lax.ppermute(x, axes, perm))  27 us
    ppermute x18, waiting for transfers between devices, shifted_copies(): copies.append(lax.ppermute(x, axes, perm))  22.8 us
    unnamed x34, local copies, waits for them, and re-layouts  3.58 us
  transfers between devices with their start and end apart: 18, of which 4 were waited for; matrix products, arithmetic and copies ran while one was open for 3% of the time, Pallas kernels for 0%

profile of v1, /device:TPU:0, one launch (start us, length us, event | category | flops | bytes accessed | tf_op | source)
XLA Modules:
  0.0 62.9 jit_solution(15304302830294679040)
XLA Ops:
  0.7 1.0 %constant_dynamic-update-slice_fusion.1 = bf16[270,512]{1,0:T(8,128)(2,1)S(1)} fusion(bf16[256,512]{1,0:T(8,128)(2,1)} %param.12), kind=kLoop, calls=%fused_computation.45 | loop fusion | bytes 524288
  2.0 0.5 copy-done.2
  3.1 5.1 %collective-permute-start.2 = (bf16[270,512]{1,0:T(8,128)(2,1)S(1)}, bf16[270,512]{1,0:T(8,128)(2,1)S(1)}, u32[]{:S(2)}, u32[]{:S(2)}) collective-permute-start(bf16[270,512]{1,0:T(8,128)(2,1)S(1)} %constant_dynamic-update-slice_fusion), channel_id=1, source_target_pairs={{0,12},{4,0},{8,4},{12,8},{1,13},{5,1},{9,5},{13,9},{2,14},{6,2},{... | collective-permute-start | bytes 829448 | tf_op jit(solution)/shard_map/ppermute | solution.py:13
  8.2 1.0 %collective-permute-start = (bf16[270,512]{1,0:T(8,128)(2,1)S(1)}, bf16[270,512]{1,0:T(8,128)(2,1)S(1)}, u32[]{:S(2)}, u32[]{:S(2)}) collective-permute-start(bf16[270,512]{1,0:T(8,128)(2,1)S(1)} %constant_dynamic-update-slice_fusion), channel_id=1, source_target_pairs={{0,4},{4,8},{8,12},{12,0},{1,5},{5,9},{9,13},{13,1},{2,6},{6,10},{... | collective-permute-start | bytes 829448 | tf_op jit(solution)/shard_map/ppermute | solution.py:13
  9.3 0.9 %copy-done = bf16[256,512]{1,0:T(8,128)(2,1)S(1)} copy-done((bf16[256,512]{1,0:T(8,128)(2,1)S(1)}, bf16[256,512]{1,0:T(8,128)(2,1)}, u32[]{:S(2)}) %copy-start) | copy-done | bytes 262168
  10.2 0.3 fusion.21
  10.7 0.6 %copy-done.4 = f32[256,4]{0,1:T(4,128)S(1)} copy-done((f32[256,4]{0,1:T(4,128)S(1)}, f32[256,4]{0,1:T(4,128)}, u32[]{:S(2)}) %copy-start.4) | copy-done | bytes 4120
  11.3 3.9 %collective-permute-done.2 = bf16[270,512]{1,0:T(8,128)(2,1)S(1)} collective-permute-done((bf16[270,512]{1,0:T(8,128)(2,1)S(1)}, bf16[270,512]{1,0:T(8,128)(2,1)S(1)}, u32[]{:S(2)}, u32[]{:S(2)}) %collective-permute-start.2) | collective-permute-done | bytes 276512 | tf_op jit(solution)/shard_map/ppermute | solution.py:13
  15.4 16.5 %collective-permute-done.1 = bf16[270,512]{1,0:T(8,128)(2,1)S(1)} collective-permute-done((bf16[270,512]{1,0:T(8,128)(2,1)S(1)}, bf16[270,512]{1,0:T(8,128)(2,1)S(1)}, u32[]{:S(2)}, u32[]{:S(2)}) %collective-permute-start.1) | collective-permute-done | bytes 276512 | tf_op jit(solution)/shard_map/ppermute | solution.py:13
  33.4 0.3 fusion.3
  33.8 0.3 fusion.2
  34.1 0.3 fusion.1
  34.5 0.6 gather_fusion.1
  35.2 1.5 %collective-permute-start.4 = (f32[4,4,256]{2,1,0:T(4,128)S(1)}, f32[4,4,256]{2,1,0:T(4,128)S(1)}, u32[]{:S(2)}, u32[]{:S(2)}) collective-permute-start(f32[4,4,256]{2,1,0:T(4,128)S(1)} %get-tuple-element.15), channel_id=1, source_target_pairs={{0,2},{1,3},{2,4},{3,5},{4,6},{5,7},{6,8},{7,9},{8,10},{9,11},{10,... | collective-permute-start | bytes 49160 | tf_op jit(solution)/shard_map/ppermute | solution.py:13
  36.7 0.8 %collective-permute-start.5 = (f32[4,4,256]{2,1,0:T(4,128)S(1)}, f32[4,4,256]{2,1,0:T(4,128)S(1)}, u32[]{:S(2)}, u32[]{:S(2)}) collective-permute-start(f32[4,4,256]{2,1,0:T(4,128)S(1)} %get-tuple-element.15), channel_id=1, source_target_pairs={{0,3},{1,4},{2,5},{3,6},{4,7},{5,8},{6,9},{7,10},{8,11},{9,12},{10... | collective-permute-start | bytes 49160 | tf_op jit(solution)/shard_map/ppermute | solution.py:13
  37.5 2.5 %collective-permute-start.6 = (f32[4,4,256]{2,1,0:T(4,128)S(1)}, f32[4,4,256]{2,1,0:T(4,128)S(1)}, u32[]{:S(2)}, u32[]{:S(2)}) collective-permute-start(f32[4,4,256]{2,1,0:T(4,128)S(1)} %get-tuple-element.15), channel_id=1, source_target_pairs={{0,4},{1,5},{2,6},{3,7},{4,8},{5,9},{6,10},{7,11},{8,12},{9,13},{1... | collective-permute-start | bytes 49160 | tf_op jit(solution)/shard_map/ppermute | solution.py:13
  40.0 1.0 %collective-permute-done.3 = f32[4,4,256]{2,1,0:T(4,128)S(1)} collective-permute-done((f32[4,4,256]{2,1,0:T(4,128)S(1)}, f32[4,4,256]{2,1,0:T(4,128)S(1)}, u32[]{:S(2)}, u32[]{:S(2)}) %collective-permute-start.3) | collective-permute-done | bytes 16416 | tf_op jit(solution)/shard_map/ppermute | solution.py:13
  41.0 1.0 %collective-permute-start.8 = (f32[4,4,256]{2,1,0:T(4,128)S(1)}, f32[4,4,256]{2,1,0:T(4,128)S(1)}, u32[]{:S(2)}, u32[]{:S(2)}) collective-permute-start(f32[4,4,256]{2,1,0:T(4,128)S(1)} %get-tuple-element.15), channel_id=1, source_target_pairs={{0,6},{1,7},{2,8},{3,9},{4,10},{5,11},{6,12},{7,13},{8,14},{9,15},... | collective-permute-start | bytes 49160 | tf_op jit(solution)/shard_map/ppermute | solution.py:13
  42.0 2.5 %collective-permute-start.9 = (f32[4,4,256]{2,1,0:T(4,128)S(1)}, f32[4,4,256]{2,1,0:T(4,128)S(1)}, u32[]{:S(2)}, u32[]{:S(2)}) collective-permute-start(f32[4,4,256]{2,1,0:T(4,128)S(1)} %get-tuple-element.15), channel_id=1, source_target_pairs={{0,7},{1,8},{2,9},{3,10},{4,11},{5,12},{6,13},{7,14},{8,15},{9,0},... | collective-permute-start | bytes 49160 | tf_op jit(solution)/shard_map/ppermute | solution.py:13
  44.6 1.1 %collective-permute-start.10 = (f32[4,4,256]{2,1,0:T(4,128)S(1)}, f32[4,4,256]{2,1,0:T(4,128)S(1)}, u32[]{:S(2)}, u32[]{:S(2)}) collective-permute-start(f32[4,4,256]{2,1,0:T(4,128)S(1)} %get-tuple-element.15), channel_id=1, source_target_pairs={{0,8},{1,9},{2,10},{3,11},{4,12},{5,13},{6,14},{7,15},{8,0},{9,1},... | collective-permute-start | bytes 49160 | tf_op jit(solution)/shard_map/ppermute | solution.py:13
  45.7 0.6 collective-permute-start.11
  46.3 2.0 %collective-permute-start.12 = (f32[4,4,256]{2,1,0:T(4,128)S(1)}, f32[4,4,256]{2,1,0:T(4,128)S(1)}, u32[]{:S(2)}, u32[]{:S(2)}) collective-permute-start(f32[4,4,256]{2,1,0:T(4,128)S(1)} %get-tuple-element.15), channel_id=1, source_target_pairs={{0,10},{1,11},{2,12},{3,13},{4,14},{5,15},{6,0},{7,1},{8,2},{9,3},... | collective-permute-start | bytes 49160 | tf_op jit(solution)/shard_map/ppermute | solution.py:13
  48.3 4.1 %collective-permute-start.13 = (f32[4,4,256]{2,1,0:T(4,128)S(1)}, f32[4,4,256]{2,1,0:T(4,128)S(1)}, u32[]{:S(2)}, u32[]{:S(2)}) collective-permute-start(f32[4,4,256]{2,1,0:T(4,128)S(1)} %get-tuple-element.15), channel_id=1, source_target_pairs={{0,11},{1,12},{2,13},{3,14},{4,15},{5,0},{6,1},{7,2},{8,3},{9,4},{... | collective-permute-start | bytes 49160 | tf_op jit(solution)/shard_map/ppermute | solution.py:13
  52.5 0.6 collective-permute-start.15
  53.1 1.9 %collective-permute-start.16 = (f32[4,4,256]{2,1,0:T(4,128)S(1)}, f32[4,4,256]{2,1,0:T(4,128)S(1)}, u32[]{:S(2)}, u32[]{:S(2)}) collective-permute-start(f32[4,4,256]{2,1,0:T(4,128)S(1)} %get-tuple-element.15), channel_id=1, source_target_pairs={{0,14},{1,15},{2,0},{3,1},{4,2},{5,3},{6,4},{7,5},{8,6},{9,7},{10,... | collective-permute-start | bytes 49160 | tf_op jit(solution)/shard_map/ppermute | solution.py:13
  55.0 2.2 %collective-permute-start.17 = (f32[4,4,256]{2,1,0:T(4,128)S(1)}, f32[4,4,256]{2,1,0:T(4,128)S(1)}, u32[]{:S(2)}, u32[]{:S(2)}) collective-permute-start(f32[4,4,256]{2,1,0:T(4,128)S(1)} %get-tuple-element.15), channel_id=1, source_target_pairs={{0,15},{1,0},{2,1},{3,2},{4,3},{5,4},{6,5},{7,6},{8,7},{9,8},{10,9... | collective-permute-start | bytes 49160 | tf_op jit(solution)/shard_map/ppermute | solution.py:13
  57.3 1.4 %collective-permute-done.17 = f32[4,4,256]{2,1,0:T(4,128)S(1)} collective-permute-done((f32[4,4,256]{2,1,0:T(4,128)S(1)}, f32[4,4,256]{2,1,0:T(4,128)S(1)}, u32[]{:S(2)}, u32[]{:S(2)}) %collective-permute-start.17) | collective-permute-done | bytes 16416 | tf_op jit(solution)/shard_map/ppermute | solution.py:13
  58.7 0.7 %gather_fusion = f32[16,4,4,256]{3,2,1,0:T(4,128)S(1)} fusion(f32[16,4,4,256]{3,2,1,0:T(4,128)S(1)} %constant_dynamic-update-slice_fusion.2, s32[1024]{0:T(1024)S(1)} %pad_clamp_fusion), kind=kCustom, calls=%fused_computation.2 | custom fusion | bytes 524352 | tf_op jit(solution)/shard_map/jit(_take)/gather | solution.py:20
  59.5 0.6 gather_fusion.2
  61.2 0.3 fusion
  61.5 0.7 %fusion.5 = f32[6,512]{1,0:T(8,128)} fusion(f32[6,64,512]{2,1,0:T(8,128)S(1)} %bitcast.95, bf16[6,64,512]{2,1,0:T(8,128)(2,1)S(1)} %copy-done.1), kind=kLoop, calls=%fused_computation.15 | loop fusion | flops 586752 | bytes 1191936 | tf_op jit(solution)/shard_map/reduce_sum | solution.py:92
  62.3 0.6 select_bitcast_fusion
  (110 shorter events, 4.2 us)
Async XLA Ops:
  0.6 1.0 %copy-start.5 = (s32[256,4]{0,1:T(4,128)S(1)}, s32[256,4]{0,1:T(4,128)}, u32[]{:S(2)}) copy-start(s32[256,4]{0,1:T(4,128)} %param.16) | copy-start | bytes 12292
  0.6 8.6 %copy-start.1 = (bf16[6,64,512]{2,1,0:T(8,128)(2,1)S(1)}, bf16[6,64,512]{2,1,0:T(8,128)(2,1)}, u32[]{:S(2)}) copy-start(bf16[6,64,512]{2,1,0:T(8,128)(2,1)} %param.10) | copy-start | bytes 1179652
  1.8 0.7 %copy-start.2 = (bf16[256,24]{0,1:T(8,128)(2,1)S(1)}, bf16[256,24]{0,1:T(8,128)(2,1)}, u32[]{:S(2)}) copy-start(bf16[256,24]{0,1:T(8,128)(2,1)} %param.13) | copy-start | bytes 36868
  2.0 0.7 %copy-start.7 = (s32[256]{0:T(256)S(1)}, s32[256]{0:T(256)}, u32[]{:S(2)}) copy-start(s32[256]{0:T(256)} %param.14) | copy-start | bytes 3076
  2.0 0.7 %copy-start.6 = (s32[256]{0:T(256)S(1)}, s32[256]{0:T(256)}, u32[]{:S(2)}) copy-start(s32[256]{0:T(256)} %param.15) | copy-start | bytes 3076
  3.0 6.1 %copy-start.3 = (bf16[6,512]{1,0:T(8,128)(2,1)S(1)}, bf16[6,512]{1,0:T(8,128)(2,1)}, u32[]{:S(2)}) copy-start(bf16[6,512]{1,0:T(8,128)(2,1)} %param.11) | copy-start | bytes 18436
  3.1 12.2 %collective-permute-start.2 = (bf16[270,512]{1,0:T(8,128)(2,1)S(1)}, bf16[270,512]{1,0:T(8,128)(2,1)S(1)}, u32[]{:S(2)}, u32[]{:S(2)}) collective-permute-start(bf16[270,512]{1,0:T(8,128)(2,1)S(1)} %constant_dynamic-update-slice_fusion), channel_id=1, source_target_pairs={{0,12},{4,0},{8,4},{12,8},{1,13},{5,1},{9,5},{13,9},{2,14},{6,2},{... | collective-permute-start | bytes 829448 | tf_op jit(solution)/shard_map/ppermute | solution.py:13
  8.2 23.7 %collective-permute-start.1 = (bf16[270,512]{1,0:T(8,128)(2,1)S(1)}, bf16[270,512]{1,0:T(8,128)(2,1)S(1)}, u32[]{:S(2)}, u32[]{:S(2)}) collective-permute-start(bf16[270,512]{1,0:T(8,128)(2,1)S(1)} %constant_dynamic-update-slice_fusion), channel_id=1, source_target_pairs={{0,8},{4,12},{8,0},{12,4},{1,9},{5,13},{9,1},{13,5},{2,10},{6,14},... | collective-permute-start | bytes 829448 | tf_op jit(solution)/shard_map/ppermute | solution.py:13
  8.2 24.7 %collective-permute-start = (bf16[270,512]{1,0:T(8,128)(2,1)S(1)}, bf16[270,512]{1,0:T(8,128)(2,1)S(1)}, u32[]{:S(2)}, u32[]{:S(2)}) collective-permute-start(bf16[270,512]{1,0:T(8,128)(2,1)S(1)} %constant_dynamic-update-slice_fusion), channel_id=1, source_target_pairs={{0,4},{4,8},{8,12},{12,0},{1,5},{5,9},{9,13},{13,1},{2,6},{6,10},{... | collective-permute-start | bytes 829448 | tf_op jit(solution)/shard_map/ppermute | solution.py:13
  9.2 1.0 %copy-start = (bf16[256,512]{1,0:T(8,128)(2,1)S(1)}, bf16[256,512]{1,0:T(8,128)(2,1)}, u32[]{:S(2)}) copy-start(bf16[256,512]{1,0:T(8,128)(2,1)} %param.12) | copy-start | bytes 786436
  10.7 0.7 %copy-start.4 = (f32[256,4]{0,1:T(4,128)S(1)}, f32[256,4]{0,1:T(4,128)}, u32[]{:S(2)}) copy-start(f32[256,4]{0,1:T(4,128)} %param.17) | copy-start | bytes 12292
  35.2 5.9 %collective-permute-start.3 = (f32[4,4,256]{2,1,0:T(4,128)S(1)}, f32[4,4,256]{2,1,0:T(4,128)S(1)}, u32[]{:S(2)}, u32[]{:S(2)}) collective-permute-start(f32[4,4,256]{2,1,0:T(4,128)S(1)} %get-tuple-element.15), channel_id=1, source_target_pairs={{0,1},{1,2},{2,3},{3,4},{4,5},{5,6},{6,7},{7,8},{8,9},{9,10},{10,1... | collective-permute-start | bytes 49160 | tf_op jit(solution)/shard_map/ppermute | solution.py:13
  35.2 6.8 %collective-permute-start.4 = (f32[4,4,256]{2,1,0:T(4,128)S(1)}, f32[4,4,256]{2,1,0:T(4,128)S(1)}, u32[]{:S(2)}, u32[]{:S(2)}) collective-permute-start(f32[4,4,256]{2,1,0:T(4,128)S(1)} %get-tuple-element.15), channel_id=1, source_target_pairs={{0,2},{1,3},{2,4},{3,5},{4,6},{5,7},{6,8},{7,9},{8,10},{9,11},{10,... | collective-permute-start | bytes 49160 | tf_op jit(solution)/shard_map/ppermute | solution.py:13
  36.7 7.8 %collective-permute-start.5 = (f32[4,4,256]{2,1,0:T(4,128)S(1)}, f32[4,4,256]{2,1,0:T(4,128)S(1)}, u32[]{:S(2)}, u32[]{:S(2)}) collective-permute-start(f32[4,4,256]{2,1,0:T(4,128)S(1)} %get-tuple-element.15), channel_id=1, source_target_pairs={{0,3},{1,4},{2,5},{3,6},{4,7},{5,8},{6,9},{7,10},{8,11},{9,12},{10... | collective-permute-start | bytes 49160 | tf_op jit(solution)/shard_map/ppermute | solution.py:13
  37.5 8.1 %collective-permute-start.6 = (f32[4,4,256]{2,1,0:T(4,128)S(1)}, f32[4,4,256]{2,1,0:T(4,128)S(1)}, u32[]{:S(2)}, u32[]{:S(2)}) collective-permute-start(f32[4,4,256]{2,1,0:T(4,128)S(1)} %get-tuple-element.15), channel_id=1, source_target_pairs={{0,4},{1,5},{2,6},{3,7},{4,8},{5,9},{6,10},{7,11},{8,12},{9,13},{1... | collective-permute-start | bytes 49160 | tf_op jit(solution)/shard_map/ppermute | solution.py:13
  40.0 6.2 %collective-permute-start.7 = (f32[4,4,256]{2,1,0:T(4,128)S(1)}, f32[4,4,256]{2,1,0:T(4,128)S(1)}, u32[]{:S(2)}, u32[]{:S(2)}) collective-permute-start(f32[4,4,256]{2,1,0:T(4,128)S(1)} %get-tuple-element.15), channel_id=1, source_target_pairs={{0,5},{1,6},{2,7},{3,8},{4,9},{5,10},{6,11},{7,12},{8,13},{9,14},{... | collective-permute-start | bytes 49160 | tf_op jit(solution)/shard_map/ppermute | solution.py:13
  41.0 7.3 %collective-permute-start.8 = (f32[4,4,256]{2,1,0:T(4,128)S(1)}, f32[4,4,256]{2,1,0:T(4,128)S(1)}, u32[]{:S(2)}, u32[]{:S(2)}) collective-permute-start(f32[4,4,256]{2,1,0:T(4,128)S(1)} %get-tuple-element.15), channel_id=1, source_target_pairs={{0,6},{1,7},{2,8},{3,9},{4,10},{5,11},{6,12},{7,13},{8,14},{9,15},... | collective-permute-start | bytes 49160 | tf_op jit(solution)/shard_map/ppermute | solution.py:13
  42.0 10.4 %collective-permute-start.9 = (f32[4,4,256]{2,1,0:T(4,128)S(1)}, f32[4,4,256]{2,1,0:T(4,128)S(1)}, u32[]{:S(2)}, u32[]{:S(2)}) collective-permute-start(f32[4,4,256]{2,1,0:T(4,128)S(1)} %get-tuple-element.15), channel_id=1, source_target_pairs={{0,7},{1,8},{2,9},{3,10},{4,11},{5,12},{6,13},{7,14},{8,15},{9,0},... | collective-permute-start | bytes 49160 | tf_op jit(solution)/shard_map/ppermute | solution.py:13
  44.6 7.9 %collective-permute-start.10 = (f32[4,4,256]{2,1,0:T(4,128)S(1)}, f32[4,4,256]{2,1,0:T(4,128)S(1)}, u32[]{:S(2)}, u32[]{:S(2)}) collective-permute-start(f32[4,4,256]{2,1,0:T(4,128)S(1)} %get-tuple-element.15), channel_id=1, source_target_pairs={{0,8},{1,9},{2,10},{3,11},{4,12},{5,13},{6,14},{7,15},{8,0},{9,1},... | collective-permute-start | bytes 49160 | tf_op jit(solution)/shard_map/ppermute | solution.py:13
  45.7 7.4 %collective-permute-start.11 = (f32[4,4,256]{2,1,0:T(4,128)S(1)}, f32[4,4,256]{2,1,0:T(4,128)S(1)}, u32[]{:S(2)}, u32[]{:S(2)}) collective-permute-start(f32[4,4,256]{2,1,0:T(4,128)S(1)} %get-tuple-element.15), channel_id=1, source_target_pairs={{0,9},{1,10},{2,11},{3,12},{4,13},{5,14},{6,15},{7,0},{8,1},{9,2},... | collective-permute-start | bytes 49160 | tf_op jit(solution)/shard_map/ppermute | solution.py:13
  46.3 8.7 %collective-permute-start.12 = (f32[4,4,256]{2,1,0:T(4,128)S(1)}, f32[4,4,256]{2,1,0:T(4,128)S(1)}, u32[]{:S(2)}, u32[]{:S(2)}) collective-permute-start(f32[4,4,256]{2,1,0:T(4,128)S(1)} %get-tuple-element.15), channel_id=1, source_target_pairs={{0,10},{1,11},{2,12},{3,13},{4,14},{5,15},{6,0},{7,1},{8,2},{9,3},... | collective-permute-start | bytes 49160 | tf_op jit(solution)/shard_map/ppermute | solution.py:13
  48.3 8.9 %collective-permute-start.13 = (f32[4,4,256]{2,1,0:T(4,128)S(1)}, f32[4,4,256]{2,1,0:T(4,128)S(1)}, u32[]{:S(2)}, u32[]{:S(2)}) collective-permute-start(f32[4,4,256]{2,1,0:T(4,128)S(1)} %get-tuple-element.15), channel_id=1, source_target_pairs={{0,11},{1,12},{2,13},{3,14},{4,15},{5,0},{6,1},{7,2},{8,3},{9,4},{... | collective-permute-start | bytes 49160 | tf_op jit(solution)/shard_map/ppermute | solution.py:13
  52.4 4.8 %collective-permute-start.14 = (f32[4,4,256]{2,1,0:T(4,128)S(1)}, f32[4,4,256]{2,1,0:T(4,128)S(1)}, u32[]{:S(2)}, u32[]{:S(2)}) collective-permute-start(f32[4,4,256]{2,1,0:T(4,128)S(1)} %get-tuple-element.15), channel_id=1, source_target_pairs={{0,12},{1,13},{2,14},{3,15},{4,0},{5,1},{6,2},{7,3},{8,4},{9,5},{1... | collective-permute-start | bytes 49160 | tf_op jit(solution)/shard_map/ppermute | solution.py:13
  52.5 4.8 %collective-permute-start.15 = (f32[4,4,256]{2,1,0:T(4,128)S(1)}, f32[4,4,256]{2,1,0:T(4,128)S(1)}, u32[]{:S(2)}, u32[]{:S(2)}) collective-permute-start(f32[4,4,256]{2,1,0:T(4,128)S(1)} %get-tuple-element.15), channel_id=1, source_target_pairs={{0,13},{1,14},{2,15},{3,0},{4,1},{5,2},{6,3},{7,4},{8,5},{9,6},{10... | collective-permute-start | bytes 49160 | tf_op jit(solution)/shard_map/ppermute | solution.py:13
  53.1 4.2 %collective-permute-start.16 = (f32[4,4,256]{2,1,0:T(4,128)S(1)}, f32[4,4,256]{2,1,0:T(4,128)S(1)}, u32[]{:S(2)}, u32[]{:S(2)}) collective-permute-start(f32[4,4,256]{2,1,0:T(4,128)S(1)} %get-tuple-element.15), channel_id=1, source_target_pairs={{0,14},{1,15},{2,0},{3,1},{4,2},{5,3},{6,4},{7,5},{8,6},{9,7},{10,... | collective-permute-start | bytes 49160 | tf_op jit(solution)/shard_map/ppermute | solution.py:13
  55.0 3.7 %collective-permute-start.17 = (f32[4,4,256]{2,1,0:T(4,128)S(1)}, f32[4,4,256]{2,1,0:T(4,128)S(1)}, u32[]{:S(2)}, u32[]{:S(2)}) collective-permute-start(f32[4,4,256]{2,1,0:T(4,128)S(1)} %get-tuple-element.15), channel_id=1, source_target_pairs={{0,15},{1,0},{2,1},{3,2},{4,3},{5,4},{6,5},{7,6},{8,7},{9,8},{10,9... | collective-permute-start | bytes 49160 | tf_op jit(solution)/shard_map/ppermute | solution.py:13

commit v2 on v1

--- a/solution.py
+++ b/solution.py
@@ -19,6 +19,15 @@
     copies = jnp.stack(shifted_copies(x, axes, count))
     copies = jnp.take(copies, (me - lax.iota(jnp.int32, count)) % count, axis=0)
     return jnp.sum(copies, axis=0)
+
+
+def butterfly_sum(x, axes, count):
+    step = 1
+    while step < count:
+        perm = [(i, i ^ step) for i in range(count)]
+        x = x + lax.ppermute(x, axes, perm)
+        step *= 2
+    return x
 
 
 def make_shards(n_paths, n_cols, n_depth):
@@ -71,8 +80,8 @@
         order = (p_idx - lax.iota(jnp.int32, n_paths)) % n_paths
         canon = jnp.take(by_shift, order, axis=0)
 
-        if group <= 16:
-            misfit_all = exchange_sum(canon, GROUP_AXES, group)
+        if group & (group - 1) == 0:
+            misfit_all = butterfly_sum(canon, GROUP_AXES, group)
         else:
             misfit_all = exchange_sum(canon, ("cols", "depth"), n_cols * n_depth)
             misfit_all = exchange_sum(misfit_all, "paths", n_paths)

time: 63.4 us -> 52.2 us (0.82)
  starting transfers between devices: 27 us -> 9.61 us
  waiting for transfers between devices: 22.8 us -> 30.2 us
  local copies, waits for them, and re-layouts: 7.25 us -> 6.45 us
    ppermute x18 -> x3, starting transfers between devices: 27 us -> 6.11 us  [shifted_copies(): copies.append(lax.ppermute(x, axes, perm))]
    ppermute x0 -> x4, waiting for transfers between devices: none -> 9.8 us  [butterfly_sum(): x = x + lax.ppermute(x, axes, perm)]
    ppermute x0 -> x4, starting transfers between devices: none -> 3.5 us  [butterfly_sum(): x = x + lax.ppermute(x, axes, perm)]
    ppermute x18 -> x3, waiting for transfers between devices: 22.8 us -> 20.4 us  [shifted_copies(): copies.append(lax.ppermute(x, axes, perm))]
    gather x1 -> x0, local copies, waits for them, and re-layouts: 0.7 us -> none  [exchange_sum(): copies = jnp.take(copies, (me - lax.iota(jnp.int32, count)) % count, axis=0)]
    unnamed x34 -> x20, local copies, waits for them, and re-layouts: 3.58 us -> 3.49 us
  transfers between devices with their start and end apart: 18 -> 7, of which waited for: 4 -> 6; matrix products, arithmetic and copies ran while one was open for 3% -> 3% of each run, Pallas kernels for 0% -> 0%
where the time goes in v2:
time: 52.2 us; the launch traced here: 51.9 us
  waiting for transfers between devices  30.2 us (58%)
  starting transfers between devices  9.61 us (18%)
  local copies, waits for them, and re-layouts  6.45 us (12%)
  other arithmetic  2.31 us (4%)
  matrix products  2.26 us (4%)
  between operations  1.06 us (2%)
    ppermute x3, waiting for transfers between devices, shifted_copies(): copies.append(lax.ppermute(x, axes, perm))  20.4 us
    ppermute x4, waiting for transfers between devices, butterfly_sum(): x = x + lax.ppermute(x, axes, perm)  9.8 us
    ppermute x3, starting transfers between devices, shifted_copies(): copies.append(lax.ppermute(x, axes, perm))  6.11 us
    ppermute x4, starting transfers between devices, butterfly_sum(): x = x + lax.ppermute(x, axes, perm)  3.5 us
    unnamed x20, local copies, waits for them, and re-layouts  3.49 us
    dot_general x4, matrix products, shards(): lax.dot_general(dw_b, scaled, (((1,), (1,)), ((), ())), preferred_element...  1.2 us
    dot_general x4, matrix products, shards(): lax.dot_general(spread, dw_b, (((0,), (0,)), ((), ())), preferred_element...  1.06 us
  transfers between devices with their start and end apart: 7, of which 6 were waited for; matrix products, arithmetic and copies ran while one was open for 3% of the time, Pallas kernels for 0%

profile of v2, /device:TPU:0, one launch (start us, length us, event | category | flops | bytes accessed | tf_op | source)
XLA Modules:
  0.0 51.9 jit_solution(15459763457381516398)
XLA Ops:
  0.7 1.0 %constant_dynamic-update-slice_fusion.1 = bf16[270,512]{1,0:T(8,128)(2,1)S(1)} fusion(bf16[256,512]{1,0:T(8,128)(2,1)} %param.12), kind=kLoop, calls=%fused_computation.53 | loop fusion | bytes 524288
  1.7 0.1 copy.51
  1.9 0.1 reshape.134
  2.0 0.5 %copy-done.2 = bf16[256,24]{0,1:T(8,128)(2,1)S(1)} copy-done((bf16[256,24]{0,1:T(8,128)(2,1)S(1)}, bf16[256,24]{0,1:T(8,128)(2,1)}, u32[]{:S(2)}) %copy-start.2) | copy-done | bytes 12312
  3.1 5.1 %collective-permute-start.2 = (bf16[270,512]{1,0:T(8,128)(2,1)S(1)}, bf16[270,512]{1,0:T(8,128)(2,1)S(1)}, u32[]{:S(2)}, u32[]{:S(2)}) collective-permute-start(bf16[270,512]{1,0:T(8,128)(2,1)S(1)} %constant_dynamic-update-slice_fusion), channel_id=1, source_target_pairs={{0,12},{4,0},{8,4},{12,8},{1,13},{5,1},{9,5},{13,9},{2,14},{6,2},{... | collective-permute-start | bytes 829448 | tf_op jit(solution)/shard_map/ppermute | solution.py:13
  8.2 1.0 %collective-permute-start = (bf16[270,512]{1,0:T(8,128)(2,1)S(1)}, bf16[270,512]{1,0:T(8,128)(2,1)S(1)}, u32[]{:S(2)}, u32[]{:S(2)}) collective-permute-start(bf16[270,512]{1,0:T(8,128)(2,1)S(1)} %constant_dynamic-update-slice_fusion), channel_id=1, source_target_pairs={{0,4},{4,8},{8,12},{12,0},{1,5},{5,9},{9,13},{13,1},{2,6},{6,10},{... | collective-permute-start | bytes 829448 | tf_op jit(solution)/shard_map/ppermute | solution.py:13
  9.3 0.9 %copy-done = bf16[256,512]{1,0:T(8,128)(2,1)S(1)} copy-done((bf16[256,512]{1,0:T(8,128)(2,1)S(1)}, bf16[256,512]{1,0:T(8,128)(2,1)}, u32[]{:S(2)}) %copy-start) | copy-done | bytes 262168
  10.2 0.3 fusion.18
  10.7 0.7 %copy-done.4 = f32[256,4]{0,1:T(4,128)S(1)} copy-done((f32[256,4]{0,1:T(4,128)S(1)}, f32[256,4]{0,1:T(4,128)}, u32[]{:S(2)}) %copy-start.4) | copy-done | bytes 4120
  11.3 4.0 %collective-permute-done.2 = bf16[270,512]{1,0:T(8,128)(2,1)S(1)} collective-permute-done((bf16[270,512]{1,0:T(8,128)(2,1)S(1)}, bf16[270,512]{1,0:T(8,128)(2,1)S(1)}, u32[]{:S(2)}, u32[]{:S(2)}) %collective-permute-start.2) | collective-permute-done | bytes 276512 | tf_op jit(solution)/shard_map/ppermute | solution.py:13
  15.4 16.5 %collective-permute-done.1 = bf16[270,512]{1,0:T(8,128)(2,1)S(1)} collective-permute-done((bf16[270,512]{1,0:T(8,128)(2,1)S(1)}, bf16[270,512]{1,0:T(8,128)(2,1)S(1)}, u32[]{:S(2)}, u32[]{:S(2)}) %collective-permute-start.1) | collective-permute-done | bytes 276512 | tf_op jit(solution)/shard_map/ppermute | solution.py:13
  32.2 0.2 reshape.164
  32.6 0.1 reshape.163
  32.8 0.1 reshape.136
  33.2 0.1 reshape.162
  33.4 0.3 fusion.3
  33.8 0.3 fusion.2
  34.1 0.3 fusion.1
  34.5 0.6 %gather_fusion = f32[4,4,256]{2,1,0:T(4,128)S(1)} fusion(f32[4,4,256]{2,1,0:T(4,128)S(1)} %pad_maximum_fusion, s32[1024]{0:T(1024)S(1)} %pad_clamp_fusion), kind=kCustom, calls=%fused_computation.clone | custom fusion | bytes 32784 | tf_op jit(solution)/shard_map/jit(_take)/gather | solution.py:81
  35.2 1.2 %collective-permute-done.3 = f32[4,4,256]{2,1,0:T(4,128)S(1)} collective-permute-done((f32[4,4,256]{2,1,0:T(4,128)S(1)}, f32[4,4,256]{2,1,0:T(4,128)S(1)}, u32[]{:S(2)}, u32[]{:S(2)}) %collective-permute-start.3) | collective-permute-done | bytes 16416 | tf_op jit(solution)/shard_map/ppermute | solution.py:28
  36.4 1.5 %collective-permute-start.4 = (f32[4,4,256]{2,1,0:T(4,128)S(1)}, f32[4,4,256]{2,1,0:T(4,128)S(1)}, u32[]{:S(2)}, u32[]{:S(2)}) collective-permute-start(f32[4,4,256]{2,1,0:T(4,128)S(1)} %fusion.30), channel_id=1, source_target_pairs={{0,2},{1,3},{2,0},{3,1},{4,6},{5,7},{6,4},{7,5},{8,10},{9,11},{10,... | collective-permute-start | bytes 49160 | tf_op jit(solution)/shard_map/ppermute | solution.py:28
  37.9 2.3 %collective-permute-done.4 = f32[4,4,256]{2,1,0:T(4,128)S(1)} collective-permute-done((f32[4,4,256]{2,1,0:T(4,128)S(1)}, f32[4,4,256]{2,1,0:T(4,128)S(1)}, u32[]{:S(2)}, u32[]{:S(2)}) %collective-permute-start.4) | collective-permute-done | bytes 16416 | tf_op jit(solution)/shard_map/ppermute | solution.py:28
  40.2 3.7 %collective-permute-done.5 = f32[4,4,256]{2,1,0:T(4,128)S(1)} collective-permute-done((f32[4,4,256]{2,1,0:T(4,128)S(1)}, f32[4,4,256]{2,1,0:T(4,128)S(1)}, u32[]{:S(2)}, u32[]{:S(2)}) %collective-permute-start.5) | collective-permute-done | bytes 16416 | tf_op jit(solution)/shard_map/ppermute | solution.py:28
  43.9 2.0 %collective-permute-start.6 = (f32[4,4,256]{2,1,0:T(4,128)S(1)}, f32[4,4,256]{2,1,0:T(4,128)S(1)}, u32[]{:S(2)}, u32[]{:S(2)}) collective-permute-start(f32[4,4,256]{2,1,0:T(4,128)S(1)} %add.56), channel_id=1, source_target_pairs={{0,8},{1,9},{2,10},{3,11},{4,12},{5,13},{6,14},{7,15},{8,0},{9,1},... | collective-permute-start | bytes 49160 | tf_op jit(solution)/shard_map/ppermute | solution.py:28
  45.9 2.6 %collective-permute-done.6 = f32[4,4,256]{2,1,0:T(4,128)S(1)} collective-permute-done((f32[4,4,256]{2,1,0:T(4,128)S(1)}, f32[4,4,256]{2,1,0:T(4,128)S(1)}, u32[]{:S(2)}, u32[]{:S(2)}) %collective-permute-start.6) | collective-permute-done | bytes 16416 | tf_op jit(solution)/shard_map/ppermute | solution.py:28
  48.6 0.6 %gather_fusion.1 = f32[4,4,256]{2,1,0:T(4,128)S(1)} fusion(f32[4,4,256]{2,1,0:T(4,128)S(1)} %add.57, s32[1024]{0:T(1024)S(1)} %pad_clamp_fusion), kind=kCustom, calls=%fused_computation.1.clone | custom fusion | bytes 32784 | tf_op jit(solution)/shard_map/jit(_take)/gather | solution.py:90
  49.4 0.3 fusion.19
  49.8 0.3 fusion.9
  50.0 0.3 convolution_add_fusion.1
  50.3 0.3 fusion
  50.6 0.7 %fusion.5 = f32[6,512]{1,0:T(8,128)} fusion(f32[6,64,512]{2,1,0:T(8,128)S(1)} %bitcast.61, bf16[6,64,512]{2,1,0:T(8,128)(2,1)S(1)} %copy-done.1), kind=kLoop, calls=%fused_computation.14 | loop fusion | flops 586752 | bytes 1191936 | tf_op jit(solution)/shard_map/reduce_sum | solution.py:101
  51.3 0.6 %select_bitcast_fusion = f32[256,4]{0,1:T(4,128)} fusion(f32[4,4,256]{2,1,0:T(4,128)S(1)} %add.57, s32[]{:T(128)S(6)} %select_n.50, pred[]{:T(512)S(6)} %and.27), kind=kLoop, calls=%fused_computation.54 | loop fusion | flops 1024 | bytes 8197 | tf_op jit(solution)/shard_map/jit(_take)/select_n | solution.py:88
  (72 shorter events, 2.4 us)
Async XLA Ops:
  0.6 1.0 %copy-start.5 = (s32[256,4]{0,1:T(4,128)S(1)}, s32[256,4]{0,1:T(4,128)}, u32[]{:S(2)}) copy-start(s32[256,4]{0,1:T(4,128)} %param.16) | copy-start | bytes 12292
  0.6 8.6 %copy-start.1 = (bf16[6,64,512]{2,1,0:T(8,128)(2,1)S(1)}, bf16[6,64,512]{2,1,0:T(8,128)(2,1)}, u32[]{:S(2)}) copy-start(bf16[6,64,512]{2,1,0:T(8,128)(2,1)} %param.10) | copy-start | bytes 1179652
  1.8 0.7 %copy-start.2 = (bf16[256,24]{0,1:T(8,128)(2,1)S(1)}, bf16[256,24]{0,1:T(8,128)(2,1)}, u32[]{:S(2)}) copy-start(bf16[256,24]{0,1:T(8,128)(2,1)} %param.13) | copy-start | bytes 36868
  2.0 0.7 %copy-start.7 = (s32[256]{0:T(256)S(1)}, s32[256]{0:T(256)}, u32[]{:S(2)}) copy-start(s32[256]{0:T(256)} %param.14) | copy-start | bytes 3076
  2.0 0.7 %copy-start.6 = (s32[256]{0:T(256)S(1)}, s32[256]{0:T(256)}, u32[]{:S(2)}) copy-start(s32[256]{0:T(256)} %param.15) | copy-start | bytes 3076
  3.0 6.1 %copy-start.3 = (bf16[6,512]{1,0:T(8,128)(2,1)S(1)}, bf16[6,512]{1,0:T(8,128)(2,1)}, u32[]{:S(2)}) copy-start(bf16[6,512]{1,0:T(8,128)(2,1)} %param.11) | copy-start | bytes 18436
  3.1 12.2 %collective-permute-start.2 = (bf16[270,512]{1,0:T(8,128)(2,1)S(1)}, bf16[270,512]{1,0:T(8,128)(2,1)S(1)}, u32[]{:S(2)}, u32[]{:S(2)}) collective-permute-start(bf16[270,512]{1,0:T(8,128)(2,1)S(1)} %constant_dynamic-update-slice_fusion), channel_id=1, source_target_pairs={{0,12},{4,0},{8,4},{12,8},{1,13},{5,1},{9,5},{13,9},{2,14},{6,2},{... | collective-permute-start | bytes 829448 | tf_op jit(solution)/shard_map/ppermute | solution.py:13
  8.2 23.7 %collective-permute-start.1 = (bf16[270,512]{1,0:T(8,128)(2,1)S(1)}, bf16[270,512]{1,0:T(8,128)(2,1)S(1)}, u32[]{:S(2)}, u32[]{:S(2)}) collective-permute-start(bf16[270,512]{1,0:T(8,128)(2,1)S(1)} %constant_dynamic-update-slice_fusion), channel_id=1, source_target_pairs={{0,8},{4,12},{8,0},{12,4},{1,9},{5,13},{9,1},{13,5},{2,10},{6,14},... | collective-permute-start | bytes 829448 | tf_op jit(solution)/shard_map/ppermute | solution.py:13
  8.2 24.7 %collective-permute-start = (bf16[270,512]{1,0:T(8,128)(2,1)S(1)}, bf16[270,512]{1,0:T(8,128)(2,1)S(1)}, u32[]{:S(2)}, u32[]{:S(2)}) collective-permute-start(bf16[270,512]{1,0:T(8,128)(2,1)S(1)} %constant_dynamic-update-slice_fusion), channel_id=1, source_target_pairs={{0,4},{4,8},{8,12},{12,0},{1,5},{5,9},{9,13},{13,1},{2,6},{6,10},{... | collective-permute-start | bytes 829448 | tf_op jit(solution)/shard_map/ppermute | solution.py:13
  9.2 1.0 %copy-start = (bf16[256,512]{1,0:T(8,128)(2,1)S(1)}, bf16[256,512]{1,0:T(8,128)(2,1)}, u32[]{:S(2)}) copy-start(bf16[256,512]{1,0:T(8,128)(2,1)} %param.12) | copy-start | bytes 786436
  10.6 0.7 %copy-start.4 = (f32[256,4]{0,1:T(4,128)S(1)}, f32[256,4]{0,1:T(4,128)}, u32[]{:S(2)}) copy-start(f32[256,4]{0,1:T(4,128)} %param.17) | copy-start | bytes 12292
  35.2 1.2 %collective-permute-start.3 = (f32[4,4,256]{2,1,0:T(4,128)S(1)}, f32[4,4,256]{2,1,0:T(4,128)S(1)}, u32[]{:S(2)}, u32[]{:S(2)}) collective-permute-start(f32[4,4,256]{2,1,0:T(4,128)S(1)} %broadcast_select_fusion.1), channel_id=1, source_target_pairs={{0,1},{1,0},{2,3},{3,2},{4,5},{5,4},{6,7},{7,6},{8,9},{9,8},{10,11... | collective-permute-start | bytes 49160 | tf_op jit(solution)/shard_map/ppermute | solution.py:28
  36.4 3.7 %collective-permute-start.4 = (f32[4,4,256]{2,1,0:T(4,128)S(1)}, f32[4,4,256]{2,1,0:T(4,128)S(1)}, u32[]{:S(2)}, u32[]{:S(2)}) collective-permute-start(f32[4,4,256]{2,1,0:T(4,128)S(1)} %fusion.30), channel_id=1, source_target_pairs={{0,2},{1,3},{2,0},{3,1},{4,6},{5,7},{6,4},{7,5},{8,10},{9,11},{10,... | collective-permute-start | bytes 49160 | tf_op jit(solution)/shard_map/ppermute | solution.py:28
  40.2 3.7 %collective-permute-start.5 = (f32[4,4,256]{2,1,0:T(4,128)S(1)}, f32[4,4,256]{2,1,0:T(4,128)S(1)}, u32[]{:S(2)}, u32[]{:S(2)}) collective-permute-start(f32[4,4,256]{2,1,0:T(4,128)S(1)} %add.55), channel_id=1, source_target_pairs={{0,4},{1,5},{2,6},{3,7},{4,0},{5,1},{6,2},{7,3},{8,12},{9,13},{10,... | collective-permute-start | bytes 49160 | tf_op jit(solution)/shard_map/ppermute | solution.py:28
  43.9 4.6 %collective-permute-start.6 = (f32[4,4,256]{2,1,0:T(4,128)S(1)}, f32[4,4,256]{2,1,0:T(4,128)S(1)}, u32[]{:S(2)}, u32[]{:S(2)}) collective-permute-start(f32[4,4,256]{2,1,0:T(4,128)S(1)} %add.56), channel_id=1, source_target_pairs={{0,8},{1,9},{2,10},{3,11},{4,12},{5,13},{6,14},{7,15},{8,0},{9,1},... | collective-permute-start | bytes 49160 | tf_op jit(solution)/shard_map/ppermute | solution.py:28

commit v3 on v2

--- a/solution.py
+++ b/solution.py
@@ -30,8 +30,14 @@
     return x
 
 
+def pack_rows(flat, width):
+    pad = (-flat.shape[0]) % width
+    return jnp.pad(flat, (0, pad)).reshape(-1, width)
+
+
 def make_shards(n_paths, n_cols, n_depth):
     group = n_cols * n_paths * n_depth
+    split = n_cols == 2
 
     def shards(panels, model, depth_weight, seg_len, path_start, path_end, mode_index, observed):
         own_cols, modes, depth_half = panels.shape
@@ -45,32 +51,54 @@
         columns = c_idx * block_cols + lax.iota(jnp.int32, block_cols)
         inside = (columns[None, :] >= path_start[:, None]) & (columns[None, :] < path_end[:, None])
         lengths = jnp.where(inside, seg_len, jnp.zeros_like(seg_len))
-
         n_len = path_rows * block_cols
         n_mi = path_rows * kept
-        small = jnp.concatenate([lengths.reshape(-1), mode_index.astype(bf16).reshape(-1)])
-        pad = (-small.shape[0]) % depth_half
-        small = jnp.pad(small, (0, pad)).reshape(-1, depth_half)
-        payload = jnp.concatenate([depth_weight, small], axis=0)
-        blocks = shifted_copies(payload, "paths", n_paths)
+        small_flat = jnp.concatenate([lengths.reshape(-1), mode_index.astype(bf16).reshape(-1)])
 
         scaled = (panels.astype(f32) * model.astype(f32)[:, None, :]).astype(bf16)
         scaled = scaled.reshape(own_cols * modes, depth_half)
+
+        if split:
+            width = depth_half // 2
+            own_off = c_idx * width
+            other_off = (1 - c_idx) * width
+            offsets = [own_off, other_off]
+            mine = lax.dynamic_slice_in_dim(depth_weight, own_off, width, axis=1)
+            theirs = lax.dynamic_slice_in_dim(depth_weight, other_off, width, axis=1)
+            payload = jnp.concatenate([mine, pack_rows(small_flat, width)], axis=0)
+            z_copies = shifted_copies(payload, "paths", n_paths)
+            blocks = [([mine, theirs], small_flat)]
+            for s in range(1, n_paths):
+                got = z_copies[s]
+                half = got[:path_rows]
+                across = lax.ppermute(half, "cols", [(0, 1), (1, 0)])
+                blocks.append(([half, across], got[path_rows:].reshape(-1)))
+        else:
+            width = depth_half
+            offsets = [0]
+            payload = jnp.concatenate([depth_weight, pack_rows(small_flat, width)], axis=0)
+            blocks = [
+                ([got[:path_rows]], got[path_rows:].reshape(-1))
+                for got in shifted_copies(payload, "paths", n_paths)
+            ]
+        scaled_parts = [lax.dynamic_slice_in_dim(scaled, off, width, axis=1) for off in offsets]
         mode_ids = lax.iota(jnp.int32, modes)
 
         unpacked = []
         parts = []
-        for s, blk in enumerate(blocks):
-            dw_b = blk[:path_rows]
-            sm = blk[path_rows:].reshape(-1)
+        for s, (dw_parts, sm) in enumerate(blocks):
             len_b = sm[:n_len].reshape(path_rows, block_cols)
             mi_b = sm[n_len:n_len + n_mi].reshape(path_rows, kept).astype(jnp.int32)
             len_own = lax.dynamic_slice_in_dim(len_b, p_idx * own_cols, own_cols, axis=1).astype(f32)
             one_hot = (mi_b[:, :, None] == mode_ids[None, None, :]).astype(f32)
-            unpacked.append((dw_b, len_own, one_hot))
-            weighted = lax.dot_general(
-                dw_b, scaled, (((1,), (1,)), ((), ())), preferred_element_type=f32
-            ).reshape(path_rows, own_cols, modes)
+            unpacked.append((dw_parts, len_own, one_hot))
+            weighted = None
+            for dw_part, sc_part in zip(dw_parts, scaled_parts):
+                term = lax.dot_general(
+                    dw_part, sc_part, (((1,), (1,)), ((), ())), preferred_element_type=f32
+                )
+                weighted = term if weighted is None else weighted + term
+            weighted = weighted.reshape(path_rows, own_cols, modes)
             per_mode = jnp.sum(len_own[:, :, None] * weighted, axis=1)
             part = jnp.sum(one_hot * per_mode[:, None, :], axis=2)
             parts.append(part.T)
@@ -88,17 +116,28 @@
         misfit = jnp.take(misfit_all, p_idx, axis=0).T
 
         mis_shift = jnp.take(misfit_all, order, axis=0)
-        summed = None
-        for s, (dw_b, len_own, one_hot) in enumerate(unpacked):
+        summed = [None] * len(offsets)
+        for s, (dw_parts, len_own, one_hot) in enumerate(unpacked):
             resid = jnp.sum(mis_shift[s].T[:, :, None] * one_hot, axis=1)
             spread = (len_own[:, :, None] * resid[:, None, :]).astype(bf16)
             spread = spread.reshape(path_rows, own_cols * modes)
-            term = lax.dot_general(
-                spread, dw_b, (((0,), (0,)), ((), ())), preferred_element_type=f32
+            for j, dw_part in enumerate(dw_parts):
+                term = lax.dot_general(
+                    spread, dw_part, (((0,), (0,)), ((), ())), preferred_element_type=f32
+                )
+                summed[j] = term if summed[j] is None else summed[j] + term
+        grads = []
+        for acc, off in zip(summed, offsets):
+            panel_part = lax.dynamic_slice_in_dim(panels, off, width, axis=2).astype(f32)
+            grads.append(jnp.sum(acc.reshape(own_cols, modes, width) * panel_part, axis=1))
+        if split:
+            gradient = jnp.where(
+                c_idx == 0,
+                jnp.concatenate([grads[0], grads[1]], axis=1),
+                jnp.concatenate([grads[1], grads[0]], axis=1),
             )
-            summed = term if summed is None else summed + term
-        summed = summed.reshape(own_cols, modes, depth_half)
-        gradient = jnp.sum(summed * panels.astype(f32), axis=1)
+        else:
+            gradient = grads[0]
         return (gradient, misfit)
 
     return shards

time: 52.2 us -> 48.2 us (0.923)
  waiting for transfers between devices: 30.2 us -> 22.8 us
  starting transfers between devices: 9.61 us -> 11.2 us
  matrix products: 2.26 us -> 3.76 us
  other arithmetic: 2.31 us -> 3.13 us
  local copies, waits for them, and re-layouts: 6.45 us -> 5.88 us
    ppermute x3, waiting for transfers between devices: 20.4 us -> 7.49 us  [shifted_copies(): copies.append(lax.ppermute(x, axes, perm))]
    ppermute x0 -> x3, starting transfers between devices: none -> 3.71 us  [shards(): across = lax.ppermute(half, 'cols', [(0, 1), (1, 0)])]
    ppermute x0 -> x3, waiting for transfers between devices: none -> 3.35 us  [shards(): across = lax.ppermute(half, 'cols', [(0, 1), (1, 0)])]
    ppermute x4, starting transfers between devices: 3.5 us -> 1.34 us  [butterfly_sum(): x = x + lax.ppermute(x, axes, perm)]
    ppermute x4, waiting for transfers between devices: 9.8 us -> 11.9 us  [butterfly_sum(): x = x + lax.ppermute(x, axes, perm)]
    dot_general x8 -> x16, matrix products: 2.26 us -> 3.76 us  [the longest x8 2.08 us: shards(): lax.dot_general(dw_part, sc_part, (((1,), (1,)), ((), ())), preferred_ele...]
    unnamed x20 -> x17, local copies, waits for them, and re-layouts: 3.49 us -> 2.23 us
    convert_element_type x4, other arithmetic: 0.06 us -> 0.75 us  [shards(): mi_b = sm[n_len:n_len + n_mi].reshape(path_rows, kept).astype(jnp.int32)]
  transfers between devices with their start and end apart: 7 -> 10, of which waited for: 6 -> 8; matrix products, arithmetic and copies ran while one was open for 3% -> 8% of each run, Pallas kernels for 0% -> 0%
where the time goes in v3:
time: 48.2 us; the launch traced here: 47.9 us
  waiting for transfers between devices  22.8 us (47%)
  starting transfers between devices  11.2 us (23%)
  local copies, waits for them, and re-layouts  5.88 us (12%)
  matrix products  3.76 us (8%)
  other arithmetic  3.13 us (6%)
  between operations  1.15 us (2%)
    ppermute x4, waiting for transfers between devices, butterfly_sum(): x = x + lax.ppermute(x, axes, perm)  11.9 us
    ppermute x3, waiting for transfers between devices, shifted_copies(): copies.append(lax.ppermute(x, axes, perm))  7.49 us
    ppermute x3, starting transfers between devices, shifted_copies(): copies.append(lax.ppermute(x, axes, perm))  6.11 us
    ppermute x3, starting transfers between devices, shards(): across = lax.ppermute(half, 'cols', [(0, 1), (1, 0)])  3.71 us
    ppermute x3, waiting for transfers between devices, shards(): across = lax.ppermute(half, 'cols', [(0, 1), (1, 0)])  3.35 us
    unnamed x17, local copies, waits for them, and re-layouts  2.23 us
    dot_general x8, matrix products, shards(): lax.dot_general(dw_part, sc_part, (((1,), (1,)), ((), ())), preferred_ele...  2.08 us
    dot_general x8, matrix products, shards(): lax.dot_general(spread, dw_part, (((0,), (0,)), ((), ())), preferred_elem...  1.68 us
  transfers between devices with their start and end apart: 10, of which 8 were waited for; matrix products, arithmetic and copies ran while one was open for 8% of the time, Pallas kernels for 0%

profile of v3, /device:TPU:0, one launch (start us, length us, event | category | flops | bytes accessed | tf_op | source)
XLA Modules:
  0.0 47.9 jit_solution(9974447815723316118)
XLA Ops:
  0.6 0.7 %fusion.34 = (s32[256,4]{0,1:T(4,128)S(1)}, bf16[256,4]{0,1:T(4,128)(2,1)S(1)}) fusion(s32[256,4]{0,1:T(4,128)} %param.16), kind=kLoop, calls=%fused_computation.95 | loop fusion | flops 2048 | bytes 10240 | tf_op jit(solution)/shard_map/convert_element_type | solution.py:91
  1.7 0.5 %copy-done.2 = bf16[256,24]{0,1:T(8,128)(2,1)S(1)} copy-done((bf16[256,24]{0,1:T(8,128)(2,1)S(1)}, bf16[256,24]{0,1:T(8,128)(2,1)}, u32[]{:S(2)}) %copy-start.2) | copy-done | bytes 12312
  2.8 5.1 %collective-permute-start.4 = (bf16[284,256]{1,0:T(8,128)(2,1)S(1)}, bf16[284,256]{1,0:T(8,128)(2,1)S(1)}, u32[]{:S(2)}, u32[]{:S(2)}) collective-permute-start(bf16[284,256]{1,0:T(8,128)(2,1)S(1)} %pad_maximum_fusion), channel_id=1, source_target_pairs={{0,12},{4,0},{8,4},{12,8},{1,13},{5,1},{9,5},{13,9},{2,14},{6,2},{... | collective-permute-start | bytes 436232 | tf_op jit(solution)/shard_map/ppermute | solution.py:13
  7.9 1.0 %collective-permute-start = (bf16[284,256]{1,0:T(8,128)(2,1)S(1)}, bf16[284,256]{1,0:T(8,128)(2,1)S(1)}, u32[]{:S(2)}, u32[]{:S(2)}) collective-permute-start(bf16[284,256]{1,0:T(8,128)(2,1)S(1)} %pad_maximum_fusion), channel_id=1, source_target_pairs={{0,4},{4,8},{8,12},{12,0},{1,5},{5,9},{9,13},{13,1},{2,6},{6,10},{... | collective-permute-start | bytes 436232 | tf_op jit(solution)/shard_map/ppermute | solution.py:13
  8.9 0.7 %copy-done.3 = bf16[6,512]{1,0:T(8,128)(2,1)S(1)} copy-done((bf16[6,512]{1,0:T(8,128)(2,1)S(1)}, bf16[6,512]{1,0:T(8,128)(2,1)}, u32[]{:S(2)}) %copy-start.3) | copy-done | bytes 6168
  9.7 0.3 fusion.12
  9.9 0.3 convolution_add_fusion.7
  10.5 0.6 %copy-done.4 = f32[256,4]{0,1:T(4,128)S(1)} copy-done((f32[256,4]{0,1:T(4,128)S(1)}, f32[256,4]{0,1:T(4,128)}, u32[]{:S(2)}) %copy-start.4) | copy-done | bytes 4120
  11.2 1.0 %collective-permute-done.4 = bf16[284,256]{1,0:T(8,128)(2,1)S(1)} collective-permute-done((bf16[284,256]{1,0:T(8,128)(2,1)S(1)}, bf16[284,256]{1,0:T(8,128)(2,1)S(1)}, u32[]{:S(2)}, u32[]{:S(2)}) %collective-permute-start.4) | collective-permute-done | bytes 145440 | tf_op jit(solution)/shard_map/ppermute | solution.py:13
  12.2 1.6 %collective-permute-start.5 = (bf16[256,256]{1,0:T(8,128)(2,1)S(1)}, bf16[256,256]{1,0:T(8,128)(2,1)S(1)}, u32[]{:S(2)}, u32[]{:S(2)}) collective-permute-start(bf16[256,256]{1,0:T(8,128)(2,1)S(1)} %slice.88), channel_id=1, source_target_pairs={{0,2},{2,0},{1,3},{3,1},{4,6},{6,4},{5,7},{7,5},{8,10},{10,8},{9,1... | collective-permute-start | bytes 393224 | tf_op jit(solution)/shard_map/ppermute | solution.py:74
  13.9 6.5 %collective-permute-done.2 = bf16[284,256]{1,0:T(8,128)(2,1)S(1)} collective-permute-done((bf16[284,256]{1,0:T(8,128)(2,1)S(1)}, bf16[284,256]{1,0:T(8,128)(2,1)S(1)}, u32[]{:S(2)}, u32[]{:S(2)}) %collective-permute-start.2) | collective-permute-done | bytes 145440 | tf_op jit(solution)/shard_map/ppermute | solution.py:13
  21.0 1.6 %collective-permute-start.3 = (bf16[256,256]{1,0:T(8,128)(2,1)S(1)}, bf16[256,256]{1,0:T(8,128)(2,1)S(1)}, u32[]{:S(2)}, u32[]{:S(2)}) collective-permute-start(bf16[256,256]{1,0:T(8,128)(2,1)S(1)} %slice.85), channel_id=1, source_target_pairs={{0,2},{2,0},{1,3},{3,1},{4,6},{6,4},{5,7},{7,5},{8,10},{10,8},{9,1... | collective-permute-start | bytes 393224 | tf_op jit(solution)/shard_map/ppermute | solution.py:74
  22.9 0.6 %collective-permute-start.1 = (bf16[256,256]{1,0:T(8,128)(2,1)S(1)}, bf16[256,256]{1,0:T(8,128)(2,1)S(1)}, u32[]{:S(2)}, u32[]{:S(2)}) collective-permute-start(bf16[256,256]{1,0:T(8,128)(2,1)S(1)} %slice.82), channel_id=1, source_target_pairs={{0,2},{2,0},{1,3},{3,1},{4,6},{6,4},{5,7},{7,5},{8,10},{10,8},{9,1... | collective-permute-start | bytes 393224 | tf_op jit(solution)/shard_map/ppermute | solution.py:74
  24.1 0.3 fusion.2
  24.3 0.3 convolution_add_fusion.4
  24.8 2.6 %collective-permute-done.3 = bf16[256,256]{1,0:T(8,128)(2,1)S(1)} collective-permute-done((bf16[256,256]{1,0:T(8,128)(2,1)S(1)}, bf16[256,256]{1,0:T(8,128)(2,1)S(1)}, u32[]{:S(2)}, u32[]{:S(2)}) %collective-permute-start.3) | collective-permute-done | bytes 131104 | tf_op jit(solution)/shard_map/ppermute | solution.py:74
  27.3 0.3 fusion.4
  27.6 0.3 convolution_add_fusion.5
  28.0 0.8 %collective-permute-done.1 = bf16[256,256]{1,0:T(8,128)(2,1)S(1)} collective-permute-done((bf16[256,256]{1,0:T(8,128)(2,1)S(1)}, bf16[256,256]{1,0:T(8,128)(2,1)S(1)}, u32[]{:S(2)}, u32[]{:S(2)}) %collective-permute-start.1) | collective-permute-done | bytes 131104 | tf_op jit(solution)/shard_map/ppermute | solution.py:74
  28.8 0.3 fusion.6
  29.1 0.3 convolution_add_fusion.6
  29.8 0.6 %gather_fusion = f32[4,4,256]{2,1,0:T(4,128)S(1)} fusion(f32[4,4,256]{2,1,0:T(4,128)S(1)} %pad_maximum_fusion.1, s32[1024]{0:T(1024)S(1)} %pad_clamp_fusion), kind=kCustom, calls=%fused_computation.clone | custom fusion | bytes 32784 | tf_op jit(solution)/shard_map/jit(_take)/gather | solution.py:109
  30.5 1.2 %collective-permute-done.6 = f32[4,4,256]{2,1,0:T(4,128)S(1)} collective-permute-done((f32[4,4,256]{2,1,0:T(4,128)S(1)}, f32[4,4,256]{2,1,0:T(4,128)S(1)}, u32[]{:S(2)}, u32[]{:S(2)}) %collective-permute-start.6) | collective-permute-done | bytes 16416 | tf_op jit(solution)/shard_map/ppermute | solution.py:28
  31.7 1.3 %collective-permute-start.7 = (f32[4,4,256]{2,1,0:T(4,128)S(1)}, f32[4,4,256]{2,1,0:T(4,128)S(1)}, u32[]{:S(2)}, u32[]{:S(2)}) collective-permute-start(f32[4,4,256]{2,1,0:T(4,128)S(1)} %fusion.53), channel_id=1, source_target_pairs={{0,2},{1,3},{2,0},{3,1},{4,6},{5,7},{6,4},{7,5},{8,10},{9,11},{10,... | collective-permute-start | bytes 49160 | tf_op jit(solution)/shard_map/ppermute | solution.py:28
  33.0 2.4 %collective-permute-done.7 = f32[4,4,256]{2,1,0:T(4,128)S(1)} collective-permute-done((f32[4,4,256]{2,1,0:T(4,128)S(1)}, f32[4,4,256]{2,1,0:T(4,128)S(1)}, u32[]{:S(2)}, u32[]{:S(2)}) %collective-permute-start.7) | collective-permute-done | bytes 16416 | tf_op jit(solution)/shard_map/ppermute | solution.py:28
  35.5 3.7 %collective-permute-done.8 = f32[4,4,256]{2,1,0:T(4,128)S(1)} collective-permute-done((f32[4,4,256]{2,1,0:T(4,128)S(1)}, f32[4,4,256]{2,1,0:T(4,128)S(1)}, u32[]{:S(2)}, u32[]{:S(2)}) %collective-permute-start.8) | collective-permute-done | bytes 16416 | tf_op jit(solution)/shard_map/ppermute | solution.py:28
  39.2 4.6 %collective-permute-done.9 = f32[4,4,256]{2,1,0:T(4,128)S(1)} collective-permute-done((f32[4,4,256]{2,1,0:T(4,128)S(1)}, f32[4,4,256]{2,1,0:T(4,128)S(1)}, u32[]{:S(2)}, u32[]{:S(2)}) %collective-permute-start.9) | collective-permute-done | bytes 16416 | tf_op jit(solution)/shard_map/ppermute | solution.py:28
  43.9 0.6 %gather_fusion.1 = f32[4,4,256]{2,1,0:T(4,128)S(1)} fusion(f32[4,4,256]{2,1,0:T(4,128)S(1)} %add.94, s32[1024]{0:T(1024)S(1)} %pad_clamp_fusion), kind=kCustom, calls=%fused_computation.1.clone | custom fusion | bytes 32784 | tf_op jit(solution)/shard_map/jit(_take)/gather | solution.py:118
  45.2 0.6 %select_bitcast_fusion = f32[256,4]{0,1:T(4,128)} fusion(f32[4,4,256]{2,1,0:T(4,128)S(1)} %add.94, s32[]{:T(128)S(6)} %select_n.72, pred[]{:T(512)S(6)} %and.27), kind=kLoop, calls=%fused_computation.62 | loop fusion | flops 1024 | bytes 8197 | tf_op jit(solution)/shard_map/jit(_take)/select_n | solution.py:116
  46.7 0.2 fusion
  46.9 0.2 fusion.1
  47.3 0.6 %maximum_select_fusion = f32[6,512]{1,0:T(8,128)} fusion(f32[6,256]{1,0:T(8,128)S(1)} %get-tuple-element.15, f32[6,256]{1,0:T(8,128)S(1)} %get-tuple-element.14, pred[]{:T(512)S(6)} %eq.29), kind=kLoop, calls=%fused_computation.53 | loop fusion | flops 9216 | bytes 24577 | tf_op jit(solution)/shard_map/jit(_where)/select_n | solution.py:134
  (95 shorter events, 5.3 us)
Async XLA Ops:
  0.6 2.1 %copy-start = (bf16[256,512]{1,0:T(8,128)(2,1)S(1)}, bf16[256,512]{1,0:T(8,128)(2,1)}, u32[]{:S(2)}) copy-start(bf16[256,512]{1,0:T(8,128)(2,1)} %param.12) | copy-start | bytes 786436
  1.5 0.7 %copy-start.2 = (bf16[256,24]{0,1:T(8,128)(2,1)S(1)}, bf16[256,24]{0,1:T(8,128)(2,1)}, u32[]{:S(2)}) copy-start(bf16[256,24]{0,1:T(8,128)(2,1)} %param.13) | copy-start | bytes 36868
  1.7 0.7 %copy-start.6 = (s32[256]{0:T(256)S(1)}, s32[256]{0:T(256)}, u32[]{:S(2)}) copy-start(s32[256]{0:T(256)} %param.14) | copy-start | bytes 3076
  1.7 0.7 %copy-start.5 = (s32[256]{0:T(256)S(1)}, s32[256]{0:T(256)}, u32[]{:S(2)}) copy-start(s32[256]{0:T(256)} %param.15) | copy-start | bytes 3076
  2.6 7.0 %copy-start.1 = (bf16[6,64,512]{2,1,0:T(8,128)(2,1)S(1)}, bf16[6,64,512]{2,1,0:T(8,128)(2,1)}, u32[]{:S(2)}) copy-start(bf16[6,64,512]{2,1,0:T(8,128)(2,1)} %param.10) | copy-start | bytes 1179652
  2.8 9.4 %collective-permute-start.4 = (bf16[284,256]{1,0:T(8,128)(2,1)S(1)}, bf16[284,256]{1,0:T(8,128)(2,1)S(1)}, u32[]{:S(2)}, u32[]{:S(2)}) collective-permute-start(bf16[284,256]{1,0:T(8,128)(2,1)S(1)} %pad_maximum_fusion), channel_id=1, source_target_pairs={{0,12},{4,0},{8,4},{12,8},{1,13},{5,1},{9,5},{13,9},{2,14},{6,2},{... | collective-permute-start | bytes 436232 | tf_op jit(solution)/shard_map/ppermute | solution.py:13
  7.9 12.5 %collective-permute-start.2 = (bf16[284,256]{1,0:T(8,128)(2,1)S(1)}, bf16[284,256]{1,0:T(8,128)(2,1)S(1)}, u32[]{:S(2)}, u32[]{:S(2)}) collective-permute-start(bf16[284,256]{1,0:T(8,128)(2,1)S(1)} %pad_maximum_fusion), channel_id=1, source_target_pairs={{0,8},{4,12},{8,0},{12,4},{1,9},{5,13},{9,1},{13,5},{2,10},{6,14},... | collective-permute-start | bytes 436232 | tf_op jit(solution)/shard_map/ppermute | solution.py:13
  7.9 15.0 %collective-permute-start = (bf16[284,256]{1,0:T(8,128)(2,1)S(1)}, bf16[284,256]{1,0:T(8,128)(2,1)S(1)}, u32[]{:S(2)}, u32[]{:S(2)}) collective-permute-start(bf16[284,256]{1,0:T(8,128)(2,1)S(1)} %pad_maximum_fusion), channel_id=1, source_target_pairs={{0,4},{4,8},{8,12},{12,0},{1,5},{5,9},{9,13},{13,1},{2,6},{6,10},{... | collective-permute-start | bytes 436232 | tf_op jit(solution)/shard_map/ppermute | solution.py:13
  8.9 0.7 %copy-start.3 = (bf16[6,512]{1,0:T(8,128)(2,1)S(1)}, bf16[6,512]{1,0:T(8,128)(2,1)}, u32[]{:S(2)}) copy-start(bf16[6,512]{1,0:T(8,128)(2,1)} %param.11) | copy-start | bytes 18436
  10.5 0.7 %copy-start.4 = (f32[256,4]{0,1:T(4,128)S(1)}, f32[256,4]{0,1:T(4,128)}, u32[]{:S(2)}) copy-start(f32[256,4]{0,1:T(4,128)} %param.17) | copy-start | bytes 12292
  12.2 11.9 %collective-permute-start.5 = (bf16[256,256]{1,0:T(8,128)(2,1)S(1)}, bf16[256,256]{1,0:T(8,128)(2,1)S(1)}, u32[]{:S(2)}, u32[]{:S(2)}) collective-permute-start(bf16[256,256]{1,0:T(8,128)(2,1)S(1)} %slice.88), channel_id=1, source_target_pairs={{0,2},{2,0},{1,3},{3,1},{4,6},{6,4},{5,7},{7,5},{8,10},{10,8},{9,1... | collective-permute-start | bytes 393224 | tf_op jit(solution)/shard_map/ppermute | solution.py:74
  21.0 6.4 %collective-permute-start.3 = (bf16[256,256]{1,0:T(8,128)(2,1)S(1)}, bf16[256,256]{1,0:T(8,128)(2,1)S(1)}, u32[]{:S(2)}, u32[]{:S(2)}) collective-permute-start(bf16[256,256]{1,0:T(8,128)(2,1)S(1)} %slice.85), channel_id=1, source_target_pairs={{0,2},{2,0},{1,3},{3,1},{4,6},{6,4},{5,7},{7,5},{8,10},{10,8},{9,1... | collective-permute-start | bytes 393224 | tf_op jit(solution)/shard_map/ppermute | solution.py:74
  22.9 5.9 %collective-permute-start.1 = (bf16[256,256]{1,0:T(8,128)(2,1)S(1)}, bf16[256,256]{1,0:T(8,128)(2,1)S(1)}, u32[]{:S(2)}, u32[]{:S(2)}) collective-permute-start(bf16[256,256]{1,0:T(8,128)(2,1)S(1)} %slice.82), channel_id=1, source_target_pairs={{0,2},{2,0},{1,3},{3,1},{4,6},{6,4},{5,7},{7,5},{8,10},{10,8},{9,1... | collective-permute-start | bytes 393224 | tf_op jit(solution)/shard_map/ppermute | solution.py:74
  30.4 1.2 %collective-permute-start.6 = (f32[4,4,256]{2,1,0:T(4,128)S(1)}, f32[4,4,256]{2,1,0:T(4,128)S(1)}, u32[]{:S(2)}, u32[]{:S(2)}) collective-permute-start(f32[4,4,256]{2,1,0:T(4,128)S(1)} %broadcast_select_fusion.1), channel_id=1, source_target_pairs={{0,1},{1,0},{2,3},{3,2},{4,5},{5,4},{6,7},{7,6},{8,9},{9,8},{10,11... | collective-permute-start | bytes 49160 | tf_op jit(solution)/shard_map/ppermute | solution.py:28
  31.7 3.7 %collective-permute-start.7 = (f32[4,4,256]{2,1,0:T(4,128)S(1)}, f32[4,4,256]{2,1,0:T(4,128)S(1)}, u32[]{:S(2)}, u32[]{:S(2)}) collective-permute-start(f32[4,4,256]{2,1,0:T(4,128)S(1)} %fusion.53), channel_id=1, source_target_pairs={{0,2},{1,3},{2,0},{3,1},{4,6},{5,7},{6,4},{7,5},{8,10},{9,11},{10,... | collective-permute-start | bytes 49160 | tf_op jit(solution)/shard_map/ppermute | solution.py:28
  35.5 3.7 %collective-permute-start.8 = (f32[4,4,256]{2,1,0:T(4,128)S(1)}, f32[4,4,256]{2,1,0:T(4,128)S(1)}, u32[]{:S(2)}, u32[]{:S(2)}) collective-permute-start(f32[4,4,256]{2,1,0:T(4,128)S(1)} %add.92), channel_id=1, source_target_pairs={{0,4},{1,5},{2,6},{3,7},{4,0},{5,1},{6,2},{7,3},{8,12},{9,13},{10,... | collective-permute-start | bytes 49160 | tf_op jit(solution)/shard_map/ppermute | solution.py:28
  39.2 4.6 %collective-permute-start.9 = (f32[4,4,256]{2,1,0:T(4,128)S(1)}, f32[4,4,256]{2,1,0:T(4,128)S(1)}, u32[]{:S(2)}, u32[]{:S(2)}) collective-permute-start(f32[4,4,256]{2,1,0:T(4,128)S(1)} %add.93), channel_id=1, source_target_pairs={{0,8},{1,9},{2,10},{3,11},{4,12},{5,13},{6,14},{7,15},{8,0},{9,1},... | collective-permute-start | bytes 49160 | tf_op jit(solution)/shard_map/ppermute | solution.py:28

commit v4 on v3

--- a/solution.py
+++ b/solution.py
@@ -2,9 +2,6 @@
 import jax.numpy as jnp
 from jax import lax
 from jax.sharding import PartitionSpec as P
-
-GROUP_AXES = ("paths", "cols", "depth")
-
 
 def shifted_copies(x, axes, count):
     copies = [x]
@@ -14,11 +11,16 @@
     return copies
 
 
+def place_by_source(copies, me, count):
+    stacked = jnp.zeros((count,) + copies[0].shape, copies[0].dtype)
+    for shift, piece in enumerate(copies):
+        stacked = lax.dynamic_update_index_in_dim(stacked, piece, (me - shift) % count, 0)
+    return stacked
+
+
 def exchange_sum(x, axes, count):
     me = lax.axis_index(axes)
-    copies = jnp.stack(shifted_copies(x, axes, count))
-    copies = jnp.take(copies, (me - lax.iota(jnp.int32, count)) % count, axis=0)
-    return jnp.sum(copies, axis=0)
+    return jnp.sum(place_by_source(shifted_copies(x, axes, count), me, count), axis=0)
 
 
 def butterfly_sum(x, axes, count):
@@ -36,7 +38,6 @@
 
 
 def make_shards(n_paths, n_cols, n_depth):
-    group = n_cols * n_paths * n_depth
     split = n_cols == 2
 
     def shards(panels, model, depth_weight, seg_len, path_start, path_end, mode_index, observed):
@@ -104,18 +105,19 @@
             parts.append(part.T)
         first = (c_idx == 0) & (d_idx == 0)
         parts[0] = parts[0] - jnp.where(first, observed.T, jnp.zeros_like(observed.T))
-        by_shift = jnp.stack(parts)
-        order = (p_idx - lax.iota(jnp.int32, n_paths)) % n_paths
-        canon = jnp.take(by_shift, order, axis=0)
+        canon = place_by_source(parts, p_idx, n_paths)
 
-        if group & (group - 1) == 0:
-            misfit_all = butterfly_sum(canon, GROUP_AXES, group)
+        local = n_cols * n_depth
+        if local & (local - 1) == 0:
+            misfit_all = butterfly_sum(canon, ("cols", "depth"), local)
         else:
-            misfit_all = exchange_sum(canon, ("cols", "depth"), n_cols * n_depth)
-            misfit_all = exchange_sum(misfit_all, "paths", n_paths)
-        misfit = jnp.take(misfit_all, p_idx, axis=0).T
-
-        mis_shift = jnp.take(misfit_all, order, axis=0)
+            misfit_all = exchange_sum(canon, ("cols", "depth"), local)
+        misfit_all = exchange_sum(misfit_all, "paths", n_paths)
+        misfit = lax.dynamic_index_in_dim(misfit_all, p_idx, 0, keepdims=False).T
+        mis_shift = [
+            lax.dynamic_index_in_dim(misfit_all, (p_idx - s) % n_paths, 0, keepdims=False)
+            for s in range(n_paths)
+        ]
         summed = [None] * len(offsets)
         for s, (dw_parts, len_own, one_hot) in enumerate(unpacked):
             resid = jnp.sum(mis_shift[s].T[:, :, None] * one_hot, axis=1)

time: 48.2 us -> 44.8 us (0.929)
  waiting for transfers between devices: 22.8 us -> 13.5 us
  starting transfers between devices: 11.2 us -> 18.3 us
  other arithmetic: 3.13 us -> 1.57 us
    ppermute x4 -> x2, waiting for transfers between devices: 11.9 us -> 3.42 us  [butterfly_sum(): x = x + lax.ppermute(x, axes, perm)]
    ppermute x3 -> x6, starting transfers between devices: 6.11 us -> 12.8 us  [shifted_copies(): copies.append(lax.ppermute(x, axes, perm))]
    gather x2 -> x0, local copies, waits for them, and re-layouts: 1.14 us -> none  [the longest x1 0.57 us: shards(): canon = jnp.take(by_shift, order, axis=0)]
    ppermute x3 -> x6, waiting for transfers between devices: 7.49 us -> 6.49 us  [shifted_copies(): copies.append(lax.ppermute(x, axes, perm))]
    select_n x4 -> x0, other arithmetic: 0.76 us -> none  [the longest x1 0.6 us: shards(): misfit = jnp.take(misfit_all, p_idx, axis=0).T]
    convert_element_type x4, other arithmetic: 0.75 us -> 0.02 us  [shards(): mi_b = sm[n_len:n_len + n_mi].reshape(path_rows, kept).astype(jnp.int32)]
    unnamed x17 -> x19, local copies, waits for them, and re-layouts: 2.23 us -> 2.89 us
    transpose x1, local copies, waits for them, and re-layouts: 0.01 us -> 0.61 us  [shards(): misfit = lax.dynamic_index_in_dim(misfit_all, p_idx, 0, keepdims=False).T]
  transfers between devices with their start and end apart: 10 -> 11, of which waited for: 8 -> 9; matrix products, arithmetic and copies ran while one was open for 8% -> 9% of each run, Pallas kernels for 0% -> 0%
where the time goes in v4:
time: 44.8 us; the launch traced here: 44.4 us
  starting transfers between devices  18.3 us (41%)
  waiting for transfers between devices  13.5 us (30%)
  local copies, waits for them, and re-layouts  6.07 us (14%)
  matrix products  3.79 us (8%)
  other arithmetic  1.57 us (4%)
  between operations  1.17 us (3%)
    ppermute x6, starting transfers between devices, shifted_copies(): copies.append(lax.ppermute(x, axes, perm))  12.8 us
    ppermute x6, waiting for transfers between devices, shifted_copies(): copies.append(lax.ppermute(x, axes, perm))  6.49 us
    ppermute x3, starting transfers between devices, shards(): across = lax.ppermute(half, 'cols', [(0, 1), (1, 0)])  3.96 us
    ppermute x3, waiting for transfers between devices, shards(): across = lax.ppermute(half, 'cols', [(0, 1), (1, 0)])  3.55 us
    ppermute x2, waiting for transfers between devices, butterfly_sum(): x = x + lax.ppermute(x, axes, perm)  3.42 us
    unnamed x19, local copies, waits for them, and re-layouts  2.89 us
    dot_general x8, matrix products, shards(): lax.dot_general(dw_part, sc_part, (((1,), (1,)), ((), ())), preferred_ele...  2.09 us
    dot_general x8, matrix products, shards(): lax.dot_general(spread, dw_part, (((0,), (0,)), ((), ())), preferred_elem...  1.7 us
  transfers between devices with their start and end apart: 11, of which 9 were waited for; matrix products, arithmetic and copies ran while one was open for 9% of the time, Pallas kernels for 0%

profile of v4, /device:TPU:0, one launch (start us, length us, event | category | flops | bytes accessed | tf_op | source)
XLA Modules:
  0.0 44.4 jit_solution(14998919283847217466)
XLA Ops:
  0.7 0.7 %copy-done.4 = s32[256,4]{0,1:T(4,128)S(1)} copy-done((s32[256,4]{0,1:T(4,128)S(1)}, s32[256,4]{0,1:T(4,128)}, u32[]{:S(2)}) %copy-start.4) | copy-done | bytes 4120
  1.7 0.5 %copy-done.2 = bf16[256,24]{0,1:T(8,128)(2,1)S(1)} copy-done((bf16[256,24]{0,1:T(8,128)(2,1)S(1)}, bf16[256,24]{0,1:T(8,128)(2,1)}, u32[]{:S(2)}) %copy-start.2) | copy-done | bytes 12312
  2.7 3.1 %collective-permute-start = (bf16[284,256]{1,0:T(8,128)(2,1)S(1)}, bf16[284,256]{1,0:T(8,128)(2,1)S(1)}, u32[]{:S(2)}, u32[]{:S(2)}) collective-permute-start(bf16[284,256]{1,0:T(8,128)(2,1)S(1)} %pad_maximum_fusion), channel_id=1, source_target_pairs={{0,4},{4,8},{8,12},{12,0},{1,5},{5,9},{9,13},{13,1},{2,6},{6,10},{... | collective-permute-start | bytes 436232 | tf_op jit(solution)/shard_map/ppermute | solution.py:10
  5.8 2.6 %collective-permute-start.2 = (bf16[284,256]{1,0:T(8,128)(2,1)S(1)}, bf16[284,256]{1,0:T(8,128)(2,1)S(1)}, u32[]{:S(2)}, u32[]{:S(2)}) collective-permute-start(bf16[284,256]{1,0:T(8,128)(2,1)S(1)} %pad_maximum_fusion), channel_id=1, source_target_pairs={{0,8},{4,12},{8,0},{12,4},{1,9},{5,13},{9,1},{13,5},{2,10},{6,14},... | collective-permute-start | bytes 436232 | tf_op jit(solution)/shard_map/ppermute | solution.py:10
  8.3 1.3 %collective-permute-start.4 = (bf16[284,256]{1,0:T(8,128)(2,1)S(1)}, bf16[284,256]{1,0:T(8,128)(2,1)S(1)}, u32[]{:S(2)}, u32[]{:S(2)}) collective-permute-start(bf16[284,256]{1,0:T(8,128)(2,1)S(1)} %pad_maximum_fusion), channel_id=1, source_target_pairs={{0,12},{4,0},{8,4},{12,8},{1,13},{5,1},{9,5},{13,9},{2,14},{6,2},{... | collective-permute-start | bytes 436232 | tf_op jit(solution)/shard_map/ppermute | solution.py:10
  9.7 0.7 %copy-done.3 = bf16[6,512]{1,0:T(8,128)(2,1)S(1)} copy-done((bf16[6,512]{1,0:T(8,128)(2,1)S(1)}, bf16[6,512]{1,0:T(8,128)(2,1)}, u32[]{:S(2)}) %copy-start.3) | copy-done | bytes 6168
  10.5 0.3 fusion.12
  10.7 0.3 convolution_add_fusion.7
  11.4 0.7 %copy-done.5 = f32[256,4]{0,1:T(4,128)S(1)} copy-done((f32[256,4]{0,1:T(4,128)S(1)}, f32[256,4]{0,1:T(4,128)}, u32[]{:S(2)}) %copy-start.5) | copy-done | bytes 4120
  12.0 0.5 %collective-permute-done = bf16[284,256]{1,0:T(8,128)(2,1)S(1)} collective-permute-done((bf16[284,256]{1,0:T(8,128)(2,1)S(1)}, bf16[284,256]{1,0:T(8,128)(2,1)S(1)}, u32[]{:S(2)}, u32[]{:S(2)}) %collective-permute-start) | collective-permute-done | bytes 145440 | tf_op jit(solution)/shard_map/ppermute | solution.py:10
  12.6 1.8 %collective-permute-start.1 = (bf16[256,256]{1,0:T(8,128)(2,1)S(1)}, bf16[256,256]{1,0:T(8,128)(2,1)S(1)}, u32[]{:S(2)}, u32[]{:S(2)}) collective-permute-start(bf16[256,256]{1,0:T(8,128)(2,1)S(1)} %slice.53), channel_id=1, source_target_pairs={{0,2},{2,0},{1,3},{3,1},{4,6},{6,4},{5,7},{7,5},{8,10},{10,8},{9,1... | collective-permute-start | bytes 393224 | tf_op jit(solution)/shard_map/ppermute | solution.py:75
  14.9 3.1 %collective-permute-done.2 = bf16[284,256]{1,0:T(8,128)(2,1)S(1)} collective-permute-done((bf16[284,256]{1,0:T(8,128)(2,1)S(1)}, bf16[284,256]{1,0:T(8,128)(2,1)S(1)}, u32[]{:S(2)}, u32[]{:S(2)}) %collective-permute-start.2) | collective-permute-done | bytes 145440 | tf_op jit(solution)/shard_map/ppermute | solution.py:10
  18.1 1.6 %collective-permute-start.3 = (bf16[256,256]{1,0:T(8,128)(2,1)S(1)}, bf16[256,256]{1,0:T(8,128)(2,1)S(1)}, u32[]{:S(2)}, u32[]{:S(2)}) collective-permute-start(bf16[256,256]{1,0:T(8,128)(2,1)S(1)} %slice.56), channel_id=1, source_target_pairs={{0,2},{2,0},{1,3},{3,1},{4,6},{6,4},{5,7},{7,5},{8,10},{10,8},{9,1... | collective-permute-start | bytes 393224 | tf_op jit(solution)/shard_map/ppermute | solution.py:75
  20.4 0.6 %collective-permute-start.5 = (bf16[256,256]{1,0:T(8,128)(2,1)S(1)}, bf16[256,256]{1,0:T(8,128)(2,1)S(1)}, u32[]{:S(2)}, u32[]{:S(2)}) collective-permute-start(bf16[256,256]{1,0:T(8,128)(2,1)S(1)} %slice.59), channel_id=1, source_target_pairs={{0,2},{2,0},{1,3},{3,1},{4,6},{6,4},{5,7},{7,5},{8,10},{10,8},{9,1... | collective-permute-start | bytes 393224 | tf_op jit(solution)/shard_map/ppermute | solution.py:75
  21.3 0.3 fusion.6
  21.6 0.3 convolution_add_fusion.6
  22.0 2.2 %collective-permute-done.3 = bf16[256,256]{1,0:T(8,128)(2,1)S(1)} collective-permute-done((bf16[256,256]{1,0:T(8,128)(2,1)S(1)}, bf16[256,256]{1,0:T(8,128)(2,1)S(1)}, u32[]{:S(2)}, u32[]{:S(2)}) %collective-permute-start.3) | collective-permute-done | bytes 131104 | tf_op jit(solution)/shard_map/ppermute | solution.py:75
  24.2 0.3 fusion.4
  24.5 0.3 convolution_add_fusion.5
  24.9 1.3 %collective-permute-done.5 = bf16[256,256]{1,0:T(8,128)(2,1)S(1)} collective-permute-done((bf16[256,256]{1,0:T(8,128)(2,1)S(1)}, bf16[256,256]{1,0:T(8,128)(2,1)S(1)}, u32[]{:S(2)}, u32[]{:S(2)}) %collective-permute-start.5) | collective-permute-done | bytes 131104 | tf_op jit(solution)/shard_map/ppermute | solution.py:75
  26.5 0.3 convolution_add_fusion.4
  27.3 1.2 %collective-permute-done.6 = f32[4,4,256]{2,1,0:T(4,128)S(1)} collective-permute-done((f32[4,4,256]{2,1,0:T(4,128)S(1)}, f32[4,4,256]{2,1,0:T(4,128)S(1)}, u32[]{:S(2)}, u32[]{:S(2)}) %collective-permute-start.6) | collective-permute-done | bytes 16416 | tf_op jit(solution)/shard_map/ppermute | solution.py:30
  28.5 1.5 %collective-permute-start.7 = (f32[4,4,256]{2,1,0:T(4,128)S(1)}, f32[4,4,256]{2,1,0:T(4,128)S(1)}, u32[]{:S(2)}, u32[]{:S(2)}) collective-permute-start(f32[4,4,256]{2,1,0:T(4,128)S(1)} %add.129), channel_id=1, source_target_pairs={{0,2},{1,3},{2,0},{3,1},{4,6},{5,7},{6,4},{7,5},{8,10},{9,11},{10,... | collective-permute-start | bytes 49160 | tf_op jit(solution)/shard_map/ppermute | solution.py:30
  30.0 2.2 %collective-permute-done.7 = f32[4,4,256]{2,1,0:T(4,128)S(1)} collective-permute-done((f32[4,4,256]{2,1,0:T(4,128)S(1)}, f32[4,4,256]{2,1,0:T(4,128)S(1)}, u32[]{:S(2)}, u32[]{:S(2)}) %collective-permute-start.7) | collective-permute-done | bytes 16416 | tf_op jit(solution)/shard_map/ppermute | solution.py:30
  32.3 2.4 %collective-permute-start.8 = (f32[4,4,256]{2,1,0:T(4,128)S(1)}, f32[4,4,256]{2,1,0:T(4,128)S(1)}, u32[]{:S(2)}, u32[]{:S(2)}) collective-permute-start(f32[4,4,256]{2,1,0:T(4,128)S(1)} %get-tuple-element.5), channel_id=1, source_target_pairs={{0,4},{4,8},{8,12},{12,0},{1,5},{5,9},{9,13},{13,1},{2,6},{6,10},{... | collective-permute-start | bytes 49160 | tf_op jit(solution)/shard_map/ppermute | solution.py:10
  34.7 2.6 %collective-permute-start.9 = (f32[4,4,256]{2,1,0:T(4,128)S(1)}, f32[4,4,256]{2,1,0:T(4,128)S(1)}, u32[]{:S(2)}, u32[]{:S(2)}) collective-permute-start(f32[4,4,256]{2,1,0:T(4,128)S(1)} %get-tuple-element.5), channel_id=1, source_target_pairs={{0,8},{4,12},{8,0},{12,4},{1,9},{5,13},{9,1},{13,5},{2,10},{6,14},... | collective-permute-start | bytes 49160 | tf_op jit(solution)/shard_map/ppermute | solution.py:10
  37.2 0.9 %collective-permute-start.10 = (f32[4,4,256]{2,1,0:T(4,128)S(1)}, f32[4,4,256]{2,1,0:T(4,128)S(1)}, u32[]{:S(2)}, u32[]{:S(2)}) collective-permute-start(f32[4,4,256]{2,1,0:T(4,128)S(1)} %get-tuple-element.5), channel_id=1, source_target_pairs={{0,12},{4,0},{8,4},{12,8},{1,13},{5,1},{9,5},{13,9},{2,14},{6,2},{... | collective-permute-start | bytes 49160 | tf_op jit(solution)/shard_map/ppermute | solution.py:10
  38.1 0.4 collective-permute-done.8
  38.6 0.7 %collective-permute-done.9 = f32[4,4,256]{2,1,0:T(4,128)S(1)} collective-permute-done((f32[4,4,256]{2,1,0:T(4,128)S(1)}, f32[4,4,256]{2,1,0:T(4,128)S(1)}, u32[]{:S(2)}, u32[]{:S(2)}) %collective-permute-start.9) | collective-permute-done | bytes 16416 | tf_op jit(solution)/shard_map/ppermute | solution.py:10
  39.3 1.7 %collective-permute-done.10 = f32[4,4,256]{2,1,0:T(4,128)S(1)} collective-permute-done((f32[4,4,256]{2,1,0:T(4,128)S(1)}, f32[4,4,256]{2,1,0:T(4,128)S(1)}, u32[]{:S(2)}, u32[]{:S(2)}) %collective-permute-start.10) | collective-permute-done | bytes 16416 | tf_op jit(solution)/shard_map/ppermute | solution.py:10
  41.0 0.6 %fusion.31 = (f32[256,4]{0,1:T(4,128)}, f32[256,4]{0,1:T(4,128)S(1)}, f32[256,4]{0,1:T(4,128)S(1)}, f32[256,4]{0,1:T(4,128)S(1)}, f32[256,4]{0,1:T(4,128)S(1)}) fusion(f32[4,4,256]{2,1,0:T(4,128)S(1)} %reduce_sum.143, s32[]{:T(128)S(6)} %select_n.114, s32[]{:T(128)S(6)} %select_n.112, s32[]{:T(128)S(6)} %select_n.110, s32[]{:T(128)S(6)} %select_n.108, ...), kind=kLoop, calls=%fused_computation.84 | loop fusion | bytes 40980 | tf_op jit(solution)/shard_map/transpose | solution.py:116
  43.8 0.6 %maximum_select_fusion = f32[6,512]{1,0:T(8,128)} fusion(f32[6,256]{1,0:T(8,128)S(1)} %get-tuple-element.3, f32[6,256]{1,0:T(8,128)S(1)} %get-tuple-element.2, pred[]{:T(512)S(6)} %eq.72), kind=kLoop, calls=%fused_computation.50 | loop fusion | flops 9216 | bytes 24577 | tf_op jit(solution)/shard_map/jit(_where)/select_n | solution.py:136
  (97 shorter events, 5.8 us)
Async XLA Ops:
  0.6 2.0 %copy-start = (bf16[256,512]{1,0:T(8,128)(2,1)S(1)}, bf16[256,512]{1,0:T(8,128)(2,1)}, u32[]{:S(2)}) copy-start(bf16[256,512]{1,0:T(8,128)(2,1)} %param.10) | copy-start | bytes 786436
  0.7 0.7 %copy-start.4 = (s32[256,4]{0,1:T(4,128)S(1)}, s32[256,4]{0,1:T(4,128)}, u32[]{:S(2)}) copy-start(s32[256,4]{0,1:T(4,128)} %param.14) | copy-start | bytes 12292
  1.5 0.7 %copy-start.2 = (bf16[256,24]{0,1:T(8,128)(2,1)S(1)}, bf16[256,24]{0,1:T(8,128)(2,1)}, u32[]{:S(2)}) copy-start(bf16[256,24]{0,1:T(8,128)(2,1)} %param.11) | copy-start | bytes 36868
  1.5 0.7 %copy-start.6 = (s32[256]{0:T(256)S(1)}, s32[256]{0:T(256)}, u32[]{:S(2)}) copy-start(s32[256]{0:T(256)} %param.13) | copy-start | bytes 3076
  1.6 0.7 %copy-start.7 = (s32[256]{0:T(256)S(1)}, s32[256]{0:T(256)}, u32[]{:S(2)}) copy-start(s32[256]{0:T(256)} %param.12) | copy-start | bytes 3076
  2.6 7.8 %copy-start.1 = (bf16[6,64,512]{2,1,0:T(8,128)(2,1)S(1)}, bf16[6,64,512]{2,1,0:T(8,128)(2,1)}, u32[]{:S(2)}) copy-start(bf16[6,64,512]{2,1,0:T(8,128)(2,1)} %param.8) | copy-start | bytes 1179652
  2.7 9.9 %collective-permute-start = (bf16[284,256]{1,0:T(8,128)(2,1)S(1)}, bf16[284,256]{1,0:T(8,128)(2,1)S(1)}, u32[]{:S(2)}, u32[]{:S(2)}) collective-permute-start(bf16[284,256]{1,0:T(8,128)(2,1)S(1)} %pad_maximum_fusion), channel_id=1, source_target_pairs={{0,4},{4,8},{8,12},{12,0},{1,5},{5,9},{9,13},{13,1},{2,6},{6,10},{... | collective-permute-start | bytes 436232 | tf_op jit(solution)/shard_map/ppermute | solution.py:10
  5.8 12.3 %collective-permute-start.2 = (bf16[284,256]{1,0:T(8,128)(2,1)S(1)}, bf16[284,256]{1,0:T(8,128)(2,1)S(1)}, u32[]{:S(2)}, u32[]{:S(2)}) collective-permute-start(bf16[284,256]{1,0:T(8,128)(2,1)S(1)} %pad_maximum_fusion), channel_id=1, source_target_pairs={{0,8},{4,12},{8,0},{12,4},{1,9},{5,13},{9,1},{13,5},{2,10},{6,14},... | collective-permute-start | bytes 436232 | tf_op jit(solution)/shard_map/ppermute | solution.py:10
  8.3 11.3 %collective-permute-start.4 = (bf16[284,256]{1,0:T(8,128)(2,1)S(1)}, bf16[284,256]{1,0:T(8,128)(2,1)S(1)}, u32[]{:S(2)}, u32[]{:S(2)}) collective-permute-start(bf16[284,256]{1,0:T(8,128)(2,1)S(1)} %pad_maximum_fusion), channel_id=1, source_target_pairs={{0,12},{4,0},{8,4},{12,8},{1,13},{5,1},{9,5},{13,9},{2,14},{6,2},{... | collective-permute-start | bytes 436232 | tf_op jit(solution)/shard_map/ppermute | solution.py:10
  9.7 0.7 %copy-start.3 = (bf16[6,512]{1,0:T(8,128)(2,1)S(1)}, bf16[6,512]{1,0:T(8,128)(2,1)}, u32[]{:S(2)}) copy-start(bf16[6,512]{1,0:T(8,128)(2,1)} %param.9) | copy-start | bytes 18436
  11.3 0.7 %copy-start.5 = (f32[256,4]{0,1:T(4,128)S(1)}, f32[256,4]{0,1:T(4,128)}, u32[]{:S(2)}) copy-start(f32[256,4]{0,1:T(4,128)} %param.15) | copy-start | bytes 12292
  12.6 8.7 %collective-permute-start.1 = (bf16[256,256]{1,0:T(8,128)(2,1)S(1)}, bf16[256,256]{1,0:T(8,128)(2,1)S(1)}, u32[]{:S(2)}, u32[]{:S(2)}) collective-permute-start(bf16[256,256]{1,0:T(8,128)(2,1)S(1)} %slice.53), channel_id=1, source_target_pairs={{0,2},{2,0},{1,3},{3,1},{4,6},{6,4},{5,7},{7,5},{8,10},{10,8},{9,1... | collective-permute-start | bytes 393224 | tf_op jit(solution)/shard_map/ppermute | solution.py:75
  18.1 6.2 %collective-permute-start.3 = (bf16[256,256]{1,0:T(8,128)(2,1)S(1)}, bf16[256,256]{1,0:T(8,128)(2,1)S(1)}, u32[]{:S(2)}, u32[]{:S(2)}) collective-permute-start(bf16[256,256]{1,0:T(8,128)(2,1)S(1)} %slice.56), channel_id=1, source_target_pairs={{0,2},{2,0},{1,3},{3,1},{4,6},{6,4},{5,7},{7,5},{8,10},{10,8},{9,1... | collective-permute-start | bytes 393224 | tf_op jit(solution)/shard_map/ppermute | solution.py:75
  20.4 5.9 %collective-permute-start.5 = (bf16[256,256]{1,0:T(8,128)(2,1)S(1)}, bf16[256,256]{1,0:T(8,128)(2,1)S(1)}, u32[]{:S(2)}, u32[]{:S(2)}) collective-permute-start(bf16[256,256]{1,0:T(8,128)(2,1)S(1)} %slice.59), channel_id=1, source_target_pairs={{0,2},{2,0},{1,3},{3,1},{4,6},{6,4},{5,7},{7,5},{8,10},{10,8},{9,1... | collective-permute-start | bytes 393224 | tf_op jit(solution)/shard_map/ppermute | solution.py:75
  27.3 1.2 %collective-permute-start.6 = (f32[4,4,256]{2,1,0:T(4,128)S(1)}, f32[4,4,256]{2,1,0:T(4,128)S(1)}, u32[]{:S(2)}, u32[]{:S(2)}) collective-permute-start(f32[4,4,256]{2,1,0:T(4,128)S(1)} %constant_dynamic-update-slice_fusion), channel_id=1, source_target_pairs={{0,1},{1,0},{2,3},{3,2},{4,5},{5,4},{6,7},{7,6},{8,9},{9,8},{10,11... | collective-permute-start | bytes 49160 | tf_op jit(solution)/shard_map/ppermute | solution.py:30
  28.5 3.7 %collective-permute-start.7 = (f32[4,4,256]{2,1,0:T(4,128)S(1)}, f32[4,4,256]{2,1,0:T(4,128)S(1)}, u32[]{:S(2)}, u32[]{:S(2)}) collective-permute-start(f32[4,4,256]{2,1,0:T(4,128)S(1)} %add.129), channel_id=1, source_target_pairs={{0,2},{1,3},{2,0},{3,1},{4,6},{5,7},{6,4},{7,5},{8,10},{9,11},{10,... | collective-permute-start | bytes 49160 | tf_op jit(solution)/shard_map/ppermute | solution.py:30
  32.3 6.2 %collective-permute-start.8 = (f32[4,4,256]{2,1,0:T(4,128)S(1)}, f32[4,4,256]{2,1,0:T(4,128)S(1)}, u32[]{:S(2)}, u32[]{:S(2)}) collective-permute-start(f32[4,4,256]{2,1,0:T(4,128)S(1)} %get-tuple-element.5), channel_id=1, source_target_pairs={{0,4},{4,8},{8,12},{12,0},{1,5},{5,9},{9,13},{13,1},{2,6},{6,10},{... | collective-permute-start | bytes 49160 | tf_op jit(solution)/shard_map/ppermute | solution.py:10
  34.7 4.6 %collective-permute-start.9 = (f32[4,4,256]{2,1,0:T(4,128)S(1)}, f32[4,4,256]{2,1,0:T(4,128)S(1)}, u32[]{:S(2)}, u32[]{:S(2)}) collective-permute-start(f32[4,4,256]{2,1,0:T(4,128)S(1)} %get-tuple-element.5), channel_id=1, source_target_pairs={{0,8},{4,12},{8,0},{12,4},{1,9},{5,13},{9,1},{13,5},{2,10},{6,14},... | collective-permute-start | bytes 49160 | tf_op jit(solution)/shard_map/ppermute | solution.py:10
  37.2 3.7 %collective-permute-start.10 = (f32[4,4,256]{2,1,0:T(4,128)S(1)}, f32[4,4,256]{2,1,0:T(4,128)S(1)}, u32[]{:S(2)}, u32[]{:S(2)}) collective-permute-start(f32[4,4,256]{2,1,0:T(4,128)S(1)} %get-tuple-element.5), channel_id=1, source_target_pairs={{0,12},{4,0},{8,4},{12,8},{1,13},{5,1},{9,5},{13,9},{2,14},{6,2},{... | collective-permute-start | bytes 49160 | tf_op jit(solution)/shard_map/ppermute | solution.py:10

commit v5 on v4

--- a/solution.py
+++ b/solution.py
@@ -52,9 +52,12 @@
         columns = c_idx * block_cols + lax.iota(jnp.int32, block_cols)
         inside = (columns[None, :] >= path_start[:, None]) & (columns[None, :] < path_end[:, None])
         lengths = jnp.where(inside, seg_len, jnp.zeros_like(seg_len))
-        n_len = path_rows * block_cols
+        def small_for(target):
+            cols_of = lax.dynamic_slice_in_dim(lengths, target * own_cols, own_cols, axis=1)
+            return jnp.concatenate([cols_of.reshape(-1), mode_index.astype(bf16).reshape(-1)])
+
+        n_len = path_rows * own_cols
         n_mi = path_rows * kept
-        small_flat = jnp.concatenate([lengths.reshape(-1), mode_index.astype(bf16).reshape(-1)])
 
         scaled = (panels.astype(f32) * model.astype(f32)[:, None, :]).astype(bf16)
         scaled = scaled.reshape(own_cols * modes, depth_half)
@@ -66,31 +69,30 @@
             offsets = [own_off, other_off]
             mine = lax.dynamic_slice_in_dim(depth_weight, own_off, width, axis=1)
             theirs = lax.dynamic_slice_in_dim(depth_weight, other_off, width, axis=1)
-            payload = jnp.concatenate([mine, pack_rows(small_flat, width)], axis=0)
-            z_copies = shifted_copies(payload, "paths", n_paths)
-            blocks = [([mine, theirs], small_flat)]
-            for s in range(1, n_paths):
-                got = z_copies[s]
-                half = got[:path_rows]
-                across = lax.ppermute(half, "cols", [(0, 1), (1, 0)])
-                blocks.append(([half, across], got[path_rows:].reshape(-1)))
+            head = [mine]
         else:
             width = depth_half
             offsets = [0]
-            payload = jnp.concatenate([depth_weight, pack_rows(small_flat, width)], axis=0)
-            blocks = [
-                ([got[:path_rows]], got[path_rows:].reshape(-1))
-                for got in shifted_copies(payload, "paths", n_paths)
-            ]
+            head = [depth_weight]
+        blocks = [(head + ([theirs] if split else []), small_for(p_idx))]
+        for shift in range(1, n_paths):
+            target = (p_idx + shift) % n_paths
+            payload = jnp.concatenate([head[0], pack_rows(small_for(target), width)], axis=0)
+            perm = [(i, (i + shift) % n_paths) for i in range(n_paths)]
+            got = lax.ppermute(payload, "paths", perm)
+            part_rows = got[:path_rows]
+            dw_parts = [part_rows]
+            if split:
+                dw_parts.append(lax.ppermute(part_rows, "cols", [(0, 1), (1, 0)]))
+            blocks.append((dw_parts, got[path_rows:].reshape(-1)))
         scaled_parts = [lax.dynamic_slice_in_dim(scaled, off, width, axis=1) for off in offsets]
         mode_ids = lax.iota(jnp.int32, modes)
 
         unpacked = []
         parts = []
         for s, (dw_parts, sm) in enumerate(blocks):
-            len_b = sm[:n_len].reshape(path_rows, block_cols)
+            len_own = sm[:n_len].reshape(path_rows, own_cols).astype(f32)
             mi_b = sm[n_len:n_len + n_mi].reshape(path_rows, kept).astype(jnp.int32)
-            len_own = lax.dynamic_slice_in_dim(len_b, p_idx * own_cols, own_cols, axis=1).astype(f32)
             one_hot = (mi_b[:, :, None] == mode_ids[None, None, :]).astype(f32)
             unpacked.append((dw_parts, len_own, one_hot))
             weighted = None
@@ -132,14 +134,9 @@
         for acc, off in zip(summed, offsets):
             panel_part = lax.dynamic_slice_in_dim(panels, off, width, axis=2).astype(f32)
             grads.append(jnp.sum(acc.reshape(own_cols, modes, width) * panel_part, axis=1))
-        if split:
-            gradient = jnp.where(
-                c_idx == 0,
-                jnp.concatenate([grads[0], grads[1]], axis=1),
-                jnp.concatenate([grads[1], grads[0]], axis=1),
-            )
-        else:
-            gradient = grads[0]
+        gradient = jnp.zeros((own_cols, depth_half), f32)
+        for g, off in zip(grads, offsets):
+            gradient = lax.dynamic_update_slice_in_dim(gradient, g, off, axis=1)
         return (gradient, misfit)
 
     return shards

time: 44.8 us -> 44.1 us (0.984)
  starting transfers between devices: 18.3 us -> 15 us
  waiting for transfers between devices: 13.5 us -> 15.7 us
  local copies, waits for them, and re-layouts: 6.07 us -> 7.1 us
  other arithmetic: 1.57 us -> 0.98 us
    ppermute x6 -> x3, starting transfers between devices: 12.8 us -> 3.87 us  [shifted_copies(): copies.append(lax.ppermute(x, axes, perm))]
    ppermute x3 -> x6, waiting for transfers between devices: 3.55 us -> 9.79 us  [the longest x3 6.47 us: shards(): got = lax.ppermute(payload, 'paths', perm)]
    ppermute x3 -> x6, starting transfers between devices: 3.96 us -> 9.83 us  [the longest x3 6.11 us: shards(): got = lax.ppermute(payload, 'paths', perm)]
    ppermute x6 -> x3, waiting for transfers between devices: 6.49 us -> 2.26 us  [shifted_copies(): copies.append(lax.ppermute(x, axes, perm))]
    convert_element_type x1 -> x7, local copies, waits for them, and re-layouts: 0.15 us -> 0.78 us  [the longest x6 0.63 us: shards(): len_own = sm[:n_len].reshape(path_rows, own_cols).astype(f32)]
    select_n x1 -> x0, other arithmetic: 0.61 us -> none  [shards(): jnp.where(c_idx == 0, jnp.concatenate([grads[0], grads[1]], axis=1), jnp....]
    unnamed x19 -> x18, local copies, waits for them, and re-layouts: 2.89 us -> 3.21 us
  transfers between devices with their start and end apart: 11 -> 11, of which waited for: 9 -> 8; matrix products, arithmetic and copies ran while one was open for 9% -> 8% of each run, Pallas kernels for 0% -> 0%
where the time goes in v5:
time: 44.1 us; the launch traced here: 43.8 us
  waiting for transfers between devices  15.7 us (36%)
  starting transfers between devices  15 us (34%)
  local copies, waits for them, and re-layouts  7.1 us (16%)
  matrix products  3.79 us (9%)
  between operations  1.23 us (3%)
  other arithmetic  0.98 us (2%)
    ppermute x3, waiting for transfers between devices, shards(): got = lax.ppermute(payload, 'paths', perm)  6.47 us
    ppermute x3, starting transfers between devices, shards(): got = lax.ppermute(payload, 'paths', perm)  6.11 us
    ppermute x3, starting transfers between devices, shifted_copies(): copies.append(lax.ppermute(x, axes, perm))  3.87 us
    ppermute x3, starting transfers between devices, shards(): dw_parts.append(lax.ppermute(part_rows, 'cols', [(0, 1), (1, 0)]))  3.71 us
    ppermute x2, waiting for transfers between devices, butterfly_sum(): x = x + lax.ppermute(x, axes, perm)  3.63 us
    ppermute x3, waiting for transfers between devices, shards(): dw_parts.append(lax.ppermute(part_rows, 'cols', [(0, 1), (1, 0)]))  3.32 us
    unnamed x18, local copies, waits for them, and re-layouts  3.21 us
    ppermute x3, waiting for transfers between devices, shifted_copies(): copies.append(lax.ppermute(x, axes, perm))  2.26 us
  transfers between devices with their start and end apart: 11, of which 8 were waited for; matrix products, arithmetic and copies ran while one was open for 8% of the time, Pallas kernels for 0%

profile of v5, /device:TPU:0, one launch (start us, length us, event | category | flops | bytes accessed | tf_op | source)
XLA Modules:
  0.0 43.8 jit_solution(11897186998310136047)
XLA Ops:
  0.8 0.7 %copy-done.3 = bf16[256,24]{0,1:T(8,128)(2,1)S(1)} copy-done((bf16[256,24]{0,1:T(8,128)(2,1)S(1)}, bf16[256,24]{0,1:T(8,128)(2,1)}, u32[]{:S(2)}) %copy-start.3) | copy-done | bytes 12312
  2.4 0.5 %copy-done.5 = s32[256,4]{0,1:T(4,128)S(1)} copy-done((s32[256,4]{0,1:T(4,128)S(1)}, s32[256,4]{0,1:T(4,128)}, u32[]{:S(2)}) %copy-start.5) | copy-done | bytes 4120
  3.4 5.1 %collective-permute-start.4 = (bf16[266,256]{1,0:T(8,128)(2,1)S(1)}, bf16[266,256]{1,0:T(8,128)(2,1)S(1)}, u32[]{:S(2)}, u32[]{:S(2)}) collective-permute-start(bf16[266,256]{1,0:T(8,128)(2,1)S(1)} %get-tuple-element.8), channel_id=1, source_target_pairs={{0,12},{4,0},{8,4},{12,8},{1,13},{5,1},{9,5},{13,9},{2,14},{6,2},{... | collective-permute-start | bytes 408584 | tf_op jit(solution)/shard_map/ppermute | solution.py:82
  8.5 1.0 %collective-permute-start = (bf16[266,256]{1,0:T(8,128)(2,1)S(1)}, bf16[266,256]{1,0:T(8,128)(2,1)S(1)}, u32[]{:S(2)}, u32[]{:S(2)}) collective-permute-start(bf16[266,256]{1,0:T(8,128)(2,1)S(1)} %get-tuple-element.10), channel_id=1, source_target_pairs={{0,4},{4,8},{8,12},{12,0},{1,5},{5,9},{9,13},{13,1},{2,6},{6,10},{... | collective-permute-start | bytes 408584 | tf_op jit(solution)/shard_map/ppermute | solution.py:82
  9.5 0.7 %copy-done.4 = bf16[6,512]{1,0:T(8,128)(2,1)S(1)} copy-done((bf16[6,512]{1,0:T(8,128)(2,1)S(1)}, bf16[6,512]{1,0:T(8,128)(2,1)}, u32[]{:S(2)}) %copy-start.4) | copy-done | bytes 6168
  10.3 0.3 fusion.12
  10.6 0.3 convolution_add_fusion.7
  11.2 0.7 %copy-done.6 = f32[256,4]{0,1:T(4,128)S(1)} copy-done((f32[256,4]{0,1:T(4,128)S(1)}, f32[256,4]{0,1:T(4,128)}, u32[]{:S(2)}) %copy-start.6) | copy-done | bytes 4120
  11.8 0.8 %collective-permute-done.4 = bf16[266,256]{1,0:T(8,128)(2,1)S(1)} collective-permute-done((bf16[266,256]{1,0:T(8,128)(2,1)S(1)}, bf16[266,256]{1,0:T(8,128)(2,1)S(1)}, u32[]{:S(2)}, u32[]{:S(2)}) %collective-permute-start.4) | collective-permute-done | bytes 136224 | tf_op jit(solution)/shard_map/ppermute | solution.py:82
  12.6 1.6 %collective-permute-start.5 = (bf16[256,256]{1,0:T(8,128)(2,1)S(1)}, bf16[256,256]{1,0:T(8,128)(2,1)S(1)}, u32[]{:S(2)}, u32[]{:S(2)}) collective-permute-start(bf16[256,256]{1,0:T(8,128)(2,1)S(1)} %slice.59), channel_id=1, source_target_pairs={{0,2},{2,0},{1,3},{3,1},{4,6},{6,4},{5,7},{7,5},{8,10},{10,8},{9,1... | collective-permute-start | bytes 393224 | tf_op jit(solution)/shard_map/ppermute | solution.py:86
  14.7 5.7 %collective-permute-done.2 = bf16[266,256]{1,0:T(8,128)(2,1)S(1)} collective-permute-done((bf16[266,256]{1,0:T(8,128)(2,1)S(1)}, bf16[266,256]{1,0:T(8,128)(2,1)S(1)}, u32[]{:S(2)}, u32[]{:S(2)}) %collective-permute-start.2) | collective-permute-done | bytes 136224 | tf_op jit(solution)/shard_map/ppermute | solution.py:82
  20.3 1.6 %collective-permute-start.3 = (bf16[256,256]{1,0:T(8,128)(2,1)S(1)}, bf16[256,256]{1,0:T(8,128)(2,1)S(1)}, u32[]{:S(2)}, u32[]{:S(2)}) collective-permute-start(bf16[256,256]{1,0:T(8,128)(2,1)S(1)} %slice.56), channel_id=1, source_target_pairs={{0,2},{2,0},{1,3},{3,1},{4,6},{6,4},{5,7},{7,5},{8,10},{10,8},{9,1... | collective-permute-start | bytes 393224 | tf_op jit(solution)/shard_map/ppermute | solution.py:86
  22.4 0.6 %collective-permute-start.1 = (bf16[256,256]{1,0:T(8,128)(2,1)S(1)}, bf16[256,256]{1,0:T(8,128)(2,1)S(1)}, u32[]{:S(2)}, u32[]{:S(2)}) collective-permute-start(bf16[256,256]{1,0:T(8,128)(2,1)S(1)} %slice.53), channel_id=1, source_target_pairs={{0,2},{2,0},{1,3},{3,1},{4,6},{6,4},{5,7},{7,5},{8,10},{10,8},{9,1... | collective-permute-start | bytes 393224 | tf_op jit(solution)/shard_map/ppermute | solution.py:86
  23.5 0.3 fusion.2
  23.7 0.3 convolution_add_fusion.4
  24.2 2.4 %collective-permute-done.3 = bf16[256,256]{1,0:T(8,128)(2,1)S(1)} collective-permute-done((bf16[256,256]{1,0:T(8,128)(2,1)S(1)}, bf16[256,256]{1,0:T(8,128)(2,1)S(1)}, u32[]{:S(2)}, u32[]{:S(2)}) %collective-permute-start.3) | collective-permute-done | bytes 131104 | tf_op jit(solution)/shard_map/ppermute | solution.py:86
  26.6 0.3 fusion.4
  26.9 0.3 convolution_add_fusion.5
  27.3 0.9 %collective-permute-done.1 = bf16[256,256]{1,0:T(8,128)(2,1)S(1)} collective-permute-done((bf16[256,256]{1,0:T(8,128)(2,1)S(1)}, bf16[256,256]{1,0:T(8,128)(2,1)S(1)}, u32[]{:S(2)}, u32[]{:S(2)}) %collective-permute-start.1) | collective-permute-done | bytes 131104 | tf_op jit(solution)/shard_map/ppermute | solution.py:86
  28.2 0.3 fusion.6
  28.4 0.3 convolution_add_fusion.6
  29.3 1.2 %collective-permute-done.6 = f32[4,4,256]{2,1,0:T(4,128)S(1)} collective-permute-done((f32[4,4,256]{2,1,0:T(4,128)S(1)}, f32[4,4,256]{2,1,0:T(4,128)S(1)}, u32[]{:S(2)}, u32[]{:S(2)}) %collective-permute-start.6) | collective-permute-done | bytes 16416 | tf_op jit(solution)/shard_map/ppermute | solution.py:30
  30.5 1.3 %collective-permute-start.7 = (f32[4,4,256]{2,1,0:T(4,128)S(1)}, f32[4,4,256]{2,1,0:T(4,128)S(1)}, u32[]{:S(2)}, u32[]{:S(2)}) collective-permute-start(f32[4,4,256]{2,1,0:T(4,128)S(1)} %add.164), channel_id=1, source_target_pairs={{0,2},{1,3},{2,0},{3,1},{4,6},{5,7},{6,4},{7,5},{8,10},{9,11},{10,... | collective-permute-start | bytes 49160 | tf_op jit(solution)/shard_map/ppermute | solution.py:30
  31.7 2.5 %collective-permute-done.7 = f32[4,4,256]{2,1,0:T(4,128)S(1)} collective-permute-done((f32[4,4,256]{2,1,0:T(4,128)S(1)}, f32[4,4,256]{2,1,0:T(4,128)S(1)}, u32[]{:S(2)}, u32[]{:S(2)}) %collective-permute-start.7) | collective-permute-done | bytes 16416 | tf_op jit(solution)/shard_map/ppermute | solution.py:30
  34.3 1.3 %collective-permute-start.9 = (f32[4,4,256]{2,1,0:T(4,128)S(1)}, f32[4,4,256]{2,1,0:T(4,128)S(1)}, u32[]{:S(2)}, u32[]{:S(2)}) collective-permute-start(f32[4,4,256]{2,1,0:T(4,128)S(1)} %get-tuple-element.5), channel_id=1, source_target_pairs={{0,8},{4,12},{8,0},{12,4},{1,9},{5,13},{9,1},{13,5},{2,10},{6,14},... | collective-permute-start | bytes 49160 | tf_op jit(solution)/shard_map/ppermute | solution.py:10
  35.6 2.5 %collective-permute-start.10 = (f32[4,4,256]{2,1,0:T(4,128)S(1)}, f32[4,4,256]{2,1,0:T(4,128)S(1)}, u32[]{:S(2)}, u32[]{:S(2)}) collective-permute-start(f32[4,4,256]{2,1,0:T(4,128)S(1)} %get-tuple-element.5), channel_id=1, source_target_pairs={{0,12},{4,0},{8,4},{12,8},{1,13},{5,1},{9,5},{13,9},{2,14},{6,2},{... | collective-permute-start | bytes 49160 | tf_op jit(solution)/shard_map/ppermute | solution.py:10
  38.1 1.7 %collective-permute-done.8 = f32[4,4,256]{2,1,0:T(4,128)S(1)} collective-permute-done((f32[4,4,256]{2,1,0:T(4,128)S(1)}, f32[4,4,256]{2,1,0:T(4,128)S(1)}, u32[]{:S(2)}, u32[]{:S(2)}) %collective-permute-start.8) | collective-permute-done | bytes 16416 | tf_op jit(solution)/shard_map/ppermute | solution.py:10
  39.8 0.5 %collective-permute-done.10 = f32[4,4,256]{2,1,0:T(4,128)S(1)} collective-permute-done((f32[4,4,256]{2,1,0:T(4,128)S(1)}, f32[4,4,256]{2,1,0:T(4,128)S(1)}, u32[]{:S(2)}, u32[]{:S(2)}) %collective-permute-start.10) | collective-permute-done | bytes 16416 | tf_op jit(solution)/shard_map/ppermute | solution.py:10
  40.4 0.6 %fusion.31 = (f32[256,4]{0,1:T(4,128)}, f32[256,4]{0,1:T(4,128)S(1)}, f32[256,4]{0,1:T(4,128)S(1)}, f32[256,4]{0,1:T(4,128)S(1)}, f32[256,4]{0,1:T(4,128)S(1)}) fusion(f32[4,4,256]{2,1,0:T(4,128)S(1)} %reduce_sum.143, s32[]{:T(128)S(6)} %select_n.130, s32[]{:T(128)S(6)} %select_n.129, s32[]{:T(128)S(6)} %select_n.125, s32[]{:T(128)S(6)} %select_n.121, ...), kind=kLoop, calls=%fused_computation.89 | loop fusion | bytes 40980 | tf_op jit(solution)/shard_map/transpose | solution.py:118
  42.6 0.2 fusion
  42.8 0.2 fusion.1
  43.2 0.6 %copy-done.2 = f32[6,512]{1,0:T(8,128)} copy-done((f32[6,512]{1,0:T(8,128)}, f32[6,512]{1,0:T(8,128)S(1)}, u32[]{:S(2)}) %copy-start.2) | copy-done | bytes 12312
  (100 shorter events, 5.7 us)
Async XLA Ops:
  0.6 2.7 %copy-start = (bf16[256,512]{1,0:T(8,128)(2,1)S(1)}, bf16[256,512]{1,0:T(8,128)(2,1)}, u32[]{:S(2)}) copy-start(bf16[256,512]{1,0:T(8,128)(2,1)} %param.10) | copy-start | bytes 786436
  0.7 0.7 %copy-start.3 = (bf16[256,24]{0,1:T(8,128)(2,1)S(1)}, bf16[256,24]{0,1:T(8,128)(2,1)}, u32[]{:S(2)}) copy-start(bf16[256,24]{0,1:T(8,128)(2,1)} %param.11) | copy-start | bytes 36868
  0.7 0.7 %copy-start.7 = (s32[256]{0:T(256)S(1)}, s32[256]{0:T(256)}, u32[]{:S(2)}) copy-start(s32[256]{0:T(256)} %param.13) | copy-start | bytes 3076
  0.7 0.7 %copy-start.8 = (s32[256]{0:T(256)S(1)}, s32[256]{0:T(256)}, u32[]{:S(2)}) copy-start(s32[256]{0:T(256)} %param.12) | copy-start | bytes 3076
  2.3 0.7 %copy-start.5 = (s32[256,4]{0,1:T(4,128)S(1)}, s32[256,4]{0,1:T(4,128)}, u32[]{:S(2)}) copy-start(s32[256,4]{0,1:T(4,128)} %param.14) | copy-start | bytes 12292
  3.4 6.9 %copy-start.1 = (bf16[6,64,512]{2,1,0:T(8,128)(2,1)S(1)}, bf16[6,64,512]{2,1,0:T(8,128)(2,1)}, u32[]{:S(2)}) copy-start(bf16[6,64,512]{2,1,0:T(8,128)(2,1)} %param.8) | copy-start | bytes 1179652
  3.4 9.2 %collective-permute-start.4 = (bf16[266,256]{1,0:T(8,128)(2,1)S(1)}, bf16[266,256]{1,0:T(8,128)(2,1)S(1)}, u32[]{:S(2)}, u32[]{:S(2)}) collective-permute-start(bf16[266,256]{1,0:T(8,128)(2,1)S(1)} %get-tuple-element.8), channel_id=1, source_target_pairs={{0,12},{4,0},{8,4},{12,8},{1,13},{5,1},{9,5},{13,9},{2,14},{6,2},{... | collective-permute-start | bytes 408584 | tf_op jit(solution)/shard_map/ppermute | solution.py:82
  8.5 11.8 %collective-permute-start.2 = (bf16[266,256]{1,0:T(8,128)(2,1)S(1)}, bf16[266,256]{1,0:T(8,128)(2,1)S(1)}, u32[]{:S(2)}, u32[]{:S(2)}) collective-permute-start(bf16[266,256]{1,0:T(8,128)(2,1)S(1)} %get-tuple-element.9), channel_id=1, source_target_pairs={{0,8},{4,12},{8,0},{12,4},{1,9},{5,13},{9,1},{13,5},{2,10},{6,14},... | collective-permute-start | bytes 408584 | tf_op jit(solution)/shard_map/ppermute | solution.py:82
  8.5 13.9 %collective-permute-start = (bf16[266,256]{1,0:T(8,128)(2,1)S(1)}, bf16[266,256]{1,0:T(8,128)(2,1)S(1)}, u32[]{:S(2)}, u32[]{:S(2)}) collective-permute-start(bf16[266,256]{1,0:T(8,128)(2,1)S(1)} %get-tuple-element.10), channel_id=1, source_target_pairs={{0,4},{4,8},{8,12},{12,0},{1,5},{5,9},{9,13},{13,1},{2,6},{6,10},{... | collective-permute-start | bytes 408584 | tf_op jit(solution)/shard_map/ppermute | solution.py:82
  9.5 0.7 %copy-start.4 = (bf16[6,512]{1,0:T(8,128)(2,1)S(1)}, bf16[6,512]{1,0:T(8,128)(2,1)}, u32[]{:S(2)}) copy-start(bf16[6,512]{1,0:T(8,128)(2,1)} %param.9) | copy-start | bytes 18436
  11.1 0.7 %copy-start.6 = (f32[256,4]{0,1:T(4,128)S(1)}, f32[256,4]{0,1:T(4,128)}, u32[]{:S(2)}) copy-start(f32[256,4]{0,1:T(4,128)} %param.15) | copy-start | bytes 12292
  12.6 10.8 %collective-permute-start.5 = (bf16[256,256]{1,0:T(8,128)(2,1)S(1)}, bf16[256,256]{1,0:T(8,128)(2,1)S(1)}, u32[]{:S(2)}, u32[]{:S(2)}) collective-permute-start(bf16[256,256]{1,0:T(8,128)(2,1)S(1)} %slice.59), channel_id=1, source_target_pairs={{0,2},{2,0},{1,3},{3,1},{4,6},{6,4},{5,7},{7,5},{8,10},{10,8},{9,1... | collective-permute-start | bytes 393224 | tf_op jit(solution)/shard_map/ppermute | solution.py:86
  20.3 6.3 %collective-permute-start.3 = (bf16[256,256]{1,0:T(8,128)(2,1)S(1)}, bf16[256,256]{1,0:T(8,128)(2,1)S(1)}, u32[]{:S(2)}, u32[]{:S(2)}) collective-permute-start(bf16[256,256]{1,0:T(8,128)(2,1)S(1)} %slice.56), channel_id=1, source_target_pairs={{0,2},{2,0},{1,3},{3,1},{4,6},{6,4},{5,7},{7,5},{8,10},{10,8},{9,1... | collective-permute-start | bytes 393224 | tf_op jit(solution)/shard_map/ppermute | solution.py:86
  22.4 5.8 %collective-permute-start.1 = (bf16[256,256]{1,0:T(8,128)(2,1)S(1)}, bf16[256,256]{1,0:T(8,128)(2,1)S(1)}, u32[]{:S(2)}, u32[]{:S(2)}) collective-permute-start(bf16[256,256]{1,0:T(8,128)(2,1)S(1)} %slice.53), channel_id=1, source_target_pairs={{0,2},{2,0},{1,3},{3,1},{4,6},{6,4},{5,7},{7,5},{8,10},{10,8},{9,1... | collective-permute-start | bytes 393224 | tf_op jit(solution)/shard_map/ppermute | solution.py:86
  29.2 1.2 %collective-permute-start.6 = (f32[4,4,256]{2,1,0:T(4,128)S(1)}, f32[4,4,256]{2,1,0:T(4,128)S(1)}, u32[]{:S(2)}, u32[]{:S(2)}) collective-permute-start(f32[4,4,256]{2,1,0:T(4,128)S(1)} %constant_dynamic-update-slice_fusion.2), channel_id=1, source_target_pairs={{0,1},{1,0},{2,3},{3,2},{4,5},{5,4},{6,7},{7,6},{8,9},{9,8},{10,11... | collective-permute-start | bytes 49160 | tf_op jit(solution)/shard_map/ppermute | solution.py:30
  30.5 3.7 %collective-permute-start.7 = (f32[4,4,256]{2,1,0:T(4,128)S(1)}, f32[4,4,256]{2,1,0:T(4,128)S(1)}, u32[]{:S(2)}, u32[]{:S(2)}) collective-permute-start(f32[4,4,256]{2,1,0:T(4,128)S(1)} %add.164), channel_id=1, source_target_pairs={{0,2},{1,3},{2,0},{3,1},{4,6},{5,7},{6,4},{7,5},{8,10},{9,11},{10,... | collective-permute-start | bytes 49160 | tf_op jit(solution)/shard_map/ppermute | solution.py:30
  34.2 5.6 %collective-permute-start.8 = (f32[4,4,256]{2,1,0:T(4,128)S(1)}, f32[4,4,256]{2,1,0:T(4,128)S(1)}, u32[]{:S(2)}, u32[]{:S(2)}) collective-permute-start(f32[4,4,256]{2,1,0:T(4,128)S(1)} %get-tuple-element.5), channel_id=1, source_target_pairs={{0,4},{4,8},{8,12},{12,0},{1,5},{5,9},{9,13},{13,1},{2,6},{6,10},{... | collective-permute-start | bytes 49160 | tf_op jit(solution)/shard_map/ppermute | solution.py:10
  34.3 5.5 %collective-permute-start.9 = (f32[4,4,256]{2,1,0:T(4,128)S(1)}, f32[4,4,256]{2,1,0:T(4,128)S(1)}, u32[]{:S(2)}, u32[]{:S(2)}) collective-permute-start(f32[4,4,256]{2,1,0:T(4,128)S(1)} %get-tuple-element.5), channel_id=1, source_target_pairs={{0,8},{4,12},{8,0},{12,4},{1,9},{5,13},{9,1},{13,5},{2,10},{6,14},... | collective-permute-start | bytes 49160 | tf_op jit(solution)/shard_map/ppermute | solution.py:10
  35.6 4.8 %collective-permute-start.10 = (f32[4,4,256]{2,1,0:T(4,128)S(1)}, f32[4,4,256]{2,1,0:T(4,128)S(1)}, u32[]{:S(2)}, u32[]{:S(2)}) collective-permute-start(f32[4,4,256]{2,1,0:T(4,128)S(1)} %get-tuple-element.5), channel_id=1, source_target_pairs={{0,12},{4,0},{8,4},{12,8},{1,13},{5,1},{9,5},{13,9},{2,14},{6,2},{... | collective-permute-start | bytes 49160 | tf_op jit(solution)/shard_map/ppermute | solution.py:10
  43.2 0.6 %copy-start.2 = (f32[6,512]{1,0:T(8,128)}, f32[6,512]{1,0:T(8,128)S(1)}, u32[]{:S(2)}) copy-start(f32[6,512]{1,0:T(8,128)S(1)} %constant_dynamic-update-slice_fusion) | copy-start | bytes 36868

commit v6 on v5

v6 whole, which is shorter than its diff:
```python
import jax
import jax.numpy as jnp
from jax import lax
from jax.sharding import PartitionSpec as P


def shifted_copies(x, axes, count):
    copies = [x]
    for shift in range(1, count):
        perm = [(i, (i + shift) % count) for i in range(count)]
        copies.append(lax.ppermute(x, axes, perm))
    return copies


def place_by_source(copies, me, count):
    stacked = jnp.zeros((count,) + copies[0].shape, copies[0].dtype)
    for shift, piece in enumerate(copies):
        stacked = lax.dynamic_update_index_in_dim(stacked, piece, (me - shift) % count, 0)
    return stacked


def exchange_sum(x, axes, count):
    me = lax.axis_index(axes)
    return jnp.sum(place_by_source(shifted_copies(x, axes, count), me, count), axis=0)


def butterfly_sum(x, axes, count):
    step = 1
    while step < count:
        perm = [(i, i ^ step) for i in range(count)]
        x = x + lax.ppermute(x, axes, perm)
        step *= 2
    return x


def pack_rows(flat, width):
    pad = (-flat.shape[0]) % width
    return jnp.pad(flat, (0, pad)).reshape(-1, width)


def make_shards(n_paths, n_cols, n_depth):
    split = n_cols == 2

    def shards(panels, model, depth_weight, seg_len, path_start, path_end, mode_index, observed):
        own_cols, modes, depth_half = panels.shape
        path_rows, block_cols = seg_len.shape
        kept = mode_index.shape[1]
        f32, bf16 = jnp.float32, jnp.bfloat16
        p_idx = lax.axis_index("paths")
        c_idx = lax.axis_index("cols")
        d_idx = lax.axis_index("depth")

        columns = c_idx * block_cols + lax.iota(jnp.int32, block_cols)
        inside = (columns[None, :] >= path_start[:, None]) & (columns[None, :] < path_end[:, None])
        lengths = jnp.where(inside, seg_len, jnp.zeros_like(seg_len))

        def lengths_of(target):
            return lax.dynamic_slice_in_dim(lengths, target * own_cols, own_cols, axis=1)

        def small_for(target):
            return jnp.concatenate(
                [lengths_of(target).reshape(-1), mode_index.astype(bf16).reshape(-1)]
            )

        n_len = path_rows * own_cols
        n_mi = path_rows * kept
        n_sets = 2 if split else 1
        width = depth_half // n_sets

        def scale(pan, mod):
            return (pan.astype(f32) * mod.astype(f32)[:, None, :]).astype(bf16)

        if split:
            own_off = c_idx * width
            other_off = (1 - c_idx) * width
            head = lax.dynamic_slice_in_dim(depth_weight, own_off, width, axis=1)
            pan_out = lax.dynamic_slice_in_dim(panels, other_off, width, axis=2)
            mod_out = lax.dynamic_slice_in_dim(model, other_off, width, axis=1)
            x_msg = jnp.concatenate(
                [
                    pan_out.reshape(own_cols * modes, width),
                    mod_out,
                    pack_rows(lengths_of(p_idx).reshape(-1), width),
                ],
                axis=0,
            )
            x_got = lax.ppermute(x_msg, "cols", [(0, 1), (1, 0)])
            n_pan = own_cols * modes
            pan_nb = x_got[:n_pan].reshape(own_cols, modes, width)
            mod_nb = x_got[n_pan:n_pan + own_cols]
            len_nb_own = x_got[n_pan + own_cols:].reshape(-1)[:n_len].reshape(path_rows, own_cols)
            pan_mine = lax.dynamic_slice_in_dim(panels, own_off, width, axis=2)
            mod_mine = lax.dynamic_slice_in_dim(model, own_off, width, axis=1)
            col_panels = [pan_mine, pan_nb]
            scaled2 = jnp.concatenate([scale(pan_mine, mod_mine), scale(pan_nb, mod_nb)], axis=0)
            scaled2 = scaled2.reshape(n_sets * own_cols * modes, width)
        else:
            head = depth_weight
            col_panels = [panels]
            scaled2 = scale(panels, model).reshape(own_cols * modes, width)

        blocks = [(head, [lengths_of(p_idx)] + ([len_nb_own] if split else []), mode_index)]
        for shift in range(1, n_paths):
            target = (p_idx + shift) % n_paths
            payload = jnp.concatenate([head, pack_rows(small_for(target), width)], axis=0)
            perm = [(i, (i + shift) % n_paths) for i in range(n_paths)]
            got = lax.ppermute(payload, "paths", perm)
            sm = got[path_rows:].reshape(-1)
            lens = [sm[:n_len].reshape(path_rows, own_cols)]
            if split:
                diag = [
                    (q * n_cols + c, ((q + shift) % n_paths) * n_cols + (1 - c))
                    for q in range(n_paths)
                    for c in range(n_cols)
                ]
                lens.append(
                    lax.ppermute(pack_rows(lengths_of(target).reshape(-1), width), ("paths", "cols"), diag)
                    .reshape(-1)[:n_len]
                    .reshape(path_rows, own_cols)
                )
            mi_b = sm[n_len:n_len + n_mi].reshape(path_rows, kept).astype(jnp.int32)
            blocks.append((got[:path_rows], lens, mi_b))
        mode_ids = lax.iota(jnp.int32, modes)

        unpacked = []
        parts = []
        for s, (dw_b, lens, mi_b) in enumerate(blocks):
            len_all = jnp.concatenate(lens, axis=1).astype(f32)
            one_hot = (mi_b[:, :, None] == mode_ids[None, None, :]).astype(f32)
            unpacked.append((dw_b, len_all, one_hot))
            weighted = lax.dot_general(
                dw_b, scaled2, (((1,), (1,)), ((), ())), preferred_element_type=f32
            ).reshape(path_rows, n_sets * own_cols, modes)
            per_mode = jnp.sum(len_all[:, :, None] * weighted, axis=1)
            part = jnp.sum(one_hot * per_mode[:, None, :], axis=2)
            parts.append(part.T)
        first = (c_idx == 0) & (d_idx == 0)
        parts[0] = parts[0] - jnp.where(first, observed.T, jnp.zeros_like(observed.T))
        canon = place_by_source(parts, p_idx, n_paths)

        local = n_cols * n_depth
        if local & (local - 1) == 0:
            misfit_all = butterfly_sum(canon, ("cols", "depth"), local)
        else:
            misfit_all = exchange_sum(canon, ("cols", "depth"), local)
        misfit_all = exchange_sum(misfit_all, "paths", n_paths)
        misfit = lax.dynamic_index_in_dim(misfit_all, p_idx, 0, keepdims=False).T

        summed = None
        for s, (dw_b, len_all, one_hot) in enumerate(unpacked):
            mis_b = lax.dynamic_index_in_dim(misfit_all, (p_idx - s) % n_paths, 0, keepdims=False)
            resid = jnp.sum(mis_b.T[:, :, None] * one_hot, axis=1)
            spread = (len_all[:, :, None] * resid[:, None, :]).astype(bf16)
            spread = spread.reshape(path_rows, n_sets * own_cols * modes)
            term = lax.dot_general(
                spread, dw_b, (((0,), (0,)), ((), ())), preferred_element_type=f32
            )
            summed = term if summed is None else summed + term
        summed = summed.reshape(n_sets, own_cols, modes, width)
        grads = [
            jnp.sum(summed[j] * col_panels[j].astype(f32), axis=1) for j in range(n_sets)
        ]
        if split:
            back = lax.ppermute(grads[1], "cols", [(0, 1), (1, 0)])
            gradient = jnp.zeros((own_cols, depth_half), f32)
            gradient = lax.dynamic_update_slice_in_dim(gradient, grads[0], own_off, axis=1)
            gradient = lax.dynamic_update_slice_in_dim(gradient, back, other_off, axis=1)
        else:
            gradient = grads[0]
        return (gradient, misfit)

    return shards


def solution(mesh):
    shards = make_shards(mesh.shape["paths"], mesh.shape["cols"], mesh.shape["depth"])
    return jax.shard_map(
        shards,
        mesh=mesh,
        in_specs=(
            P(("groups", "cols", "paths"), None, "depth"),
            P(("groups", "cols", "paths"), "depth"),
            P(("groups", "paths"), "depth"),
            P(("groups", "paths"), "cols"),
            P(("groups", "paths")),
            P(("groups", "paths")),
            P(("groups", "paths"), None),
            P(("groups", "paths"), None),
        ),
        out_specs=(P(("groups", "cols", "paths"), "depth"), P(("groups", "paths"), None)),
        check_vma=False,
    )
```

time: 44.1 us -> 48.1 us (1.091)
  starting transfers between devices: 15 us -> 20.7 us
  waiting for transfers between devices: 15.7 us -> 13.8 us
  local copies, waits for them, and re-layouts: 7.1 us -> 8.71 us
  matrix products: 3.79 us -> 2.26 us
    ppermute x3 -> x5, starting transfers between devices: 3.71 us -> 11.1 us  [the longest x3 6.55 us: shards(): lax.ppermute(pack_rows(lengths_of(target).reshape(-1), width), ('paths',...]
    ppermute x3, starting transfers between devices: 6.11 us -> 3.72 us  [shards(): got = lax.ppermute(payload, 'paths', perm)]
    ppermute x3, waiting for transfers between devices: 6.47 us -> 4.6 us  [shards(): got = lax.ppermute(payload, 'paths', perm)]
    concatenate x0 -> x14, local copies, waits for them, and re-layouts: none -> 1.72 us  [shards(): len_all = jnp.concatenate(lens, axis=1).astype(f32)]
    dot_general x16 -> x8, matrix products: 3.79 us -> 2.26 us  [the longest x4 1.22 us: shards(): lax.dot_general(dw_b, scaled2, (((1,), (1,)), ((), ())), preferred_elemen...]
    ppermute x3, waiting for transfers between devices: 2.26 us -> 3.43 us  [shifted_copies(): copies.append(lax.ppermute(x, axes, perm))]
    dynamic_slice x4 -> x7, local copies, waits for them, and re-layouts: 0.44 us -> 1.55 us  [the longest x1 0.95 us: shards(): pan_out = lax.dynamic_slice_in_dim(panels, other_off, width, axis=2)]
    ppermute x3 -> x5, waiting for transfers between devices: 3.32 us -> 2.46 us  [the longest x1 2.2 us: shards(): back = lax.ppermute(grads[1], 'cols', [(0, 1), (1, 0)])]
  transfers between devices with their start and end apart: 11 -> 13, of which waited for: 8 -> 8; matrix products, arithmetic and copies ran while one was open for 8% -> 8% of each run, Pallas kernels for 0% -> 0%
where the time goes in v6:
time: 48.1 us; the launch traced here: 47.8 us
  starting transfers between devices  20.7 us (43%)
  waiting for transfers between devices  13.8 us (29%)
  local copies, waits for them, and re-layouts  8.71 us (18%)
  matrix products  2.26 us (5%)
  between operations  1.33 us (3%)
  other arithmetic  1.07 us (2%)
    ppermute x3, starting transfers between devices, shards(): lax.ppermute(pack_rows(lengths_of(target).reshape(-1), width), ('paths',...  6.55 us
    ppermute x3, waiting for transfers between devices, shards(): got = lax.ppermute(payload, 'paths', perm)  4.6 us
    ppermute x3, starting transfers between devices, shifted_copies(): copies.append(lax.ppermute(x, axes, perm))  4.21 us
    ppermute x3, starting transfers between devices, shards(): got = lax.ppermute(payload, 'paths', perm)  3.72 us
    ppermute x3, waiting for transfers between devices, shifted_copies(): copies.append(lax.ppermute(x, axes, perm))  3.43 us
    ppermute x2, waiting for transfers between devices, butterfly_sum(): x = x + lax.ppermute(x, axes, perm)  3.3 us
    ppermute x1, starting transfers between devices, shards(): x_got = lax.ppermute(x_msg, 'cols', [(0, 1), (1, 0)])  3 us
    unnamed x18, local copies, waits for them, and re-layouts  2.64 us
  transfers between devices with their start and end apart: 13, of which 8 were waited for; matrix products, arithmetic and copies ran while one was open for 8% of the time, Pallas kernels for 0%

profile of v6, /device:TPU:0, one launch (start us, length us, event | category | flops | bytes accessed | tf_op | source)
XLA Modules:
  0.0 47.8 jit_solution(15510067475214942363)
XLA Ops:
  0.8 0.7 %copy-done.4 = bf16[256,24]{0,1:T(8,128)(2,1)S(1)} copy-done((bf16[256,24]{0,1:T(8,128)(2,1)S(1)}, bf16[256,24]{0,1:T(8,128)(2,1)}, u32[]{:S(2)}) %copy-start.4) | copy-done | bytes 12312
  1.9 0.9 %constant_dynamic-slice_fusion.11 = bf16[6,64,256]{2,1,0:T(8,128)(2,1)S(1)} fusion(bf16[6,64,512]{2,1,0:T(8,128)(2,1)} %param.8, s32[]{:T(128)S(6)} %select_n.115), kind=kLoop, calls=%fused_computation.80 | loop fusion | bytes 393220 | tf_op jit(solution)/shard_map/dynamic_slice | solution.py:77
  2.9 3.0 %collective-permute-start = (bf16[396,256]{1,0:T(8,128)(2,1)S(1)}, bf16[396,256]{1,0:T(8,128)(2,1)S(1)}, u32[]{:S(2)}, u32[]{:S(2)}) collective-permute-start(bf16[396,256]{1,0:T(8,128)(2,1)S(1)} %pad_maximum_fusion.1), channel_id=1, source_target_pairs={{0,2},{2,0},{1,3},{3,1},{4,6},{6,4},{5,7},{7,5},{8,10},{10,8},{9,1... | collective-permute-start | bytes 608264 | tf_op jit(solution)/shard_map/ppermute | solution.py:87
  6.2 1.6 %collective-permute-start.2 = (bf16[6,256]{1,0:T(8,128)(2,1)S(1)}, bf16[6,256]{1,0:T(8,128)(2,1)S(1)}, u32[]{:S(2)}, u32[]{:S(2)}) collective-permute-start(bf16[6,256]{1,0:T(8,128)(2,1)S(1)} %reshape.226), channel_id=1, source_target_pairs={{0,6},{2,4},{4,10},{6,8},{8,14},{10,12},{12,2},{14,0},{1,7},{3,5},... | collective-permute-start | bytes 9224 | tf_op jit(solution)/shard_map/ppermute | solution.py:117
  8.0 0.7 %copy-done.2 = s32[256,4]{0,1:T(4,128)S(1)} copy-done((s32[256,4]{0,1:T(4,128)S(1)}, s32[256,4]{0,1:T(4,128)}, u32[]{:S(2)}) %copy-start.2) | copy-done | bytes 4120
  9.6 1.6 %collective-permute-start.1 = (bf16[266,256]{1,0:T(8,128)(2,1)S(1)}, bf16[266,256]{1,0:T(8,128)(2,1)S(1)}, u32[]{:S(2)}, u32[]{:S(2)}) collective-permute-start(bf16[266,256]{1,0:T(8,128)(2,1)S(1)} %get-tuple-element.10), channel_id=1, source_target_pairs={{0,4},{4,8},{8,12},{12,0},{1,5},{5,9},{9,13},{13,1},{2,6},{6,10},{... | collective-permute-start | bytes 408584 | tf_op jit(solution)/shard_map/ppermute | solution.py:107
  11.4 2.2 %collective-permute-start.4 = (bf16[6,256]{1,0:T(8,128)(2,1)S(1)}, bf16[6,256]{1,0:T(8,128)(2,1)S(1)}, u32[]{:S(2)}, u32[]{:S(2)}) collective-permute-start(bf16[6,256]{1,0:T(8,128)(2,1)S(1)} %reshape.229), channel_id=1, source_target_pairs={{0,10},{2,8},{4,14},{6,12},{8,2},{10,0},{12,6},{14,4},{1,11},{3,9}... | collective-permute-start | bytes 9224 | tf_op jit(solution)/shard_map/ppermute | solution.py:117
  13.8 2.7 %collective-permute-start.6 = (bf16[6,256]{1,0:T(8,128)(2,1)S(1)}, bf16[6,256]{1,0:T(8,128)(2,1)S(1)}, u32[]{:S(2)}, u32[]{:S(2)}) collective-permute-start(bf16[6,256]{1,0:T(8,128)(2,1)S(1)} %reshape.232), channel_id=1, source_target_pairs={{0,14},{2,12},{4,2},{6,0},{8,6},{10,4},{12,10},{14,8},{1,15},{3,13... | collective-permute-start | bytes 9224 | tf_op jit(solution)/shard_map/ppermute | solution.py:117
  16.6 0.4 collective-permute-start.3
  17.5 1.7 %collective-permute-start.5 = (bf16[266,256]{1,0:T(8,128)(2,1)S(1)}, bf16[266,256]{1,0:T(8,128)(2,1)S(1)}, u32[]{:S(2)}, u32[]{:S(2)}) collective-permute-start(bf16[266,256]{1,0:T(8,128)(2,1)S(1)} %get-tuple-element.8), channel_id=1, source_target_pairs={{0,12},{4,0},{8,4},{12,8},{1,13},{5,1},{9,5},{13,9},{2,14},{6,2},{... | collective-permute-start | bytes 408584 | tf_op jit(solution)/shard_map/ppermute | solution.py:107
  20.3 4.6 %collective-permute-done.3 = bf16[266,256]{1,0:T(8,128)(2,1)S(1)} collective-permute-done((bf16[266,256]{1,0:T(8,128)(2,1)S(1)}, bf16[266,256]{1,0:T(8,128)(2,1)S(1)}, u32[]{:S(2)}, u32[]{:S(2)}) %collective-permute-start.3) | collective-permute-done | bytes 136224 | tf_op jit(solution)/shard_map/ppermute | solution.py:107
  26.3 0.3 fusion.1
  26.7 0.3 fusion.2
  27.0 0.3 fusion.3
  27.4 0.3 fusion.4
  27.8 0.7 %copy-done.6 = f32[256,4]{0,1:T(4,128)S(1)} copy-done((f32[256,4]{0,1:T(4,128)S(1)}, f32[256,4]{0,1:T(4,128)}, u32[]{:S(2)}) %copy-start.6) | copy-done | bytes 4120
  28.6 1.2 %collective-permute-done.7 = f32[4,4,256]{2,1,0:T(4,128)S(1)} collective-permute-done((f32[4,4,256]{2,1,0:T(4,128)S(1)}, f32[4,4,256]{2,1,0:T(4,128)S(1)}, u32[]{:S(2)}, u32[]{:S(2)}) %collective-permute-start.7) | collective-permute-done | bytes 16416 | tf_op jit(solution)/shard_map/ppermute | solution.py:31
  29.7 1.6 %collective-permute-start.8 = (f32[4,4,256]{2,1,0:T(4,128)S(1)}, f32[4,4,256]{2,1,0:T(4,128)S(1)}, u32[]{:S(2)}, u32[]{:S(2)}) collective-permute-start(f32[4,4,256]{2,1,0:T(4,128)S(1)} %add.142), channel_id=1, source_target_pairs={{0,2},{1,3},{2,0},{3,1},{4,6},{5,7},{6,4},{7,5},{8,10},{9,11},{10,... | collective-permute-start | bytes 49160 | tf_op jit(solution)/shard_map/ppermute | solution.py:31
  31.3 2.1 %collective-permute-done.8 = f32[4,4,256]{2,1,0:T(4,128)S(1)} collective-permute-done((f32[4,4,256]{2,1,0:T(4,128)S(1)}, f32[4,4,256]{2,1,0:T(4,128)S(1)}, u32[]{:S(2)}, u32[]{:S(2)}) %collective-permute-start.8) | collective-permute-done | bytes 16416 | tf_op jit(solution)/shard_map/ppermute | solution.py:31
  33.5 1.8 %collective-permute-start.9 = (f32[4,4,256]{2,1,0:T(4,128)S(1)}, f32[4,4,256]{2,1,0:T(4,128)S(1)}, u32[]{:S(2)}, u32[]{:S(2)}) collective-permute-start(f32[4,4,256]{2,1,0:T(4,128)S(1)} %get-tuple-element.3), channel_id=1, source_target_pairs={{0,4},{4,8},{8,12},{12,0},{1,5},{5,9},{9,13},{13,1},{2,6},{6,10},{... | collective-permute-start | bytes 49160 | tf_op jit(solution)/shard_map/ppermute | solution.py:11
  35.3 2.2 %collective-permute-start.10 = (f32[4,4,256]{2,1,0:T(4,128)S(1)}, f32[4,4,256]{2,1,0:T(4,128)S(1)}, u32[]{:S(2)}, u32[]{:S(2)}) collective-permute-start(f32[4,4,256]{2,1,0:T(4,128)S(1)} %get-tuple-element.3), channel_id=1, source_target_pairs={{0,8},{4,12},{8,0},{12,4},{1,9},{5,13},{9,1},{13,5},{2,10},{6,14},... | collective-permute-start | bytes 49160 | tf_op jit(solution)/shard_map/ppermute | solution.py:11
  37.4 0.3 collective-permute-start.11
  37.7 1.4 %collective-permute-done.9 = f32[4,4,256]{2,1,0:T(4,128)S(1)} collective-permute-done((f32[4,4,256]{2,1,0:T(4,128)S(1)}, f32[4,4,256]{2,1,0:T(4,128)S(1)}, u32[]{:S(2)}, u32[]{:S(2)}) %collective-permute-start.9) | collective-permute-done | bytes 16416 | tf_op jit(solution)/shard_map/ppermute | solution.py:11
  39.1 0.8 %collective-permute-done.10 = f32[4,4,256]{2,1,0:T(4,128)S(1)} collective-permute-done((f32[4,4,256]{2,1,0:T(4,128)S(1)}, f32[4,4,256]{2,1,0:T(4,128)S(1)}, u32[]{:S(2)}, u32[]{:S(2)}) %collective-permute-start.10) | collective-permute-done | bytes 16416 | tf_op jit(solution)/shard_map/ppermute | solution.py:11
  39.9 1.2 %collective-permute-done.11 = f32[4,4,256]{2,1,0:T(4,128)S(1)} collective-permute-done((f32[4,4,256]{2,1,0:T(4,128)S(1)}, f32[4,4,256]{2,1,0:T(4,128)S(1)}, u32[]{:S(2)}, u32[]{:S(2)}) %collective-permute-start.11) | collective-permute-done | bytes 16416 | tf_op jit(solution)/shard_map/ppermute | solution.py:11
  41.2 0.6 %fusion.25 = (f32[256,4]{0,1:T(4,128)}, f32[256,4]{0,1:T(4,128)S(1)}, f32[256,4]{0,1:T(4,128)S(1)}, f32[256,4]{0,1:T(4,128)S(1)}, f32[256,4]{0,1:T(4,128)S(1)}) fusion(f32[4,4,256]{2,1,0:T(4,128)S(1)} %reduce_sum.143, s32[]{:T(128)S(6)} %select_n.133, s32[]{:T(128)S(6)} %select_n.132, s32[]{:T(128)S(6)} %select_n.128, s32[]{:T(128)S(6)} %select_n.124, ...), kind=kLoop, calls=%fused_computation.87 | loop fusion | bytes 40980 | tf_op jit(solution)/shard_map/transpose | solution.py:147
  42.5 0.3 fusion.13
  42.8 0.3 convolution_add_fusion.1
  43.0 0.3 fusion
  43.5 1.5 %collective-permute-start.12 = (f32[6,256]{1,0:T(8,128)S(1)}, f32[6,256]{1,0:T(8,128)S(1)}, u32[]{:S(2)}, u32[]{:S(2)}) collective-permute-start(f32[6,256]{1,0:T(8,128)S(1)} %fusion.8), channel_id=1, source_target_pairs={{0,2},{2,0},{1,3},{3,1},{4,6},{6,4},{5,7},{7,5},{8,10},{10,8},{9,1... | collective-permute-start | bytes 18440 | tf_op jit(solution)/shard_map/ppermute | solution.py:164
  45.0 2.2 %collective-permute-done.12 = f32[6,256]{1,0:T(8,128)S(1)} collective-permute-done((f32[6,256]{1,0:T(8,128)S(1)}, f32[6,256]{1,0:T(8,128)S(1)}, u32[]{:S(2)}, u32[]{:S(2)}) %collective-permute-start.12) | collective-permute-done | bytes 6176 | tf_op jit(solution)/shard_map/ppermute | solution.py:164
  47.2 0.6 %copy-done.3 = f32[6,512]{1,0:T(8,128)} copy-done((f32[6,512]{1,0:T(8,128)}, f32[6,512]{1,0:T(8,128)S(1)}, u32[]{:S(2)}) %copy-start.3) | copy-done | bytes 12312
  (109 shorter events, 6.2 us)
Async XLA Ops:
  0.6 7.3 %copy-start = (bf16[256,512]{1,0:T(8,128)(2,1)S(1)}, bf16[256,512]{1,0:T(8,128)(2,1)}, u32[]{:S(2)}) copy-start(bf16[256,512]{1,0:T(8,128)(2,1)} %param.10) | copy-start | bytes 786436
  0.7 0.7 %copy-start.4 = (bf16[256,24]{0,1:T(8,128)(2,1)S(1)}, bf16[256,24]{0,1:T(8,128)(2,1)}, u32[]{:S(2)}) copy-start(bf16[256,24]{0,1:T(8,128)(2,1)} %param.11) | copy-start | bytes 36868
  0.7 0.7 %copy-start.7 = (s32[256]{0:T(256)S(1)}, s32[256]{0:T(256)}, u32[]{:S(2)}) copy-start(s32[256]{0:T(256)} %param.13) | copy-start | bytes 3076
  0.7 0.7 %copy-start.8 = (s32[256]{0:T(256)S(1)}, s32[256]{0:T(256)}, u32[]{:S(2)}) copy-start(s32[256]{0:T(256)} %param.12) | copy-start | bytes 3076
  1.8 1.0 %copy-start.5 = (bf16[6,512]{1,0:T(8,128)(2,1)S(1)}, bf16[6,512]{1,0:T(8,128)(2,1)}, u32[]{:S(2)}) copy-start(bf16[6,512]{1,0:T(8,128)(2,1)} %param.9) | copy-start | bytes 18436
  2.9 23.1 %collective-permute-start = (bf16[396,256]{1,0:T(8,128)(2,1)S(1)}, bf16[396,256]{1,0:T(8,128)(2,1)S(1)}, u32[]{:S(2)}, u32[]{:S(2)}) collective-permute-start(bf16[396,256]{1,0:T(8,128)(2,1)S(1)} %pad_maximum_fusion.1), channel_id=1, source_target_pairs={{0,2},{2,0},{1,3},{3,1},{4,6},{6,4},{5,7},{7,5},{8,10},{10,8},{9,1... | collective-permute-start | bytes 608264 | tf_op jit(solution)/shard_map/ppermute | solution.py:87
  6.2 10.5 %collective-permute-start.2 = (bf16[6,256]{1,0:T(8,128)(2,1)S(1)}, bf16[6,256]{1,0:T(8,128)(2,1)S(1)}, u32[]{:S(2)}, u32[]{:S(2)}) collective-permute-start(bf16[6,256]{1,0:T(8,128)(2,1)S(1)} %reshape.226), channel_id=1, source_target_pairs={{0,6},{2,4},{4,10},{6,8},{8,14},{10,12},{12,2},{14,0},{1,7},{3,5},... | collective-permute-start | bytes 9224 | tf_op jit(solution)/shard_map/ppermute | solution.py:117
  7.9 0.7 %copy-start.2 = (s32[256,4]{0,1:T(4,128)S(1)}, s32[256,4]{0,1:T(4,128)}, u32[]{:S(2)}) copy-start(s32[256,4]{0,1:T(4,128)} %param.14) | copy-start | bytes 12292
  9.5 7.0 %copy-start.1 = (bf16[6,64,512]{2,1,0:T(8,128)(2,1)S(1)}, bf16[6,64,512]{2,1,0:T(8,128)(2,1)}, u32[]{:S(2)}) copy-start(bf16[6,64,512]{2,1,0:T(8,128)(2,1)} %param.8) | copy-start | bytes 1179652
  9.6 10.1 %collective-permute-start.1 = (bf16[266,256]{1,0:T(8,128)(2,1)S(1)}, bf16[266,256]{1,0:T(8,128)(2,1)S(1)}, u32[]{:S(2)}, u32[]{:S(2)}) collective-permute-start(bf16[266,256]{1,0:T(8,128)(2,1)S(1)} %get-tuple-element.10), channel_id=1, source_target_pairs={{0,4},{4,8},{8,12},{12,0},{1,5},{5,9},{9,13},{13,1},{2,6},{6,10},{... | collective-permute-start | bytes 408584 | tf_op jit(solution)/shard_map/ppermute | solution.py:107
  11.4 6.1 %collective-permute-start.4 = (bf16[6,256]{1,0:T(8,128)(2,1)S(1)}, bf16[6,256]{1,0:T(8,128)(2,1)S(1)}, u32[]{:S(2)}, u32[]{:S(2)}) collective-permute-start(bf16[6,256]{1,0:T(8,128)(2,1)S(1)} %reshape.229), channel_id=1, source_target_pairs={{0,10},{2,8},{4,14},{6,12},{8,2},{10,0},{12,6},{14,4},{1,11},{3,9}... | collective-permute-start | bytes 9224 | tf_op jit(solution)/shard_map/ppermute | solution.py:117
  13.8 5.7 %collective-permute-start.6 = (bf16[6,256]{1,0:T(8,128)(2,1)S(1)}, bf16[6,256]{1,0:T(8,128)(2,1)S(1)}, u32[]{:S(2)}, u32[]{:S(2)}) collective-permute-start(bf16[6,256]{1,0:T(8,128)(2,1)S(1)} %reshape.232), channel_id=1, source_target_pairs={{0,14},{2,12},{4,2},{6,0},{8,6},{10,4},{12,10},{14,8},{1,15},{3,13... | collective-permute-start | bytes 9224 | tf_op jit(solution)/shard_map/ppermute | solution.py:117
  16.6 8.2 %collective-permute-start.3 = (bf16[266,256]{1,0:T(8,128)(2,1)S(1)}, bf16[266,256]{1,0:T(8,128)(2,1)S(1)}, u32[]{:S(2)}, u32[]{:S(2)}) collective-permute-start(bf16[266,256]{1,0:T(8,128)(2,1)S(1)} %get-tuple-element.9), channel_id=1, source_target_pairs={{0,8},{4,12},{8,0},{12,4},{1,9},{5,13},{9,1},{13,5},{2,10},{6,14},... | collective-permute-start | bytes 408584 | tf_op jit(solution)/shard_map/ppermute | solution.py:107
  17.5 7.8 %collective-permute-start.5 = (bf16[266,256]{1,0:T(8,128)(2,1)S(1)}, bf16[266,256]{1,0:T(8,128)(2,1)S(1)}, u32[]{:S(2)}, u32[]{:S(2)}) collective-permute-start(bf16[266,256]{1,0:T(8,128)(2,1)S(1)} %get-tuple-element.8), channel_id=1, source_target_pairs={{0,12},{4,0},{8,4},{12,8},{1,13},{5,1},{9,5},{13,9},{2,14},{6,2},{... | collective-permute-start | bytes 408584 | tf_op jit(solution)/shard_map/ppermute | solution.py:107
  27.7 0.7 %copy-start.6 = (f32[256,4]{0,1:T(4,128)S(1)}, f32[256,4]{0,1:T(4,128)}, u32[]{:S(2)}) copy-start(f32[256,4]{0,1:T(4,128)} %param.15) | copy-start | bytes 12292
  28.5 1.2 %collective-permute-start.7 = (f32[4,4,256]{2,1,0:T(4,128)S(1)}, f32[4,4,256]{2,1,0:T(4,128)S(1)}, u32[]{:S(2)}, u32[]{:S(2)}) collective-permute-start(f32[4,4,256]{2,1,0:T(4,128)S(1)} %constant_dynamic-update-slice_fusion.2), channel_id=1, source_target_pairs={{0,1},{1,0},{2,3},{3,2},{4,5},{5,4},{6,7},{7,6},{8,9},{9,8},{10,11... | collective-permute-start | bytes 49160 | tf_op jit(solution)/shard_map/ppermute | solution.py:31
  29.7 3.7 %collective-permute-start.8 = (f32[4,4,256]{2,1,0:T(4,128)S(1)}, f32[4,4,256]{2,1,0:T(4,128)S(1)}, u32[]{:S(2)}, u32[]{:S(2)}) collective-permute-start(f32[4,4,256]{2,1,0:T(4,128)S(1)} %add.142), channel_id=1, source_target_pairs={{0,2},{1,3},{2,0},{3,1},{4,6},{5,7},{6,4},{7,5},{8,10},{9,11},{10,... | collective-permute-start | bytes 49160 | tf_op jit(solution)/shard_map/ppermute | solution.py:31
  33.5 5.6 %collective-permute-start.9 = (f32[4,4,256]{2,1,0:T(4,128)S(1)}, f32[4,4,256]{2,1,0:T(4,128)S(1)}, u32[]{:S(2)}, u32[]{:S(2)}) collective-permute-start(f32[4,4,256]{2,1,0:T(4,128)S(1)} %get-tuple-element.3), channel_id=1, source_target_pairs={{0,4},{4,8},{8,12},{12,0},{1,5},{5,9},{9,13},{13,1},{2,6},{6,10},{... | collective-permute-start | bytes 49160 | tf_op jit(solution)/shard_map/ppermute | solution.py:11
  35.3 4.6 %collective-permute-start.10 = (f32[4,4,256]{2,1,0:T(4,128)S(1)}, f32[4,4,256]{2,1,0:T(4,128)S(1)}, u32[]{:S(2)}, u32[]{:S(2)}) collective-permute-start(f32[4,4,256]{2,1,0:T(4,128)S(1)} %get-tuple-element.3), channel_id=1, source_target_pairs={{0,8},{4,12},{8,0},{12,4},{1,9},{5,13},{9,1},{13,5},{2,10},{6,14},... | collective-permute-start | bytes 49160 | tf_op jit(solution)/shard_map/ppermute | solution.py:11
  37.4 3.7 %collective-permute-start.11 = (f32[4,4,256]{2,1,0:T(4,128)S(1)}, f32[4,4,256]{2,1,0:T(4,128)S(1)}, u32[]{:S(2)}, u32[]{:S(2)}) collective-permute-start(f32[4,4,256]{2,1,0:T(4,128)S(1)} %get-tuple-element.3), channel_id=1, source_target_pairs={{0,12},{4,0},{8,4},{12,8},{1,13},{5,1},{9,5},{13,9},{2,14},{6,2},{... | collective-permute-start | bytes 49160 | tf_op jit(solution)/shard_map/ppermute | solution.py:11
  43.5 3.7 %collective-permute-start.12 = (f32[6,256]{1,0:T(8,128)S(1)}, f32[6,256]{1,0:T(8,128)S(1)}, u32[]{:S(2)}, u32[]{:S(2)}) collective-permute-start(f32[6,256]{1,0:T(8,128)S(1)} %fusion.8), channel_id=1, source_target_pairs={{0,2},{2,0},{1,3},{3,1},{4,6},{6,4},{5,7},{7,5},{8,10},{10,8},{9,1... | collective-permute-start | bytes 18440 | tf_op jit(solution)/shard_map/ppermute | solution.py:164
  47.2 0.6 %copy-start.3 = (f32[6,512]{1,0:T(8,128)}, f32[6,512]{1,0:T(8,128)S(1)}, u32[]{:S(2)}) copy-start(f32[6,512]{1,0:T(8,128)S(1)} %constant_dynamic-update-slice_fusion) | copy-start | bytes 36868

commit v7 on v5

--- a/solution.py
+++ b/solution.py
@@ -116,20 +116,23 @@
             misfit_all = exchange_sum(canon, ("cols", "depth"), local)
         misfit_all = exchange_sum(misfit_all, "paths", n_paths)
         misfit = lax.dynamic_index_in_dim(misfit_all, p_idx, 0, keepdims=False).T
-        mis_shift = [
-            lax.dynamic_index_in_dim(misfit_all, (p_idx - s) % n_paths, 0, keepdims=False)
-            for s in range(n_paths)
-        ]
-        summed = [None] * len(offsets)
-        for s, (dw_parts, len_own, one_hot) in enumerate(unpacked):
-            resid = jnp.sum(mis_shift[s].T[:, :, None] * one_hot, axis=1)
-            spread = (len_own[:, :, None] * resid[:, None, :]).astype(bf16)
-            spread = spread.reshape(path_rows, own_cols * modes)
-            for j, dw_part in enumerate(dw_parts):
-                term = lax.dot_general(
-                    spread, dw_part, (((0,), (0,)), ((), ())), preferred_element_type=f32
+        rev = list(reversed(range(n_paths)))
+        doubled = jnp.concatenate([misfit_all, misfit_all], axis=0)
+        mis_rev = lax.dynamic_slice_in_dim(doubled, (p_idx + 1) % n_paths, n_paths, axis=0)
+        mis_rows = jnp.swapaxes(mis_rev, 1, 2).reshape(n_paths * path_rows, kept)
+        len_all = jnp.concatenate([unpacked[s][1] for s in rev], axis=0)
+        hot_all = jnp.concatenate([unpacked[s][2] for s in rev], axis=0)
+        resid = jnp.sum(mis_rows[:, :, None] * hot_all, axis=1)
+        spread = (len_all[:, :, None] * resid[:, None, :]).astype(bf16)
+        spread = spread.reshape(n_paths * path_rows, own_cols * modes)
+        summed = []
+        for j in range(len(offsets)):
+            dw_all = jnp.concatenate([unpacked[s][0][j] for s in rev], axis=0)
+            summed.append(
+                lax.dot_general(
+                    spread, dw_all, (((0,), (0,)), ((), ())), preferred_element_type=f32
                 )
-                summed[j] = term if summed[j] is None else summed[j] + term
+            )
         grads = []
         for acc, off in zip(summed, offsets):
             panel_part = lax.dynamic_slice_in_dim(panels, off, width, axis=2).astype(f32)

time: 44.1 us -> 43.5 us (0.986)
  local copies, waits for them, and re-layouts: 7.1 us -> 6.13 us
  matrix products: 3.79 us -> 2.83 us
  other arithmetic: 0.98 us -> 1.74 us
  waiting for transfers between devices: 15.7 us -> 16.3 us
    unnamed x18 -> x14, local copies, waits for them, and re-layouts: 3.21 us -> 1.58 us
    dot_general x8 -> x2, matrix products: 1.71 us -> 0.77 us  [shards(): lax.dot_general(spread, dw_all, (((0,), (0,)), ((), ())), preferred_eleme...]
    ppermute x3, waiting for transfers between devices: 6.47 us -> 7.28 us  [shards(): got = lax.ppermute(payload, 'paths', perm)]
    select_n x1, other arithmetic: 0.07 us -> 0.83 us  [shards(): lengths = jnp.where(inside, seg_len, jnp.zeros_like(seg_len))]
    dynamic_slice x1, local copies, waits for them, and re-layouts: 0.02 us -> 0.66 us  [shards(): theirs = lax.dynamic_slice_in_dim(depth_weight, other_off, width, axis=1)]
  transfers between devices with their start and end apart: 11 -> 11, of which waited for: 8 -> 8; matrix products, arithmetic and copies ran while one was open for 8% -> 9% of each run, Pallas kernels for 0% -> 0%
where the time goes in v7:
time: 43.5 us; the launch traced here: 43.3 us
  waiting for transfers between devices  16.3 us (37%)
  starting transfers between devices  15.1 us (35%)
  local copies, waits for them, and re-layouts  6.13 us (14%)
  matrix products  2.83 us (7%)
  other arithmetic  1.74 us (4%)
  between operations  1.2 us (3%)
    ppermute x3, waiting for transfers between devices, shards(): got = lax.ppermute(payload, 'paths', perm)  7.28 us
    ppermute x3, starting transfers between devices, shards(): got = lax.ppermute(payload, 'paths', perm)  6.11 us
    ppermute x3, starting transfers between devices, shifted_copies(): copies.append(lax.ppermute(x, axes, perm))  3.92 us
    ppermute x3, starting transfers between devices, shards(): dw_parts.append(lax.ppermute(part_rows, 'cols', [(0, 1), (1, 0)]))  3.71 us
    ppermute x2, waiting for transfers between devices, butterfly_sum(): x = x + lax.ppermute(x, axes, perm)  3.54 us
    ppermute x3, waiting for transfers between devices, shards(): dw_parts.append(lax.ppermute(part_rows, 'cols', [(0, 1), (1, 0)]))  3.26 us
    ppermute x3, waiting for transfers between devices, shifted_copies(): copies.append(lax.ppermute(x, axes, perm))  2.2 us
    dot_general x8, matrix products, shards(): lax.dot_general(dw_part, sc_part, (((1,), (1,)), ((), ())), preferred_ele...  2.06 us
  transfers between devices with their start and end apart: 11, of which 8 were waited for; matrix products, arithmetic and copies ran while one was open for 9% of the time, Pallas kernels for 0%

profile of v7, /device:TPU:0, one launch (start us, length us, event | category | flops | bytes accessed | tf_op | source)
XLA Modules:
  0.0 43.3 jit_solution(17719676989194040609)
XLA Ops:
  0.7 0.8 %and_select_fusion = bf16[256,24]{0,1:T(8,128)(2,1)S(1)} fusion(bf16[256,24]{0,1:T(8,128)(2,1)} %param.11, s32[256]{0:T(256)} %param.13, s32[256]{0:T(256)} %param.12, s32[24]{0:T(128)S(1)} %iota_add_fusion), kind=kLoop, calls=%fused_computation.60 | loop fusion | flops 24576 | bytes 26720 | tf_op jit(solution)/shard_map/jit(_where)/select_n | solution.py:54
  2.9 0.7 %constant_dynamic-slice_fusion.1 = (bf16[256,256]{1,0:T(8,128)(2,1)}, bf16[256,256]{1,0:T(8,128)(2,1)S(1)}) fusion(bf16[256,512]{1,0:T(8,128)(2,1)S(1)} %copy-done, s32[]{:T(128)S(6)} %select_n.112, s32[]{:T(128)S(6)} %select_n.103), kind=kLoop, calls=%fused_computation.83 | loop fusion | bytes 524296 | tf_op jit(solution)/shard_map/dynamic_slice | solution.py:71
  3.6 5.1 %collective-permute-start = (bf16[266,256]{1,0:T(8,128)(2,1)S(1)}, bf16[266,256]{1,0:T(8,128)(2,1)S(1)}, u32[]{:S(2)}, u32[]{:S(2)}) collective-permute-start(bf16[266,256]{1,0:T(8,128)(2,1)S(1)} %get-tuple-element.8), channel_id=1, source_target_pairs={{0,12},{4,0},{8,4},{12,8},{1,13},{5,1},{9,5},{13,9},{2,14},{6,2},{... | collective-permute-start | bytes 408584 | tf_op jit(solution)/shard_map/ppermute | solution.py:82
  8.7 1.0 %collective-permute-start.2 = (bf16[266,256]{1,0:T(8,128)(2,1)S(1)}, bf16[266,256]{1,0:T(8,128)(2,1)S(1)}, u32[]{:S(2)}, u32[]{:S(2)}) collective-permute-start(bf16[266,256]{1,0:T(8,128)(2,1)S(1)} %get-tuple-element.9), channel_id=1, source_target_pairs={{0,4},{4,8},{8,12},{12,0},{1,5},{5,9},{9,13},{13,1},{2,6},{6,10},{... | collective-permute-start | bytes 408584 | tf_op jit(solution)/shard_map/ppermute | solution.py:82
  9.8 0.3 fusion.31
  10.0 0.3 convolution_add_fusion.3
  10.7 0.5 %copy-done.6 = f32[256,4]{0,1:T(4,128)S(1)} copy-done((f32[256,4]{0,1:T(4,128)S(1)}, f32[256,4]{0,1:T(4,128)}, u32[]{:S(2)}) %copy-start.6) | copy-done | bytes 4120
  11.2 1.6 %collective-permute-done = bf16[266,256]{1,0:T(8,128)(2,1)S(1)} collective-permute-done((bf16[266,256]{1,0:T(8,128)(2,1)S(1)}, bf16[266,256]{1,0:T(8,128)(2,1)S(1)}, u32[]{:S(2)}, u32[]{:S(2)}) %collective-permute-start) | collective-permute-done | bytes 136224 | tf_op jit(solution)/shard_map/ppermute | solution.py:82
  12.8 1.6 %collective-permute-start.5 = (bf16[256,256]{1,0:T(8,128)(2,1)S(1)}, bf16[256,256]{1,0:T(8,128)(2,1)S(1)}, u32[]{:S(2)}, u32[]{:S(2)}) collective-permute-start(bf16[256,256]{1,0:T(8,128)(2,1)S(1)} %slice.59), channel_id=1, source_target_pairs={{0,2},{2,0},{1,3},{3,1},{4,6},{6,4},{5,7},{7,5},{8,10},{10,8},{9,1... | collective-permute-start | bytes 393224 | tf_op jit(solution)/shard_map/ppermute | solution.py:86
  14.8 5.7 %collective-permute-done.1 = bf16[266,256]{1,0:T(8,128)(2,1)S(1)} collective-permute-done((bf16[266,256]{1,0:T(8,128)(2,1)S(1)}, bf16[266,256]{1,0:T(8,128)(2,1)S(1)}, u32[]{:S(2)}, u32[]{:S(2)}) %collective-permute-start.1) | collective-permute-done | bytes 136224 | tf_op jit(solution)/shard_map/ppermute | solution.py:82
  20.5 1.6 %collective-permute-start.4 = (bf16[256,256]{1,0:T(8,128)(2,1)S(1)}, bf16[256,256]{1,0:T(8,128)(2,1)S(1)}, u32[]{:S(2)}, u32[]{:S(2)}) collective-permute-start(bf16[256,256]{1,0:T(8,128)(2,1)S(1)} %slice.58), channel_id=1, source_target_pairs={{0,2},{2,0},{1,3},{3,1},{4,6},{6,4},{5,7},{7,5},{8,10},{10,8},{9,1... | collective-permute-start | bytes 393224 | tf_op jit(solution)/shard_map/ppermute | solution.py:86
  22.6 0.6 %collective-permute-start.3 = (bf16[256,256]{1,0:T(8,128)(2,1)S(1)}, bf16[256,256]{1,0:T(8,128)(2,1)S(1)}, u32[]{:S(2)}, u32[]{:S(2)}) collective-permute-start(bf16[256,256]{1,0:T(8,128)(2,1)S(1)} %slice.57), channel_id=1, source_target_pairs={{0,2},{2,0},{1,3},{3,1},{4,6},{6,4},{5,7},{7,5},{8,10},{10,8},{9,1... | collective-permute-start | bytes 393224 | tf_op jit(solution)/shard_map/ppermute | solution.py:86
  23.7 0.3 fusion.21
  24.0 0.3 convolution_add_fusion
  24.4 2.4 %collective-permute-done.4 = bf16[256,256]{1,0:T(8,128)(2,1)S(1)} collective-permute-done((bf16[256,256]{1,0:T(8,128)(2,1)S(1)}, bf16[256,256]{1,0:T(8,128)(2,1)S(1)}, u32[]{:S(2)}, u32[]{:S(2)}) %collective-permute-start.4) | collective-permute-done | bytes 131104 | tf_op jit(solution)/shard_map/ppermute | solution.py:86
  26.8 0.3 fusion.23
  27.0 0.3 convolution_add_fusion.1
  27.5 0.9 %collective-permute-done.3 = bf16[256,256]{1,0:T(8,128)(2,1)S(1)} collective-permute-done((bf16[256,256]{1,0:T(8,128)(2,1)S(1)}, bf16[256,256]{1,0:T(8,128)(2,1)S(1)}, u32[]{:S(2)}, u32[]{:S(2)}) %collective-permute-start.3) | collective-permute-done | bytes 131104 | tf_op jit(solution)/shard_map/ppermute | solution.py:86
  28.3 0.3 fusion.25
  28.6 0.3 convolution_add_fusion.2
  29.5 1.1 %collective-permute-done.6 = f32[4,4,256]{2,1,0:T(4,128)S(1)} collective-permute-done((f32[4,4,256]{2,1,0:T(4,128)S(1)}, f32[4,4,256]{2,1,0:T(4,128)S(1)}, u32[]{:S(2)}, u32[]{:S(2)}) %collective-permute-start.6) | collective-permute-done | bytes 16416 | tf_op jit(solution)/shard_map/ppermute | solution.py:30
  30.6 1.3 %collective-permute-start.7 = (f32[4,4,256]{2,1,0:T(4,128)S(1)}, f32[4,4,256]{2,1,0:T(4,128)S(1)}, u32[]{:S(2)}, u32[]{:S(2)}) collective-permute-start(f32[4,4,256]{2,1,0:T(4,128)S(1)} %add.143), channel_id=1, source_target_pairs={{0,2},{1,3},{2,0},{3,1},{4,6},{5,7},{6,4},{7,5},{8,10},{9,11},{10,... | collective-permute-start | bytes 49160 | tf_op jit(solution)/shard_map/ppermute | solution.py:30
  31.9 2.4 %collective-permute-done.7 = f32[4,4,256]{2,1,0:T(4,128)S(1)} collective-permute-done((f32[4,4,256]{2,1,0:T(4,128)S(1)}, f32[4,4,256]{2,1,0:T(4,128)S(1)}, u32[]{:S(2)}, u32[]{:S(2)}) %collective-permute-start.7) | collective-permute-done | bytes 16416 | tf_op jit(solution)/shard_map/ppermute | solution.py:30
  34.5 1.3 %collective-permute-start.9 = (f32[4,4,256]{2,1,0:T(4,128)S(1)}, f32[4,4,256]{2,1,0:T(4,128)S(1)}, u32[]{:S(2)}, u32[]{:S(2)}) collective-permute-start(f32[4,4,256]{2,1,0:T(4,128)S(1)} %get-tuple-element.3), channel_id=1, source_target_pairs={{0,8},{4,12},{8,0},{12,4},{1,9},{5,13},{9,1},{13,5},{2,10},{6,14},... | collective-permute-start | bytes 49160 | tf_op jit(solution)/shard_map/ppermute | solution.py:10
  35.8 2.5 %collective-permute-start.10 = (f32[4,4,256]{2,1,0:T(4,128)S(1)}, f32[4,4,256]{2,1,0:T(4,128)S(1)}, u32[]{:S(2)}, u32[]{:S(2)}) collective-permute-start(f32[4,4,256]{2,1,0:T(4,128)S(1)} %get-tuple-element.3), channel_id=1, source_target_pairs={{0,12},{4,0},{8,4},{12,8},{1,13},{5,1},{9,5},{13,9},{2,14},{6,2},{... | collective-permute-start | bytes 49160 | tf_op jit(solution)/shard_map/ppermute | solution.py:10
  38.3 1.6 %collective-permute-done.8 = f32[4,4,256]{2,1,0:T(4,128)S(1)} collective-permute-done((f32[4,4,256]{2,1,0:T(4,128)S(1)}, f32[4,4,256]{2,1,0:T(4,128)S(1)}, u32[]{:S(2)}, u32[]{:S(2)}) %collective-permute-start.8) | collective-permute-done | bytes 16416 | tf_op jit(solution)/shard_map/ppermute | solution.py:10
  40.0 0.6 %collective-permute-done.10 = f32[4,4,256]{2,1,0:T(4,128)S(1)} collective-permute-done((f32[4,4,256]{2,1,0:T(4,128)S(1)}, f32[4,4,256]{2,1,0:T(4,128)S(1)}, u32[]{:S(2)}, u32[]{:S(2)}) %collective-permute-start.10) | collective-permute-done | bytes 16416 | tf_op jit(solution)/shard_map/ppermute | solution.py:10
  40.6 0.6 %fusion.43 = f32[256,4]{0,1:T(4,128)} fusion(f32[4,4,256]{2,1,0:T(4,128)S(1)} %reduce_sum.116, s32[]{:T(128)S(6)} %select_n.124), kind=kLoop, calls=%fused_computation.91 | loop fusion | bytes 8196 | tf_op jit(solution)/shard_map/transpose | solution.py:118
  41.4 0.4 fusion
  41.8 0.5 %copy-done.2 = bf16[256,256]{1,0:T(8,128)(2,1)S(1)} copy-done((bf16[256,256]{1,0:T(8,128)(2,1)S(1)}, bf16[256,256]{1,0:T(8,128)(2,1)}, u32[]{:S(2)}) %copy-start.2) | copy-done | bytes 131096
  42.3 0.4 fusion.1
  42.7 0.6 %copy-done.3 = f32[6,512]{1,0:T(8,128)} copy-done((f32[6,512]{1,0:T(8,128)}, f32[6,512]{1,0:T(8,128)S(1)}, u32[]{:S(2)}) %copy-start.3) | copy-done | bytes 12312
  (90 shorter events, 4.3 us)
Async XLA Ops:
  0.6 1.9 %copy-start.5 = (s32[256,4]{0,1:T(4,128)S(1)}, s32[256,4]{0,1:T(4,128)}, u32[]{:S(2)}) copy-start(s32[256,4]{0,1:T(4,128)} %param.14) | copy-start | bytes 12292
  0.7 2.2 %copy-start = (bf16[256,512]{1,0:T(8,128)(2,1)S(1)}, bf16[256,512]{1,0:T(8,128)(2,1)}, u32[]{:S(2)}) copy-start(bf16[256,512]{1,0:T(8,128)(2,1)} %param.10) | copy-start | bytes 786436
  3.5 6.2 %copy-start.4 = (bf16[6,512]{1,0:T(8,128)(2,1)S(1)}, bf16[6,512]{1,0:T(8,128)(2,1)}, u32[]{:S(2)}) copy-start(bf16[6,512]{1,0:T(8,128)(2,1)} %param.9) | copy-start | bytes 18436
  3.5 6.2 %copy-start.1 = (bf16[6,64,512]{2,1,0:T(8,128)(2,1)S(1)}, bf16[6,64,512]{2,1,0:T(8,128)(2,1)}, u32[]{:S(2)}) copy-start(bf16[6,64,512]{2,1,0:T(8,128)(2,1)} %param.8) | copy-start | bytes 1179652
  3.6 9.2 %collective-permute-start = (bf16[266,256]{1,0:T(8,128)(2,1)S(1)}, bf16[266,256]{1,0:T(8,128)(2,1)S(1)}, u32[]{:S(2)}, u32[]{:S(2)}) collective-permute-start(bf16[266,256]{1,0:T(8,128)(2,1)S(1)} %get-tuple-element.8), channel_id=1, source_target_pairs={{0,12},{4,0},{8,4},{12,8},{1,13},{5,1},{9,5},{13,9},{2,14},{6,2},{... | collective-permute-start | bytes 408584 | tf_op jit(solution)/shard_map/ppermute | solution.py:82
  8.7 11.8 %collective-permute-start.1 = (bf16[266,256]{1,0:T(8,128)(2,1)S(1)}, bf16[266,256]{1,0:T(8,128)(2,1)S(1)}, u32[]{:S(2)}, u32[]{:S(2)}) collective-permute-start(bf16[266,256]{1,0:T(8,128)(2,1)S(1)} %get-tuple-element.10), channel_id=1, source_target_pairs={{0,8},{4,12},{8,0},{12,4},{1,9},{5,13},{9,1},{13,5},{2,10},{6,14},... | collective-permute-start | bytes 408584 | tf_op jit(solution)/shard_map/ppermute | solution.py:82
  8.7 13.9 %collective-permute-start.2 = (bf16[266,256]{1,0:T(8,128)(2,1)S(1)}, bf16[266,256]{1,0:T(8,128)(2,1)S(1)}, u32[]{:S(2)}, u32[]{:S(2)}) collective-permute-start(bf16[266,256]{1,0:T(8,128)(2,1)S(1)} %get-tuple-element.9), channel_id=1, source_target_pairs={{0,4},{4,8},{8,12},{12,0},{1,5},{5,9},{9,13},{13,1},{2,6},{6,10},{... | collective-permute-start | bytes 408584 | tf_op jit(solution)/shard_map/ppermute | solution.py:82
  10.5 0.7 %copy-start.6 = (f32[256,4]{0,1:T(4,128)S(1)}, f32[256,4]{0,1:T(4,128)}, u32[]{:S(2)}) copy-start(f32[256,4]{0,1:T(4,128)} %param.15) | copy-start | bytes 12292
  12.8 10.9 %collective-permute-start.5 = (bf16[256,256]{1,0:T(8,128)(2,1)S(1)}, bf16[256,256]{1,0:T(8,128)(2,1)S(1)}, u32[]{:S(2)}, u32[]{:S(2)}) collective-permute-start(bf16[256,256]{1,0:T(8,128)(2,1)S(1)} %slice.59), channel_id=1, source_target_pairs={{0,2},{2,0},{1,3},{3,1},{4,6},{6,4},{5,7},{7,5},{8,10},{10,8},{9,1... | collective-permute-start | bytes 393224 | tf_op jit(solution)/shard_map/ppermute | solution.py:86
  20.5 6.3 %collective-permute-start.4 = (bf16[256,256]{1,0:T(8,128)(2,1)S(1)}, bf16[256,256]{1,0:T(8,128)(2,1)S(1)}, u32[]{:S(2)}, u32[]{:S(2)}) collective-permute-start(bf16[256,256]{1,0:T(8,128)(2,1)S(1)} %slice.58), channel_id=1, source_target_pairs={{0,2},{2,0},{1,3},{3,1},{4,6},{6,4},{5,7},{7,5},{8,10},{10,8},{9,1... | collective-permute-start | bytes 393224 | tf_op jit(solution)/shard_map/ppermute | solution.py:86
  22.6 5.8 %collective-permute-start.3 = (bf16[256,256]{1,0:T(8,128)(2,1)S(1)}, bf16[256,256]{1,0:T(8,128)(2,1)S(1)}, u32[]{:S(2)}, u32[]{:S(2)}) collective-permute-start(bf16[256,256]{1,0:T(8,128)(2,1)S(1)} %slice.57), channel_id=1, source_target_pairs={{0,2},{2,0},{1,3},{3,1},{4,6},{6,4},{5,7},{7,5},{8,10},{10,8},{9,1... | collective-permute-start | bytes 393224 | tf_op jit(solution)/shard_map/ppermute | solution.py:86
  29.4 1.2 %collective-permute-start.6 = (f32[4,4,256]{2,1,0:T(4,128)S(1)}, f32[4,4,256]{2,1,0:T(4,128)S(1)}, u32[]{:S(2)}, u32[]{:S(2)}) collective-permute-start(f32[4,4,256]{2,1,0:T(4,128)S(1)} %constant_dynamic-update-slice_fusion.2), channel_id=1, source_target_pairs={{0,1},{1,0},{2,3},{3,2},{4,5},{5,4},{6,7},{7,6},{8,9},{9,8},{10,11... | collective-permute-start | bytes 49160 | tf_op jit(solution)/shard_map/ppermute | solution.py:30
  30.6 3.7 %collective-permute-start.7 = (f32[4,4,256]{2,1,0:T(4,128)S(1)}, f32[4,4,256]{2,1,0:T(4,128)S(1)}, u32[]{:S(2)}, u32[]{:S(2)}) collective-permute-start(f32[4,4,256]{2,1,0:T(4,128)S(1)} %add.143), channel_id=1, source_target_pairs={{0,2},{1,3},{2,0},{3,1},{4,6},{5,7},{6,4},{7,5},{8,10},{9,11},{10,... | collective-permute-start | bytes 49160 | tf_op jit(solution)/shard_map/ppermute | solution.py:30
  34.4 5.6 %collective-permute-start.8 = (f32[4,4,256]{2,1,0:T(4,128)S(1)}, f32[4,4,256]{2,1,0:T(4,128)S(1)}, u32[]{:S(2)}, u32[]{:S(2)}) collective-permute-start(f32[4,4,256]{2,1,0:T(4,128)S(1)} %get-tuple-element.3), channel_id=1, source_target_pairs={{0,4},{4,8},{8,12},{12,0},{1,5},{5,9},{9,13},{13,1},{2,6},{6,10},{... | collective-permute-start | bytes 49160 | tf_op jit(solution)/shard_map/ppermute | solution.py:10
  34.5 5.5 %collective-permute-start.9 = (f32[4,4,256]{2,1,0:T(4,128)S(1)}, f32[4,4,256]{2,1,0:T(4,128)S(1)}, u32[]{:S(2)}, u32[]{:S(2)}) collective-permute-start(f32[4,4,256]{2,1,0:T(4,128)S(1)} %get-tuple-element.3), channel_id=1, source_target_pairs={{0,8},{4,12},{8,0},{12,4},{1,9},{5,13},{9,1},{13,5},{2,10},{6,14},... | collective-permute-start | bytes 49160 | tf_op jit(solution)/shard_map/ppermute | solution.py:10
  35.8 4.8 %collective-permute-start.10 = (f32[4,4,256]{2,1,0:T(4,128)S(1)}, f32[4,4,256]{2,1,0:T(4,128)S(1)}, u32[]{:S(2)}, u32[]{:S(2)}) collective-permute-start(f32[4,4,256]{2,1,0:T(4,128)S(1)} %get-tuple-element.3), channel_id=1, source_target_pairs={{0,12},{4,0},{8,4},{12,8},{1,13},{5,1},{9,5},{13,9},{2,14},{6,2},{... | collective-permute-start | bytes 49160 | tf_op jit(solution)/shard_map/ppermute | solution.py:10
  41.4 0.9 %copy-start.2 = (bf16[256,256]{1,0:T(8,128)(2,1)S(1)}, bf16[256,256]{1,0:T(8,128)(2,1)}, u32[]{:S(2)}) copy-start(bf16[256,256]{1,0:T(8,128)(2,1)} %get-tuple-element.6) | copy-start | bytes 393220
  42.7 0.6 %copy-start.3 = (f32[6,512]{1,0:T(8,128)}, f32[6,512]{1,0:T(8,128)S(1)}, u32[]{:S(2)}) copy-start(f32[6,512]{1,0:T(8,128)S(1)} %constant_dynamic-update-slice_fusion) | copy-start | bytes 36868

commit v8 on v7

--- a/solution.py
+++ b/solution.py
@@ -50,20 +50,43 @@
         d_idx = lax.axis_index("depth")
 
         columns = c_idx * block_cols + lax.iota(jnp.int32, block_cols)
-        inside = (columns[None, :] >= path_start[:, None]) & (columns[None, :] < path_end[:, None])
-        lengths = jnp.where(inside, seg_len, jnp.zeros_like(seg_len))
-        def small_for(target):
-            cols_of = lax.dynamic_slice_in_dim(lengths, target * own_cols, own_cols, axis=1)
-            return jnp.concatenate([cols_of.reshape(-1), mode_index.astype(bf16).reshape(-1)])
-
         n_len = path_rows * own_cols
         n_mi = path_rows * kept
+        if split:
+            width = depth_half // 2
+        else:
+            width = depth_half
+        if path_rows == width:
+            inside_t = (columns[:, None] >= path_start[None, :]) & (columns[:, None] < path_end[None, :])
+            seg_t = seg_len.T
+            lengths_t = jnp.where(inside_t, seg_t, jnp.zeros_like(seg_t))
+            mi_t = mode_index.T.astype(bf16)
+
+            def small_for(target):
+                cols_of = lax.dynamic_slice_in_dim(lengths_t, target * own_cols, own_cols, axis=0)
+                return jnp.concatenate([cols_of, mi_t], axis=0)
+
+            def decode(rows):
+                len_b = rows[:own_cols].T.astype(f32)
+                return len_b, rows[own_cols:own_cols + kept].T.astype(jnp.int32)
+        else:
+            inside = (columns[None, :] >= path_start[:, None]) & (columns[None, :] < path_end[:, None])
+            lengths = jnp.where(inside, seg_len, jnp.zeros_like(seg_len))
+
+            def small_for(target):
+                cols_of = lax.dynamic_slice_in_dim(lengths, target * own_cols, own_cols, axis=1)
+                flat = jnp.concatenate([cols_of.reshape(-1), mode_index.astype(bf16).reshape(-1)])
+                return pack_rows(flat, width)
+
+            def decode(rows):
+                flat = rows.reshape(-1)
+                len_b = flat[:n_len].reshape(path_rows, own_cols).astype(f32)
+                return len_b, flat[n_len:n_len + n_mi].reshape(path_rows, kept).astype(jnp.int32)
 
         scaled = (panels.astype(f32) * model.astype(f32)[:, None, :]).astype(bf16)
         scaled = scaled.reshape(own_cols * modes, depth_half)
 
         if split:
-            width = depth_half // 2
             own_off = c_idx * width
             other_off = (1 - c_idx) * width
             offsets = [own_off, other_off]
@@ -71,28 +94,26 @@
             theirs = lax.dynamic_slice_in_dim(depth_weight, other_off, width, axis=1)
             head = [mine]
         else:
-            width = depth_half
             offsets = [0]
             head = [depth_weight]
         blocks = [(head + ([theirs] if split else []), small_for(p_idx))]
         for shift in range(1, n_paths):
             target = (p_idx + shift) % n_paths
-            payload = jnp.concatenate([head[0], pack_rows(small_for(target), width)], axis=0)
+            payload = jnp.concatenate([head[0], small_for(target)], axis=0)
             perm = [(i, (i + shift) % n_paths) for i in range(n_paths)]
             got = lax.ppermute(payload, "paths", perm)
             part_rows = got[:path_rows]
             dw_parts = [part_rows]
             if split:
                 dw_parts.append(lax.ppermute(part_rows, "cols", [(0, 1), (1, 0)]))
-            blocks.append((dw_parts, got[path_rows:].reshape(-1)))
+            blocks.append((dw_parts, got[path_rows:]))
         scaled_parts = [lax.dynamic_slice_in_dim(scaled, off, width, axis=1) for off in offsets]
         mode_ids = lax.iota(jnp.int32, modes)
 
         unpacked = []
         parts = []
         for s, (dw_parts, sm) in enumerate(blocks):
-            len_own = sm[:n_len].reshape(path_rows, own_cols).astype(f32)
-            mi_b = sm[n_len:n_len + n_mi].reshape(path_rows, kept).astype(jnp.int32)
+            len_own, mi_b = decode(sm)
             one_hot = (mi_b[:, :, None] == mode_ids[None, None, :]).astype(f32)
             unpacked.append((dw_parts, len_own, one_hot))
             weighted = None

time: 43.5 us -> 43.2 us (level)
  starting transfers between devices: 15.1 us -> 19.7 us
  waiting for transfers between devices: 16.3 us -> 13.3 us
  local copies, waits for them, and re-layouts: 6.13 us -> 4.35 us
    ppermute x3, waiting for transfers between devices: 7.28 us -> 4.34 us  [shards(): got = lax.ppermute(payload, 'paths', perm)]
    ppermute x3, starting transfers between devices: 3.92 us -> 6.38 us  [shifted_copies(): copies.append(lax.ppermute(x, axes, perm))]
    ppermute x3, starting transfers between devices: 6.11 us -> 7.93 us  [shards(): got = lax.ppermute(payload, 'paths', perm)]
    convert_element_type x13 -> x0, local copies, waits for them, and re-layouts: 1.45 us -> none  [the longest x6 0.67 us: shards(): mi_b = sm[n_len:n_len + n_mi].reshape(path_rows, kept).astype(jnp.int32)]
    ppermute x3, waiting for transfers between devices: 2.2 us -> 1.42 us  [shifted_copies(): copies.append(lax.ppermute(x, axes, perm))]
    select_n x1, other arithmetic: 0.83 us -> 0.08 us  [shards(): lengths_t = jnp.where(inside_t, seg_t, jnp.zeros_like(seg_t))]
    convert_element_type x8, other arithmetic: 0.07 us -> 0.76 us  [the longest x1 0.7 us: shards(): mi_t = mode_index.T.astype(bf16)]
    ppermute x3, waiting for transfers between devices: 3.26 us -> 3.93 us  [shards(): dw_parts.append(lax.ppermute(part_rows, 'cols', [(0, 1), (1, 0)]))]
  transfers between devices with their start and end apart: 11 -> 11, of which waited for: 8 -> 5; matrix products, arithmetic and copies ran while one was open for 9% -> 6% of each run, Pallas kernels for 0% -> 0%
where the time goes in v8:
time: 43.2 us; the launch traced here: 42.9 us
  starting transfers between devices  19.7 us (46%)
  waiting for transfers between devices  13.3 us (31%)
  local copies, waits for them, and re-layouts  4.35 us (10%)
  matrix products  2.84 us (7%)
  other arithmetic  1.66 us (4%)
  between operations  1.14 us (3%)
    ppermute x3, starting transfers between devices, shards(): got = lax.ppermute(payload, 'paths', perm)  7.93 us
    ppermute x3, starting transfers between devices, shifted_copies(): copies.append(lax.ppermute(x, axes, perm))  6.38 us
    ppermute x3, waiting for transfers between devices, shards(): got = lax.ppermute(payload, 'paths', perm)  4.34 us
    ppermute x3, starting transfers between devices, shards(): dw_parts.append(lax.ppermute(part_rows, 'cols', [(0, 1), (1, 0)]))  4.06 us
    ppermute x3, waiting for transfers between devices, shards(): dw_parts.append(lax.ppermute(part_rows, 'cols', [(0, 1), (1, 0)]))  3.93 us
    ppermute x2, waiting for transfers between devices, butterfly_sum(): x = x + lax.ppermute(x, axes, perm)  3.58 us
    dot_general x8, matrix products, shards(): lax.dot_general(dw_part, sc_part, (((1,), (1,)), ((), ())), preferred_ele...  2.07 us
    unnamed x16, local copies, waits for them, and re-layouts  1.98 us
  transfers between devices with their start and end apart: 11, of which 5 were waited for; matrix products, arithmetic and copies ran while one was open for 6% of the time, Pallas kernels for 0%

profile of v8, /device:TPU:0, one launch (start us, length us, event | category | flops | bytes accessed | tf_op | source)
XLA Modules:
  0.0 42.9 jit_solution(4374642097678036692)
XLA Ops:
  0.7 0.7 %convert_bitcast_fusion.7 = (bf16[4,256]{1,0:T(4,128)(2,1)S(1)}, s32[256,4]{0,1:T(4,128)S(1)}) fusion(s32[256,4]{0,1:T(4,128)} %param.14), kind=kLoop, calls=%fused_computation.96 | loop fusion | flops 2048 | bytes 10240 | tf_op jit(solution)/shard_map/convert_element_type | solution.py:63
  1.4 1.0 %constant_dynamic-slice_fusion.1 = (bf16[256,256]{1,0:T(8,128)(2,1)S(1)}, bf16[256,256]{1,0:T(8,128)(2,1)S(1)}) fusion(bf16[256,512]{1,0:T(8,128)(2,1)} %param.10, s32[]{:T(128)S(6)} %select_n.112, s32[]{:T(128)S(6)} %select_n.103), kind=kLoop, calls=%fused_computation.84 | loop fusion | bytes 524296 | tf_op jit(solution)/shard_map/dynamic_slice | solution.py:94
  2.6 4.1 %collective-permute-start.1 = (bf16[266,256]{1,0:T(8,128)(2,1)S(1)}, bf16[266,256]{1,0:T(8,128)(2,1)S(1)}, u32[]{:S(2)}, u32[]{:S(2)}) collective-permute-start(bf16[266,256]{1,0:T(8,128)(2,1)S(1)} %get-tuple-element.7), channel_id=1, source_target_pairs={{0,8},{4,12},{8,0},{12,4},{1,9},{5,13},{9,1},{13,5},{2,10},{6,14},... | collective-permute-start | bytes 408584 | tf_op jit(solution)/shard_map/ppermute | solution.py:104
  6.7 1.6 %collective-permute-start.2 = (bf16[266,256]{1,0:T(8,128)(2,1)S(1)}, bf16[266,256]{1,0:T(8,128)(2,1)S(1)}, u32[]{:S(2)}, u32[]{:S(2)}) collective-permute-start(bf16[266,256]{1,0:T(8,128)(2,1)S(1)} %get-tuple-element.8), channel_id=1, source_target_pairs={{0,4},{4,8},{8,12},{12,0},{1,5},{5,9},{9,13},{13,1},{2,6},{6,10},{... | collective-permute-start | bytes 408584 | tf_op jit(solution)/shard_map/ppermute | solution.py:104
  8.3 2.2 %collective-permute-start = (bf16[266,256]{1,0:T(8,128)(2,1)S(1)}, bf16[266,256]{1,0:T(8,128)(2,1)S(1)}, u32[]{:S(2)}, u32[]{:S(2)}) collective-permute-start(bf16[266,256]{1,0:T(8,128)(2,1)S(1)} %get-tuple-element.6), channel_id=1, source_target_pairs={{0,12},{4,0},{8,4},{12,8},{1,13},{5,1},{9,5},{13,9},{2,14},{6,2},{... | collective-permute-start | bytes 408584 | tf_op jit(solution)/shard_map/ppermute | solution.py:104
  10.6 0.9 %copy-done = bf16[256,512]{1,0:T(8,128)(2,1)S(1)} copy-done((bf16[256,512]{1,0:T(8,128)(2,1)S(1)}, bf16[256,512]{1,0:T(8,128)(2,1)}, u32[]{:S(2)}) %copy-start) | copy-done | bytes 262168
  11.5 0.3 fusion.31
  11.8 0.3 convolution_add_fusion.3
  12.4 0.5 %copy-done.5 = f32[256,4]{0,1:T(4,128)S(1)} copy-done((f32[256,4]{0,1:T(4,128)S(1)}, f32[256,4]{0,1:T(4,128)}, u32[]{:S(2)}) %copy-start.5) | copy-done | bytes 4120
  12.9 4.3 %collective-permute-done.1 = bf16[266,256]{1,0:T(8,128)(2,1)S(1)} collective-permute-done((bf16[266,256]{1,0:T(8,128)(2,1)S(1)}, bf16[266,256]{1,0:T(8,128)(2,1)S(1)}, u32[]{:S(2)}, u32[]{:S(2)}) %collective-permute-start.1) | collective-permute-done | bytes 136224 | tf_op jit(solution)/shard_map/ppermute | solution.py:104
  17.2 1.9 %collective-permute-start.4 = (bf16[256,256]{1,0:T(8,128)(2,1)S(1)}, bf16[256,256]{1,0:T(8,128)(2,1)S(1)}, u32[]{:S(2)}, u32[]{:S(2)}) collective-permute-start(bf16[256,256]{1,0:T(8,128)(2,1)S(1)} %slice.52), channel_id=1, source_target_pairs={{0,2},{2,0},{1,3},{3,1},{4,6},{6,4},{5,7},{7,5},{8,10},{10,8},{9,1... | collective-permute-start | bytes 393224 | tf_op jit(solution)/shard_map/ppermute | solution.py:108
  19.2 0.3 collective-permute-start.3
  19.4 1.9 %collective-permute-start.5 = (bf16[256,256]{1,0:T(8,128)(2,1)S(1)}, bf16[256,256]{1,0:T(8,128)(2,1)S(1)}, u32[]{:S(2)}, u32[]{:S(2)}) collective-permute-start(bf16[256,256]{1,0:T(8,128)(2,1)S(1)} %slice.53), channel_id=1, source_target_pairs={{0,2},{2,0},{1,3},{3,1},{4,6},{6,4},{5,7},{7,5},{8,10},{10,8},{9,1... | collective-permute-start | bytes 393224 | tf_op jit(solution)/shard_map/ppermute | solution.py:108
  21.5 3.9 %collective-permute-done.3 = bf16[256,256]{1,0:T(8,128)(2,1)S(1)} collective-permute-done((bf16[256,256]{1,0:T(8,128)(2,1)S(1)}, bf16[256,256]{1,0:T(8,128)(2,1)S(1)}, u32[]{:S(2)}, u32[]{:S(2)}) %collective-permute-start.3) | collective-permute-done | bytes 131104 | tf_op jit(solution)/shard_map/ppermute | solution.py:108
  25.4 0.3 fusion.25
  25.6 0.3 convolution_add_fusion.2
  25.9 0.2 copy.41
  26.1 0.3 fusion.23
  26.3 0.3 convolution_add_fusion.1
  26.9 0.3 fusion.21
  27.1 0.3 convolution_add_fusion
  27.9 1.1 %collective-permute-done.6 = f32[4,4,256]{2,1,0:T(4,128)S(1)} collective-permute-done((f32[4,4,256]{2,1,0:T(4,128)S(1)}, f32[4,4,256]{2,1,0:T(4,128)S(1)}, u32[]{:S(2)}, u32[]{:S(2)}) %collective-permute-start.6) | collective-permute-done | bytes 16416 | tf_op jit(solution)/shard_map/ppermute | solution.py:30
  29.1 1.2 %collective-permute-start.7 = (f32[4,4,256]{2,1,0:T(4,128)S(1)}, f32[4,4,256]{2,1,0:T(4,128)S(1)}, u32[]{:S(2)}, u32[]{:S(2)}) collective-permute-start(f32[4,4,256]{2,1,0:T(4,128)S(1)} %add.143), channel_id=1, source_target_pairs={{0,2},{1,3},{2,0},{3,1},{4,6},{5,7},{6,4},{7,5},{8,10},{9,11},{10,... | collective-permute-start | bytes 49160 | tf_op jit(solution)/shard_map/ppermute | solution.py:30
  30.4 2.5 %collective-permute-done.7 = f32[4,4,256]{2,1,0:T(4,128)S(1)} collective-permute-done((f32[4,4,256]{2,1,0:T(4,128)S(1)}, f32[4,4,256]{2,1,0:T(4,128)S(1)}, u32[]{:S(2)}, u32[]{:S(2)}) %collective-permute-start.7) | collective-permute-done | bytes 16416 | tf_op jit(solution)/shard_map/ppermute | solution.py:30
  32.8 1.5 %collective-permute-start.8 = (f32[4,4,256]{2,1,0:T(4,128)S(1)}, f32[4,4,256]{2,1,0:T(4,128)S(1)}, u32[]{:S(2)}, u32[]{:S(2)}) collective-permute-start(f32[4,4,256]{2,1,0:T(4,128)S(1)} %get-tuple-element.3), channel_id=1, source_target_pairs={{0,4},{4,8},{8,12},{12,0},{1,5},{5,9},{9,13},{13,1},{2,6},{6,10},{... | collective-permute-start | bytes 49160 | tf_op jit(solution)/shard_map/ppermute | solution.py:10
  34.4 2.0 %collective-permute-start.9 = (f32[4,4,256]{2,1,0:T(4,128)S(1)}, f32[4,4,256]{2,1,0:T(4,128)S(1)}, u32[]{:S(2)}, u32[]{:S(2)}) collective-permute-start(f32[4,4,256]{2,1,0:T(4,128)S(1)} %get-tuple-element.3), channel_id=1, source_target_pairs={{0,8},{4,12},{8,0},{12,4},{1,9},{5,13},{9,1},{13,5},{2,10},{6,14},... | collective-permute-start | bytes 49160 | tf_op jit(solution)/shard_map/ppermute | solution.py:10
  36.4 2.8 %collective-permute-start.10 = (f32[4,4,256]{2,1,0:T(4,128)S(1)}, f32[4,4,256]{2,1,0:T(4,128)S(1)}, u32[]{:S(2)}, u32[]{:S(2)}) collective-permute-start(f32[4,4,256]{2,1,0:T(4,128)S(1)} %get-tuple-element.3), channel_id=1, source_target_pairs={{0,12},{4,0},{8,4},{12,8},{1,13},{5,1},{9,5},{13,9},{2,14},{6,2},{... | collective-permute-start | bytes 49160 | tf_op jit(solution)/shard_map/ppermute | solution.py:10
  39.3 1.4 %collective-permute-done.10 = f32[4,4,256]{2,1,0:T(4,128)S(1)} collective-permute-done((f32[4,4,256]{2,1,0:T(4,128)S(1)}, f32[4,4,256]{2,1,0:T(4,128)S(1)}, u32[]{:S(2)}, u32[]{:S(2)}) %collective-permute-start.10) | collective-permute-done | bytes 16416 | tf_op jit(solution)/shard_map/ppermute | solution.py:10
  40.7 0.6 %fusion.42 = f32[256,4]{0,1:T(4,128)} fusion(f32[4,4,256]{2,1,0:T(4,128)S(1)} %reduce_sum.116, s32[]{:T(128)S(6)} %select_n.124), kind=kLoop, calls=%fused_computation.91 | loop fusion | bytes 8196 | tf_op jit(solution)/shard_map/transpose | solution.py:139
  41.5 0.4 fusion
  41.9 0.4 fusion.1
  42.3 0.6 %copy-done.2 = f32[6,512]{1,0:T(8,128)} copy-done((f32[6,512]{1,0:T(8,128)}, f32[6,512]{1,0:T(8,128)S(1)}, u32[]{:S(2)}) %copy-start.2) | copy-done | bytes 12312
  (68 shorter events, 1.7 us)
Async XLA Ops:
  0.6 1.8 %copy-start.3 = (bf16[256,24]{0,1:T(8,128)(2,1)S(1)}, bf16[256,24]{0,1:T(8,128)(2,1)}, u32[]{:S(2)}) copy-start(bf16[256,24]{0,1:T(8,128)(2,1)} %param.11) | copy-start | bytes 36868
  0.6 1.8 %copy-start.7 = (s32[256]{0:T(256)S(1)}, s32[256]{0:T(256)}, u32[]{:S(2)}) copy-start(s32[256]{0:T(256)} %param.12) | copy-start | bytes 3076
  0.7 1.8 %copy-start.6 = (s32[256]{0:T(256)S(1)}, s32[256]{0:T(256)}, u32[]{:S(2)}) copy-start(s32[256]{0:T(256)} %param.13) | copy-start | bytes 3076
  2.4 8.1 %copy-start.4 = (bf16[6,512]{1,0:T(8,128)(2,1)S(1)}, bf16[6,512]{1,0:T(8,128)(2,1)}, u32[]{:S(2)}) copy-start(bf16[6,512]{1,0:T(8,128)(2,1)} %param.9) | copy-start | bytes 18436
  2.5 8.1 %copy-start.1 = (bf16[6,64,512]{2,1,0:T(8,128)(2,1)S(1)}, bf16[6,64,512]{2,1,0:T(8,128)(2,1)}, u32[]{:S(2)}) copy-start(bf16[6,64,512]{2,1,0:T(8,128)(2,1)} %param.8) | copy-start | bytes 1179652
  2.6 14.6 %collective-permute-start.1 = (bf16[266,256]{1,0:T(8,128)(2,1)S(1)}, bf16[266,256]{1,0:T(8,128)(2,1)S(1)}, u32[]{:S(2)}, u32[]{:S(2)}) collective-permute-start(bf16[266,256]{1,0:T(8,128)(2,1)S(1)} %get-tuple-element.7), channel_id=1, source_target_pairs={{0,8},{4,12},{8,0},{12,4},{1,9},{5,13},{9,1},{13,5},{2,10},{6,14},... | collective-permute-start | bytes 408584 | tf_op jit(solution)/shard_map/ppermute | solution.py:104
  6.7 12.4 %collective-permute-start.2 = (bf16[266,256]{1,0:T(8,128)(2,1)S(1)}, bf16[266,256]{1,0:T(8,128)(2,1)S(1)}, u32[]{:S(2)}, u32[]{:S(2)}) collective-permute-start(bf16[266,256]{1,0:T(8,128)(2,1)S(1)} %get-tuple-element.8), channel_id=1, source_target_pairs={{0,4},{4,8},{8,12},{12,0},{1,5},{5,9},{9,13},{13,1},{2,6},{6,10},{... | collective-permute-start | bytes 408584 | tf_op jit(solution)/shard_map/ppermute | solution.py:104
  8.3 11.1 %collective-permute-start = (bf16[266,256]{1,0:T(8,128)(2,1)S(1)}, bf16[266,256]{1,0:T(8,128)(2,1)S(1)}, u32[]{:S(2)}, u32[]{:S(2)}) collective-permute-start(bf16[266,256]{1,0:T(8,128)(2,1)S(1)} %get-tuple-element.6), channel_id=1, source_target_pairs={{0,12},{4,0},{8,4},{12,8},{1,13},{5,1},{9,5},{13,9},{2,14},{6,2},{... | collective-permute-start | bytes 408584 | tf_op jit(solution)/shard_map/ppermute | solution.py:104
  10.5 1.0 %copy-start = (bf16[256,512]{1,0:T(8,128)(2,1)S(1)}, bf16[256,512]{1,0:T(8,128)(2,1)}, u32[]{:S(2)}) copy-start(bf16[256,512]{1,0:T(8,128)(2,1)} %param.10) | copy-start | bytes 786436
  12.2 0.7 %copy-start.5 = (f32[256,4]{0,1:T(4,128)S(1)}, f32[256,4]{0,1:T(4,128)}, u32[]{:S(2)}) copy-start(f32[256,4]{0,1:T(4,128)} %param.15) | copy-start | bytes 12292
  17.2 8.8 %collective-permute-start.4 = (bf16[256,256]{1,0:T(8,128)(2,1)S(1)}, bf16[256,256]{1,0:T(8,128)(2,1)S(1)}, u32[]{:S(2)}, u32[]{:S(2)}) collective-permute-start(bf16[256,256]{1,0:T(8,128)(2,1)S(1)} %slice.52), channel_id=1, source_target_pairs={{0,2},{2,0},{1,3},{3,1},{4,6},{6,4},{5,7},{7,5},{8,10},{10,8},{9,1... | collective-permute-start | bytes 393224 | tf_op jit(solution)/shard_map/ppermute | solution.py:108
  19.2 6.2 %collective-permute-start.3 = (bf16[256,256]{1,0:T(8,128)(2,1)S(1)}, bf16[256,256]{1,0:T(8,128)(2,1)S(1)}, u32[]{:S(2)}, u32[]{:S(2)}) collective-permute-start(bf16[256,256]{1,0:T(8,128)(2,1)S(1)} %slice.51), channel_id=1, source_target_pairs={{0,2},{2,0},{1,3},{3,1},{4,6},{6,4},{5,7},{7,5},{8,10},{10,8},{9,1... | collective-permute-start | bytes 393224 | tf_op jit(solution)/shard_map/ppermute | solution.py:108
  19.4 7.4 %collective-permute-start.5 = (bf16[256,256]{1,0:T(8,128)(2,1)S(1)}, bf16[256,256]{1,0:T(8,128)(2,1)S(1)}, u32[]{:S(2)}, u32[]{:S(2)}) collective-permute-start(bf16[256,256]{1,0:T(8,128)(2,1)S(1)} %slice.53), channel_id=1, source_target_pairs={{0,2},{2,0},{1,3},{3,1},{4,6},{6,4},{5,7},{7,5},{8,10},{10,8},{9,1... | collective-permute-start | bytes 393224 | tf_op jit(solution)/shard_map/ppermute | solution.py:108
  27.8 1.2 %collective-permute-start.6 = (f32[4,4,256]{2,1,0:T(4,128)S(1)}, f32[4,4,256]{2,1,0:T(4,128)S(1)}, u32[]{:S(2)}, u32[]{:S(2)}) collective-permute-start(f32[4,4,256]{2,1,0:T(4,128)S(1)} %constant_dynamic-update-slice_fusion.2), channel_id=1, source_target_pairs={{0,1},{1,0},{2,3},{3,2},{4,5},{5,4},{6,7},{7,6},{8,9},{9,8},{10,11... | collective-permute-start | bytes 49160 | tf_op jit(solution)/shard_map/ppermute | solution.py:30
  29.1 3.7 %collective-permute-start.7 = (f32[4,4,256]{2,1,0:T(4,128)S(1)}, f32[4,4,256]{2,1,0:T(4,128)S(1)}, u32[]{:S(2)}, u32[]{:S(2)}) collective-permute-start(f32[4,4,256]{2,1,0:T(4,128)S(1)} %add.143), channel_id=1, source_target_pairs={{0,2},{1,3},{2,0},{3,1},{4,6},{5,7},{6,4},{7,5},{8,10},{9,11},{10,... | collective-permute-start | bytes 49160 | tf_op jit(solution)/shard_map/ppermute | solution.py:30
  32.8 6.4 %collective-permute-start.8 = (f32[4,4,256]{2,1,0:T(4,128)S(1)}, f32[4,4,256]{2,1,0:T(4,128)S(1)}, u32[]{:S(2)}, u32[]{:S(2)}) collective-permute-start(f32[4,4,256]{2,1,0:T(4,128)S(1)} %get-tuple-element.3), channel_id=1, source_target_pairs={{0,4},{4,8},{8,12},{12,0},{1,5},{5,9},{9,13},{13,1},{2,6},{6,10},{... | collective-permute-start | bytes 49160 | tf_op jit(solution)/shard_map/ppermute | solution.py:10
  34.4 4.9 %collective-permute-start.9 = (f32[4,4,256]{2,1,0:T(4,128)S(1)}, f32[4,4,256]{2,1,0:T(4,128)S(1)}, u32[]{:S(2)}, u32[]{:S(2)}) collective-permute-start(f32[4,4,256]{2,1,0:T(4,128)S(1)} %get-tuple-element.3), channel_id=1, source_target_pairs={{0,8},{4,12},{8,0},{12,4},{1,9},{5,13},{9,1},{13,5},{2,10},{6,14},... | collective-permute-start | bytes 49160 | tf_op jit(solution)/shard_map/ppermute | solution.py:10
  36.4 4.3 %collective-permute-start.10 = (f32[4,4,256]{2,1,0:T(4,128)S(1)}, f32[4,4,256]{2,1,0:T(4,128)S(1)}, u32[]{:S(2)}, u32[]{:S(2)}) collective-permute-start(f32[4,4,256]{2,1,0:T(4,128)S(1)} %get-tuple-element.3), channel_id=1, source_target_pairs={{0,12},{4,0},{8,4},{12,8},{1,13},{5,1},{9,5},{13,9},{2,14},{6,2},{... | collective-permute-start | bytes 49160 | tf_op jit(solution)/shard_map/ppermute | solution.py:10
  42.3 0.6 %copy-start.2 = (f32[6,512]{1,0:T(8,128)}, f32[6,512]{1,0:T(8,128)S(1)}, u32[]{:S(2)}) copy-start(f32[6,512]{1,0:T(8,128)S(1)} %constant_dynamic-update-slice_fusion) | copy-start | bytes 36868

commit v9 on v8

--- a/solution.py
+++ b/solution.py
@@ -131,10 +131,7 @@
         canon = place_by_source(parts, p_idx, n_paths)
 
         local = n_cols * n_depth
-        if local & (local - 1) == 0:
-            misfit_all = butterfly_sum(canon, ("cols", "depth"), local)
-        else:
-            misfit_all = exchange_sum(canon, ("cols", "depth"), local)
+        misfit_all = exchange_sum(canon, ("cols", "depth"), local)
         misfit_all = exchange_sum(misfit_all, "paths", n_paths)
         misfit = lax.dynamic_index_in_dim(misfit_all, p_idx, 0, keepdims=False).T
         rev = list(reversed(range(n_paths)))

time: 43.2 us -> 42.5 us (0.984)
  waiting for transfers between devices: 13.3 us -> 10.7 us
  starting transfers between devices: 19.7 us -> 21.5 us
    ppermute x2 -> x0, waiting for transfers between devices: 3.58 us -> none  [butterfly_sum(): x = x + lax.ppermute(x, axes, perm)]
    ppermute x3 -> x6, starting transfers between devices: 6.38 us -> 9.49 us  [shifted_copies(): copies.append(lax.ppermute(x, axes, perm))]
    ppermute x3 -> x6, waiting for transfers between devices: 1.42 us -> 2.76 us  [shifted_copies(): copies.append(lax.ppermute(x, axes, perm))]
    ppermute x2 -> x0, starting transfers between devices: 1.32 us -> none  [butterfly_sum(): x = x + lax.ppermute(x, axes, perm)]
  transfers between devices with their start and end apart: 11 -> 12, of which waited for: 5 -> 8; matrix products, arithmetic and copies ran while one was open for 6% -> 6% of each run, Pallas kernels for 0% -> 0%
where the time goes in v9:
time: 42.5 us; the launch traced here: 42.3 us
  starting transfers between devices  21.5 us (51%)
  waiting for transfers between devices  10.7 us (25%)
  local copies, waits for them, and re-layouts  4.4 us (10%)
  matrix products  2.83 us (7%)
  other arithmetic  1.65 us (4%)
  between operations  1.18 us (3%)
    ppermute x6, starting transfers between devices, shifted_copies(): copies.append(lax.ppermute(x, axes, perm))  9.49 us
    ppermute x3, starting transfers between devices, shards(): got = lax.ppermute(payload, 'paths', perm)  7.93 us
    ppermute x3, waiting for transfers between devices, shards(): got = lax.ppermute(payload, 'paths', perm)  4.34 us
    ppermute x3, starting transfers between devices, shards(): dw_parts.append(lax.ppermute(part_rows, 'cols', [(0, 1), (1, 0)]))  4.06 us
    ppermute x3, waiting for transfers between devices, shards(): dw_parts.append(lax.ppermute(part_rows, 'cols', [(0, 1), (1, 0)]))  3.65 us
    ppermute x6, waiting for transfers between devices, shifted_copies(): copies.append(lax.ppermute(x, axes, perm))  2.76 us
    dot_general x8, matrix products, shards(): lax.dot_general(dw_part, sc_part, (((1,), (1,)), ((), ())), preferred_ele...  2.06 us
    unnamed x16, local copies, waits for them, and re-layouts  1.96 us
  transfers between devices with their start and end apart: 12, of which 8 were waited for; matrix products, arithmetic and copies ran while one was open for 6% of the time, Pallas kernels for 0%

profile of v9, /device:TPU:0, one launch (start us, length us, event | category | flops | bytes accessed | tf_op | source)
XLA Modules:
  0.0 42.3 jit_solution(10059936987186992834)
XLA Ops:
  0.7 0.7 %convert_bitcast_fusion.7 = (bf16[4,256]{1,0:T(4,128)(2,1)S(1)}, s32[256,4]{0,1:T(4,128)S(1)}) fusion(s32[256,4]{0,1:T(4,128)} %param.14), kind=kLoop, calls=%fused_computation.100 | loop fusion | flops 2048 | bytes 10240 | tf_op jit(solution)/shard_map/convert_element_type | solution.py:63
  1.4 1.0 %constant_dynamic-slice_fusion.1 = (bf16[256,256]{1,0:T(8,128)(2,1)S(1)}, bf16[256,256]{1,0:T(8,128)(2,1)S(1)}) fusion(bf16[256,512]{1,0:T(8,128)(2,1)} %param.10, s32[]{:T(128)S(6)} %select_n.140, s32[]{:T(128)S(6)} %select_n.131), kind=kLoop, calls=%fused_computation.88 | loop fusion | bytes 524296 | tf_op jit(solution)/shard_map/dynamic_slice | solution.py:94
  2.6 4.1 %collective-permute-start.1 = (bf16[266,256]{1,0:T(8,128)(2,1)S(1)}, bf16[266,256]{1,0:T(8,128)(2,1)S(1)}, u32[]{:S(2)}, u32[]{:S(2)}) collective-permute-start(bf16[266,256]{1,0:T(8,128)(2,1)S(1)} %get-tuple-element.5), channel_id=1, source_target_pairs={{0,8},{4,12},{8,0},{12,4},{1,9},{5,13},{9,1},{13,5},{2,10},{6,14},... | collective-permute-start | bytes 408584 | tf_op jit(solution)/shard_map/ppermute | solution.py:104
  6.7 1.6 %collective-permute-start.2 = (bf16[266,256]{1,0:T(8,128)(2,1)S(1)}, bf16[266,256]{1,0:T(8,128)(2,1)S(1)}, u32[]{:S(2)}, u32[]{:S(2)}) collective-permute-start(bf16[266,256]{1,0:T(8,128)(2,1)S(1)} %get-tuple-element.6), channel_id=1, source_target_pairs={{0,4},{4,8},{8,12},{12,0},{1,5},{5,9},{9,13},{13,1},{2,6},{6,10},{... | collective-permute-start | bytes 408584 | tf_op jit(solution)/shard_map/ppermute | solution.py:104
  8.3 2.2 %collective-permute-start = (bf16[266,256]{1,0:T(8,128)(2,1)S(1)}, bf16[266,256]{1,0:T(8,128)(2,1)S(1)}, u32[]{:S(2)}, u32[]{:S(2)}) collective-permute-start(bf16[266,256]{1,0:T(8,128)(2,1)S(1)} %get-tuple-element.4), channel_id=1, source_target_pairs={{0,12},{4,0},{8,4},{12,8},{1,13},{5,1},{9,5},{13,9},{2,14},{6,2},{... | collective-permute-start | bytes 408584 | tf_op jit(solution)/shard_map/ppermute | solution.py:104
  10.6 0.9 %copy-done = bf16[256,512]{1,0:T(8,128)(2,1)S(1)} copy-done((bf16[256,512]{1,0:T(8,128)(2,1)S(1)}, bf16[256,512]{1,0:T(8,128)(2,1)}, u32[]{:S(2)}) %copy-start) | copy-done | bytes 262168
  11.8 0.3 convolution_add_fusion.3
  12.4 0.5 %copy-done.5 = f32[256,4]{0,1:T(4,128)S(1)} copy-done((f32[256,4]{0,1:T(4,128)S(1)}, f32[256,4]{0,1:T(4,128)}, u32[]{:S(2)}) %copy-start.5) | copy-done | bytes 4120
  12.9 4.3 %collective-permute-done.1 = bf16[266,256]{1,0:T(8,128)(2,1)S(1)} collective-permute-done((bf16[266,256]{1,0:T(8,128)(2,1)S(1)}, bf16[266,256]{1,0:T(8,128)(2,1)S(1)}, u32[]{:S(2)}, u32[]{:S(2)}) %collective-permute-start.1) | collective-permute-done | bytes 136224 | tf_op jit(solution)/shard_map/ppermute | solution.py:104
  17.2 1.9 %collective-permute-start.4 = (bf16[256,256]{1,0:T(8,128)(2,1)S(1)}, bf16[256,256]{1,0:T(8,128)(2,1)S(1)}, u32[]{:S(2)}, u32[]{:S(2)}) collective-permute-start(bf16[256,256]{1,0:T(8,128)(2,1)S(1)} %slice.52), channel_id=1, source_target_pairs={{0,2},{2,0},{1,3},{3,1},{4,6},{6,4},{5,7},{7,5},{8,10},{10,8},{9,1... | collective-permute-start | bytes 393224 | tf_op jit(solution)/shard_map/ppermute | solution.py:108
  19.2 0.3 collective-permute-start.3
  19.4 1.9 %collective-permute-start.5 = (bf16[256,256]{1,0:T(8,128)(2,1)S(1)}, bf16[256,256]{1,0:T(8,128)(2,1)S(1)}, u32[]{:S(2)}, u32[]{:S(2)}) collective-permute-start(bf16[256,256]{1,0:T(8,128)(2,1)S(1)} %slice.53), channel_id=1, source_target_pairs={{0,2},{2,0},{1,3},{3,1},{4,6},{6,4},{5,7},{7,5},{8,10},{10,8},{9,1... | collective-permute-start | bytes 393224 | tf_op jit(solution)/shard_map/ppermute | solution.py:108
  21.6 2.2 %collective-permute-done.4 = bf16[256,256]{1,0:T(8,128)(2,1)S(1)} collective-permute-done((bf16[256,256]{1,0:T(8,128)(2,1)S(1)}, bf16[256,256]{1,0:T(8,128)(2,1)S(1)}, u32[]{:S(2)}, u32[]{:S(2)}) %collective-permute-start.4) | collective-permute-done | bytes 131104 | tf_op jit(solution)/shard_map/ppermute | solution.py:108
  24.0 0.3 convolution_add_fusion.1
  24.5 0.9 %collective-permute-done.3 = bf16[256,256]{1,0:T(8,128)(2,1)S(1)} collective-permute-done((bf16[256,256]{1,0:T(8,128)(2,1)S(1)}, bf16[256,256]{1,0:T(8,128)(2,1)S(1)}, u32[]{:S(2)}, u32[]{:S(2)}) %collective-permute-start.3) | collective-permute-done | bytes 131104 | tf_op jit(solution)/shard_map/ppermute | solution.py:108
  25.4 0.3 fusion.25
  25.6 0.3 convolution_add_fusion.2
  26.2 0.6 %collective-permute-done.5 = bf16[256,256]{1,0:T(8,128)(2,1)S(1)} collective-permute-done((bf16[256,256]{1,0:T(8,128)(2,1)S(1)}, bf16[256,256]{1,0:T(8,128)(2,1)S(1)}, u32[]{:S(2)}, u32[]{:S(2)}) %collective-permute-start.5) | collective-permute-done | bytes 131104 | tf_op jit(solution)/shard_map/ppermute | solution.py:108
  27.0 0.3 convolution_add_fusion
  27.7 1.3 %collective-permute-start.7 = (f32[4,4,256]{2,1,0:T(4,128)S(1)}, f32[4,4,256]{2,1,0:T(4,128)S(1)}, u32[]{:S(2)}, u32[]{:S(2)}) collective-permute-start(f32[4,4,256]{2,1,0:T(4,128)S(1)} %constant_dynamic-update-slice_fusion.2), channel_id=1, source_target_pairs={{0,2},{1,3},{2,0},{3,1},{4,6},{5,7},{6,4},{7,5},{8,10},{9,11},{10,... | collective-permute-start | bytes 49160 | tf_op jit(solution)/shard_map/ppermute | solution.py:10
  29.0 1.4 %collective-permute-start.8 = (f32[4,4,256]{2,1,0:T(4,128)S(1)}, f32[4,4,256]{2,1,0:T(4,128)S(1)}, u32[]{:S(2)}, u32[]{:S(2)}) collective-permute-start(f32[4,4,256]{2,1,0:T(4,128)S(1)} %constant_dynamic-update-slice_fusion.2), channel_id=1, source_target_pairs={{0,3},{1,0},{2,1},{3,2},{4,7},{5,4},{6,5},{7,6},{8,11},{9,8},{10,9... | collective-permute-start | bytes 49160 | tf_op jit(solution)/shard_map/ppermute | solution.py:10
  30.4 0.4 collective-permute-done.6
  30.8 0.6 %collective-permute-done.7 = f32[4,4,256]{2,1,0:T(4,128)S(1)} collective-permute-done((f32[4,4,256]{2,1,0:T(4,128)S(1)}, f32[4,4,256]{2,1,0:T(4,128)S(1)}, u32[]{:S(2)}, u32[]{:S(2)}) %collective-permute-start.7) | collective-permute-done | bytes 16416 | tf_op jit(solution)/shard_map/ppermute | solution.py:10
  31.5 0.3 collective-permute-done.8
  31.8 1.9 %collective-permute-start.9 = (f32[4,4,256]{2,1,0:T(4,128)S(1)}, f32[4,4,256]{2,1,0:T(4,128)S(1)}, u32[]{:S(2)}, u32[]{:S(2)}) collective-permute-start(f32[4,4,256]{2,1,0:T(4,128)S(1)} %reduce_sum.125), channel_id=1, source_target_pairs={{0,4},{4,8},{8,12},{12,0},{1,5},{5,9},{9,13},{13,1},{2,6},{6,10},{... | collective-permute-start | bytes 49160 | tf_op jit(solution)/shard_map/ppermute | solution.py:10
  33.7 2.0 %collective-permute-start.10 = (f32[4,4,256]{2,1,0:T(4,128)S(1)}, f32[4,4,256]{2,1,0:T(4,128)S(1)}, u32[]{:S(2)}, u32[]{:S(2)}) collective-permute-start(f32[4,4,256]{2,1,0:T(4,128)S(1)} %reduce_sum.125), channel_id=1, source_target_pairs={{0,8},{4,12},{8,0},{12,4},{1,9},{5,13},{9,1},{13,5},{2,10},{6,14},... | collective-permute-start | bytes 49160 | tf_op jit(solution)/shard_map/ppermute | solution.py:10
  35.7 2.8 %collective-permute-start.11 = (f32[4,4,256]{2,1,0:T(4,128)S(1)}, f32[4,4,256]{2,1,0:T(4,128)S(1)}, u32[]{:S(2)}, u32[]{:S(2)}) collective-permute-start(f32[4,4,256]{2,1,0:T(4,128)S(1)} %reduce_sum.125), channel_id=1, source_target_pairs={{0,12},{4,0},{8,4},{12,8},{1,13},{5,1},{9,5},{13,9},{2,14},{6,2},{... | collective-permute-start | bytes 49160 | tf_op jit(solution)/shard_map/ppermute | solution.py:10
  38.7 1.4 %collective-permute-done.11 = f32[4,4,256]{2,1,0:T(4,128)S(1)} collective-permute-done((f32[4,4,256]{2,1,0:T(4,128)S(1)}, f32[4,4,256]{2,1,0:T(4,128)S(1)}, u32[]{:S(2)}, u32[]{:S(2)}) %collective-permute-start.11) | collective-permute-done | bytes 16416 | tf_op jit(solution)/shard_map/ppermute | solution.py:10
  40.1 0.6 %fusion.42 = f32[256,4]{0,1:T(4,128)} fusion(f32[4,4,256]{2,1,0:T(4,128)S(1)} %reduce_sum.126, s32[]{:T(128)S(6)} %select_n.160), kind=kLoop, calls=%fused_computation.95 | loop fusion | bytes 8196 | tf_op jit(solution)/shard_map/transpose | solution.py:136
  40.8 0.4 fusion
  41.3 0.4 fusion.1
  41.7 0.6 %copy-done.2 = f32[6,512]{1,0:T(8,128)} copy-done((f32[6,512]{1,0:T(8,128)}, f32[6,512]{1,0:T(8,128)S(1)}, u32[]{:S(2)}) %copy-start.2) | copy-done | bytes 12312
  (75 shorter events, 2.7 us)
Async XLA Ops:
  0.6 1.8 %copy-start.3 = (bf16[256,24]{0,1:T(8,128)(2,1)S(1)}, bf16[256,24]{0,1:T(8,128)(2,1)}, u32[]{:S(2)}) copy-start(bf16[256,24]{0,1:T(8,128)(2,1)} %param.11) | copy-start | bytes 36868
  0.6 1.8 %copy-start.7 = (s32[256]{0:T(256)S(1)}, s32[256]{0:T(256)}, u32[]{:S(2)}) copy-start(s32[256]{0:T(256)} %param.12) | copy-start | bytes 3076
  0.7 1.8 %copy-start.6 = (s32[256]{0:T(256)S(1)}, s32[256]{0:T(256)}, u32[]{:S(2)}) copy-start(s32[256]{0:T(256)} %param.13) | copy-start | bytes 3076
  2.5 8.0 %copy-start.4 = (bf16[6,512]{1,0:T(8,128)(2,1)S(1)}, bf16[6,512]{1,0:T(8,128)(2,1)}, u32[]{:S(2)}) copy-start(bf16[6,512]{1,0:T(8,128)(2,1)} %param.9) | copy-start | bytes 18436
  2.6 8.0 %copy-start.1 = (bf16[6,64,512]{2,1,0:T(8,128)(2,1)S(1)}, bf16[6,64,512]{2,1,0:T(8,128)(2,1)}, u32[]{:S(2)}) copy-start(bf16[6,64,512]{2,1,0:T(8,128)(2,1)} %param.8) | copy-start | bytes 1179652
  2.6 14.6 %collective-permute-start.1 = (bf16[266,256]{1,0:T(8,128)(2,1)S(1)}, bf16[266,256]{1,0:T(8,128)(2,1)S(1)}, u32[]{:S(2)}, u32[]{:S(2)}) collective-permute-start(bf16[266,256]{1,0:T(8,128)(2,1)S(1)} %get-tuple-element.5), channel_id=1, source_target_pairs={{0,8},{4,12},{8,0},{12,4},{1,9},{5,13},{9,1},{13,5},{2,10},{6,14},... | collective-permute-start | bytes 408584 | tf_op jit(solution)/shard_map/ppermute | solution.py:104
  6.7 12.4 %collective-permute-start.2 = (bf16[266,256]{1,0:T(8,128)(2,1)S(1)}, bf16[266,256]{1,0:T(8,128)(2,1)S(1)}, u32[]{:S(2)}, u32[]{:S(2)}) collective-permute-start(bf16[266,256]{1,0:T(8,128)(2,1)S(1)} %get-tuple-element.6), channel_id=1, source_target_pairs={{0,4},{4,8},{8,12},{12,0},{1,5},{5,9},{9,13},{13,1},{2,6},{6,10},{... | collective-permute-start | bytes 408584 | tf_op jit(solution)/shard_map/ppermute | solution.py:104
  8.3 11.1 %collective-permute-start = (bf16[266,256]{1,0:T(8,128)(2,1)S(1)}, bf16[266,256]{1,0:T(8,128)(2,1)S(1)}, u32[]{:S(2)}, u32[]{:S(2)}) collective-permute-start(bf16[266,256]{1,0:T(8,128)(2,1)S(1)} %get-tuple-element.4), channel_id=1, source_target_pairs={{0,12},{4,0},{8,4},{12,8},{1,13},{5,1},{9,5},{13,9},{2,14},{6,2},{... | collective-permute-start | bytes 408584 | tf_op jit(solution)/shard_map/ppermute | solution.py:104
  10.5 1.0 %copy-start = (bf16[256,512]{1,0:T(8,128)(2,1)S(1)}, bf16[256,512]{1,0:T(8,128)(2,1)}, u32[]{:S(2)}) copy-start(bf16[256,512]{1,0:T(8,128)(2,1)} %param.10) | copy-start | bytes 786436
  12.2 0.7 %copy-start.5 = (f32[256,4]{0,1:T(4,128)S(1)}, f32[256,4]{0,1:T(4,128)}, u32[]{:S(2)}) copy-start(f32[256,4]{0,1:T(4,128)} %param.15) | copy-start | bytes 12292
  17.2 6.5 %collective-permute-start.4 = (bf16[256,256]{1,0:T(8,128)(2,1)S(1)}, bf16[256,256]{1,0:T(8,128)(2,1)S(1)}, u32[]{:S(2)}, u32[]{:S(2)}) collective-permute-start(bf16[256,256]{1,0:T(8,128)(2,1)S(1)} %slice.52), channel_id=1, source_target_pairs={{0,2},{2,0},{1,3},{3,1},{4,6},{6,4},{5,7},{7,5},{8,10},{10,8},{9,1... | collective-permute-start | bytes 393224 | tf_op jit(solution)/shard_map/ppermute | solution.py:108
  19.2 6.2 %collective-permute-start.3 = (bf16[256,256]{1,0:T(8,128)(2,1)S(1)}, bf16[256,256]{1,0:T(8,128)(2,1)S(1)}, u32[]{:S(2)}, u32[]{:S(2)}) collective-permute-start(bf16[256,256]{1,0:T(8,128)(2,1)S(1)} %slice.51), channel_id=1, source_target_pairs={{0,2},{2,0},{1,3},{3,1},{4,6},{6,4},{5,7},{7,5},{8,10},{10,8},{9,1... | collective-permute-start | bytes 393224 | tf_op jit(solution)/shard_map/ppermute | solution.py:108
  19.4 7.3 %collective-permute-start.5 = (bf16[256,256]{1,0:T(8,128)(2,1)S(1)}, bf16[256,256]{1,0:T(8,128)(2,1)S(1)}, u32[]{:S(2)}, u32[]{:S(2)}) collective-permute-start(bf16[256,256]{1,0:T(8,128)(2,1)S(1)} %slice.53), channel_id=1, source_target_pairs={{0,2},{2,0},{1,3},{3,1},{4,6},{6,4},{5,7},{7,5},{8,10},{10,8},{9,1... | collective-permute-start | bytes 393224 | tf_op jit(solution)/shard_map/ppermute | solution.py:108
  27.6 3.2 %collective-permute-start.6 = (f32[4,4,256]{2,1,0:T(4,128)S(1)}, f32[4,4,256]{2,1,0:T(4,128)S(1)}, u32[]{:S(2)}, u32[]{:S(2)}) collective-permute-start(f32[4,4,256]{2,1,0:T(4,128)S(1)} %constant_dynamic-update-slice_fusion.2), channel_id=1, source_target_pairs={{0,1},{1,2},{2,3},{3,0},{4,5},{5,6},{6,7},{7,4},{8,9},{9,10},{10,1... | collective-permute-start | bytes 49160 | tf_op jit(solution)/shard_map/ppermute | solution.py:10
  27.7 3.8 %collective-permute-start.7 = (f32[4,4,256]{2,1,0:T(4,128)S(1)}, f32[4,4,256]{2,1,0:T(4,128)S(1)}, u32[]{:S(2)}, u32[]{:S(2)}) collective-permute-start(f32[4,4,256]{2,1,0:T(4,128)S(1)} %constant_dynamic-update-slice_fusion.2), channel_id=1, source_target_pairs={{0,2},{1,3},{2,0},{3,1},{4,6},{5,7},{6,4},{7,5},{8,10},{9,11},{10,... | collective-permute-start | bytes 49160 | tf_op jit(solution)/shard_map/ppermute | solution.py:10
  29.0 2.8 %collective-permute-start.8 = (f32[4,4,256]{2,1,0:T(4,128)S(1)}, f32[4,4,256]{2,1,0:T(4,128)S(1)}, u32[]{:S(2)}, u32[]{:S(2)}) collective-permute-start(f32[4,4,256]{2,1,0:T(4,128)S(1)} %constant_dynamic-update-slice_fusion.2), channel_id=1, source_target_pairs={{0,3},{1,0},{2,1},{3,2},{4,7},{5,4},{6,5},{7,6},{8,11},{9,8},{10,9... | collective-permute-start | bytes 49160 | tf_op jit(solution)/shard_map/ppermute | solution.py:10
  31.8 6.8 %collective-permute-start.9 = (f32[4,4,256]{2,1,0:T(4,128)S(1)}, f32[4,4,256]{2,1,0:T(4,128)S(1)}, u32[]{:S(2)}, u32[]{:S(2)}) collective-permute-start(f32[4,4,256]{2,1,0:T(4,128)S(1)} %reduce_sum.125), channel_id=1, source_target_pairs={{0,4},{4,8},{8,12},{12,0},{1,5},{5,9},{9,13},{13,1},{2,6},{6,10},{... | collective-permute-start | bytes 49160 | tf_op jit(solution)/shard_map/ppermute | solution.py:10
  33.7 4.9 %collective-permute-start.10 = (f32[4,4,256]{2,1,0:T(4,128)S(1)}, f32[4,4,256]{2,1,0:T(4,128)S(1)}, u32[]{:S(2)}, u32[]{:S(2)}) collective-permute-start(f32[4,4,256]{2,1,0:T(4,128)S(1)} %reduce_sum.125), channel_id=1, source_target_pairs={{0,8},{4,12},{8,0},{12,4},{1,9},{5,13},{9,1},{13,5},{2,10},{6,14},... | collective-permute-start | bytes 49160 | tf_op jit(solution)/shard_map/ppermute | solution.py:10
  35.7 4.3 %collective-permute-start.11 = (f32[4,4,256]{2,1,0:T(4,128)S(1)}, f32[4,4,256]{2,1,0:T(4,128)S(1)}, u32[]{:S(2)}, u32[]{:S(2)}) collective-permute-start(f32[4,4,256]{2,1,0:T(4,128)S(1)} %reduce_sum.125), channel_id=1, source_target_pairs={{0,12},{4,0},{8,4},{12,8},{1,13},{5,1},{9,5},{13,9},{2,14},{6,2},{... | collective-permute-start | bytes 49160 | tf_op jit(solution)/shard_map/ppermute | solution.py:10
  41.7 0.6 %copy-start.2 = (f32[6,512]{1,0:T(8,128)}, f32[6,512]{1,0:T(8,128)S(1)}, u32[]{:S(2)}) copy-start(f32[6,512]{1,0:T(8,128)S(1)} %constant_dynamic-update-slice_fusion) | copy-start | bytes 36868

commit v10 on v9

--- a/solution.py
+++ b/solution.py
@@ -143,21 +143,18 @@
         resid = jnp.sum(mis_rows[:, :, None] * hot_all, axis=1)
         spread = (len_all[:, :, None] * resid[:, None, :]).astype(bf16)
         spread = spread.reshape(n_paths * path_rows, own_cols * modes)
-        summed = []
-        for j in range(len(offsets)):
-            dw_all = jnp.concatenate([unpacked[s][0][j] for s in rev], axis=0)
-            summed.append(
-                lax.dot_general(
-                    spread, dw_all, (((0,), (0,)), ((), ())), preferred_element_type=f32
-                )
-            )
-        grads = []
-        for acc, off in zip(summed, offsets):
-            panel_part = lax.dynamic_slice_in_dim(panels, off, width, axis=2).astype(f32)
-            grads.append(jnp.sum(acc.reshape(own_cols, modes, width) * panel_part, axis=1))
-        gradient = jnp.zeros((own_cols, depth_half), f32)
-        for g, off in zip(grads, offsets):
-            gradient = lax.dynamic_update_slice_in_dim(gradient, g, off, axis=1)
+        full_blocks = []
+        for s in rev:
+            full = unpacked[s][0][0] if len(offsets) == 1 else jnp.zeros((path_rows, depth_half), bf16)
+            if len(offsets) > 1:
+                for dw_part, off in zip(unpacked[s][0], offsets):
+                    full = lax.dynamic_update_slice_in_dim(full, dw_part, off, axis=1)
+            full_blocks.append(full)
+        dw_all = jnp.concatenate(full_blocks, axis=0)
+        summed = lax.dot_general(
+            spread, dw_all, (((0,), (0,)), ((), ())), preferred_element_type=f32
+        ).reshape(own_cols, modes, depth_half)
+        gradient = jnp.sum(summed * panels.astype(f32), axis=1)
         return (gradient, misfit)
 
     return shards

time: 42.5 us -> 43 us (1.012)
    slice x3, local copies, waits for them, and re-layouts: 0.03 us -> 1.38 us  [shards(): part_rows = got[:path_rows]]
    dynamic_slice x1, local copies, waits for them, and re-layouts: 0.98 us -> 0.02 us  [shards(): mine = lax.dynamic_slice_in_dim(depth_weight, own_off, width, axis=1)]
    ppermute x3, waiting for transfers between devices: 4.34 us -> 5.19 us  [shards(): got = lax.ppermute(payload, 'paths', perm)]
    ppermute x3, waiting for transfers between devices: 3.65 us -> 2.82 us  [shards(): dw_parts.append(lax.ppermute(part_rows, 'cols', [(0, 1), (1, 0)]))]
    convert_element_type x3 -> x4, other arithmetic: 0.03 us -> 0.74 us  [decode(): return (len_b, rows[own_cols:own_cols + kept].T.astype(jnp.int32))]
    convert_element_type x1 -> x0, other arithmetic: 0.7 us -> none  [shards(): mi_t = mode_index.T.astype(bf16)]
    unnamed x16 -> x18, local copies, waits for them, and re-layouts: 1.96 us -> 1.35 us
    dot_general x2 -> x1, matrix products: 0.77 us -> 1.19 us  [shards(): lax.dot_general(spread, dw_all, (((0,), (0,)), ((), ())), preferred_eleme...]
  transfers between devices with their start and end apart: 12 -> 12, of which waited for: 8 -> 7; matrix products, arithmetic and copies ran while one was open for 6% -> 10% of each run, Pallas kernels for 0% -> 0%
where the time goes in v10:
time: 43 us; the launch traced here: 42.8 us
  starting transfers between devices  21.5 us (50%)
  waiting for transfers between devices  10.9 us (25%)
  local copies, waits for them, and re-layouts  4.28 us (10%)
  matrix products  3.26 us (8%)
  other arithmetic  1.67 us (4%)
  between operations  1.15 us (3%)
    ppermute x6, starting transfers between devices, shifted_copies(): copies.append(lax.ppermute(x, axes, perm))  9.69 us
    ppermute x3, starting transfers between devices, shards(): got = lax.ppermute(payload, 'paths', perm)  7.93 us
    ppermute x3, waiting for transfers between devices, shards(): got = lax.ppermute(payload, 'paths', perm)  5.19 us
    ppermute x3, starting transfers between devices, shards(): dw_parts.append(lax.ppermute(part_rows, 'cols', [(0, 1), (1, 0)]))  3.93 us
    ppermute x6, waiting for transfers between devices, shifted_copies(): copies.append(lax.ppermute(x, axes, perm))  2.84 us
    ppermute x3, waiting for transfers between devices, shards(): dw_parts.append(lax.ppermute(part_rows, 'cols', [(0, 1), (1, 0)]))  2.82 us
    dot_general x8, matrix products, shards(): lax.dot_general(dw_part, sc_part, (((1,), (1,)), ((), ())), preferred_ele...  2.07 us
    slice x3, local copies, waits for them, and re-layouts, shards(): part_rows = got[:path_rows]  1.38 us
  transfers between devices with their start and end apart: 12, of which 7 were waited for; matrix products, arithmetic and copies ran while one was open for 10% of the time, Pallas kernels for 0%

profile of v10, /device:TPU:0, one launch (start us, length us, event | category | flops | bytes accessed | tf_op | source)
XLA Modules:
  0.0 42.8 jit_solution(9209398952256983353)
XLA Ops:
  0.7 0.7 %convert_convert_fusion = (s32[256,4]{0,1:T(4,128)S(1)}, bf16[4,256]{1,0:T(4,128)(2,1)S(1)}) fusion(s32[256,4]{0,1:T(4,128)} %param.14), kind=kLoop, calls=%fused_computation.95 | loop fusion | flops 2048 | bytes 10240 | tf_op jit(solution)/shard_map/convert_element_type | solution.py:71
  1.8 4.1 %collective-permute-start.1 = (bf16[266,256]{1,0:T(8,128)(2,1)S(1)}, bf16[266,256]{1,0:T(8,128)(2,1)S(1)}, u32[]{:S(2)}, u32[]{:S(2)}) collective-permute-start(bf16[266,256]{1,0:T(8,128)(2,1)S(1)} %get-tuple-element.11), channel_id=1, source_target_pairs={{0,8},{4,12},{8,0},{12,4},{1,9},{5,13},{9,1},{13,5},{2,10},{6,14},... | collective-permute-start | bytes 408584 | tf_op jit(solution)/shard_map/ppermute | solution.py:104
  5.9 1.6 %collective-permute-start.2 = (bf16[266,256]{1,0:T(8,128)(2,1)S(1)}, bf16[266,256]{1,0:T(8,128)(2,1)S(1)}, u32[]{:S(2)}, u32[]{:S(2)}) collective-permute-start(bf16[266,256]{1,0:T(8,128)(2,1)S(1)} %get-tuple-element.12), channel_id=1, source_target_pairs={{0,4},{4,8},{8,12},{12,0},{1,5},{5,9},{9,13},{13,1},{2,6},{6,10},{... | collective-permute-start | bytes 408584 | tf_op jit(solution)/shard_map/ppermute | solution.py:104
  7.5 2.2 %collective-permute-start = (bf16[266,256]{1,0:T(8,128)(2,1)S(1)}, bf16[266,256]{1,0:T(8,128)(2,1)S(1)}, u32[]{:S(2)}, u32[]{:S(2)}) collective-permute-start(bf16[266,256]{1,0:T(8,128)(2,1)S(1)} %get-tuple-element.10), channel_id=1, source_target_pairs={{0,12},{4,0},{8,4},{12,8},{1,13},{5,1},{9,5},{13,9},{2,14},{6,2},{... | collective-permute-start | bytes 408584 | tf_op jit(solution)/shard_map/ppermute | solution.py:104
  9.8 0.3 fusion.22
  10.1 0.3 convolution_add_fusion.3
  10.7 0.5 %copy-done.6 = f32[256,4]{0,1:T(4,128)S(1)} copy-done((f32[256,4]{0,1:T(4,128)S(1)}, f32[256,4]{0,1:T(4,128)}, u32[]{:S(2)}) %copy-start.6) | copy-done | bytes 4120
  11.2 5.2 %collective-permute-done.1 = bf16[266,256]{1,0:T(8,128)(2,1)S(1)} collective-permute-done((bf16[266,256]{1,0:T(8,128)(2,1)S(1)}, bf16[266,256]{1,0:T(8,128)(2,1)S(1)}, u32[]{:S(2)}, u32[]{:S(2)}) %collective-permute-start.1) | collective-permute-done | bytes 136224 | tf_op jit(solution)/shard_map/ppermute | solution.py:104
  16.5 1.9 %collective-permute-start.4 = (bf16[256,256]{1,0:T(8,128)(2,1)S(1)}, bf16[256,256]{1,0:T(8,128)(2,1)S(1)}, u32[]{:S(2)}, u32[]{:S(2)}) collective-permute-start(bf16[256,256]{1,0:T(8,128)(2,1)S(1)} %get-tuple-element.6), channel_id=1, source_target_pairs={{0,2},{2,0},{1,3},{3,1},{4,6},{6,4},{5,7},{7,5},{8,10},{10,8},{9,1... | collective-permute-start | bytes 393224 | tf_op jit(solution)/shard_map/ppermute | solution.py:108
  18.4 0.7 %fusion.41 = (bf16[256,256]{1,0:T(8,128)(2,1)}, bf16[256,512]{1,0:T(8,128)(2,1)S(1)}) fusion(bf16[266,256]{1,0:T(8,128)(2,1)S(1)} %collective-permute-done.2, bf16[256,512]{1,0:T(8,128)(2,1)S(1)} %broadcast.56.clone.1, s32[]{:T(128)S(6)} %select_n.135), kind=kLoop, calls=%fused_computation.104 | loop fusion | bytes 393220 | tf_op jit(solution)/shard_map/slice | solution.py:105
  19.1 0.7 %copy-done.2 = bf16[256,512]{1,0:T(8,128)(2,1)} copy-done((bf16[256,512]{1,0:T(8,128)(2,1)}, bf16[256,512]{1,0:T(8,128)(2,1)S(1)}, u32[]{:S(2)}) %copy-start.2) | copy-done | bytes 262168
  19.8 0.2 collective-permute-start.3
  20.0 0.7 %fusion.39 = (bf16[256,256]{1,0:T(8,128)(2,1)}, bf16[256,512]{1,0:T(8,128)(2,1)S(1)}) fusion(bf16[266,256]{1,0:T(8,128)(2,1)S(1)} %collective-permute-done, bf16[256,512]{1,0:T(8,128)(2,1)S(1)} %broadcast.56.clone.3, s32[]{:T(128)S(6)} %select_n.135), kind=kLoop, calls=%fused_computation.102 | loop fusion | bytes 393220 | tf_op jit(solution)/shard_map/slice | solution.py:105
  20.7 1.8 %collective-permute-start.5 = (bf16[256,256]{1,0:T(8,128)(2,1)}, bf16[256,256]{1,0:T(8,128)(2,1)S(1)}, u32[]{:S(2)}, u32[]{:S(2)}) collective-permute-start(bf16[256,256]{1,0:T(8,128)(2,1)} %get-tuple-element.4), channel_id=1, source_target_pairs={{0,2},{2,0},{1,3},{3,1},{4,6},{6,4},{5,7},{7,5},{8,10},{10,8},{9,1... | collective-permute-start | bytes 393224 | tf_op jit(solution)/shard_map/ppermute | solution.py:108
  22.9 0.3 fusion.14
  23.1 0.3 convolution_add_fusion.1
  23.6 2.1 %collective-permute-done.3 = bf16[256,256]{1,0:T(8,128)(2,1)S(1)} collective-permute-done((bf16[256,256]{1,0:T(8,128)(2,1)}, bf16[256,256]{1,0:T(8,128)(2,1)S(1)}, u32[]{:S(2)}, u32[]{:S(2)}) %collective-permute-start.3) | collective-permute-done | bytes 131104 | tf_op jit(solution)/shard_map/ppermute | solution.py:108
  25.7 0.3 fusion.16
  26.0 0.3 convolution_add_fusion.2
  26.6 0.6 %collective-permute-done.5 = bf16[256,256]{1,0:T(8,128)(2,1)S(1)} collective-permute-done((bf16[256,256]{1,0:T(8,128)(2,1)}, bf16[256,256]{1,0:T(8,128)(2,1)S(1)}, u32[]{:S(2)}, u32[]{:S(2)}) %collective-permute-start.5) | collective-permute-done | bytes 131104 | tf_op jit(solution)/shard_map/ppermute | solution.py:108
  27.1 0.3 fusion.12
  27.4 0.3 convolution_add_fusion
  28.0 0.9 %collective-permute-start.7 = (f32[4,4,256]{2,1,0:T(4,128)S(1)}, f32[4,4,256]{2,1,0:T(4,128)S(1)}, u32[]{:S(2)}, u32[]{:S(2)}) collective-permute-start(f32[4,4,256]{2,1,0:T(4,128)S(1)} %constant_dynamic-update-slice_fusion.7), channel_id=1, source_target_pairs={{0,2},{1,3},{2,0},{3,1},{4,6},{5,7},{6,4},{7,5},{8,10},{9,11},{10,... | collective-permute-start | bytes 49160 | tf_op jit(solution)/shard_map/ppermute | solution.py:10
  28.9 1.4 %collective-permute-start.8 = (f32[4,4,256]{2,1,0:T(4,128)S(1)}, f32[4,4,256]{2,1,0:T(4,128)S(1)}, u32[]{:S(2)}, u32[]{:S(2)}) collective-permute-start(f32[4,4,256]{2,1,0:T(4,128)S(1)} %constant_dynamic-update-slice_fusion.7), channel_id=1, source_target_pairs={{0,3},{1,0},{2,1},{3,2},{4,7},{5,4},{6,5},{7,6},{8,11},{9,8},{10,9... | collective-permute-start | bytes 49160 | tf_op jit(solution)/shard_map/ppermute | solution.py:10
  30.4 0.7 %collective-permute-done.6 = f32[4,4,256]{2,1,0:T(4,128)S(1)} collective-permute-done((f32[4,4,256]{2,1,0:T(4,128)S(1)}, f32[4,4,256]{2,1,0:T(4,128)S(1)}, u32[]{:S(2)}, u32[]{:S(2)}) %collective-permute-start.6) | collective-permute-done | bytes 16416 | tf_op jit(solution)/shard_map/ppermute | solution.py:10
  31.2 0.7 %collective-permute-done.7 = f32[4,4,256]{2,1,0:T(4,128)S(1)} collective-permute-done((f32[4,4,256]{2,1,0:T(4,128)S(1)}, f32[4,4,256]{2,1,0:T(4,128)S(1)}, u32[]{:S(2)}, u32[]{:S(2)}) %collective-permute-start.7) | collective-permute-done | bytes 16416 | tf_op jit(solution)/shard_map/ppermute | solution.py:10
  32.0 2.5 %collective-permute-start.9 = (f32[4,4,256]{2,1,0:T(4,128)S(1)}, f32[4,4,256]{2,1,0:T(4,128)S(1)}, u32[]{:S(2)}, u32[]{:S(2)}) collective-permute-start(f32[4,4,256]{2,1,0:T(4,128)S(1)} %reduce_sum.116), channel_id=1, source_target_pairs={{0,4},{4,8},{8,12},{12,0},{1,5},{5,9},{9,13},{13,1},{2,6},{6,10},{... | collective-permute-start | bytes 49160 | tf_op jit(solution)/shard_map/ppermute | solution.py:10
  34.5 2.0 %collective-permute-start.10 = (f32[4,4,256]{2,1,0:T(4,128)S(1)}, f32[4,4,256]{2,1,0:T(4,128)S(1)}, u32[]{:S(2)}, u32[]{:S(2)}) collective-permute-start(f32[4,4,256]{2,1,0:T(4,128)S(1)} %reduce_sum.116), channel_id=1, source_target_pairs={{0,8},{4,12},{8,0},{12,4},{1,9},{5,13},{9,1},{13,5},{2,10},{6,14},... | collective-permute-start | bytes 49160 | tf_op jit(solution)/shard_map/ppermute | solution.py:10
  36.5 2.8 %collective-permute-start.11 = (f32[4,4,256]{2,1,0:T(4,128)S(1)}, f32[4,4,256]{2,1,0:T(4,128)S(1)}, u32[]{:S(2)}, u32[]{:S(2)}) collective-permute-start(f32[4,4,256]{2,1,0:T(4,128)S(1)} %reduce_sum.116), channel_id=1, source_target_pairs={{0,12},{4,0},{8,4},{12,8},{1,13},{5,1},{9,5},{13,9},{2,14},{6,2},{... | collective-permute-start | bytes 49160 | tf_op jit(solution)/shard_map/ppermute | solution.py:10
  39.4 1.4 %collective-permute-done.11 = f32[4,4,256]{2,1,0:T(4,128)S(1)} collective-permute-done((f32[4,4,256]{2,1,0:T(4,128)S(1)}, f32[4,4,256]{2,1,0:T(4,128)S(1)}, u32[]{:S(2)}, u32[]{:S(2)}) %collective-permute-start.11) | collective-permute-done | bytes 16416 | tf_op jit(solution)/shard_map/ppermute | solution.py:10
  40.8 0.6 %fusion.34 = f32[256,4]{0,1:T(4,128)} fusion(f32[4,4,256]{2,1,0:T(4,128)S(1)} %reduce_sum.117, s32[]{:T(128)S(6)} %select_n.164), kind=kLoop, calls=%fused_computation.91 | loop fusion | bytes 8196 | tf_op jit(solution)/shard_map/transpose | solution.py:136
  41.6 1.2 %fusion = f32[6,512]{1,0:T(8,128)} fusion(bf16[256,512]{1,0:T(8,128)(2,1)S(1)} %dynamic-slice_dynamic-update-slice_fusion, bf16[256,512]{1,0:T(8,128)(2,1)S(1)} %constant_dynamic-update-slice_fusion.1, bf16[256,512]{1,0:T(8,128)(2,1)S(1)} %constant_dynamic-update-slice_fusion.3, bf16[256,512]{1,0:T(8,128)(2,1)S(1)} %constant_dynamic-update-slice_fusion.5, ...), kind=kOutput, calls=%fused_computation.2 | convolution fusion | flops 408220672 | bytes 1740800 | tf_op jit(solution)/shard_map/dot_general | solution.py:154
  (81 shorter events, 2.3 us)
Async XLA Ops:
  0.6 1.0 %copy-start = (bf16[256,512]{1,0:T(8,128)(2,1)S(1)}, bf16[256,512]{1,0:T(8,128)(2,1)}, u32[]{:S(2)}) copy-start(bf16[256,512]{1,0:T(8,128)(2,1)} %param.10) | copy-start | bytes 786436
  0.6 1.0 %copy-start.4 = (bf16[256,24]{0,1:T(8,128)(2,1)S(1)}, bf16[256,24]{0,1:T(8,128)(2,1)}, u32[]{:S(2)}) copy-start(bf16[256,24]{0,1:T(8,128)(2,1)} %param.11) | copy-start | bytes 36868
  0.7 1.0 %copy-start.7 = (s32[256]{0:T(256)S(1)}, s32[256]{0:T(256)}, u32[]{:S(2)}) copy-start(s32[256]{0:T(256)} %param.13) | copy-start | bytes 3076
  0.7 1.0 %copy-start.8 = (s32[256]{0:T(256)S(1)}, s32[256]{0:T(256)}, u32[]{:S(2)}) copy-start(s32[256]{0:T(256)} %param.12) | copy-start | bytes 3076
  1.6 8.1 %copy-start.5 = (bf16[6,512]{1,0:T(8,128)(2,1)S(1)}, bf16[6,512]{1,0:T(8,128)(2,1)}, u32[]{:S(2)}) copy-start(bf16[6,512]{1,0:T(8,128)(2,1)} %param.9) | copy-start | bytes 18436
  1.6 8.1 %copy-start.1 = (bf16[6,64,512]{2,1,0:T(8,128)(2,1)S(1)}, bf16[6,64,512]{2,1,0:T(8,128)(2,1)}, u32[]{:S(2)}) copy-start(bf16[6,64,512]{2,1,0:T(8,128)(2,1)} %param.8) | copy-start | bytes 1179652
  1.8 14.6 %collective-permute-start.1 = (bf16[266,256]{1,0:T(8,128)(2,1)S(1)}, bf16[266,256]{1,0:T(8,128)(2,1)S(1)}, u32[]{:S(2)}, u32[]{:S(2)}) collective-permute-start(bf16[266,256]{1,0:T(8,128)(2,1)S(1)} %get-tuple-element.11), channel_id=1, source_target_pairs={{0,8},{4,12},{8,0},{12,4},{1,9},{5,13},{9,1},{13,5},{2,10},{6,14},... | collective-permute-start | bytes 408584 | tf_op jit(solution)/shard_map/ppermute | solution.py:104
  5.9 12.5 %collective-permute-start.2 = (bf16[266,256]{1,0:T(8,128)(2,1)S(1)}, bf16[266,256]{1,0:T(8,128)(2,1)S(1)}, u32[]{:S(2)}, u32[]{:S(2)}) collective-permute-start(bf16[266,256]{1,0:T(8,128)(2,1)S(1)} %get-tuple-element.12), channel_id=1, source_target_pairs={{0,4},{4,8},{8,12},{12,0},{1,5},{5,9},{9,13},{13,1},{2,6},{6,10},{... | collective-permute-start | bytes 408584 | tf_op jit(solution)/shard_map/ppermute | solution.py:104
  7.5 12.5 %collective-permute-start = (bf16[266,256]{1,0:T(8,128)(2,1)S(1)}, bf16[266,256]{1,0:T(8,128)(2,1)S(1)}, u32[]{:S(2)}, u32[]{:S(2)}) collective-permute-start(bf16[266,256]{1,0:T(8,128)(2,1)S(1)} %get-tuple-element.10), channel_id=1, source_target_pairs={{0,12},{4,0},{8,4},{12,8},{1,13},{5,1},{9,5},{13,9},{2,14},{6,2},{... | collective-permute-start | bytes 408584 | tf_op jit(solution)/shard_map/ppermute | solution.py:104
  10.5 0.7 %copy-start.6 = (f32[256,4]{0,1:T(4,128)S(1)}, f32[256,4]{0,1:T(4,128)}, u32[]{:S(2)}) copy-start(f32[256,4]{0,1:T(4,128)} %param.15) | copy-start | bytes 12292
  16.5 6.4 %collective-permute-start.4 = (bf16[256,256]{1,0:T(8,128)(2,1)S(1)}, bf16[256,256]{1,0:T(8,128)(2,1)S(1)}, u32[]{:S(2)}, u32[]{:S(2)}) collective-permute-start(bf16[256,256]{1,0:T(8,128)(2,1)S(1)} %get-tuple-element.6), channel_id=1, source_target_pairs={{0,2},{2,0},{1,3},{3,1},{4,6},{6,4},{5,7},{7,5},{8,10},{10,8},{9,1... | collective-permute-start | bytes 393224 | tf_op jit(solution)/shard_map/ppermute | solution.py:108
  19.1 0.7 %copy-start.2 = (bf16[256,512]{1,0:T(8,128)(2,1)}, bf16[256,512]{1,0:T(8,128)(2,1)S(1)}, u32[]{:S(2)}) copy-start(bf16[256,512]{1,0:T(8,128)(2,1)S(1)} %get-tuple-element.9) | copy-start | bytes 786436
  19.8 5.9 %collective-permute-start.3 = (bf16[256,256]{1,0:T(8,128)(2,1)}, bf16[256,256]{1,0:T(8,128)(2,1)S(1)}, u32[]{:S(2)}, u32[]{:S(2)}) collective-permute-start(bf16[256,256]{1,0:T(8,128)(2,1)} %get-tuple-element.8), channel_id=1, source_target_pairs={{0,2},{2,0},{1,3},{3,1},{4,6},{6,4},{5,7},{7,5},{8,10},{10,8},{9,1... | collective-permute-start | bytes 393224 | tf_op jit(solution)/shard_map/ppermute | solution.py:108
  20.7 6.5 %collective-permute-start.5 = (bf16[256,256]{1,0:T(8,128)(2,1)}, bf16[256,256]{1,0:T(8,128)(2,1)S(1)}, u32[]{:S(2)}, u32[]{:S(2)}) collective-permute-start(bf16[256,256]{1,0:T(8,128)(2,1)} %get-tuple-element.4), channel_id=1, source_target_pairs={{0,2},{2,0},{1,3},{3,1},{4,6},{6,4},{5,7},{7,5},{8,10},{10,8},{9,1... | collective-permute-start | bytes 393224 | tf_op jit(solution)/shard_map/ppermute | solution.py:108
  27.9 2.5 %copy-start.3 = (bf16[256,512]{1,0:T(8,128)(2,1)S(1)}, bf16[256,512]{1,0:T(8,128)(2,1)}, u32[]{:S(2)}) copy-start(bf16[256,512]{1,0:T(8,128)(2,1)} %copy-done.2) | copy-start | bytes 786436
  28.0 3.2 %collective-permute-start.6 = (f32[4,4,256]{2,1,0:T(4,128)S(1)}, f32[4,4,256]{2,1,0:T(4,128)S(1)}, u32[]{:S(2)}, u32[]{:S(2)}) collective-permute-start(f32[4,4,256]{2,1,0:T(4,128)S(1)} %constant_dynamic-update-slice_fusion.7), channel_id=1, source_target_pairs={{0,1},{1,2},{2,3},{3,0},{4,5},{5,6},{6,7},{7,4},{8,9},{9,10},{10,1... | collective-permute-start | bytes 49160 | tf_op jit(solution)/shard_map/ppermute | solution.py:10
  28.0 3.9 %collective-permute-start.7 = (f32[4,4,256]{2,1,0:T(4,128)S(1)}, f32[4,4,256]{2,1,0:T(4,128)S(1)}, u32[]{:S(2)}, u32[]{:S(2)}) collective-permute-start(f32[4,4,256]{2,1,0:T(4,128)S(1)} %constant_dynamic-update-slice_fusion.7), channel_id=1, source_target_pairs={{0,2},{1,3},{2,0},{3,1},{4,6},{5,7},{6,4},{7,5},{8,10},{9,11},{10,... | collective-permute-start | bytes 49160 | tf_op jit(solution)/shard_map/ppermute | solution.py:10
  28.9 3.0 %collective-permute-start.8 = (f32[4,4,256]{2,1,0:T(4,128)S(1)}, f32[4,4,256]{2,1,0:T(4,128)S(1)}, u32[]{:S(2)}, u32[]{:S(2)}) collective-permute-start(f32[4,4,256]{2,1,0:T(4,128)S(1)} %constant_dynamic-update-slice_fusion.7), channel_id=1, source_target_pairs={{0,3},{1,0},{2,1},{3,2},{4,7},{5,4},{6,5},{7,6},{8,11},{9,8},{10,9... | collective-permute-start | bytes 49160 | tf_op jit(solution)/shard_map/ppermute | solution.py:10
  32.0 7.4 %collective-permute-start.9 = (f32[4,4,256]{2,1,0:T(4,128)S(1)}, f32[4,4,256]{2,1,0:T(4,128)S(1)}, u32[]{:S(2)}, u32[]{:S(2)}) collective-permute-start(f32[4,4,256]{2,1,0:T(4,128)S(1)} %reduce_sum.116), channel_id=1, source_target_pairs={{0,4},{4,8},{8,12},{12,0},{1,5},{5,9},{9,13},{13,1},{2,6},{6,10},{... | collective-permute-start | bytes 49160 | tf_op jit(solution)/shard_map/ppermute | solution.py:10
  34.5 4.9 %collective-permute-start.10 = (f32[4,4,256]{2,1,0:T(4,128)S(1)}, f32[4,4,256]{2,1,0:T(4,128)S(1)}, u32[]{:S(2)}, u32[]{:S(2)}) collective-permute-start(f32[4,4,256]{2,1,0:T(4,128)S(1)} %reduce_sum.116), channel_id=1, source_target_pairs={{0,8},{4,12},{8,0},{12,4},{1,9},{5,13},{9,1},{13,5},{2,10},{6,14},... | collective-permute-start | bytes 49160 | tf_op jit(solution)/shard_map/ppermute | solution.py:10
  36.5 4.3 %collective-permute-start.11 = (f32[4,4,256]{2,1,0:T(4,128)S(1)}, f32[4,4,256]{2,1,0:T(4,128)S(1)}, u32[]{:S(2)}, u32[]{:S(2)}) collective-permute-start(f32[4,4,256]{2,1,0:T(4,128)S(1)} %reduce_sum.116), channel_id=1, source_target_pairs={{0,12},{4,0},{8,4},{12,8},{1,13},{5,1},{9,5},{13,9},{2,14},{6,2},{... | collective-permute-start | bytes 49160 | tf_op jit(solution)/shard_map/ppermute | solution.py:10

commit v11 on v9

--- a/solution.py
+++ b/solution.py
@@ -133,11 +133,11 @@
         local = n_cols * n_depth
         misfit_all = exchange_sum(canon, ("cols", "depth"), local)
         misfit_all = exchange_sum(misfit_all, "paths", n_paths)
-        misfit = lax.dynamic_index_in_dim(misfit_all, p_idx, 0, keepdims=False).T
         rev = list(reversed(range(n_paths)))
         doubled = jnp.concatenate([misfit_all, misfit_all], axis=0)
         mis_rev = lax.dynamic_slice_in_dim(doubled, (p_idx + 1) % n_paths, n_paths, axis=0)
         mis_rows = jnp.swapaxes(mis_rev, 1, 2).reshape(n_paths * path_rows, kept)
+        misfit = mis_rev[n_paths - 1].T
         len_all = jnp.concatenate([unpacked[s][1] for s in rev], axis=0)
         hot_all = jnp.concatenate([unpacked[s][2] for s in rev], axis=0)
         resid = jnp.sum(mis_rows[:, :, None] * hot_all, axis=1)

time: 42.5 us -> 42.5 us (level)
  no operation moved by 1% of the time
where the time goes in v11:
time: 42.5 us; the launch traced here: 42.3 us
  starting transfers between devices  21.5 us (51%)
  waiting for transfers between devices  10.7 us (25%)
  local copies, waits for them, and re-layouts  4.39 us (10%)
  matrix products  2.83 us (7%)
  other arithmetic  1.65 us (4%)
  between operations  1.18 us (3%)
    ppermute x6, starting transfers between devices, shifted_copies(): copies.append(lax.ppermute(x, axes, perm))  9.49 us
    ppermute x3, starting transfers between devices, shards(): got = lax.ppermute(payload, 'paths', perm)  7.93 us
    ppermute x3, waiting for transfers between devices, shards(): got = lax.ppermute(payload, 'paths', perm)  4.34 us
    ppermute x3, starting transfers between devices, shards(): dw_parts.append(lax.ppermute(part_rows, 'cols', [(0, 1), (1, 0)]))  4.06 us
    ppermute x3, waiting for transfers between devices, shards(): dw_parts.append(lax.ppermute(part_rows, 'cols', [(0, 1), (1, 0)]))  3.65 us
    ppermute x6, waiting for transfers between devices, shifted_copies(): copies.append(lax.ppermute(x, axes, perm))  2.76 us
    dot_general x8, matrix products, shards(): lax.dot_general(dw_part, sc_part, (((1,), (1,)), ((), ())), preferred_ele...  2.06 us
    unnamed x16, local copies, waits for them, and re-layouts  1.96 us
  transfers between devices with their start and end apart: 12, of which 8 were waited for; matrix products, arithmetic and copies ran while one was open for 6% of the time, Pallas kernels for 0%

profile of v11, /device:TPU:0, one launch (start us, length us, event | category | flops | bytes accessed | tf_op | source)
XLA Modules:
  0.0 42.3 jit_solution(17524872310416515216)
XLA Ops:
  0.7 0.7 %convert_bitcast_fusion.7 = (bf16[4,256]{1,0:T(4,128)(2,1)S(1)}, s32[256,4]{0,1:T(4,128)S(1)}) fusion(s32[256,4]{0,1:T(4,128)} %param.14), kind=kLoop, calls=%fused_computation.99 | loop fusion | flops 2048 | bytes 10240 | tf_op jit(solution)/shard_map/convert_element_type | solution.py:63
  1.4 1.0 %constant_dynamic-slice_fusion = (bf16[256,256]{1,0:T(8,128)(2,1)S(1)}, bf16[256,256]{1,0:T(8,128)(2,1)S(1)}) fusion(bf16[256,512]{1,0:T(8,128)(2,1)} %param.10, s32[]{:T(128)S(6)} %select_n.136, s32[]{:T(128)S(6)} %select_n.127), kind=kLoop, calls=%fused_computation.87 | loop fusion | bytes 524296 | tf_op jit(solution)/shard_map/dynamic_slice | solution.py:94
  2.6 4.1 %collective-permute-start.1 = (bf16[266,256]{1,0:T(8,128)(2,1)S(1)}, bf16[266,256]{1,0:T(8,128)(2,1)S(1)}, u32[]{:S(2)}, u32[]{:S(2)}) collective-permute-start(bf16[266,256]{1,0:T(8,128)(2,1)S(1)} %get-tuple-element.5), channel_id=1, source_target_pairs={{0,8},{4,12},{8,0},{12,4},{1,9},{5,13},{9,1},{13,5},{2,10},{6,14},... | collective-permute-start | bytes 408584 | tf_op jit(solution)/shard_map/ppermute | solution.py:104
  6.7 1.6 %collective-permute-start.2 = (bf16[266,256]{1,0:T(8,128)(2,1)S(1)}, bf16[266,256]{1,0:T(8,128)(2,1)S(1)}, u32[]{:S(2)}, u32[]{:S(2)}) collective-permute-start(bf16[266,256]{1,0:T(8,128)(2,1)S(1)} %get-tuple-element.6), channel_id=1, source_target_pairs={{0,4},{4,8},{8,12},{12,0},{1,5},{5,9},{9,13},{13,1},{2,6},{6,10},{... | collective-permute-start | bytes 408584 | tf_op jit(solution)/shard_map/ppermute | solution.py:104
  8.3 2.2 %collective-permute-start = (bf16[266,256]{1,0:T(8,128)(2,1)S(1)}, bf16[266,256]{1,0:T(8,128)(2,1)S(1)}, u32[]{:S(2)}, u32[]{:S(2)}) collective-permute-start(bf16[266,256]{1,0:T(8,128)(2,1)S(1)} %get-tuple-element.4), channel_id=1, source_target_pairs={{0,12},{4,0},{8,4},{12,8},{1,13},{5,1},{9,5},{13,9},{2,14},{6,2},{... | collective-permute-start | bytes 408584 | tf_op jit(solution)/shard_map/ppermute | solution.py:104
  10.6 0.9 %copy-done = bf16[256,512]{1,0:T(8,128)(2,1)S(1)} copy-done((bf16[256,512]{1,0:T(8,128)(2,1)S(1)}, bf16[256,512]{1,0:T(8,128)(2,1)}, u32[]{:S(2)}) %copy-start) | copy-done | bytes 262168
  11.8 0.3 convolution_add_fusion.3
  12.4 0.5 %copy-done.5 = f32[256,4]{0,1:T(4,128)S(1)} copy-done((f32[256,4]{0,1:T(4,128)S(1)}, f32[256,4]{0,1:T(4,128)}, u32[]{:S(2)}) %copy-start.5) | copy-done | bytes 4120
  12.9 4.3 %collective-permute-done.1 = bf16[266,256]{1,0:T(8,128)(2,1)S(1)} collective-permute-done((bf16[266,256]{1,0:T(8,128)(2,1)S(1)}, bf16[266,256]{1,0:T(8,128)(2,1)S(1)}, u32[]{:S(2)}, u32[]{:S(2)}) %collective-permute-start.1) | collective-permute-done | bytes 136224 | tf_op jit(solution)/shard_map/ppermute | solution.py:104
  17.2 1.9 %collective-permute-start.4 = (bf16[256,256]{1,0:T(8,128)(2,1)S(1)}, bf16[256,256]{1,0:T(8,128)(2,1)S(1)}, u32[]{:S(2)}, u32[]{:S(2)}) collective-permute-start(bf16[256,256]{1,0:T(8,128)(2,1)S(1)} %slice.56), channel_id=1, source_target_pairs={{0,2},{2,0},{1,3},{3,1},{4,6},{6,4},{5,7},{7,5},{8,10},{10,8},{9,1... | collective-permute-start | bytes 393224 | tf_op jit(solution)/shard_map/ppermute | solution.py:108
  19.2 0.3 collective-permute-start.3
  19.4 1.9 %collective-permute-start.5 = (bf16[256,256]{1,0:T(8,128)(2,1)S(1)}, bf16[256,256]{1,0:T(8,128)(2,1)S(1)}, u32[]{:S(2)}, u32[]{:S(2)}) collective-permute-start(bf16[256,256]{1,0:T(8,128)(2,1)S(1)} %slice.57), channel_id=1, source_target_pairs={{0,2},{2,0},{1,3},{3,1},{4,6},{6,4},{5,7},{7,5},{8,10},{10,8},{9,1... | collective-permute-start | bytes 393224 | tf_op jit(solution)/shard_map/ppermute | solution.py:108
  21.6 2.2 %collective-permute-done.4 = bf16[256,256]{1,0:T(8,128)(2,1)S(1)} collective-permute-done((bf16[256,256]{1,0:T(8,128)(2,1)S(1)}, bf16[256,256]{1,0:T(8,128)(2,1)S(1)}, u32[]{:S(2)}, u32[]{:S(2)}) %collective-permute-start.4) | collective-permute-done | bytes 131104 | tf_op jit(solution)/shard_map/ppermute | solution.py:108
  24.0 0.3 convolution_add_fusion.1
  24.5 0.9 %collective-permute-done.3 = bf16[256,256]{1,0:T(8,128)(2,1)S(1)} collective-permute-done((bf16[256,256]{1,0:T(8,128)(2,1)S(1)}, bf16[256,256]{1,0:T(8,128)(2,1)S(1)}, u32[]{:S(2)}, u32[]{:S(2)}) %collective-permute-start.3) | collective-permute-done | bytes 131104 | tf_op jit(solution)/shard_map/ppermute | solution.py:108
  25.4 0.3 fusion.25
  25.6 0.3 convolution_add_fusion.2
  26.2 0.6 %collective-permute-done.5 = bf16[256,256]{1,0:T(8,128)(2,1)S(1)} collective-permute-done((bf16[256,256]{1,0:T(8,128)(2,1)S(1)}, bf16[256,256]{1,0:T(8,128)(2,1)S(1)}, u32[]{:S(2)}, u32[]{:S(2)}) %collective-permute-start.5) | collective-permute-done | bytes 131104 | tf_op jit(solution)/shard_map/ppermute | solution.py:108
  27.0 0.3 convolution_add_fusion
  27.7 1.3 %collective-permute-start.7 = (f32[4,4,256]{2,1,0:T(4,128)S(1)}, f32[4,4,256]{2,1,0:T(4,128)S(1)}, u32[]{:S(2)}, u32[]{:S(2)}) collective-permute-start(f32[4,4,256]{2,1,0:T(4,128)S(1)} %constant_dynamic-update-slice_fusion.2), channel_id=1, source_target_pairs={{0,2},{1,3},{2,0},{3,1},{4,6},{5,7},{6,4},{7,5},{8,10},{9,11},{10,... | collective-permute-start | bytes 49160 | tf_op jit(solution)/shard_map/ppermute | solution.py:10
  29.0 1.4 %collective-permute-start.8 = (f32[4,4,256]{2,1,0:T(4,128)S(1)}, f32[4,4,256]{2,1,0:T(4,128)S(1)}, u32[]{:S(2)}, u32[]{:S(2)}) collective-permute-start(f32[4,4,256]{2,1,0:T(4,128)S(1)} %constant_dynamic-update-slice_fusion.2), channel_id=1, source_target_pairs={{0,3},{1,0},{2,1},{3,2},{4,7},{5,4},{6,5},{7,6},{8,11},{9,8},{10,9... | collective-permute-start | bytes 49160 | tf_op jit(solution)/shard_map/ppermute | solution.py:10
  30.4 0.4 collective-permute-done.6
  30.8 0.6 %collective-permute-done.7 = f32[4,4,256]{2,1,0:T(4,128)S(1)} collective-permute-done((f32[4,4,256]{2,1,0:T(4,128)S(1)}, f32[4,4,256]{2,1,0:T(4,128)S(1)}, u32[]{:S(2)}, u32[]{:S(2)}) %collective-permute-start.7) | collective-permute-done | bytes 16416 | tf_op jit(solution)/shard_map/ppermute | solution.py:10
  31.5 0.3 collective-permute-done.8
  31.8 1.9 %collective-permute-start.9 = (f32[4,4,256]{2,1,0:T(4,128)S(1)}, f32[4,4,256]{2,1,0:T(4,128)S(1)}, u32[]{:S(2)}, u32[]{:S(2)}) collective-permute-start(f32[4,4,256]{2,1,0:T(4,128)S(1)} %reduce_sum.125), channel_id=1, source_target_pairs={{0,4},{4,8},{8,12},{12,0},{1,5},{5,9},{9,13},{13,1},{2,6},{6,10},{... | collective-permute-start | bytes 49160 | tf_op jit(solution)/shard_map/ppermute | solution.py:10
  33.7 2.0 %collective-permute-start.10 = (f32[4,4,256]{2,1,0:T(4,128)S(1)}, f32[4,4,256]{2,1,0:T(4,128)S(1)}, u32[]{:S(2)}, u32[]{:S(2)}) collective-permute-start(f32[4,4,256]{2,1,0:T(4,128)S(1)} %reduce_sum.125), channel_id=1, source_target_pairs={{0,8},{4,12},{8,0},{12,4},{1,9},{5,13},{9,1},{13,5},{2,10},{6,14},... | collective-permute-start | bytes 49160 | tf_op jit(solution)/shard_map/ppermute | solution.py:10
  35.7 2.8 %collective-permute-start.11 = (f32[4,4,256]{2,1,0:T(4,128)S(1)}, f32[4,4,256]{2,1,0:T(4,128)S(1)}, u32[]{:S(2)}, u32[]{:S(2)}) collective-permute-start(f32[4,4,256]{2,1,0:T(4,128)S(1)} %reduce_sum.125), channel_id=1, source_target_pairs={{0,12},{4,0},{8,4},{12,8},{1,13},{5,1},{9,5},{13,9},{2,14},{6,2},{... | collective-permute-start | bytes 49160 | tf_op jit(solution)/shard_map/ppermute | solution.py:10
  38.7 1.4 %collective-permute-done.11 = f32[4,4,256]{2,1,0:T(4,128)S(1)} collective-permute-done((f32[4,4,256]{2,1,0:T(4,128)S(1)}, f32[4,4,256]{2,1,0:T(4,128)S(1)}, u32[]{:S(2)}, u32[]{:S(2)}) %collective-permute-start.11) | collective-permute-done | bytes 16416 | tf_op jit(solution)/shard_map/ppermute | solution.py:10
  40.1 0.6 %slice_bitcast_fusion = f32[256,4]{0,1:T(4,128)} fusion(f32[4,4,256]{2,1,0:T(4,128)S(1)} %fusion.33), kind=kLoop, calls=%fused_computation.94 | loop fusion | bytes 8192 | tf_op jit(solution)/shard_map/transpose | solution.py:140
  40.8 0.4 fusion
  41.3 0.4 fusion.1
  41.7 0.6 %copy-done.2 = f32[6,512]{1,0:T(8,128)} copy-done((f32[6,512]{1,0:T(8,128)}, f32[6,512]{1,0:T(8,128)S(1)}, u32[]{:S(2)}) %copy-start.2) | copy-done | bytes 12312
  (75 shorter events, 2.7 us)
Async XLA Ops:
  0.6 1.8 %copy-start.3 = (bf16[256,24]{0,1:T(8,128)(2,1)S(1)}, bf16[256,24]{0,1:T(8,128)(2,1)}, u32[]{:S(2)}) copy-start(bf16[256,24]{0,1:T(8,128)(2,1)} %param.11) | copy-start | bytes 36868
  0.6 1.8 %copy-start.7 = (s32[256]{0:T(256)S(1)}, s32[256]{0:T(256)}, u32[]{:S(2)}) copy-start(s32[256]{0:T(256)} %param.12) | copy-start | bytes 3076
  0.7 1.8 %copy-start.6 = (s32[256]{0:T(256)S(1)}, s32[256]{0:T(256)}, u32[]{:S(2)}) copy-start(s32[256]{0:T(256)} %param.13) | copy-start | bytes 3076
  2.5 8.0 %copy-start.4 = (bf16[6,512]{1,0:T(8,128)(2,1)S(1)}, bf16[6,512]{1,0:T(8,128)(2,1)}, u32[]{:S(2)}) copy-start(bf16[6,512]{1,0:T(8,128)(2,1)} %param.9) | copy-start | bytes 18436
  2.6 8.0 %copy-start.1 = (bf16[6,64,512]{2,1,0:T(8,128)(2,1)S(1)}, bf16[6,64,512]{2,1,0:T(8,128)(2,1)}, u32[]{:S(2)}) copy-start(bf16[6,64,512]{2,1,0:T(8,128)(2,1)} %param.8) | copy-start | bytes 1179652
  2.6 14.6 %collective-permute-start.1 = (bf16[266,256]{1,0:T(8,128)(2,1)S(1)}, bf16[266,256]{1,0:T(8,128)(2,1)S(1)}, u32[]{:S(2)}, u32[]{:S(2)}) collective-permute-start(bf16[266,256]{1,0:T(8,128)(2,1)S(1)} %get-tuple-element.5), channel_id=1, source_target_pairs={{0,8},{4,12},{8,0},{12,4},{1,9},{5,13},{9,1},{13,5},{2,10},{6,14},... | collective-permute-start | bytes 408584 | tf_op jit(solution)/shard_map/ppermute | solution.py:104
  6.7 12.4 %collective-permute-start.2 = (bf16[266,256]{1,0:T(8,128)(2,1)S(1)}, bf16[266,256]{1,0:T(8,128)(2,1)S(1)}, u32[]{:S(2)}, u32[]{:S(2)}) collective-permute-start(bf16[266,256]{1,0:T(8,128)(2,1)S(1)} %get-tuple-element.6), channel_id=1, source_target_pairs={{0,4},{4,8},{8,12},{12,0},{1,5},{5,9},{9,13},{13,1},{2,6},{6,10},{... | collective-permute-start | bytes 408584 | tf_op jit(solution)/shard_map/ppermute | solution.py:104
  8.3 11.1 %collective-permute-start = (bf16[266,256]{1,0:T(8,128)(2,1)S(1)}, bf16[266,256]{1,0:T(8,128)(2,1)S(1)}, u32[]{:S(2)}, u32[]{:S(2)}) collective-permute-start(bf16[266,256]{1,0:T(8,128)(2,1)S(1)} %get-tuple-element.4), channel_id=1, source_target_pairs={{0,12},{4,0},{8,4},{12,8},{1,13},{5,1},{9,5},{13,9},{2,14},{6,2},{... | collective-permute-start | bytes 408584 | tf_op jit(solution)/shard_map/ppermute | solution.py:104
  10.5 1.0 %copy-start = (bf16[256,512]{1,0:T(8,128)(2,1)S(1)}, bf16[256,512]{1,0:T(8,128)(2,1)}, u32[]{:S(2)}) copy-start(bf16[256,512]{1,0:T(8,128)(2,1)} %param.10) | copy-start | bytes 786436
  12.2 0.7 %copy-start.5 = (f32[256,4]{0,1:T(4,128)S(1)}, f32[256,4]{0,1:T(4,128)}, u32[]{:S(2)}) copy-start(f32[256,4]{0,1:T(4,128)} %param.15) | copy-start | bytes 12292
  17.2 6.5 %collective-permute-start.4 = (bf16[256,256]{1,0:T(8,128)(2,1)S(1)}, bf16[256,256]{1,0:T(8,128)(2,1)S(1)}, u32[]{:S(2)}, u32[]{:S(2)}) collective-permute-start(bf16[256,256]{1,0:T(8,128)(2,1)S(1)} %slice.56), channel_id=1, source_target_pairs={{0,2},{2,0},{1,3},{3,1},{4,6},{6,4},{5,7},{7,5},{8,10},{10,8},{9,1... | collective-permute-start | bytes 393224 | tf_op jit(solution)/shard_map/ppermute | solution.py:108
  19.2 6.2 %collective-permute-start.3 = (bf16[256,256]{1,0:T(8,128)(2,1)S(1)}, bf16[256,256]{1,0:T(8,128)(2,1)S(1)}, u32[]{:S(2)}, u32[]{:S(2)}) collective-permute-start(bf16[256,256]{1,0:T(8,128)(2,1)S(1)} %slice.55), channel_id=1, source_target_pairs={{0,2},{2,0},{1,3},{3,1},{4,6},{6,4},{5,7},{7,5},{8,10},{10,8},{9,1... | collective-permute-start | bytes 393224 | tf_op jit(solution)/shard_map/ppermute | solution.py:108
  19.4 7.3 %collective-permute-start.5 = (bf16[256,256]{1,0:T(8,128)(2,1)S(1)}, bf16[256,256]{1,0:T(8,128)(2,1)S(1)}, u32[]{:S(2)}, u32[]{:S(2)}) collective-permute-start(bf16[256,256]{1,0:T(8,128)(2,1)S(1)} %slice.57), channel_id=1, source_target_pairs={{0,2},{2,0},{1,3},{3,1},{4,6},{6,4},{5,7},{7,5},{8,10},{10,8},{9,1... | collective-permute-start | bytes 393224 | tf_op jit(solution)/shard_map/ppermute | solution.py:108
  27.6 3.2 %collective-permute-start.6 = (f32[4,4,256]{2,1,0:T(4,128)S(1)}, f32[4,4,256]{2,1,0:T(4,128)S(1)}, u32[]{:S(2)}, u32[]{:S(2)}) collective-permute-start(f32[4,4,256]{2,1,0:T(4,128)S(1)} %constant_dynamic-update-slice_fusion.2), channel_id=1, source_target_pairs={{0,1},{1,2},{2,3},{3,0},{4,5},{5,6},{6,7},{7,4},{8,9},{9,10},{10,1... | collective-permute-start | bytes 49160 | tf_op jit(solution)/shard_map/ppermute | solution.py:10
  27.7 3.8 %collective-permute-start.7 = (f32[4,4,256]{2,1,0:T(4,128)S(1)}, f32[4,4,256]{2,1,0:T(4,128)S(1)}, u32[]{:S(2)}, u32[]{:S(2)}) collective-permute-start(f32[4,4,256]{2,1,0:T(4,128)S(1)} %constant_dynamic-update-slice_fusion.2), channel_id=1, source_target_pairs={{0,2},{1,3},{2,0},{3,1},{4,6},{5,7},{6,4},{7,5},{8,10},{9,11},{10,... | collective-permute-start | bytes 49160 | tf_op jit(solution)/shard_map/ppermute | solution.py:10
  29.0 2.8 %collective-permute-start.8 = (f32[4,4,256]{2,1,0:T(4,128)S(1)}, f32[4,4,256]{2,1,0:T(4,128)S(1)}, u32[]{:S(2)}, u32[]{:S(2)}) collective-permute-start(f32[4,4,256]{2,1,0:T(4,128)S(1)} %constant_dynamic-update-slice_fusion.2), channel_id=1, source_target_pairs={{0,3},{1,0},{2,1},{3,2},{4,7},{5,4},{6,5},{7,6},{8,11},{9,8},{10,9... | collective-permute-start | bytes 49160 | tf_op jit(solution)/shard_map/ppermute | solution.py:10
  31.8 6.8 %collective-permute-start.9 = (f32[4,4,256]{2,1,0:T(4,128)S(1)}, f32[4,4,256]{2,1,0:T(4,128)S(1)}, u32[]{:S(2)}, u32[]{:S(2)}) collective-permute-start(f32[4,4,256]{2,1,0:T(4,128)S(1)} %reduce_sum.125), channel_id=1, source_target_pairs={{0,4},{4,8},{8,12},{12,0},{1,5},{5,9},{9,13},{13,1},{2,6},{6,10},{... | collective-permute-start | bytes 49160 | tf_op jit(solution)/shard_map/ppermute | solution.py:10
  33.7 4.9 %collective-permute-start.10 = (f32[4,4,256]{2,1,0:T(4,128)S(1)}, f32[4,4,256]{2,1,0:T(4,128)S(1)}, u32[]{:S(2)}, u32[]{:S(2)}) collective-permute-start(f32[4,4,256]{2,1,0:T(4,128)S(1)} %reduce_sum.125), channel_id=1, source_target_pairs={{0,8},{4,12},{8,0},{12,4},{1,9},{5,13},{9,1},{13,5},{2,10},{6,14},... | collective-permute-start | bytes 49160 | tf_op jit(solution)/shard_map/ppermute | solution.py:10
  35.7 4.3 %collective-permute-start.11 = (f32[4,4,256]{2,1,0:T(4,128)S(1)}, f32[4,4,256]{2,1,0:T(4,128)S(1)}, u32[]{:S(2)}, u32[]{:S(2)}) collective-permute-start(f32[4,4,256]{2,1,0:T(4,128)S(1)} %reduce_sum.125), channel_id=1, source_target_pairs={{0,12},{4,0},{8,4},{12,8},{1,13},{5,1},{9,5},{13,9},{2,14},{6,2},{... | collective-permute-start | bytes 49160 | tf_op jit(solution)/shard_map/ppermute | solution.py:10
  41.7 0.6 %copy-start.2 = (f32[6,512]{1,0:T(8,128)}, f32[6,512]{1,0:T(8,128)S(1)}, u32[]{:S(2)}) copy-start(f32[6,512]{1,0:T(8,128)S(1)} %constant_dynamic-update-slice_fusion) | copy-start | bytes 36868

commit v12 on v9

--- a/solution.py
+++ b/solution.py
@@ -132,7 +132,10 @@
 
         local = n_cols * n_depth
         misfit_all = exchange_sum(canon, ("cols", "depth"), local)
-        misfit_all = exchange_sum(misfit_all, "paths", n_paths)
+        if n_paths & (n_paths - 1) == 0:
+            misfit_all = butterfly_sum(misfit_all, "paths", n_paths)
+        else:
+            misfit_all = exchange_sum(misfit_all, "paths", n_paths)
         misfit = lax.dynamic_index_in_dim(misfit_all, p_idx, 0, keepdims=False).T
         rev = list(reversed(range(n_paths)))
         doubled = jnp.concatenate([misfit_all, misfit_all], axis=0)

time: 42.5 us -> 43.6 us (1.026)
  waiting for transfers between devices: 10.7 us -> 13.1 us
  starting transfers between devices: 21.5 us -> 20.3 us
    ppermute x6 -> x3, starting transfers between devices: 9.49 us -> 2.75 us  [shifted_copies(): copies.append(lax.ppermute(x, axes, perm))]
    ppermute x0 -> x2, starting transfers between devices: none -> 5.58 us  [butterfly_sum(): x = x + lax.ppermute(x, axes, perm)]
    ppermute x0 -> x2, waiting for transfers between devices: none -> 3.64 us  [butterfly_sum(): x = x + lax.ppermute(x, axes, perm)]
    ppermute x6 -> x3, waiting for transfers between devices: 2.76 us -> 1.4 us  [shifted_copies(): copies.append(lax.ppermute(x, axes, perm))]
  transfers between devices with their start and end apart: 12 -> 11, of which waited for: 8 -> 9; matrix products, arithmetic and copies ran while one was open for 6% -> 6% of each run, Pallas kernels for 0% -> 0%
where the time goes in v12:
time: 43.6 us; the launch traced here: 43.4 us
  starting transfers between devices  20.3 us (47%)
  waiting for transfers between devices  13.1 us (30%)
  local copies, waits for them, and re-layouts  4.34 us (10%)
  matrix products  2.84 us (7%)
  other arithmetic  1.63 us (4%)
  between operations  1.14 us (3%)
    ppermute x3, starting transfers between devices, shards(): got = lax.ppermute(payload, 'paths', perm)  7.93 us
    ppermute x2, starting transfers between devices, butterfly_sum(): x = x + lax.ppermute(x, axes, perm)  5.58 us
    ppermute x3, waiting for transfers between devices, shards(): got = lax.ppermute(payload, 'paths', perm)  4.34 us
    ppermute x3, starting transfers between devices, shards(): dw_parts.append(lax.ppermute(part_rows, 'cols', [(0, 1), (1, 0)]))  4.06 us
    ppermute x3, waiting for transfers between devices, shards(): dw_parts.append(lax.ppermute(part_rows, 'cols', [(0, 1), (1, 0)]))  3.71 us
    ppermute x2, waiting for transfers between devices, butterfly_sum(): x = x + lax.ppermute(x, axes, perm)  3.64 us
    ppermute x3, starting transfers between devices, shifted_copies(): copies.append(lax.ppermute(x, axes, perm))  2.75 us
    dot_general x8, matrix products, shards(): lax.dot_general(dw_part, sc_part, (((1,), (1,)), ((), ())), preferred_ele...  2.06 us
  transfers between devices with their start and end apart: 11, of which 9 were waited for; matrix products, arithmetic and copies ran while one was open for 6% of the time, Pallas kernels for 0%

profile of v12, /device:TPU:0, one launch (start us, length us, event | category | flops | bytes accessed | tf_op | source)
XLA Modules:
  0.0 43.4 jit_solution(11279052578603803737)
XLA Ops:
  0.7 0.7 %convert_bitcast_fusion.7 = (bf16[4,256]{1,0:T(4,128)(2,1)S(1)}, s32[256,4]{0,1:T(4,128)S(1)}) fusion(s32[256,4]{0,1:T(4,128)} %param.14), kind=kLoop, calls=%fused_computation.96 | loop fusion | flops 2048 | bytes 10240 | tf_op jit(solution)/shard_map/convert_element_type | solution.py:63
  1.4 1.0 %constant_dynamic-slice_fusion.1 = (bf16[256,256]{1,0:T(8,128)(2,1)S(1)}, bf16[256,256]{1,0:T(8,128)(2,1)S(1)}) fusion(bf16[256,512]{1,0:T(8,128)(2,1)} %param.10, s32[]{:T(128)S(6)} %select_n.128, s32[]{:T(128)S(6)} %select_n.119), kind=kLoop, calls=%fused_computation.84 | loop fusion | bytes 524296 | tf_op jit(solution)/shard_map/dynamic_slice | solution.py:94
  2.6 4.1 %collective-permute-start.1 = (bf16[266,256]{1,0:T(8,128)(2,1)S(1)}, bf16[266,256]{1,0:T(8,128)(2,1)S(1)}, u32[]{:S(2)}, u32[]{:S(2)}) collective-permute-start(bf16[266,256]{1,0:T(8,128)(2,1)S(1)} %get-tuple-element.5), channel_id=1, source_target_pairs={{0,8},{4,12},{8,0},{12,4},{1,9},{5,13},{9,1},{13,5},{2,10},{6,14},... | collective-permute-start | bytes 408584 | tf_op jit(solution)/shard_map/ppermute | solution.py:104
  6.7 1.6 %collective-permute-start.2 = (bf16[266,256]{1,0:T(8,128)(2,1)S(1)}, bf16[266,256]{1,0:T(8,128)(2,1)S(1)}, u32[]{:S(2)}, u32[]{:S(2)}) collective-permute-start(bf16[266,256]{1,0:T(8,128)(2,1)S(1)} %get-tuple-element.6), channel_id=1, source_target_pairs={{0,4},{4,8},{8,12},{12,0},{1,5},{5,9},{9,13},{13,1},{2,6},{6,10},{... | collective-permute-start | bytes 408584 | tf_op jit(solution)/shard_map/ppermute | solution.py:104
  8.3 2.2 %collective-permute-start = (bf16[266,256]{1,0:T(8,128)(2,1)S(1)}, bf16[266,256]{1,0:T(8,128)(2,1)S(1)}, u32[]{:S(2)}, u32[]{:S(2)}) collective-permute-start(bf16[266,256]{1,0:T(8,128)(2,1)S(1)} %get-tuple-element.4), channel_id=1, source_target_pairs={{0,12},{4,0},{8,4},{12,8},{1,13},{5,1},{9,5},{13,9},{2,14},{6,2},{... | collective-permute-start | bytes 408584 | tf_op jit(solution)/shard_map/ppermute | solution.py:104
  10.6 0.9 %copy-done = bf16[256,512]{1,0:T(8,128)(2,1)S(1)} copy-done((bf16[256,512]{1,0:T(8,128)(2,1)S(1)}, bf16[256,512]{1,0:T(8,128)(2,1)}, u32[]{:S(2)}) %copy-start) | copy-done | bytes 262168
  11.8 0.3 convolution_add_fusion.3
  12.4 0.5 %copy-done.5 = f32[256,4]{0,1:T(4,128)S(1)} copy-done((f32[256,4]{0,1:T(4,128)S(1)}, f32[256,4]{0,1:T(4,128)}, u32[]{:S(2)}) %copy-start.5) | copy-done | bytes 4120
  12.9 4.3 %collective-permute-done.1 = bf16[266,256]{1,0:T(8,128)(2,1)S(1)} collective-permute-done((bf16[266,256]{1,0:T(8,128)(2,1)S(1)}, bf16[266,256]{1,0:T(8,128)(2,1)S(1)}, u32[]{:S(2)}, u32[]{:S(2)}) %collective-permute-start.1) | collective-permute-done | bytes 136224 | tf_op jit(solution)/shard_map/ppermute | solution.py:104
  17.2 1.9 %collective-permute-start.4 = (bf16[256,256]{1,0:T(8,128)(2,1)S(1)}, bf16[256,256]{1,0:T(8,128)(2,1)S(1)}, u32[]{:S(2)}, u32[]{:S(2)}) collective-permute-start(bf16[256,256]{1,0:T(8,128)(2,1)S(1)} %slice.52), channel_id=1, source_target_pairs={{0,2},{2,0},{1,3},{3,1},{4,6},{6,4},{5,7},{7,5},{8,10},{10,8},{9,1... | collective-permute-start | bytes 393224 | tf_op jit(solution)/shard_map/ppermute | solution.py:108
  19.4 1.9 %collective-permute-start.5 = (bf16[256,256]{1,0:T(8,128)(2,1)S(1)}, bf16[256,256]{1,0:T(8,128)(2,1)S(1)}, u32[]{:S(2)}, u32[]{:S(2)}) collective-permute-start(bf16[256,256]{1,0:T(8,128)(2,1)S(1)} %slice.53), channel_id=1, source_target_pairs={{0,2},{2,0},{1,3},{3,1},{4,6},{6,4},{5,7},{7,5},{8,10},{10,8},{9,1... | collective-permute-start | bytes 393224 | tf_op jit(solution)/shard_map/ppermute | solution.py:108
  21.5 2.2 %collective-permute-done.4 = bf16[256,256]{1,0:T(8,128)(2,1)S(1)} collective-permute-done((bf16[256,256]{1,0:T(8,128)(2,1)S(1)}, bf16[256,256]{1,0:T(8,128)(2,1)S(1)}, u32[]{:S(2)}, u32[]{:S(2)}) %collective-permute-start.4) | collective-permute-done | bytes 131104 | tf_op jit(solution)/shard_map/ppermute | solution.py:108
  23.7 0.3 fusion.23
  24.0 0.3 convolution_add_fusion.1
  24.4 0.9 %collective-permute-done.3 = bf16[256,256]{1,0:T(8,128)(2,1)S(1)} collective-permute-done((bf16[256,256]{1,0:T(8,128)(2,1)S(1)}, bf16[256,256]{1,0:T(8,128)(2,1)S(1)}, u32[]{:S(2)}, u32[]{:S(2)}) %collective-permute-start.3) | collective-permute-done | bytes 131104 | tf_op jit(solution)/shard_map/ppermute | solution.py:108
  25.4 0.3 fusion.25
  25.6 0.3 convolution_add_fusion.2
  26.2 0.5 %collective-permute-done.5 = bf16[256,256]{1,0:T(8,128)(2,1)S(1)} collective-permute-done((bf16[256,256]{1,0:T(8,128)(2,1)S(1)}, bf16[256,256]{1,0:T(8,128)(2,1)S(1)}, u32[]{:S(2)}, u32[]{:S(2)}) %collective-permute-start.5) | collective-permute-done | bytes 131104 | tf_op jit(solution)/shard_map/ppermute | solution.py:108
  27.0 0.3 convolution_add_fusion
  27.7 1.3 %collective-permute-start.7 = (f32[4,4,256]{2,1,0:T(4,128)S(1)}, f32[4,4,256]{2,1,0:T(4,128)S(1)}, u32[]{:S(2)}, u32[]{:S(2)}) collective-permute-start(f32[4,4,256]{2,1,0:T(4,128)S(1)} %constant_dynamic-update-slice_fusion.2), channel_id=1, source_target_pairs={{0,2},{1,3},{2,0},{3,1},{4,6},{5,7},{6,4},{7,5},{8,10},{9,11},{10,... | collective-permute-start | bytes 49160 | tf_op jit(solution)/shard_map/ppermute | solution.py:10
  29.0 1.4 %collective-permute-start.8 = (f32[4,4,256]{2,1,0:T(4,128)S(1)}, f32[4,4,256]{2,1,0:T(4,128)S(1)}, u32[]{:S(2)}, u32[]{:S(2)}) collective-permute-start(f32[4,4,256]{2,1,0:T(4,128)S(1)} %constant_dynamic-update-slice_fusion.2), channel_id=1, source_target_pairs={{0,3},{1,0},{2,1},{3,2},{4,7},{5,4},{6,5},{7,6},{8,11},{9,8},{10,9... | collective-permute-start | bytes 49160 | tf_op jit(solution)/shard_map/ppermute | solution.py:10
  30.4 0.4 collective-permute-done.6
  30.8 0.6 %collective-permute-done.7 = f32[4,4,256]{2,1,0:T(4,128)S(1)} collective-permute-done((f32[4,4,256]{2,1,0:T(4,128)S(1)}, f32[4,4,256]{2,1,0:T(4,128)S(1)}, u32[]{:S(2)}, u32[]{:S(2)}) %collective-permute-start.7) | collective-permute-done | bytes 16416 | tf_op jit(solution)/shard_map/ppermute | solution.py:10
  31.5 0.3 collective-permute-done.8
  31.8 1.9 %collective-permute-start.9 = (f32[4,4,256]{2,1,0:T(4,128)S(1)}, f32[4,4,256]{2,1,0:T(4,128)S(1)}, u32[]{:S(2)}, u32[]{:S(2)}) collective-permute-start(f32[4,4,256]{2,1,0:T(4,128)S(1)} %reduce_sum.116), channel_id=1, source_target_pairs={{0,4},{4,0},{8,12},{12,8},{1,5},{5,1},{9,13},{13,9},{2,6},{6,2},{1... | collective-permute-start | bytes 49160 | tf_op jit(solution)/shard_map/ppermute | solution.py:30
  33.8 1.9 %collective-permute-done.9 = f32[4,4,256]{2,1,0:T(4,128)S(1)} collective-permute-done((f32[4,4,256]{2,1,0:T(4,128)S(1)}, f32[4,4,256]{2,1,0:T(4,128)S(1)}, u32[]{:S(2)}, u32[]{:S(2)}) %collective-permute-start.9) | collective-permute-done | bytes 16416 | tf_op jit(solution)/shard_map/ppermute | solution.py:30
  35.7 3.7 %collective-permute-start.10 = (f32[4,4,256]{2,1,0:T(4,128)S(1)}, f32[4,4,256]{2,1,0:T(4,128)S(1)}, u32[]{:S(2)}, u32[]{:S(2)}) collective-permute-start(f32[4,4,256]{2,1,0:T(4,128)S(1)} %add.174), channel_id=1, source_target_pairs={{0,8},{4,12},{8,0},{12,4},{1,9},{5,13},{9,1},{13,5},{2,10},{6,14},... | collective-permute-start | bytes 49160 | tf_op jit(solution)/shard_map/ppermute | solution.py:30
  39.4 1.7 %collective-permute-done.10 = f32[4,4,256]{2,1,0:T(4,128)S(1)} collective-permute-done((f32[4,4,256]{2,1,0:T(4,128)S(1)}, f32[4,4,256]{2,1,0:T(4,128)S(1)}, u32[]{:S(2)}, u32[]{:S(2)}) %collective-permute-start.10) | collective-permute-done | bytes 16416 | tf_op jit(solution)/shard_map/ppermute | solution.py:30
  41.2 0.6 %fusion.42 = f32[256,4]{0,1:T(4,128)} fusion(f32[4,4,256]{2,1,0:T(4,128)S(1)} %add.175, s32[]{:T(128)S(6)} %select_n.148), kind=kLoop, calls=%fused_computation.91 | loop fusion | bytes 8196 | tf_op jit(solution)/shard_map/transpose | solution.py:139
  41.9 0.4 fusion
  42.3 0.4 fusion.1
  42.8 0.6 %copy-done.2 = f32[6,512]{1,0:T(8,128)} copy-done((f32[6,512]{1,0:T(8,128)}, f32[6,512]{1,0:T(8,128)S(1)}, u32[]{:S(2)}) %copy-start.2) | copy-done | bytes 12312
  (69 shorter events, 2.6 us)
Async XLA Ops:
  0.6 1.8 %copy-start.3 = (bf16[256,24]{0,1:T(8,128)(2,1)S(1)}, bf16[256,24]{0,1:T(8,128)(2,1)}, u32[]{:S(2)}) copy-start(bf16[256,24]{0,1:T(8,128)(2,1)} %param.11) | copy-start | bytes 36868
  0.6 1.8 %copy-start.7 = (s32[256]{0:T(256)S(1)}, s32[256]{0:T(256)}, u32[]{:S(2)}) copy-start(s32[256]{0:T(256)} %param.12) | copy-start | bytes 3076
  0.7 1.8 %copy-start.6 = (s32[256]{0:T(256)S(1)}, s32[256]{0:T(256)}, u32[]{:S(2)}) copy-start(s32[256]{0:T(256)} %param.13) | copy-start | bytes 3076
  2.5 8.0 %copy-start.4 = (bf16[6,512]{1,0:T(8,128)(2,1)S(1)}, bf16[6,512]{1,0:T(8,128)(2,1)}, u32[]{:S(2)}) copy-start(bf16[6,512]{1,0:T(8,128)(2,1)} %param.9) | copy-start | bytes 18436
  2.6 8.0 %copy-start.1 = (bf16[6,64,512]{2,1,0:T(8,128)(2,1)S(1)}, bf16[6,64,512]{2,1,0:T(8,128)(2,1)}, u32[]{:S(2)}) copy-start(bf16[6,64,512]{2,1,0:T(8,128)(2,1)} %param.8) | copy-start | bytes 1179652
  2.6 14.6 %collective-permute-start.1 = (bf16[266,256]{1,0:T(8,128)(2,1)S(1)}, bf16[266,256]{1,0:T(8,128)(2,1)S(1)}, u32[]{:S(2)}, u32[]{:S(2)}) collective-permute-start(bf16[266,256]{1,0:T(8,128)(2,1)S(1)} %get-tuple-element.5), channel_id=1, source_target_pairs={{0,8},{4,12},{8,0},{12,4},{1,9},{5,13},{9,1},{13,5},{2,10},{6,14},... | collective-permute-start | bytes 408584 | tf_op jit(solution)/shard_map/ppermute | solution.py:104
  6.7 12.4 %collective-permute-start.2 = (bf16[266,256]{1,0:T(8,128)(2,1)S(1)}, bf16[266,256]{1,0:T(8,128)(2,1)S(1)}, u32[]{:S(2)}, u32[]{:S(2)}) collective-permute-start(bf16[266,256]{1,0:T(8,128)(2,1)S(1)} %get-tuple-element.6), channel_id=1, source_target_pairs={{0,4},{4,8},{8,12},{12,0},{1,5},{5,9},{9,13},{13,1},{2,6},{6,10},{... | collective-permute-start | bytes 408584 | tf_op jit(solution)/shard_map/ppermute | solution.py:104
  8.3 11.1 %collective-permute-start = (bf16[266,256]{1,0:T(8,128)(2,1)S(1)}, bf16[266,256]{1,0:T(8,128)(2,1)S(1)}, u32[]{:S(2)}, u32[]{:S(2)}) collective-permute-start(bf16[266,256]{1,0:T(8,128)(2,1)S(1)} %get-tuple-element.4), channel_id=1, source_target_pairs={{0,12},{4,0},{8,4},{12,8},{1,13},{5,1},{9,5},{13,9},{2,14},{6,2},{... | collective-permute-start | bytes 408584 | tf_op jit(solution)/shard_map/ppermute | solution.py:104
  10.5 1.0 %copy-start = (bf16[256,512]{1,0:T(8,128)(2,1)S(1)}, bf16[256,512]{1,0:T(8,128)(2,1)}, u32[]{:S(2)}) copy-start(bf16[256,512]{1,0:T(8,128)(2,1)} %param.10) | copy-start | bytes 786436
  12.2 0.7 %copy-start.5 = (f32[256,4]{0,1:T(4,128)S(1)}, f32[256,4]{0,1:T(4,128)}, u32[]{:S(2)}) copy-start(f32[256,4]{0,1:T(4,128)} %param.15) | copy-start | bytes 12292
  17.2 6.5 %collective-permute-start.4 = (bf16[256,256]{1,0:T(8,128)(2,1)S(1)}, bf16[256,256]{1,0:T(8,128)(2,1)S(1)}, u32[]{:S(2)}, u32[]{:S(2)}) collective-permute-start(bf16[256,256]{1,0:T(8,128)(2,1)S(1)} %slice.52), channel_id=1, source_target_pairs={{0,2},{2,0},{1,3},{3,1},{4,6},{6,4},{5,7},{7,5},{8,10},{10,8},{9,1... | collective-permute-start | bytes 393224 | tf_op jit(solution)/shard_map/ppermute | solution.py:108
  19.2 6.2 %collective-permute-start.3 = (bf16[256,256]{1,0:T(8,128)(2,1)S(1)}, bf16[256,256]{1,0:T(8,128)(2,1)S(1)}, u32[]{:S(2)}, u32[]{:S(2)}) collective-permute-start(bf16[256,256]{1,0:T(8,128)(2,1)S(1)} %slice.51), channel_id=1, source_target_pairs={{0,2},{2,0},{1,3},{3,1},{4,6},{6,4},{5,7},{7,5},{8,10},{10,8},{9,1... | collective-permute-start | bytes 393224 | tf_op jit(solution)/shard_map/ppermute | solution.py:108
  19.4 7.3 %collective-permute-start.5 = (bf16[256,256]{1,0:T(8,128)(2,1)S(1)}, bf16[256,256]{1,0:T(8,128)(2,1)S(1)}, u32[]{:S(2)}, u32[]{:S(2)}) collective-permute-start(bf16[256,256]{1,0:T(8,128)(2,1)S(1)} %slice.53), channel_id=1, source_target_pairs={{0,2},{2,0},{1,3},{3,1},{4,6},{6,4},{5,7},{7,5},{8,10},{10,8},{9,1... | collective-permute-start | bytes 393224 | tf_op jit(solution)/shard_map/ppermute | solution.py:108
  27.6 3.2 %collective-permute-start.6 = (f32[4,4,256]{2,1,0:T(4,128)S(1)}, f32[4,4,256]{2,1,0:T(4,128)S(1)}, u32[]{:S(2)}, u32[]{:S(2)}) collective-permute-start(f32[4,4,256]{2,1,0:T(4,128)S(1)} %constant_dynamic-update-slice_fusion.2), channel_id=1, source_target_pairs={{0,1},{1,2},{2,3},{3,0},{4,5},{5,6},{6,7},{7,4},{8,9},{9,10},{10,1... | collective-permute-start | bytes 49160 | tf_op jit(solution)/shard_map/ppermute | solution.py:10
  27.7 3.8 %collective-permute-start.7 = (f32[4,4,256]{2,1,0:T(4,128)S(1)}, f32[4,4,256]{2,1,0:T(4,128)S(1)}, u32[]{:S(2)}, u32[]{:S(2)}) collective-permute-start(f32[4,4,256]{2,1,0:T(4,128)S(1)} %constant_dynamic-update-slice_fusion.2), channel_id=1, source_target_pairs={{0,2},{1,3},{2,0},{3,1},{4,6},{5,7},{6,4},{7,5},{8,10},{9,11},{10,... | collective-permute-start | bytes 49160 | tf_op jit(solution)/shard_map/ppermute | solution.py:10
  29.0 2.8 %collective-permute-start.8 = (f32[4,4,256]{2,1,0:T(4,128)S(1)}, f32[4,4,256]{2,1,0:T(4,128)S(1)}, u32[]{:S(2)}, u32[]{:S(2)}) collective-permute-start(f32[4,4,256]{2,1,0:T(4,128)S(1)} %constant_dynamic-update-slice_fusion.2), channel_id=1, source_target_pairs={{0,3},{1,0},{2,1},{3,2},{4,7},{5,4},{6,5},{7,6},{8,11},{9,8},{10,9... | collective-permute-start | bytes 49160 | tf_op jit(solution)/shard_map/ppermute | solution.py:10
  31.8 3.9 %collective-permute-start.9 = (f32[4,4,256]{2,1,0:T(4,128)S(1)}, f32[4,4,256]{2,1,0:T(4,128)S(1)}, u32[]{:S(2)}, u32[]{:S(2)}) collective-permute-start(f32[4,4,256]{2,1,0:T(4,128)S(1)} %reduce_sum.116), channel_id=1, source_target_pairs={{0,4},{4,0},{8,12},{12,8},{1,5},{5,1},{9,13},{13,9},{2,6},{6,2},{1... | collective-permute-start | bytes 49160 | tf_op jit(solution)/shard_map/ppermute | solution.py:30
  35.7 5.4 %collective-permute-start.10 = (f32[4,4,256]{2,1,0:T(4,128)S(1)}, f32[4,4,256]{2,1,0:T(4,128)S(1)}, u32[]{:S(2)}, u32[]{:S(2)}) collective-permute-start(f32[4,4,256]{2,1,0:T(4,128)S(1)} %add.174), channel_id=1, source_target_pairs={{0,8},{4,12},{8,0},{12,4},{1,9},{5,13},{9,1},{13,5},{2,10},{6,14},... | collective-permute-start | bytes 49160 | tf_op jit(solution)/shard_map/ppermute | solution.py:30
  42.7 0.6 %copy-start.2 = (f32[6,512]{1,0:T(8,128)}, f32[6,512]{1,0:T(8,128)S(1)}, u32[]{:S(2)}) copy-start(f32[6,512]{1,0:T(8,128)S(1)} %constant_dynamic-update-slice_fusion) | copy-start | bytes 36868

commit v13 on v9

--- a/solution.py
+++ b/solution.py
@@ -116,15 +116,14 @@
             len_own, mi_b = decode(sm)
             one_hot = (mi_b[:, :, None] == mode_ids[None, None, :]).astype(f32)
             unpacked.append((dw_parts, len_own, one_hot))
-            weighted = None
+            part = None
             for dw_part, sc_part in zip(dw_parts, scaled_parts):
-                term = lax.dot_general(
+                weighted = lax.dot_general(
                     dw_part, sc_part, (((1,), (1,)), ((), ())), preferred_element_type=f32
-                )
-                weighted = term if weighted is None else weighted + term
-            weighted = weighted.reshape(path_rows, own_cols, modes)
-            per_mode = jnp.sum(len_own[:, :, None] * weighted, axis=1)
-            part = jnp.sum(one_hot * per_mode[:, None, :], axis=2)
+                ).reshape(path_rows, own_cols, modes)
+                per_mode = jnp.sum(len_own[:, :, None] * weighted, axis=1)
+                term = jnp.sum(one_hot * per_mode[:, None, :], axis=2)
+                part = term if part is None else part + term
             parts.append(part.T)
         first = (c_idx == 0) & (d_idx == 0)
         parts[0] = parts[0] - jnp.where(first, observed.T, jnp.zeros_like(observed.T))

time: 42.5 us -> 40.7 us (0.958)
  starting transfers between devices: 21.5 us -> 16.7 us
  waiting for transfers between devices: 10.7 us -> 14.3 us
  local copies, waits for them, and re-layouts: 4.4 us -> 3.7 us
    ppermute x6, starting transfers between devices: 9.49 us -> 6.87 us  [shifted_copies(): copies.append(lax.ppermute(x, axes, perm))]
    ppermute x3, waiting for transfers between devices: 4.34 us -> 6.89 us  [shards(): got = lax.ppermute(payload, 'paths', perm)]
    ppermute x3, starting transfers between devices: 7.93 us -> 6.12 us  [shards(): got = lax.ppermute(payload, 'paths', perm)]
    ppermute x6, waiting for transfers between devices: 2.76 us -> 3.62 us  [shifted_copies(): copies.append(lax.ppermute(x, axes, perm))]
    add x4 -> x0, local copies, waits for them, and re-layouts: 0.65 us -> none  [shards(): weighted = term if weighted is None else weighted + term]
  transfers between devices with their start and end apart: 12 -> 12, of which waited for: 8 -> 9; matrix products, arithmetic and copies ran while one was open for 6% -> 6% of each run, Pallas kernels for 0% -> 0%
where the time goes in v13:
time: 40.7 us; the launch traced here: 40.5 us
  starting transfers between devices  16.7 us (41%)
  waiting for transfers between devices  14.3 us (35%)
  local copies, waits for them, and re-layouts  3.7 us (9%)
  matrix products  2.65 us (7%)
  other arithmetic  1.9 us (5%)
  between operations  1.29 us (3%)
    ppermute x3, waiting for transfers between devices, shards(): got = lax.ppermute(payload, 'paths', perm)  6.89 us
    ppermute x6, starting transfers between devices, shifted_copies(): copies.append(lax.ppermute(x, axes, perm))  6.87 us
    ppermute x3, starting transfers between devices, shards(): got = lax.ppermute(payload, 'paths', perm)  6.12 us
    ppermute x3, waiting for transfers between devices, shards(): dw_parts.append(lax.ppermute(part_rows, 'cols', [(0, 1), (1, 0)]))  3.74 us
    ppermute x3, starting transfers between devices, shards(): dw_parts.append(lax.ppermute(part_rows, 'cols', [(0, 1), (1, 0)]))  3.71 us
    ppermute x6, waiting for transfers between devices, shifted_copies(): copies.append(lax.ppermute(x, axes, perm))  3.62 us
    unnamed x16, local copies, waits for them, and re-layouts  1.97 us
    dot_general x8, matrix products, shards(): lax.dot_general(dw_part, sc_part, (((1,), (1,)), ((), ())), preferred_ele...  1.89 us
  transfers between devices with their start and end apart: 12, of which 9 were waited for; matrix products, arithmetic and copies ran while one was open for 6% of the time, Pallas kernels for 0%

profile of v13, /device:TPU:0, one launch (start us, length us, event | category | flops | bytes accessed | tf_op | source)
XLA Modules:
  0.0 40.5 jit_solution(8023548684813546210)
XLA Ops:
  0.7 0.7 %convert_bitcast_fusion.7 = (bf16[4,256]{1,0:T(4,128)(2,1)S(1)}, s32[256,4]{0,1:T(4,128)S(1)}) fusion(s32[256,4]{0,1:T(4,128)} %param.14), kind=kLoop, calls=%fused_computation.108 | loop fusion | flops 2048 | bytes 10240 | tf_op jit(solution)/shard_map/convert_element_type | solution.py:63
  1.4 1.0 %constant_dynamic-slice_fusion.1 = (bf16[256,256]{1,0:T(8,128)(2,1)S(1)}, bf16[256,256]{1,0:T(8,128)(2,1)S(1)}) fusion(bf16[256,512]{1,0:T(8,128)(2,1)} %param.10, s32[]{:T(128)S(6)} %select_n.140, s32[]{:T(128)S(6)} %select_n.131), kind=kLoop, calls=%fused_computation.96 | loop fusion | bytes 524296 | tf_op jit(solution)/shard_map/dynamic_slice | solution.py:94
  2.6 5.1 %collective-permute-start = (bf16[266,256]{1,0:T(8,128)(2,1)S(1)}, bf16[266,256]{1,0:T(8,128)(2,1)S(1)}, u32[]{:S(2)}, u32[]{:S(2)}) collective-permute-start(bf16[266,256]{1,0:T(8,128)(2,1)S(1)} %get-tuple-element.20), channel_id=1, source_target_pairs={{0,12},{4,0},{8,4},{12,8},{1,13},{5,1},{9,5},{13,9},{2,14},{6,2},{... | collective-permute-start | bytes 408584 | tf_op jit(solution)/shard_map/ppermute | solution.py:104
  7.7 1.0 %collective-permute-start.2 = (bf16[266,256]{1,0:T(8,128)(2,1)S(1)}, bf16[266,256]{1,0:T(8,128)(2,1)S(1)}, u32[]{:S(2)}, u32[]{:S(2)}) collective-permute-start(bf16[266,256]{1,0:T(8,128)(2,1)S(1)} %get-tuple-element.22), channel_id=1, source_target_pairs={{0,4},{4,8},{8,12},{12,0},{1,5},{5,9},{9,13},{13,1},{2,6},{6,10},{... | collective-permute-start | bytes 408584 | tf_op jit(solution)/shard_map/ppermute | solution.py:104
  8.8 0.9 %copy-done = bf16[256,512]{1,0:T(8,128)(2,1)S(1)} copy-done((bf16[256,512]{1,0:T(8,128)(2,1)S(1)}, bf16[256,512]{1,0:T(8,128)(2,1)}, u32[]{:S(2)}) %copy-start) | copy-done | bytes 262168
  9.7 0.2 fusion.27
  9.9 0.2 fusion.35
  10.6 0.5 %copy-done.5 = f32[256,4]{0,1:T(4,128)S(1)} copy-done((f32[256,4]{0,1:T(4,128)S(1)}, f32[256,4]{0,1:T(4,128)}, u32[]{:S(2)}) %copy-start.5) | copy-done | bytes 4120
  11.1 0.7 %collective-permute-done = bf16[266,256]{1,0:T(8,128)(2,1)S(1)} collective-permute-done((bf16[266,256]{1,0:T(8,128)(2,1)S(1)}, bf16[266,256]{1,0:T(8,128)(2,1)S(1)}, u32[]{:S(2)}, u32[]{:S(2)}) %collective-permute-start) | collective-permute-done | bytes 136224 | tf_op jit(solution)/shard_map/ppermute | solution.py:104
  11.8 1.6 %collective-permute-start.5 = (bf16[256,256]{1,0:T(8,128)(2,1)S(1)}, bf16[256,256]{1,0:T(8,128)(2,1)S(1)}, u32[]{:S(2)}, u32[]{:S(2)}) collective-permute-start(bf16[256,256]{1,0:T(8,128)(2,1)S(1)} %slice.53), channel_id=1, source_target_pairs={{0,2},{2,0},{1,3},{3,1},{4,6},{6,4},{5,7},{7,5},{8,10},{10,8},{9,1... | collective-permute-start | bytes 393224 | tf_op jit(solution)/shard_map/ppermute | solution.py:108
  13.4 6.2 %collective-permute-done.1 = bf16[266,256]{1,0:T(8,128)(2,1)S(1)} collective-permute-done((bf16[266,256]{1,0:T(8,128)(2,1)S(1)}, bf16[266,256]{1,0:T(8,128)(2,1)S(1)}, u32[]{:S(2)}, u32[]{:S(2)}) %collective-permute-start.1) | collective-permute-done | bytes 136224 | tf_op jit(solution)/shard_map/ppermute | solution.py:104
  19.5 1.6 %collective-permute-start.4 = (bf16[256,256]{1,0:T(8,128)(2,1)S(1)}, bf16[256,256]{1,0:T(8,128)(2,1)S(1)}, u32[]{:S(2)}, u32[]{:S(2)}) collective-permute-start(bf16[256,256]{1,0:T(8,128)(2,1)S(1)} %slice.52), channel_id=1, source_target_pairs={{0,2},{2,0},{1,3},{3,1},{4,6},{6,4},{5,7},{7,5},{8,10},{10,8},{9,1... | collective-permute-start | bytes 393224 | tf_op jit(solution)/shard_map/ppermute | solution.py:108
  21.1 0.6 %collective-permute-start.3 = (bf16[256,256]{1,0:T(8,128)(2,1)S(1)}, bf16[256,256]{1,0:T(8,128)(2,1)S(1)}, u32[]{:S(2)}, u32[]{:S(2)}) collective-permute-start(bf16[256,256]{1,0:T(8,128)(2,1)S(1)} %slice.51), channel_id=1, source_target_pairs={{0,2},{2,0},{1,3},{3,1},{4,6},{6,4},{5,7},{7,5},{8,10},{10,8},{9,1... | collective-permute-start | bytes 393224 | tf_op jit(solution)/shard_map/ppermute | solution.py:108
  21.9 0.2 fusion.29
  22.1 0.2 fusion.31
  22.4 0.2 fusion.33
  22.7 0.2 fusion.21
  23.0 2.8 %collective-permute-done.4 = bf16[256,256]{1,0:T(8,128)(2,1)S(1)} collective-permute-done((bf16[256,256]{1,0:T(8,128)(2,1)S(1)}, bf16[256,256]{1,0:T(8,128)(2,1)S(1)}, u32[]{:S(2)}, u32[]{:S(2)}) %collective-permute-start.4) | collective-permute-done | bytes 131104 | tf_op jit(solution)/shard_map/ppermute | solution.py:108
  25.8 0.2 fusion.23
  26.2 1.0 %collective-permute-done.3 = bf16[256,256]{1,0:T(8,128)(2,1)S(1)} collective-permute-done((bf16[256,256]{1,0:T(8,128)(2,1)S(1)}, bf16[256,256]{1,0:T(8,128)(2,1)S(1)}, u32[]{:S(2)}, u32[]{:S(2)}) %collective-permute-start.3) | collective-permute-done | bytes 131104 | tf_op jit(solution)/shard_map/ppermute | solution.py:108
  27.7 1.6 %collective-permute-start.7 = (f32[4,4,256]{2,1,0:T(4,128)S(1)}, f32[4,4,256]{2,1,0:T(4,128)S(1)}, u32[]{:S(2)}, u32[]{:S(2)}) collective-permute-start(f32[4,4,256]{2,1,0:T(4,128)S(1)} %constant_dynamic-update-slice_fusion.2), channel_id=1, source_target_pairs={{0,2},{1,3},{2,0},{3,1},{4,6},{5,7},{6,4},{7,5},{8,10},{9,11},{10,... | collective-permute-start | bytes 49160 | tf_op jit(solution)/shard_map/ppermute | solution.py:10
  29.2 1.4 %collective-permute-start.8 = (f32[4,4,256]{2,1,0:T(4,128)S(1)}, f32[4,4,256]{2,1,0:T(4,128)S(1)}, u32[]{:S(2)}, u32[]{:S(2)}) collective-permute-start(f32[4,4,256]{2,1,0:T(4,128)S(1)} %constant_dynamic-update-slice_fusion.2), channel_id=1, source_target_pairs={{0,3},{1,0},{2,1},{3,2},{4,7},{5,4},{6,5},{7,6},{8,11},{9,8},{10,9... | collective-permute-start | bytes 49160 | tf_op jit(solution)/shard_map/ppermute | solution.py:10
  30.8 0.6 %collective-permute-done.7 = f32[4,4,256]{2,1,0:T(4,128)S(1)} collective-permute-done((f32[4,4,256]{2,1,0:T(4,128)S(1)}, f32[4,4,256]{2,1,0:T(4,128)S(1)}, u32[]{:S(2)}, u32[]{:S(2)}) %collective-permute-start.7) | collective-permute-done | bytes 16416 | tf_op jit(solution)/shard_map/ppermute | solution.py:10
  31.5 0.6 %collective-permute-done.8 = f32[4,4,256]{2,1,0:T(4,128)S(1)} collective-permute-done((f32[4,4,256]{2,1,0:T(4,128)S(1)}, f32[4,4,256]{2,1,0:T(4,128)S(1)}, u32[]{:S(2)}, u32[]{:S(2)}) %collective-permute-start.8) | collective-permute-done | bytes 16416 | tf_op jit(solution)/shard_map/ppermute | solution.py:10
  32.2 1.1 %collective-permute-start.10 = (f32[4,4,256]{2,1,0:T(4,128)S(1)}, f32[4,4,256]{2,1,0:T(4,128)S(1)}, u32[]{:S(2)}, u32[]{:S(2)}) collective-permute-start(f32[4,4,256]{2,1,0:T(4,128)S(1)} %reduce_sum.205), channel_id=1, source_target_pairs={{0,8},{4,12},{8,0},{12,4},{1,9},{5,13},{9,1},{13,5},{2,10},{6,14},... | collective-permute-start | bytes 49160 | tf_op jit(solution)/shard_map/ppermute | solution.py:10
  33.2 2.7 %collective-permute-start.11 = (f32[4,4,256]{2,1,0:T(4,128)S(1)}, f32[4,4,256]{2,1,0:T(4,128)S(1)}, u32[]{:S(2)}, u32[]{:S(2)}) collective-permute-start(f32[4,4,256]{2,1,0:T(4,128)S(1)} %reduce_sum.205), channel_id=1, source_target_pairs={{0,12},{4,0},{8,4},{12,8},{1,13},{5,1},{9,5},{13,9},{2,14},{6,2},{... | collective-permute-start | bytes 49160 | tf_op jit(solution)/shard_map/ppermute | solution.py:10
  36.0 1.8 %collective-permute-done.9 = f32[4,4,256]{2,1,0:T(4,128)S(1)} collective-permute-done((f32[4,4,256]{2,1,0:T(4,128)S(1)}, f32[4,4,256]{2,1,0:T(4,128)S(1)}, u32[]{:S(2)}, u32[]{:S(2)}) %collective-permute-start.9) | collective-permute-done | bytes 16416 | tf_op jit(solution)/shard_map/ppermute | solution.py:10
  37.9 0.4 collective-permute-done.11
  38.3 0.6 %fusion.46 = f32[256,4]{0,1:T(4,128)} fusion(f32[4,4,256]{2,1,0:T(4,128)S(1)} %reduce_sum.206, s32[]{:T(128)S(6)} %select_n.160), kind=kLoop, calls=%fused_computation.103 | loop fusion | bytes 8196 | tf_op jit(solution)/shard_map/transpose | solution.py:135
  39.1 0.4 fusion
  39.5 0.4 fusion.1
  39.9 0.6 %copy-done.2 = f32[6,512]{1,0:T(8,128)} copy-done((f32[6,512]{1,0:T(8,128)}, f32[6,512]{1,0:T(8,128)S(1)}, u32[]{:S(2)}) %copy-start.2) | copy-done | bytes 12312
  (71 shorter events, 1.9 us)
Async XLA Ops:
  0.6 1.8 %copy-start.3 = (bf16[256,24]{0,1:T(8,128)(2,1)S(1)}, bf16[256,24]{0,1:T(8,128)(2,1)}, u32[]{:S(2)}) copy-start(bf16[256,24]{0,1:T(8,128)(2,1)} %param.11) | copy-start | bytes 36868
  0.6 1.8 %copy-start.7 = (s32[256]{0:T(256)S(1)}, s32[256]{0:T(256)}, u32[]{:S(2)}) copy-start(s32[256]{0:T(256)} %param.12) | copy-start | bytes 3076
  0.7 1.8 %copy-start.6 = (s32[256]{0:T(256)S(1)}, s32[256]{0:T(256)}, u32[]{:S(2)}) copy-start(s32[256]{0:T(256)} %param.13) | copy-start | bytes 3076
  2.4 6.3 %copy-start.4 = (bf16[6,512]{1,0:T(8,128)(2,1)S(1)}, bf16[6,512]{1,0:T(8,128)(2,1)}, u32[]{:S(2)}) copy-start(bf16[6,512]{1,0:T(8,128)(2,1)} %param.9) | copy-start | bytes 18436
  2.5 6.3 %copy-start.1 = (bf16[6,64,512]{2,1,0:T(8,128)(2,1)S(1)}, bf16[6,64,512]{2,1,0:T(8,128)(2,1)}, u32[]{:S(2)}) copy-start(bf16[6,64,512]{2,1,0:T(8,128)(2,1)} %param.8) | copy-start | bytes 1179652
  2.6 9.2 %collective-permute-start = (bf16[266,256]{1,0:T(8,128)(2,1)S(1)}, bf16[266,256]{1,0:T(8,128)(2,1)S(1)}, u32[]{:S(2)}, u32[]{:S(2)}) collective-permute-start(bf16[266,256]{1,0:T(8,128)(2,1)S(1)} %get-tuple-element.20), channel_id=1, source_target_pairs={{0,12},{4,0},{8,4},{12,8},{1,13},{5,1},{9,5},{13,9},{2,14},{6,2},{... | collective-permute-start | bytes 408584 | tf_op jit(solution)/shard_map/ppermute | solution.py:104
  7.7 11.8 %collective-permute-start.1 = (bf16[266,256]{1,0:T(8,128)(2,1)S(1)}, bf16[266,256]{1,0:T(8,128)(2,1)S(1)}, u32[]{:S(2)}, u32[]{:S(2)}) collective-permute-start(bf16[266,256]{1,0:T(8,128)(2,1)S(1)} %get-tuple-element.21), channel_id=1, source_target_pairs={{0,8},{4,12},{8,0},{12,4},{1,9},{5,13},{9,1},{13,5},{2,10},{6,14},... | collective-permute-start | bytes 408584 | tf_op jit(solution)/shard_map/ppermute | solution.py:104
  7.7 13.4 %collective-permute-start.2 = (bf16[266,256]{1,0:T(8,128)(2,1)S(1)}, bf16[266,256]{1,0:T(8,128)(2,1)S(1)}, u32[]{:S(2)}, u32[]{:S(2)}) collective-permute-start(bf16[266,256]{1,0:T(8,128)(2,1)S(1)} %get-tuple-element.22), channel_id=1, source_target_pairs={{0,4},{4,8},{8,12},{12,0},{1,5},{5,9},{9,13},{13,1},{2,6},{6,10},{... | collective-permute-start | bytes 408584 | tf_op jit(solution)/shard_map/ppermute | solution.py:104
  8.7 1.0 %copy-start = (bf16[256,512]{1,0:T(8,128)(2,1)S(1)}, bf16[256,512]{1,0:T(8,128)(2,1)}, u32[]{:S(2)}) copy-start(bf16[256,512]{1,0:T(8,128)(2,1)} %param.10) | copy-start | bytes 786436
  10.4 0.7 %copy-start.5 = (f32[256,4]{0,1:T(4,128)S(1)}, f32[256,4]{0,1:T(4,128)}, u32[]{:S(2)}) copy-start(f32[256,4]{0,1:T(4,128)} %param.15) | copy-start | bytes 12292
  11.8 10.8 %collective-permute-start.5 = (bf16[256,256]{1,0:T(8,128)(2,1)S(1)}, bf16[256,256]{1,0:T(8,128)(2,1)S(1)}, u32[]{:S(2)}, u32[]{:S(2)}) collective-permute-start(bf16[256,256]{1,0:T(8,128)(2,1)S(1)} %slice.53), channel_id=1, source_target_pairs={{0,2},{2,0},{1,3},{3,1},{4,6},{6,4},{5,7},{7,5},{8,10},{10,8},{9,1... | collective-permute-start | bytes 393224 | tf_op jit(solution)/shard_map/ppermute | solution.py:108
  19.5 6.2 %collective-permute-start.4 = (bf16[256,256]{1,0:T(8,128)(2,1)S(1)}, bf16[256,256]{1,0:T(8,128)(2,1)S(1)}, u32[]{:S(2)}, u32[]{:S(2)}) collective-permute-start(bf16[256,256]{1,0:T(8,128)(2,1)S(1)} %slice.52), channel_id=1, source_target_pairs={{0,2},{2,0},{1,3},{3,1},{4,6},{6,4},{5,7},{7,5},{8,10},{10,8},{9,1... | collective-permute-start | bytes 393224 | tf_op jit(solution)/shard_map/ppermute | solution.py:108
  21.1 6.1 %collective-permute-start.3 = (bf16[256,256]{1,0:T(8,128)(2,1)S(1)}, bf16[256,256]{1,0:T(8,128)(2,1)S(1)}, u32[]{:S(2)}, u32[]{:S(2)}) collective-permute-start(bf16[256,256]{1,0:T(8,128)(2,1)S(1)} %slice.51), channel_id=1, source_target_pairs={{0,2},{2,0},{1,3},{3,1},{4,6},{6,4},{5,7},{7,5},{8,10},{10,8},{9,1... | collective-permute-start | bytes 393224 | tf_op jit(solution)/shard_map/ppermute | solution.py:108
  27.6 3.2 %collective-permute-start.6 = (f32[4,4,256]{2,1,0:T(4,128)S(1)}, f32[4,4,256]{2,1,0:T(4,128)S(1)}, u32[]{:S(2)}, u32[]{:S(2)}) collective-permute-start(f32[4,4,256]{2,1,0:T(4,128)S(1)} %constant_dynamic-update-slice_fusion.2), channel_id=1, source_target_pairs={{0,1},{1,2},{2,3},{3,0},{4,5},{5,6},{6,7},{7,4},{8,9},{9,10},{10,1... | collective-permute-start | bytes 49160 | tf_op jit(solution)/shard_map/ppermute | solution.py:10
  27.7 3.8 %collective-permute-start.7 = (f32[4,4,256]{2,1,0:T(4,128)S(1)}, f32[4,4,256]{2,1,0:T(4,128)S(1)}, u32[]{:S(2)}, u32[]{:S(2)}) collective-permute-start(f32[4,4,256]{2,1,0:T(4,128)S(1)} %constant_dynamic-update-slice_fusion.2), channel_id=1, source_target_pairs={{0,2},{1,3},{2,0},{3,1},{4,6},{5,7},{6,4},{7,5},{8,10},{9,11},{10,... | collective-permute-start | bytes 49160 | tf_op jit(solution)/shard_map/ppermute | solution.py:10
  29.2 2.8 %collective-permute-start.8 = (f32[4,4,256]{2,1,0:T(4,128)S(1)}, f32[4,4,256]{2,1,0:T(4,128)S(1)}, u32[]{:S(2)}, u32[]{:S(2)}) collective-permute-start(f32[4,4,256]{2,1,0:T(4,128)S(1)} %constant_dynamic-update-slice_fusion.2), channel_id=1, source_target_pairs={{0,3},{1,0},{2,1},{3,2},{4,7},{5,4},{6,5},{7,6},{8,11},{9,8},{10,9... | collective-permute-start | bytes 49160 | tf_op jit(solution)/shard_map/ppermute | solution.py:10
  32.1 5.8 %collective-permute-start.9 = (f32[4,4,256]{2,1,0:T(4,128)S(1)}, f32[4,4,256]{2,1,0:T(4,128)S(1)}, u32[]{:S(2)}, u32[]{:S(2)}) collective-permute-start(f32[4,4,256]{2,1,0:T(4,128)S(1)} %reduce_sum.205), channel_id=1, source_target_pairs={{0,4},{4,8},{8,12},{12,0},{1,5},{5,9},{9,13},{13,1},{2,6},{6,10},{... | collective-permute-start | bytes 49160 | tf_op jit(solution)/shard_map/ppermute | solution.py:10
  32.2 5.7 %collective-permute-start.10 = (f32[4,4,256]{2,1,0:T(4,128)S(1)}, f32[4,4,256]{2,1,0:T(4,128)S(1)}, u32[]{:S(2)}, u32[]{:S(2)}) collective-permute-start(f32[4,4,256]{2,1,0:T(4,128)S(1)} %reduce_sum.205), channel_id=1, source_target_pairs={{0,8},{4,12},{8,0},{12,4},{1,9},{5,13},{9,1},{13,5},{2,10},{6,14},... | collective-permute-start | bytes 49160 | tf_op jit(solution)/shard_map/ppermute | solution.py:10
  33.2 5.0 %collective-permute-start.11 = (f32[4,4,256]{2,1,0:T(4,128)S(1)}, f32[4,4,256]{2,1,0:T(4,128)S(1)}, u32[]{:S(2)}, u32[]{:S(2)}) collective-permute-start(f32[4,4,256]{2,1,0:T(4,128)S(1)} %reduce_sum.205), channel_id=1, source_target_pairs={{0,12},{4,0},{8,4},{12,8},{1,13},{5,1},{9,5},{13,9},{2,14},{6,2},{... | collective-permute-start | bytes 49160 | tf_op jit(solution)/shard_map/ppermute | solution.py:10
  39.9 0.6 %copy-start.2 = (f32[6,512]{1,0:T(8,128)}, f32[6,512]{1,0:T(8,128)S(1)}, u32[]{:S(2)}) copy-start(f32[6,512]{1,0:T(8,128)S(1)} %constant_dynamic-update-slice_fusion) | copy-start | bytes 36868

commit v14 on v13

--- a/solution.py
+++ b/solution.py
@@ -91,12 +91,11 @@
             other_off = (1 - c_idx) * width
             offsets = [own_off, other_off]
             mine = lax.dynamic_slice_in_dim(depth_weight, own_off, width, axis=1)
-            theirs = lax.dynamic_slice_in_dim(depth_weight, other_off, width, axis=1)
             head = [mine]
         else:
             offsets = [0]
             head = [depth_weight]
-        blocks = [(head + ([theirs] if split else []), small_for(p_idx))]
+        blocks = [(list(head), small_for(p_idx))]
         for shift in range(1, n_paths):
             target = (p_idx + shift) % n_paths
             payload = jnp.concatenate([head[0], small_for(target)], axis=0)
@@ -107,6 +106,11 @@
             if split:
                 dw_parts.append(lax.ppermute(part_rows, "cols", [(0, 1), (1, 0)]))
             blocks.append((dw_parts, got[path_rows:]))
+        if split:
+            late_dw = depth_weight
+            if len(blocks) > 1:
+                late_dw, _ = lax.optimization_barrier((depth_weight, blocks[1][0][0]))
+            blocks[0][0].append(lax.dynamic_slice_in_dim(late_dw, other_off, width, axis=1))
         scaled_parts = [lax.dynamic_slice_in_dim(scaled, off, width, axis=1) for off in offsets]
         mode_ids = lax.iota(jnp.int32, modes)
 

time: 40.7 us -> 44 us (1.081)
  starting transfers between devices: 16.7 us -> 20.8 us
  local copies, waits for them, and re-layouts: 3.7 us -> 2.09 us
  waiting for transfers between devices: 14.3 us -> 15.1 us
    ppermute x6, starting transfers between devices: 6.87 us -> 11 us  [shifted_copies(): copies.append(lax.ppermute(x, axes, perm))]
    ppermute x3, waiting for transfers between devices: 6.89 us -> 8.34 us  [shards(): got = lax.ppermute(payload, 'paths', perm)]
    dynamic_slice x1 -> x2, local copies, waits for them, and re-layouts: 0.98 us -> 0.03 us  [the longest x1 0.02 us: shards(): lax.dynamic_slice_in_dim(late_dw, other_off, width, axis=1)]
    ppermute x6, waiting for transfers between devices: 3.62 us -> 2.76 us  [shifted_copies(): copies.append(lax.ppermute(x, axes, perm))]
    unnamed x16, local copies, waits for them, and re-layouts: 1.97 us -> 1.3 us
  transfers between devices with their start and end apart: 12 -> 12, of which waited for: 9 -> 7; matrix products, arithmetic and copies ran while one was open for 6% -> 6% of each run, Pallas kernels for 0% -> 0%
where the time goes in v14:
time: 44 us; the launch traced here: 43.8 us
  starting transfers between devices  20.8 us (47%)
  waiting for transfers between devices  15.1 us (34%)
  matrix products  2.68 us (6%)
  local copies, waits for them, and re-layouts  2.09 us (5%)
  other arithmetic  1.92 us (4%)
  between operations  1.24 us (3%)
    ppermute x6, starting transfers between devices, shifted_copies(): copies.append(lax.ppermute(x, axes, perm))  11 us
    ppermute x3, waiting for transfers between devices, shards(): got = lax.ppermute(payload, 'paths', perm)  8.34 us
    ppermute x3, starting transfers between devices, shards(): got = lax.ppermute(payload, 'paths', perm)  6.12 us
    ppermute x3, waiting for transfers between devices, shards(): dw_parts.append(lax.ppermute(part_rows, 'cols', [(0, 1), (1, 0)]))  4.01 us
    ppermute x3, starting transfers between devices, shards(): dw_parts.append(lax.ppermute(part_rows, 'cols', [(0, 1), (1, 0)]))  3.71 us
    ppermute x6, waiting for transfers between devices, shifted_copies(): copies.append(lax.ppermute(x, axes, perm))  2.76 us
    dot_general x8, matrix products, shards(): lax.dot_general(dw_part, sc_part, (((1,), (1,)), ((), ())), preferred_ele...  1.91 us
    unnamed x16, local copies, waits for them, and re-layouts  1.3 us
  transfers between devices with their start and end apart: 12, of which 7 were waited for; matrix products, arithmetic and copies ran while one was open for 6% of the time, Pallas kernels for 0%

profile of v14, /device:TPU:0, one launch (start us, length us, event | category | flops | bytes accessed | tf_op | source)
XLA Modules:
  0.0 43.8 jit_solution(11759091371074441006)
XLA Ops:
  0.7 0.7 %convert_bitcast_fusion.7 = (bf16[4,256]{1,0:T(4,128)(2,1)S(1)}, s32[256,4]{0,1:T(4,128)S(1)}) fusion(s32[256,4]{0,1:T(4,128)} %param.14), kind=kLoop, calls=%fused_computation.108 | loop fusion | flops 2048 | bytes 10240 | tf_op jit(solution)/shard_map/convert_element_type | solution.py:63
  1.8 5.1 %collective-permute-start = (bf16[266,256]{1,0:T(8,128)(2,1)S(1)}, bf16[266,256]{1,0:T(8,128)(2,1)S(1)}, u32[]{:S(2)}, u32[]{:S(2)}) collective-permute-start(bf16[266,256]{1,0:T(8,128)(2,1)S(1)} %get-tuple-element.20), channel_id=1, source_target_pairs={{0,12},{4,0},{8,4},{12,8},{1,13},{5,1},{9,5},{13,9},{2,14},{6,2},{... | collective-permute-start | bytes 408584 | tf_op jit(solution)/shard_map/ppermute | solution.py:103
  6.9 1.0 %collective-permute-start.2 = (bf16[266,256]{1,0:T(8,128)(2,1)S(1)}, bf16[266,256]{1,0:T(8,128)(2,1)S(1)}, u32[]{:S(2)}, u32[]{:S(2)}) collective-permute-start(bf16[266,256]{1,0:T(8,128)(2,1)S(1)} %get-tuple-element.22), channel_id=1, source_target_pairs={{0,4},{4,8},{8,12},{12,0},{1,5},{5,9},{9,13},{13,1},{2,6},{6,10},{... | collective-permute-start | bytes 408584 | tf_op jit(solution)/shard_map/ppermute | solution.py:103
  8.2 0.2 fusion.35
  8.5 8.3 %collective-permute-done.2 = bf16[266,256]{1,0:T(8,128)(2,1)S(1)} collective-permute-done((bf16[266,256]{1,0:T(8,128)(2,1)S(1)}, bf16[266,256]{1,0:T(8,128)(2,1)S(1)}, u32[]{:S(2)}, u32[]{:S(2)}) %collective-permute-start.2) | collective-permute-done | bytes 136224 | tf_op jit(solution)/shard_map/ppermute | solution.py:103
  16.8 1.6 %collective-permute-start.3 = (bf16[256,256]{1,0:T(8,128)(2,1)S(1)}, bf16[256,256]{1,0:T(8,128)(2,1)S(1)}, u32[]{:S(2)}, u32[]{:S(2)}) collective-permute-start(bf16[256,256]{1,0:T(8,128)(2,1)S(1)} %slice.51), channel_id=1, source_target_pairs={{0,2},{2,0},{1,3},{3,1},{4,6},{6,4},{5,7},{7,5},{8,10},{10,8},{9,1... | collective-permute-start | bytes 393224 | tf_op jit(solution)/shard_map/ppermute | solution.py:107
  18.4 0.6 %collective-permute-start.5 = (bf16[256,256]{1,0:T(8,128)(2,1)S(1)}, bf16[256,256]{1,0:T(8,128)(2,1)S(1)}, u32[]{:S(2)}, u32[]{:S(2)}) collective-permute-start(bf16[256,256]{1,0:T(8,128)(2,1)S(1)} %slice.53), channel_id=1, source_target_pairs={{0,2},{2,0},{1,3},{3,1},{4,6},{6,4},{5,7},{7,5},{8,10},{10,8},{9,1... | collective-permute-start | bytes 393224 | tf_op jit(solution)/shard_map/ppermute | solution.py:107
  19.0 1.6 %collective-permute-start.4 = (bf16[256,256]{1,0:T(8,128)(2,1)S(1)}, bf16[256,256]{1,0:T(8,128)(2,1)S(1)}, u32[]{:S(2)}, u32[]{:S(2)}) collective-permute-start(bf16[256,256]{1,0:T(8,128)(2,1)S(1)} %slice.52), channel_id=1, source_target_pairs={{0,2},{2,0},{1,3},{3,1},{4,6},{6,4},{5,7},{7,5},{8,10},{10,8},{9,1... | collective-permute-start | bytes 393224 | tf_op jit(solution)/shard_map/ppermute | solution.py:107
  20.7 0.2 fusion.27
  21.1 0.5 %copy-done.5 = f32[256,4]{0,1:T(4,128)S(1)} copy-done((f32[256,4]{0,1:T(4,128)S(1)}, f32[256,4]{0,1:T(4,128)}, u32[]{:S(2)}) %copy-start.5) | copy-done | bytes 4120
  21.7 0.2 fusion.29
  21.9 0.2 fusion.31
  22.2 0.2 fusion.33
  22.5 2.9 %collective-permute-done.5 = bf16[256,256]{1,0:T(8,128)(2,1)S(1)} collective-permute-done((bf16[256,256]{1,0:T(8,128)(2,1)S(1)}, bf16[256,256]{1,0:T(8,128)(2,1)S(1)}, u32[]{:S(2)}, u32[]{:S(2)}) %collective-permute-start.5) | collective-permute-done | bytes 131104 | tf_op jit(solution)/shard_map/ppermute | solution.py:107
  25.4 0.2 fusion.21
  25.7 1.1 %collective-permute-done.4 = bf16[256,256]{1,0:T(8,128)(2,1)S(1)} collective-permute-done((bf16[256,256]{1,0:T(8,128)(2,1)S(1)}, bf16[256,256]{1,0:T(8,128)(2,1)S(1)}, u32[]{:S(2)}, u32[]{:S(2)}) %collective-permute-start.4) | collective-permute-done | bytes 131104 | tf_op jit(solution)/shard_map/ppermute | solution.py:107
  26.8 0.2 fusion.23
  27.3 0.2 fusion.25
  27.8 1.6 %collective-permute-start.7 = (f32[4,4,256]{2,1,0:T(4,128)S(1)}, f32[4,4,256]{2,1,0:T(4,128)S(1)}, u32[]{:S(2)}, u32[]{:S(2)}) collective-permute-start(f32[4,4,256]{2,1,0:T(4,128)S(1)} %constant_dynamic-update-slice_fusion.2), channel_id=1, source_target_pairs={{0,2},{1,3},{2,0},{3,1},{4,6},{5,7},{6,4},{7,5},{8,10},{9,11},{10,... | collective-permute-start | bytes 49160 | tf_op jit(solution)/shard_map/ppermute | solution.py:10
  29.3 1.4 %collective-permute-start.8 = (f32[4,4,256]{2,1,0:T(4,128)S(1)}, f32[4,4,256]{2,1,0:T(4,128)S(1)}, u32[]{:S(2)}, u32[]{:S(2)}) collective-permute-start(f32[4,4,256]{2,1,0:T(4,128)S(1)} %constant_dynamic-update-slice_fusion.2), channel_id=1, source_target_pairs={{0,3},{1,0},{2,1},{3,2},{4,7},{5,4},{6,5},{7,6},{8,11},{9,8},{10,9... | collective-permute-start | bytes 49160 | tf_op jit(solution)/shard_map/ppermute | solution.py:10
  30.7 0.2 collective-permute-done.6
  30.9 0.6 %collective-permute-done.7 = f32[4,4,256]{2,1,0:T(4,128)S(1)} collective-permute-done((f32[4,4,256]{2,1,0:T(4,128)S(1)}, f32[4,4,256]{2,1,0:T(4,128)S(1)}, u32[]{:S(2)}, u32[]{:S(2)}) %collective-permute-start.7) | collective-permute-done | bytes 16416 | tf_op jit(solution)/shard_map/ppermute | solution.py:10
  31.6 0.6 %collective-permute-done.8 = f32[4,4,256]{2,1,0:T(4,128)S(1)} collective-permute-done((f32[4,4,256]{2,1,0:T(4,128)S(1)}, f32[4,4,256]{2,1,0:T(4,128)S(1)}, u32[]{:S(2)}, u32[]{:S(2)}) %collective-permute-start.8) | collective-permute-done | bytes 16416 | tf_op jit(solution)/shard_map/ppermute | solution.py:10
  32.2 3.1 %collective-permute-start.9 = (f32[4,4,256]{2,1,0:T(4,128)S(1)}, f32[4,4,256]{2,1,0:T(4,128)S(1)}, u32[]{:S(2)}, u32[]{:S(2)}) collective-permute-start(f32[4,4,256]{2,1,0:T(4,128)S(1)} %reduce_sum.205), channel_id=1, source_target_pairs={{0,4},{4,8},{8,12},{12,0},{1,5},{5,9},{9,13},{13,1},{2,6},{6,10},{... | collective-permute-start | bytes 49160 | tf_op jit(solution)/shard_map/ppermute | solution.py:10
  35.3 2.0 %collective-permute-start.10 = (f32[4,4,256]{2,1,0:T(4,128)S(1)}, f32[4,4,256]{2,1,0:T(4,128)S(1)}, u32[]{:S(2)}, u32[]{:S(2)}) collective-permute-start(f32[4,4,256]{2,1,0:T(4,128)S(1)} %reduce_sum.205), channel_id=1, source_target_pairs={{0,8},{4,12},{8,0},{12,4},{1,9},{5,13},{9,1},{13,5},{2,10},{6,14},... | collective-permute-start | bytes 49160 | tf_op jit(solution)/shard_map/ppermute | solution.py:10
  37.3 2.8 %collective-permute-start.11 = (f32[4,4,256]{2,1,0:T(4,128)S(1)}, f32[4,4,256]{2,1,0:T(4,128)S(1)}, u32[]{:S(2)}, u32[]{:S(2)}) collective-permute-start(f32[4,4,256]{2,1,0:T(4,128)S(1)} %reduce_sum.205), channel_id=1, source_target_pairs={{0,12},{4,0},{8,4},{12,8},{1,13},{5,1},{9,5},{13,9},{2,14},{6,2},{... | collective-permute-start | bytes 49160 | tf_op jit(solution)/shard_map/ppermute | solution.py:10
  40.2 1.4 %collective-permute-done.11 = f32[4,4,256]{2,1,0:T(4,128)S(1)} collective-permute-done((f32[4,4,256]{2,1,0:T(4,128)S(1)}, f32[4,4,256]{2,1,0:T(4,128)S(1)}, u32[]{:S(2)}, u32[]{:S(2)}) %collective-permute-start.11) | collective-permute-done | bytes 16416 | tf_op jit(solution)/shard_map/ppermute | solution.py:10
  41.6 0.6 %fusion.46 = f32[256,4]{0,1:T(4,128)} fusion(f32[4,4,256]{2,1,0:T(4,128)S(1)} %reduce_sum.206, s32[]{:T(128)S(6)} %select_n.160), kind=kLoop, calls=%fused_computation.103 | loop fusion | bytes 8196 | tf_op jit(solution)/shard_map/transpose | solution.py:139
  42.3 0.1 select_reduce_fusion
  42.4 0.4 fusion
  42.8 0.4 fusion.1
  43.2 0.6 %copy-done.2 = f32[6,512]{1,0:T(8,128)} copy-done((f32[6,512]{1,0:T(8,128)}, f32[6,512]{1,0:T(8,128)S(1)}, u32[]{:S(2)}) %copy-start.2) | copy-done | bytes 12312
  (72 shorter events, 1.5 us)
Async XLA Ops:
  0.6 1.0 %copy-start = (bf16[256,512]{1,0:T(8,128)(2,1)S(1)}, bf16[256,512]{1,0:T(8,128)(2,1)}, u32[]{:S(2)}) copy-start(bf16[256,512]{1,0:T(8,128)(2,1)} %param.10) | copy-start | bytes 786436
  0.6 1.0 %copy-start.3 = (bf16[256,24]{0,1:T(8,128)(2,1)S(1)}, bf16[256,24]{0,1:T(8,128)(2,1)}, u32[]{:S(2)}) copy-start(bf16[256,24]{0,1:T(8,128)(2,1)} %param.11) | copy-start | bytes 36868
  0.7 1.0 %copy-start.7 = (s32[256]{0:T(256)S(1)}, s32[256]{0:T(256)}, u32[]{:S(2)}) copy-start(s32[256]{0:T(256)} %param.12) | copy-start | bytes 3076
  0.7 1.0 %copy-start.6 = (s32[256]{0:T(256)S(1)}, s32[256]{0:T(256)}, u32[]{:S(2)}) copy-start(s32[256]{0:T(256)} %param.13) | copy-start | bytes 3076
  1.6 6.3 %copy-start.4 = (bf16[6,512]{1,0:T(8,128)(2,1)S(1)}, bf16[6,512]{1,0:T(8,128)(2,1)}, u32[]{:S(2)}) copy-start(bf16[6,512]{1,0:T(8,128)(2,1)} %param.9) | copy-start | bytes 18436
  1.6 6.3 %copy-start.1 = (bf16[6,64,512]{2,1,0:T(8,128)(2,1)S(1)}, bf16[6,64,512]{2,1,0:T(8,128)(2,1)}, u32[]{:S(2)}) copy-start(bf16[6,64,512]{2,1,0:T(8,128)(2,1)} %param.8) | copy-start | bytes 1179652
  1.8 16.6 %collective-permute-start = (bf16[266,256]{1,0:T(8,128)(2,1)S(1)}, bf16[266,256]{1,0:T(8,128)(2,1)S(1)}, u32[]{:S(2)}, u32[]{:S(2)}) collective-permute-start(bf16[266,256]{1,0:T(8,128)(2,1)S(1)} %get-tuple-element.20), channel_id=1, source_target_pairs={{0,12},{4,0},{8,4},{12,8},{1,13},{5,1},{9,5},{13,9},{2,14},{6,2},{... | collective-permute-start | bytes 408584 | tf_op jit(solution)/shard_map/ppermute | solution.py:103
  6.9 12.1 %collective-permute-start.1 = (bf16[266,256]{1,0:T(8,128)(2,1)S(1)}, bf16[266,256]{1,0:T(8,128)(2,1)S(1)}, u32[]{:S(2)}, u32[]{:S(2)}) collective-permute-start(bf16[266,256]{1,0:T(8,128)(2,1)S(1)} %get-tuple-element.21), channel_id=1, source_target_pairs={{0,8},{4,12},{8,0},{12,4},{1,9},{5,13},{9,1},{13,5},{2,10},{6,14},... | collective-permute-start | bytes 408584 | tf_op jit(solution)/shard_map/ppermute | solution.py:103
  6.9 9.9 %collective-permute-start.2 = (bf16[266,256]{1,0:T(8,128)(2,1)S(1)}, bf16[266,256]{1,0:T(8,128)(2,1)S(1)}, u32[]{:S(2)}, u32[]{:S(2)}) collective-permute-start(bf16[266,256]{1,0:T(8,128)(2,1)S(1)} %get-tuple-element.22), channel_id=1, source_target_pairs={{0,4},{4,8},{8,12},{12,0},{1,5},{5,9},{9,13},{13,1},{2,6},{6,10},{... | collective-permute-start | bytes 408584 | tf_op jit(solution)/shard_map/ppermute | solution.py:103
  16.8 10.4 %collective-permute-start.3 = (bf16[256,256]{1,0:T(8,128)(2,1)S(1)}, bf16[256,256]{1,0:T(8,128)(2,1)S(1)}, u32[]{:S(2)}, u32[]{:S(2)}) collective-permute-start(bf16[256,256]{1,0:T(8,128)(2,1)S(1)} %slice.51), channel_id=1, source_target_pairs={{0,2},{2,0},{1,3},{3,1},{4,6},{6,4},{5,7},{7,5},{8,10},{10,8},{9,1... | collective-permute-start | bytes 393224 | tf_op jit(solution)/shard_map/ppermute | solution.py:107
  18.4 7.0 %collective-permute-start.5 = (bf16[256,256]{1,0:T(8,128)(2,1)S(1)}, bf16[256,256]{1,0:T(8,128)(2,1)S(1)}, u32[]{:S(2)}, u32[]{:S(2)}) collective-permute-start(bf16[256,256]{1,0:T(8,128)(2,1)S(1)} %slice.53), channel_id=1, source_target_pairs={{0,2},{2,0},{1,3},{3,1},{4,6},{6,4},{5,7},{7,5},{8,10},{10,8},{9,1... | collective-permute-start | bytes 393224 | tf_op jit(solution)/shard_map/ppermute | solution.py:107
  19.0 7.8 %collective-permute-start.4 = (bf16[256,256]{1,0:T(8,128)(2,1)S(1)}, bf16[256,256]{1,0:T(8,128)(2,1)S(1)}, u32[]{:S(2)}, u32[]{:S(2)}) collective-permute-start(bf16[256,256]{1,0:T(8,128)(2,1)S(1)} %slice.52), channel_id=1, source_target_pairs={{0,2},{2,0},{1,3},{3,1},{4,6},{6,4},{5,7},{7,5},{8,10},{10,8},{9,1... | collective-permute-start | bytes 393224 | tf_op jit(solution)/shard_map/ppermute | solution.py:107
  21.0 0.7 %copy-start.5 = (f32[256,4]{0,1:T(4,128)S(1)}, f32[256,4]{0,1:T(4,128)}, u32[]{:S(2)}) copy-start(f32[256,4]{0,1:T(4,128)} %param.15) | copy-start | bytes 12292
  27.7 3.2 %collective-permute-start.6 = (f32[4,4,256]{2,1,0:T(4,128)S(1)}, f32[4,4,256]{2,1,0:T(4,128)S(1)}, u32[]{:S(2)}, u32[]{:S(2)}) collective-permute-start(f32[4,4,256]{2,1,0:T(4,128)S(1)} %constant_dynamic-update-slice_fusion.2), channel_id=1, source_target_pairs={{0,1},{1,2},{2,3},{3,0},{4,5},{5,6},{6,7},{7,4},{8,9},{9,10},{10,1... | collective-permute-start | bytes 49160 | tf_op jit(solution)/shard_map/ppermute | solution.py:10
  27.8 3.8 %collective-permute-start.7 = (f32[4,4,256]{2,1,0:T(4,128)S(1)}, f32[4,4,256]{2,1,0:T(4,128)S(1)}, u32[]{:S(2)}, u32[]{:S(2)}) collective-permute-start(f32[4,4,256]{2,1,0:T(4,128)S(1)} %constant_dynamic-update-slice_fusion.2), channel_id=1, source_target_pairs={{0,2},{1,3},{2,0},{3,1},{4,6},{5,7},{6,4},{7,5},{8,10},{9,11},{10,... | collective-permute-start | bytes 49160 | tf_op jit(solution)/shard_map/ppermute | solution.py:10
  29.3 2.8 %collective-permute-start.8 = (f32[4,4,256]{2,1,0:T(4,128)S(1)}, f32[4,4,256]{2,1,0:T(4,128)S(1)}, u32[]{:S(2)}, u32[]{:S(2)}) collective-permute-start(f32[4,4,256]{2,1,0:T(4,128)S(1)} %constant_dynamic-update-slice_fusion.2), channel_id=1, source_target_pairs={{0,3},{1,0},{2,1},{3,2},{4,7},{5,4},{6,5},{7,6},{8,11},{9,8},{10,9... | collective-permute-start | bytes 49160 | tf_op jit(solution)/shard_map/ppermute | solution.py:10
  32.2 8.0 %collective-permute-start.9 = (f32[4,4,256]{2,1,0:T(4,128)S(1)}, f32[4,4,256]{2,1,0:T(4,128)S(1)}, u32[]{:S(2)}, u32[]{:S(2)}) collective-permute-start(f32[4,4,256]{2,1,0:T(4,128)S(1)} %reduce_sum.205), channel_id=1, source_target_pairs={{0,4},{4,8},{8,12},{12,0},{1,5},{5,9},{9,13},{13,1},{2,6},{6,10},{... | collective-permute-start | bytes 49160 | tf_op jit(solution)/shard_map/ppermute | solution.py:10
  35.3 4.9 %collective-permute-start.10 = (f32[4,4,256]{2,1,0:T(4,128)S(1)}, f32[4,4,256]{2,1,0:T(4,128)S(1)}, u32[]{:S(2)}, u32[]{:S(2)}) collective-permute-start(f32[4,4,256]{2,1,0:T(4,128)S(1)} %reduce_sum.205), channel_id=1, source_target_pairs={{0,8},{4,12},{8,0},{12,4},{1,9},{5,13},{9,1},{13,5},{2,10},{6,14},... | collective-permute-start | bytes 49160 | tf_op jit(solution)/shard_map/ppermute | solution.py:10
  37.3 4.3 %collective-permute-start.11 = (f32[4,4,256]{2,1,0:T(4,128)S(1)}, f32[4,4,256]{2,1,0:T(4,128)S(1)}, u32[]{:S(2)}, u32[]{:S(2)}) collective-permute-start(f32[4,4,256]{2,1,0:T(4,128)S(1)} %reduce_sum.205), channel_id=1, source_target_pairs={{0,12},{4,0},{8,4},{12,8},{1,13},{5,1},{9,5},{13,9},{2,14},{6,2},{... | collective-permute-start | bytes 49160 | tf_op jit(solution)/shard_map/ppermute | solution.py:10
  43.2 0.6 %copy-start.2 = (f32[6,512]{1,0:T(8,128)}, f32[6,512]{1,0:T(8,128)S(1)}, u32[]{:S(2)}) copy-start(f32[6,512]{1,0:T(8,128)S(1)} %constant_dynamic-update-slice_fusion) | copy-start | bytes 36868

commit v15 on v13

--- a/solution.py
+++ b/solution.py
@@ -97,16 +97,24 @@
             offsets = [0]
             head = [depth_weight]
         blocks = [(head + ([theirs] if split else []), small_for(p_idx))]
-        for shift in range(1, n_paths):
-            target = (p_idx + shift) % n_paths
+        sources = [p_idx]
+        pairwise = n_paths & (n_paths - 1) == 0
+        for k in reversed(range(1, n_paths)):
+            if pairwise:
+                target = source = p_idx ^ k
+                perm = [(i, i ^ k) for i in range(n_paths)]
+            else:
+                target = (p_idx + k) % n_paths
+                source = (p_idx - k) % n_paths
+                perm = [(i, (i + k) % n_paths) for i in range(n_paths)]
             payload = jnp.concatenate([head[0], small_for(target)], axis=0)
-            perm = [(i, (i + shift) % n_paths) for i in range(n_paths)]
             got = lax.ppermute(payload, "paths", perm)
             part_rows = got[:path_rows]
             dw_parts = [part_rows]
             if split:
                 dw_parts.append(lax.ppermute(part_rows, "cols", [(0, 1), (1, 0)]))
             blocks.append((dw_parts, got[path_rows:]))
+            sources.append(source)
         scaled_parts = [lax.dynamic_slice_in_dim(scaled, off, width, axis=1) for off in offsets]
         mode_ids = lax.iota(jnp.int32, modes)
 
@@ -127,16 +135,18 @@
             parts.append(part.T)
         first = (c_idx == 0) & (d_idx == 0)
         parts[0] = parts[0] - jnp.where(first, observed.T, jnp.zeros_like(observed.T))
-        canon = place_by_source(parts, p_idx, n_paths)
+        canon = jnp.zeros((n_paths,) + parts[0].shape, f32)
+        for piece, source in zip(parts, sources):
+            canon = lax.dynamic_update_index_in_dim(canon, piece, source, 0)
 
         local = n_cols * n_depth
         misfit_all = exchange_sum(canon, ("cols", "depth"), local)
         misfit_all = exchange_sum(misfit_all, "paths", n_paths)
         misfit = lax.dynamic_index_in_dim(misfit_all, p_idx, 0, keepdims=False).T
-        rev = list(reversed(range(n_paths)))
-        doubled = jnp.concatenate([misfit_all, misfit_all], axis=0)
-        mis_rev = lax.dynamic_slice_in_dim(doubled, (p_idx + 1) % n_paths, n_paths, axis=0)
-        mis_rows = jnp.swapaxes(mis_rev, 1, 2).reshape(n_paths * path_rows, kept)
+        rev = list(range(n_paths))
+        mis_rows = jnp.concatenate(
+            [lax.dynamic_index_in_dim(misfit_all, src, 0, keepdims=False).T for src in sources], axis=0
+        )
         len_all = jnp.concatenate([unpacked[s][1] for s in rev], axis=0)
         hot_all = jnp.concatenate([unpacked[s][2] for s in rev], axis=0)
         resid = jnp.sum(mis_rows[:, :, None] * hot_all, axis=1)

time: 40.7 us -> 39.1 us (0.961)
  waiting for transfers between devices: 14.3 us -> 12.7 us
  local copies, waits for them, and re-layouts: 3.7 us -> 3.12 us
  starting transfers between devices: 16.7 us -> 17.2 us
    ppermute x3, waiting for transfers between devices: 3.74 us -> 2.72 us  [shards(): dw_parts.append(lax.ppermute(part_rows, 'cols', [(0, 1), (1, 0)]))]
    convert_element_type x3 -> x4, other arithmetic: 0.03 us -> 0.72 us  [decode(): return (len_b, rows[own_cols:own_cols + kept].T.astype(jnp.int32))]
    convert_element_type x1 -> x0, other arithmetic: 0.7 us -> none  [shards(): mi_t = mode_index.T.astype(bf16)]
    ppermute x6, starting transfers between devices: 6.87 us -> 7.54 us  [shifted_copies(): copies.append(lax.ppermute(x, axes, perm))]
    transpose x1, local copies, waits for them, and re-layouts: 0.6 us -> 0.02 us  [shards(): lax.dynamic_index_in_dim(misfit_all, src, 0, keepdims=False)]
    ppermute x3, starting transfers between devices: 6.12 us -> 5.68 us  [shards(): got = lax.ppermute(payload, 'paths', perm)]
    unnamed x16 -> x18, local copies, waits for them, and re-layouts: 1.97 us -> 1.99 us
  transfers between devices with their start and end apart: 12 -> 12, of which waited for: 9 -> 10; matrix products, arithmetic and copies ran while one was open for 6% -> 6% of each run, Pallas kernels for 0% -> 0%
where the time goes in v15:
time: 39.1 us; the launch traced here: 38.8 us
  starting transfers between devices  17.2 us (44%)
  waiting for transfers between devices  12.7 us (32%)
  local copies, waits for them, and re-layouts  3.12 us (8%)
  matrix products  2.66 us (7%)
  other arithmetic  1.89 us (5%)
  between operations  1.29 us (3%)
    ppermute x6, starting transfers between devices, shifted_copies(): copies.append(lax.ppermute(x, axes, perm))  7.54 us
    ppermute x3, waiting for transfers between devices, shards(): got = lax.ppermute(payload, 'paths', perm)  6.71 us
    ppermute x3, starting transfers between devices, shards(): got = lax.ppermute(payload, 'paths', perm)  5.68 us
    ppermute x3, starting transfers between devices, shards(): dw_parts.append(lax.ppermute(part_rows, 'cols', [(0, 1), (1, 0)]))  3.93 us
    ppermute x6, waiting for transfers between devices, shifted_copies(): copies.append(lax.ppermute(x, axes, perm))  3.29 us
    ppermute x3, waiting for transfers between devices, shards(): dw_parts.append(lax.ppermute(part_rows, 'cols', [(0, 1), (1, 0)]))  2.72 us
    unnamed x18, local copies, waits for them, and re-layouts  1.99 us
    dot_general x8, matrix products, shards(): lax.dot_general(dw_part, sc_part, (((1,), (1,)), ((), ())), preferred_ele...  1.9 us
  transfers between devices with their start and end apart: 12, of which 10 were waited for; matrix products, arithmetic and copies ran while one was open for 6% of the time, Pallas kernels for 0%

profile of v15, /device:TPU:0, one launch (start us, length us, event | category | flops | bytes accessed | tf_op | source)
XLA Modules:
  0.0 38.8 jit_solution(3436954861965865020)
XLA Ops:
  0.7 0.7 %convert_convert_fusion = (s32[256,4]{0,1:T(4,128)S(1)}, bf16[4,256]{1,0:T(4,128)(2,1)S(1)}) fusion(s32[256,4]{0,1:T(4,128)} %param.14), kind=kLoop, calls=%fused_computation.111 | loop fusion | flops 2048 | bytes 10240 | tf_op jit(solution)/shard_map/convert_element_type | solution.py:71
  1.4 1.0 %constant_dynamic-slice_fusion.4 = (bf16[256,256]{1,0:T(8,128)(2,1)S(1)}, bf16[256,256]{1,0:T(8,128)(2,1)S(1)}) fusion(bf16[256,512]{1,0:T(8,128)(2,1)} %param.10, s32[]{:T(128)S(6)} %select_n.122, s32[]{:T(128)S(6)} %select_n.118), kind=kLoop, calls=%fused_computation.97 | loop fusion | bytes 524296 | tf_op jit(solution)/shard_map/dynamic_slice | solution.py:94
  2.6 3.1 %collective-permute-start.2 = (bf16[266,256]{1,0:T(8,128)(2,1)S(1)}, bf16[266,256]{1,0:T(8,128)(2,1)S(1)}, u32[]{:S(2)}, u32[]{:S(2)}) collective-permute-start(bf16[266,256]{1,0:T(8,128)(2,1)S(1)} %get-tuple-element.22), channel_id=1, source_target_pairs={{0,4},{4,0},{8,12},{12,8},{1,5},{5,1},{9,13},{13,9},{2,6},{6,2},{1... | collective-permute-start | bytes 408584 | tf_op jit(solution)/shard_map/ppermute | solution.py:111
  5.7 2.6 %collective-permute-start.1 = (bf16[266,256]{1,0:T(8,128)(2,1)S(1)}, bf16[266,256]{1,0:T(8,128)(2,1)S(1)}, u32[]{:S(2)}, u32[]{:S(2)}) collective-permute-start(bf16[266,256]{1,0:T(8,128)(2,1)S(1)} %get-tuple-element.21), channel_id=1, source_target_pairs={{0,8},{4,12},{8,0},{12,4},{1,9},{5,13},{9,1},{13,5},{2,10},{6,14},... | collective-permute-start | bytes 408584 | tf_op jit(solution)/shard_map/ppermute | solution.py:111
  8.4 0.9 %copy-done = bf16[256,512]{1,0:T(8,128)(2,1)S(1)} copy-done((bf16[256,512]{1,0:T(8,128)(2,1)S(1)}, bf16[256,512]{1,0:T(8,128)(2,1)}, u32[]{:S(2)}) %copy-start) | copy-done | bytes 262168
  9.2 0.2 fusion.27
  9.5 0.2 fusion.35
  10.2 0.5 %copy-done.6 = f32[256,4]{0,1:T(4,128)S(1)} copy-done((f32[256,4]{0,1:T(4,128)S(1)}, f32[256,4]{0,1:T(4,128)}, u32[]{:S(2)}) %copy-start.6) | copy-done | bytes 4120
  10.6 0.5 %collective-permute-done.2 = bf16[266,256]{1,0:T(8,128)(2,1)S(1)} collective-permute-done((bf16[266,256]{1,0:T(8,128)(2,1)S(1)}, bf16[266,256]{1,0:T(8,128)(2,1)S(1)}, u32[]{:S(2)}, u32[]{:S(2)}) %collective-permute-start.2) | collective-permute-done | bytes 136224 | tf_op jit(solution)/shard_map/ppermute | solution.py:111
  11.1 1.8 %collective-permute-start.5 = (bf16[256,256]{1,0:T(8,128)(2,1)S(1)}, bf16[256,256]{1,0:T(8,128)(2,1)S(1)}, u32[]{:S(2)}, u32[]{:S(2)}) collective-permute-start(bf16[256,256]{1,0:T(8,128)(2,1)S(1)} %slice.53), channel_id=1, source_target_pairs={{0,2},{2,0},{1,3},{3,1},{4,6},{6,4},{5,7},{7,5},{8,10},{10,8},{9,1... | collective-permute-start | bytes 393224 | tf_op jit(solution)/shard_map/ppermute | solution.py:115
  12.9 6.2 %collective-permute-done.1 = bf16[266,256]{1,0:T(8,128)(2,1)S(1)} collective-permute-done((bf16[266,256]{1,0:T(8,128)(2,1)S(1)}, bf16[266,256]{1,0:T(8,128)(2,1)S(1)}, u32[]{:S(2)}, u32[]{:S(2)}) %collective-permute-start.1) | collective-permute-done | bytes 136224 | tf_op jit(solution)/shard_map/ppermute | solution.py:111
  19.2 1.6 %collective-permute-start.4 = (bf16[256,256]{1,0:T(8,128)(2,1)S(1)}, bf16[256,256]{1,0:T(8,128)(2,1)S(1)}, u32[]{:S(2)}, u32[]{:S(2)}) collective-permute-start(bf16[256,256]{1,0:T(8,128)(2,1)S(1)} %slice.52), channel_id=1, source_target_pairs={{0,2},{2,0},{1,3},{3,1},{4,6},{6,4},{5,7},{7,5},{8,10},{10,8},{9,1... | collective-permute-start | bytes 393224 | tf_op jit(solution)/shard_map/ppermute | solution.py:115
  20.7 0.6 %collective-permute-start.3 = (bf16[256,256]{1,0:T(8,128)(2,1)S(1)}, bf16[256,256]{1,0:T(8,128)(2,1)S(1)}, u32[]{:S(2)}, u32[]{:S(2)}) collective-permute-start(bf16[256,256]{1,0:T(8,128)(2,1)S(1)} %slice.51), channel_id=1, source_target_pairs={{0,2},{2,0},{1,3},{3,1},{4,6},{6,4},{5,7},{7,5},{8,10},{10,8},{9,1... | collective-permute-start | bytes 393224 | tf_op jit(solution)/shard_map/ppermute | solution.py:115
  21.8 0.2 fusion.31
  22.0 0.2 fusion.33
  22.3 0.2 fusion.21
  22.6 1.6 %collective-permute-done.4 = bf16[256,256]{1,0:T(8,128)(2,1)S(1)} collective-permute-done((bf16[256,256]{1,0:T(8,128)(2,1)S(1)}, bf16[256,256]{1,0:T(8,128)(2,1)S(1)}, u32[]{:S(2)}, u32[]{:S(2)}) %collective-permute-start.4) | collective-permute-done | bytes 131104 | tf_op jit(solution)/shard_map/ppermute | solution.py:115
  24.6 1.1 %collective-permute-done.3 = bf16[256,256]{1,0:T(8,128)(2,1)S(1)} collective-permute-done((bf16[256,256]{1,0:T(8,128)(2,1)S(1)}, bf16[256,256]{1,0:T(8,128)(2,1)S(1)}, u32[]{:S(2)}, u32[]{:S(2)}) %collective-permute-start.3) | collective-permute-done | bytes 131104 | tf_op jit(solution)/shard_map/ppermute | solution.py:115
  26.3 1.4 %collective-permute-start.7 = (f32[4,4,256]{2,1,0:T(4,128)S(1)}, f32[4,4,256]{2,1,0:T(4,128)S(1)}, u32[]{:S(2)}, u32[]{:S(2)}) collective-permute-start(f32[4,4,256]{2,1,0:T(4,128)S(1)} %constant_dynamic-update-slice_fusion.2), channel_id=1, source_target_pairs={{0,2},{1,3},{2,0},{3,1},{4,6},{5,7},{6,4},{7,5},{8,10},{9,11},{10,... | collective-permute-start | bytes 49160 | tf_op jit(solution)/shard_map/ppermute | solution.py:10
  27.6 1.4 %collective-permute-start.8 = (f32[4,4,256]{2,1,0:T(4,128)S(1)}, f32[4,4,256]{2,1,0:T(4,128)S(1)}, u32[]{:S(2)}, u32[]{:S(2)}) collective-permute-start(f32[4,4,256]{2,1,0:T(4,128)S(1)} %constant_dynamic-update-slice_fusion.2), channel_id=1, source_target_pairs={{0,3},{1,0},{2,1},{3,2},{4,7},{5,4},{6,5},{7,6},{8,11},{9,8},{10,9... | collective-permute-start | bytes 49160 | tf_op jit(solution)/shard_map/ppermute | solution.py:10
  29.1 0.3 collective-permute-done.6
  29.4 0.6 %collective-permute-done.7 = f32[4,4,256]{2,1,0:T(4,128)S(1)} collective-permute-done((f32[4,4,256]{2,1,0:T(4,128)S(1)}, f32[4,4,256]{2,1,0:T(4,128)S(1)}, u32[]{:S(2)}, u32[]{:S(2)}) %collective-permute-start.7) | collective-permute-done | bytes 16416 | tf_op jit(solution)/shard_map/ppermute | solution.py:10
  30.1 0.4 %collective-permute-done.8 = f32[4,4,256]{2,1,0:T(4,128)S(1)} collective-permute-done((f32[4,4,256]{2,1,0:T(4,128)S(1)}, f32[4,4,256]{2,1,0:T(4,128)S(1)}, u32[]{:S(2)}, u32[]{:S(2)}) %collective-permute-start.8) | collective-permute-done | bytes 16416 | tf_op jit(solution)/shard_map/ppermute | solution.py:10
  30.5 0.9 %collective-permute-start.9 = (f32[4,4,256]{2,1,0:T(4,128)S(1)}, f32[4,4,256]{2,1,0:T(4,128)S(1)}, u32[]{:S(2)}, u32[]{:S(2)}) collective-permute-start(f32[4,4,256]{2,1,0:T(4,128)S(1)} %reduce_sum.205), channel_id=1, source_target_pairs={{0,4},{4,8},{8,12},{12,0},{1,5},{5,9},{9,13},{13,1},{2,6},{6,10},{... | collective-permute-start | bytes 49160 | tf_op jit(solution)/shard_map/ppermute | solution.py:10
  31.4 2.0 %collective-permute-start.10 = (f32[4,4,256]{2,1,0:T(4,128)S(1)}, f32[4,4,256]{2,1,0:T(4,128)S(1)}, u32[]{:S(2)}, u32[]{:S(2)}) collective-permute-start(f32[4,4,256]{2,1,0:T(4,128)S(1)} %reduce_sum.205), channel_id=1, source_target_pairs={{0,8},{4,12},{8,0},{12,4},{1,9},{5,13},{9,1},{13,5},{2,10},{6,14},... | collective-permute-start | bytes 49160 | tf_op jit(solution)/shard_map/ppermute | solution.py:10
  33.4 1.8 %collective-permute-start.11 = (f32[4,4,256]{2,1,0:T(4,128)S(1)}, f32[4,4,256]{2,1,0:T(4,128)S(1)}, u32[]{:S(2)}, u32[]{:S(2)}) collective-permute-start(f32[4,4,256]{2,1,0:T(4,128)S(1)} %reduce_sum.205), channel_id=1, source_target_pairs={{0,12},{4,0},{8,4},{12,8},{1,13},{5,1},{9,5},{13,9},{2,14},{6,2},{... | collective-permute-start | bytes 49160 | tf_op jit(solution)/shard_map/ppermute | solution.py:10
  35.3 0.9 %collective-permute-done.9 = f32[4,4,256]{2,1,0:T(4,128)S(1)} collective-permute-done((f32[4,4,256]{2,1,0:T(4,128)S(1)}, f32[4,4,256]{2,1,0:T(4,128)S(1)}, u32[]{:S(2)}, u32[]{:S(2)}) %collective-permute-start.9) | collective-permute-done | bytes 16416 | tf_op jit(solution)/shard_map/ppermute | solution.py:10
  36.1 0.4 %collective-permute-done.10 = f32[4,4,256]{2,1,0:T(4,128)S(1)} collective-permute-done((f32[4,4,256]{2,1,0:T(4,128)S(1)}, f32[4,4,256]{2,1,0:T(4,128)S(1)}, u32[]{:S(2)}, u32[]{:S(2)}) %collective-permute-start.10) | collective-permute-done | bytes 16416 | tf_op jit(solution)/shard_map/ppermute | solution.py:10
  36.6 0.6 %collective-permute-done.11 = f32[4,4,256]{2,1,0:T(4,128)S(1)} collective-permute-done((f32[4,4,256]{2,1,0:T(4,128)S(1)}, f32[4,4,256]{2,1,0:T(4,128)S(1)}, u32[]{:S(2)}, u32[]{:S(2)}) %collective-permute-start.11) | collective-permute-done | bytes 16416 | tf_op jit(solution)/shard_map/ppermute | solution.py:10
  37.4 0.4 fusion
  37.8 0.4 fusion.1
  38.2 0.6 %copy-done.2 = f32[6,512]{1,0:T(8,128)} copy-done((f32[6,512]{1,0:T(8,128)}, f32[6,512]{1,0:T(8,128)S(1)}, u32[]{:S(2)}) %copy-start.2) | copy-done | bytes 12312
  (73 shorter events, 2.2 us)
Async XLA Ops:
  0.6 1.8 %copy-start.4 = (bf16[256,24]{0,1:T(8,128)(2,1)S(1)}, bf16[256,24]{0,1:T(8,128)(2,1)}, u32[]{:S(2)}) copy-start(bf16[256,24]{0,1:T(8,128)(2,1)} %param.11) | copy-start | bytes 36868
  0.6 1.8 %copy-start.8 = (s32[256]{0:T(256)S(1)}, s32[256]{0:T(256)}, u32[]{:S(2)}) copy-start(s32[256]{0:T(256)} %param.12) | copy-start | bytes 3076
  0.7 1.8 %copy-start.7 = (s32[256]{0:T(256)S(1)}, s32[256]{0:T(256)}, u32[]{:S(2)}) copy-start(s32[256]{0:T(256)} %param.13) | copy-start | bytes 3076
  2.4 5.9 %copy-start.5 = (bf16[6,512]{1,0:T(8,128)(2,1)S(1)}, bf16[6,512]{1,0:T(8,128)(2,1)}, u32[]{:S(2)}) copy-start(bf16[6,512]{1,0:T(8,128)(2,1)} %param.9) | copy-start | bytes 18436
  2.4 5.9 %copy-start.1 = (bf16[6,64,512]{2,1,0:T(8,128)(2,1)S(1)}, bf16[6,64,512]{2,1,0:T(8,128)(2,1)}, u32[]{:S(2)}) copy-start(bf16[6,64,512]{2,1,0:T(8,128)(2,1)} %param.8) | copy-start | bytes 1179652
  2.6 8.5 %collective-permute-start.2 = (bf16[266,256]{1,0:T(8,128)(2,1)S(1)}, bf16[266,256]{1,0:T(8,128)(2,1)S(1)}, u32[]{:S(2)}, u32[]{:S(2)}) collective-permute-start(bf16[266,256]{1,0:T(8,128)(2,1)S(1)} %get-tuple-element.22), channel_id=1, source_target_pairs={{0,4},{4,0},{8,12},{12,8},{1,5},{5,1},{9,13},{13,9},{2,6},{6,2},{1... | collective-permute-start | bytes 408584 | tf_op jit(solution)/shard_map/ppermute | solution.py:111
  5.7 13.5 %collective-permute-start.1 = (bf16[266,256]{1,0:T(8,128)(2,1)S(1)}, bf16[266,256]{1,0:T(8,128)(2,1)S(1)}, u32[]{:S(2)}, u32[]{:S(2)}) collective-permute-start(bf16[266,256]{1,0:T(8,128)(2,1)S(1)} %get-tuple-element.21), channel_id=1, source_target_pairs={{0,8},{4,12},{8,0},{12,4},{1,9},{5,13},{9,1},{13,5},{2,10},{6,14},... | collective-permute-start | bytes 408584 | tf_op jit(solution)/shard_map/ppermute | solution.py:111
  8.3 12.5 %collective-permute-start = (bf16[266,256]{1,0:T(8,128)(2,1)S(1)}, bf16[266,256]{1,0:T(8,128)(2,1)S(1)}, u32[]{:S(2)}, u32[]{:S(2)}) collective-permute-start(bf16[266,256]{1,0:T(8,128)(2,1)S(1)} %get-tuple-element.20), channel_id=1, source_target_pairs={{0,12},{4,8},{8,4},{12,0},{1,13},{5,9},{9,5},{13,1},{2,14},{6,10},... | collective-permute-start | bytes 408584 | tf_op jit(solution)/shard_map/ppermute | solution.py:111
  8.3 1.0 %copy-start = (bf16[256,512]{1,0:T(8,128)(2,1)S(1)}, bf16[256,512]{1,0:T(8,128)(2,1)}, u32[]{:S(2)}) copy-start(bf16[256,512]{1,0:T(8,128)(2,1)} %param.10) | copy-start | bytes 786436
  9.9 0.7 %copy-start.6 = (f32[256,4]{0,1:T(4,128)S(1)}, f32[256,4]{0,1:T(4,128)}, u32[]{:S(2)}) copy-start(f32[256,4]{0,1:T(4,128)} %param.15) | copy-start | bytes 12292
  11.1 11.2 %collective-permute-start.5 = (bf16[256,256]{1,0:T(8,128)(2,1)S(1)}, bf16[256,256]{1,0:T(8,128)(2,1)S(1)}, u32[]{:S(2)}, u32[]{:S(2)}) collective-permute-start(bf16[256,256]{1,0:T(8,128)(2,1)S(1)} %slice.53), channel_id=1, source_target_pairs={{0,2},{2,0},{1,3},{3,1},{4,6},{6,4},{5,7},{7,5},{8,10},{10,8},{9,1... | collective-permute-start | bytes 393224 | tf_op jit(solution)/shard_map/ppermute | solution.py:115
  19.2 5.0 %collective-permute-start.4 = (bf16[256,256]{1,0:T(8,128)(2,1)S(1)}, bf16[256,256]{1,0:T(8,128)(2,1)S(1)}, u32[]{:S(2)}, u32[]{:S(2)}) collective-permute-start(bf16[256,256]{1,0:T(8,128)(2,1)S(1)} %slice.52), channel_id=1, source_target_pairs={{0,2},{2,0},{1,3},{3,1},{4,6},{6,4},{5,7},{7,5},{8,10},{10,8},{9,1... | collective-permute-start | bytes 393224 | tf_op jit(solution)/shard_map/ppermute | solution.py:115
  20.7 5.0 %collective-permute-start.3 = (bf16[256,256]{1,0:T(8,128)(2,1)S(1)}, bf16[256,256]{1,0:T(8,128)(2,1)S(1)}, u32[]{:S(2)}, u32[]{:S(2)}) collective-permute-start(bf16[256,256]{1,0:T(8,128)(2,1)S(1)} %slice.51), channel_id=1, source_target_pairs={{0,2},{2,0},{1,3},{3,1},{4,6},{6,4},{5,7},{7,5},{8,10},{10,8},{9,1... | collective-permute-start | bytes 393224 | tf_op jit(solution)/shard_map/ppermute | solution.py:115
  26.2 3.2 %collective-permute-start.6 = (f32[4,4,256]{2,1,0:T(4,128)S(1)}, f32[4,4,256]{2,1,0:T(4,128)S(1)}, u32[]{:S(2)}, u32[]{:S(2)}) collective-permute-start(f32[4,4,256]{2,1,0:T(4,128)S(1)} %constant_dynamic-update-slice_fusion.2), channel_id=1, source_target_pairs={{0,1},{1,2},{2,3},{3,0},{4,5},{5,6},{6,7},{7,4},{8,9},{9,10},{10,1... | collective-permute-start | bytes 49160 | tf_op jit(solution)/shard_map/ppermute | solution.py:10
  26.3 3.8 %collective-permute-start.7 = (f32[4,4,256]{2,1,0:T(4,128)S(1)}, f32[4,4,256]{2,1,0:T(4,128)S(1)}, u32[]{:S(2)}, u32[]{:S(2)}) collective-permute-start(f32[4,4,256]{2,1,0:T(4,128)S(1)} %constant_dynamic-update-slice_fusion.2), channel_id=1, source_target_pairs={{0,2},{1,3},{2,0},{3,1},{4,6},{5,7},{6,4},{7,5},{8,10},{9,11},{10,... | collective-permute-start | bytes 49160 | tf_op jit(solution)/shard_map/ppermute | solution.py:10
  27.6 2.8 %collective-permute-start.8 = (f32[4,4,256]{2,1,0:T(4,128)S(1)}, f32[4,4,256]{2,1,0:T(4,128)S(1)}, u32[]{:S(2)}, u32[]{:S(2)}) collective-permute-start(f32[4,4,256]{2,1,0:T(4,128)S(1)} %constant_dynamic-update-slice_fusion.2), channel_id=1, source_target_pairs={{0,3},{1,0},{2,1},{3,2},{4,7},{5,4},{6,5},{7,6},{8,11},{9,8},{10,9... | collective-permute-start | bytes 49160 | tf_op jit(solution)/shard_map/ppermute | solution.py:10
  30.5 5.6 %collective-permute-start.9 = (f32[4,4,256]{2,1,0:T(4,128)S(1)}, f32[4,4,256]{2,1,0:T(4,128)S(1)}, u32[]{:S(2)}, u32[]{:S(2)}) collective-permute-start(f32[4,4,256]{2,1,0:T(4,128)S(1)} %reduce_sum.205), channel_id=1, source_target_pairs={{0,4},{4,8},{8,12},{12,0},{1,5},{5,9},{9,13},{13,1},{2,6},{6,10},{... | collective-permute-start | bytes 49160 | tf_op jit(solution)/shard_map/ppermute | solution.py:10
  31.4 5.1 %collective-permute-start.10 = (f32[4,4,256]{2,1,0:T(4,128)S(1)}, f32[4,4,256]{2,1,0:T(4,128)S(1)}, u32[]{:S(2)}, u32[]{:S(2)}) collective-permute-start(f32[4,4,256]{2,1,0:T(4,128)S(1)} %reduce_sum.205), channel_id=1, source_target_pairs={{0,8},{4,12},{8,0},{12,4},{1,9},{5,13},{9,1},{13,5},{2,10},{6,14},... | collective-permute-start | bytes 49160 | tf_op jit(solution)/shard_map/ppermute | solution.py:10
  33.4 3.7 %collective-permute-start.11 = (f32[4,4,256]{2,1,0:T(4,128)S(1)}, f32[4,4,256]{2,1,0:T(4,128)S(1)}, u32[]{:S(2)}, u32[]{:S(2)}) collective-permute-start(f32[4,4,256]{2,1,0:T(4,128)S(1)} %reduce_sum.205), channel_id=1, source_target_pairs={{0,12},{4,0},{8,4},{12,8},{1,13},{5,1},{9,5},{13,9},{2,14},{6,2},{... | collective-permute-start | bytes 49160 | tf_op jit(solution)/shard_map/ppermute | solution.py:10
  37.2 0.6 %copy-start.3 = (f32[256,4]{0,1:T(4,128)}, f32[256,4]{0,1:T(4,128)S(1)}, u32[]{:S(2)}) copy-start(f32[256,4]{0,1:T(4,128)S(1)} %get-tuple-element.23) | copy-start | bytes 12292
  38.2 0.6 %copy-start.2 = (f32[6,512]{1,0:T(8,128)}, f32[6,512]{1,0:T(8,128)S(1)}, u32[]{:S(2)}) copy-start(f32[6,512]{1,0:T(8,128)S(1)} %constant_dynamic-update-slice_fusion) | copy-start | bytes 36868

commit v16 on v15

--- a/solution.py
+++ b/solution.py
@@ -20,7 +20,14 @@
 
 def exchange_sum(x, axes, count):
     me = lax.axis_index(axes)
-    return jnp.sum(place_by_source(shifted_copies(x, axes, count), me, count), axis=0)
+    if count & (count - 1):
+        return jnp.sum(place_by_source(shifted_copies(x, axes, count), me, count), axis=0)
+    stacked = jnp.zeros((count,) + x.shape, x.dtype)
+    stacked = lax.dynamic_update_index_in_dim(stacked, x, me, 0)
+    for k in reversed(range(1, count)):
+        got = lax.ppermute(x, axes, [(i, i ^ k) for i in range(count)])
+        stacked = lax.dynamic_update_index_in_dim(stacked, got, me ^ k, 0)
+    return jnp.sum(stacked, axis=0)
 
 
 def butterfly_sum(x, axes, count):

time: 39.1 us -> 39.1 us (level)
  waiting for transfers between devices: 12.7 us -> 14 us
  starting transfers between devices: 17.2 us -> 16 us
    ppermute x6, starting transfers between devices: 7.54 us -> 6.37 us  [exchange_sum(): got = lax.ppermute(x, axes, [(i, i ^ k) for i in range(count)])]
    ppermute x6, waiting for transfers between devices: 3.29 us -> 4.42 us  [exchange_sum(): got = lax.ppermute(x, axes, [(i, i ^ k) for i in range(count)])]
  transfers between devices with their start and end apart: 12 -> 12, of which waited for: 10 -> 8; matrix products, arithmetic and copies ran while one was open for 6% -> 6% of each run, Pallas kernels for 0% -> 0%
where the time goes in v16:
time: 39.1 us; the launch traced here: 38.8 us
  starting transfers between devices  16 us (41%)
  waiting for transfers between devices  14 us (36%)
  local copies, waits for them, and re-layouts  3.15 us (8%)
  matrix products  2.66 us (7%)
  other arithmetic  1.89 us (5%)
  between operations  1.14 us (3%)
    ppermute x3, waiting for transfers between devices, shards(): got = lax.ppermute(payload, 'paths', perm)  6.84 us
    ppermute x6, starting transfers between devices, exchange_sum(): got = lax.ppermute(x, axes, [(i, i ^ k) for i in range(count)])  6.37 us
    ppermute x3, starting transfers between devices, shards(): got = lax.ppermute(payload, 'paths', perm)  5.68 us
    ppermute x6, waiting for transfers between devices, exchange_sum(): got = lax.ppermute(x, axes, [(i, i ^ k) for i in range(count)])  4.42 us
    ppermute x3, starting transfers between devices, shards(): dw_parts.append(lax.ppermute(part_rows, 'cols', [(0, 1), (1, 0)]))  3.93 us
    ppermute x3, waiting for transfers between devices, shards(): dw_parts.append(lax.ppermute(part_rows, 'cols', [(0, 1), (1, 0)]))  2.72 us
    unnamed x18, local copies, waits for them, and re-layouts  2.01 us
    dot_general x8, matrix products, shards(): lax.dot_general(dw_part, sc_part, (((1,), (1,)), ((), ())), preferred_ele...  1.9 us
  transfers between devices with their start and end apart: 12, of which 8 were waited for; matrix products, arithmetic and copies ran while one was open for 6% of the time, Pallas kernels for 0%

profile of v16, /device:TPU:0, one launch (start us, length us, event | category | flops | bytes accessed | tf_op | source)
XLA Modules:
  0.0 38.8 jit_solution(18029144289699962641)
XLA Ops:
  0.7 0.7 %convert_convert_fusion = (s32[256,4]{0,1:T(4,128)S(1)}, bf16[4,256]{1,0:T(4,128)(2,1)S(1)}) fusion(s32[256,4]{0,1:T(4,128)} %param.14), kind=kLoop, calls=%fused_computation.111 | loop fusion | flops 2048 | bytes 10240 | tf_op jit(solution)/shard_map/convert_element_type | solution.py:78
  1.4 1.0 %constant_dynamic-slice_fusion.4 = (bf16[256,256]{1,0:T(8,128)(2,1)S(1)}, bf16[256,256]{1,0:T(8,128)(2,1)S(1)}) fusion(bf16[256,512]{1,0:T(8,128)(2,1)} %param.10, s32[]{:T(128)S(6)} %select_n.79, s32[]{:T(128)S(6)} %select_n.75), kind=kLoop, calls=%fused_computation.97 | loop fusion | bytes 524296 | tf_op jit(solution)/shard_map/dynamic_slice | solution.py:101
  2.6 3.1 %collective-permute-start.2 = (bf16[266,256]{1,0:T(8,128)(2,1)S(1)}, bf16[266,256]{1,0:T(8,128)(2,1)S(1)}, u32[]{:S(2)}, u32[]{:S(2)}) collective-permute-start(bf16[266,256]{1,0:T(8,128)(2,1)S(1)} %get-tuple-element.22), channel_id=1, source_target_pairs={{0,4},{4,0},{8,12},{12,8},{1,5},{5,1},{9,13},{13,9},{2,6},{6,2},{1... | collective-permute-start | bytes 408584 | tf_op jit(solution)/shard_map/ppermute | solution.py:118
  5.7 2.6 %collective-permute-start.1 = (bf16[266,256]{1,0:T(8,128)(2,1)S(1)}, bf16[266,256]{1,0:T(8,128)(2,1)S(1)}, u32[]{:S(2)}, u32[]{:S(2)}) collective-permute-start(bf16[266,256]{1,0:T(8,128)(2,1)S(1)} %get-tuple-element.21), channel_id=1, source_target_pairs={{0,8},{4,12},{8,0},{12,4},{1,9},{5,13},{9,1},{13,5},{2,10},{6,14},... | collective-permute-start | bytes 408584 | tf_op jit(solution)/shard_map/ppermute | solution.py:118
  8.4 0.9 %copy-done = bf16[256,512]{1,0:T(8,128)(2,1)S(1)} copy-done((bf16[256,512]{1,0:T(8,128)(2,1)S(1)}, bf16[256,512]{1,0:T(8,128)(2,1)}, u32[]{:S(2)}) %copy-start) | copy-done | bytes 262168
  9.2 0.2 fusion.27
  9.5 0.2 fusion.35
  10.0 0.5 %copy-done.6 = f32[256,4]{0,1:T(4,128)S(1)} copy-done((f32[256,4]{0,1:T(4,128)S(1)}, f32[256,4]{0,1:T(4,128)}, u32[]{:S(2)}) %copy-start.6) | copy-done | bytes 4120
  10.5 0.6 %collective-permute-done.2 = bf16[266,256]{1,0:T(8,128)(2,1)S(1)} collective-permute-done((bf16[266,256]{1,0:T(8,128)(2,1)S(1)}, bf16[266,256]{1,0:T(8,128)(2,1)S(1)}, u32[]{:S(2)}, u32[]{:S(2)}) %collective-permute-start.2) | collective-permute-done | bytes 136224 | tf_op jit(solution)/shard_map/ppermute | solution.py:118
  11.1 1.8 %collective-permute-start.5 = (bf16[256,256]{1,0:T(8,128)(2,1)S(1)}, bf16[256,256]{1,0:T(8,128)(2,1)S(1)}, u32[]{:S(2)}, u32[]{:S(2)}) collective-permute-start(bf16[256,256]{1,0:T(8,128)(2,1)S(1)} %slice.53), channel_id=1, source_target_pairs={{0,2},{2,0},{1,3},{3,1},{4,6},{6,4},{5,7},{7,5},{8,10},{10,8},{9,1... | collective-permute-start | bytes 393224 | tf_op jit(solution)/shard_map/ppermute | solution.py:122
  12.9 6.2 %collective-permute-done.1 = bf16[266,256]{1,0:T(8,128)(2,1)S(1)} collective-permute-done((bf16[266,256]{1,0:T(8,128)(2,1)S(1)}, bf16[266,256]{1,0:T(8,128)(2,1)S(1)}, u32[]{:S(2)}, u32[]{:S(2)}) %collective-permute-start.1) | collective-permute-done | bytes 136224 | tf_op jit(solution)/shard_map/ppermute | solution.py:118
  19.2 1.6 %collective-permute-start.4 = (bf16[256,256]{1,0:T(8,128)(2,1)S(1)}, bf16[256,256]{1,0:T(8,128)(2,1)S(1)}, u32[]{:S(2)}, u32[]{:S(2)}) collective-permute-start(bf16[256,256]{1,0:T(8,128)(2,1)S(1)} %slice.52), channel_id=1, source_target_pairs={{0,2},{2,0},{1,3},{3,1},{4,6},{6,4},{5,7},{7,5},{8,10},{10,8},{9,1... | collective-permute-start | bytes 393224 | tf_op jit(solution)/shard_map/ppermute | solution.py:122
  20.7 0.6 %collective-permute-start.3 = (bf16[256,256]{1,0:T(8,128)(2,1)S(1)}, bf16[256,256]{1,0:T(8,128)(2,1)S(1)}, u32[]{:S(2)}, u32[]{:S(2)}) collective-permute-start(bf16[256,256]{1,0:T(8,128)(2,1)S(1)} %slice.51), channel_id=1, source_target_pairs={{0,2},{2,0},{1,3},{3,1},{4,6},{6,4},{5,7},{7,5},{8,10},{10,8},{9,1... | collective-permute-start | bytes 393224 | tf_op jit(solution)/shard_map/ppermute | solution.py:122
  21.5 0.2 fusion.29
  21.8 0.2 fusion.31
  22.0 0.2 fusion.33
  22.3 0.2 fusion.21
  22.6 1.6 %collective-permute-done.4 = bf16[256,256]{1,0:T(8,128)(2,1)S(1)} collective-permute-done((bf16[256,256]{1,0:T(8,128)(2,1)S(1)}, bf16[256,256]{1,0:T(8,128)(2,1)S(1)}, u32[]{:S(2)}, u32[]{:S(2)}) %collective-permute-start.4) | collective-permute-done | bytes 131104 | tf_op jit(solution)/shard_map/ppermute | solution.py:122
  24.2 0.2 fusion.23
  24.6 1.1 %collective-permute-done.3 = bf16[256,256]{1,0:T(8,128)(2,1)S(1)} collective-permute-done((bf16[256,256]{1,0:T(8,128)(2,1)S(1)}, bf16[256,256]{1,0:T(8,128)(2,1)S(1)}, u32[]{:S(2)}, u32[]{:S(2)}) %collective-permute-start.3) | collective-permute-done | bytes 131104 | tf_op jit(solution)/shard_map/ppermute | solution.py:122
  25.8 0.2 fusion.25
  26.3 1.4 %collective-permute-start.7 = (f32[4,4,256]{2,1,0:T(4,128)S(1)}, f32[4,4,256]{2,1,0:T(4,128)S(1)}, u32[]{:S(2)}, u32[]{:S(2)}) collective-permute-start(f32[4,4,256]{2,1,0:T(4,128)S(1)} %constant_dynamic-update-slice_fusion.2), channel_id=1, source_target_pairs={{0,2},{1,3},{2,0},{3,1},{4,6},{5,7},{6,4},{7,5},{8,10},{9,11},{10,... | collective-permute-start | bytes 49160 | tf_op jit(solution)/shard_map/ppermute | solution.py:28
  27.7 0.5 %collective-permute-start.8 = (f32[4,4,256]{2,1,0:T(4,128)S(1)}, f32[4,4,256]{2,1,0:T(4,128)S(1)}, u32[]{:S(2)}, u32[]{:S(2)}) collective-permute-start(f32[4,4,256]{2,1,0:T(4,128)S(1)} %constant_dynamic-update-slice_fusion.2), channel_id=1, source_target_pairs={{0,1},{1,0},{2,3},{3,2},{4,5},{5,4},{6,7},{7,6},{8,9},{9,8},{10,11... | collective-permute-start | bytes 49160 | tf_op jit(solution)/shard_map/ppermute | solution.py:28
  28.2 1.3 %collective-permute-done.6 = f32[4,4,256]{2,1,0:T(4,128)S(1)} collective-permute-done((f32[4,4,256]{2,1,0:T(4,128)S(1)}, f32[4,4,256]{2,1,0:T(4,128)S(1)}, u32[]{:S(2)}, u32[]{:S(2)}) %collective-permute-start.6) | collective-permute-done | bytes 16416 | tf_op jit(solution)/shard_map/ppermute | solution.py:28
  29.5 0.6 %collective-permute-done.7 = f32[4,4,256]{2,1,0:T(4,128)S(1)} collective-permute-done((f32[4,4,256]{2,1,0:T(4,128)S(1)}, f32[4,4,256]{2,1,0:T(4,128)S(1)}, u32[]{:S(2)}, u32[]{:S(2)}) %collective-permute-start.7) | collective-permute-done | bytes 16416 | tf_op jit(solution)/shard_map/ppermute | solution.py:28
  30.1 2.4 %collective-permute-start.9 = (f32[4,4,256]{2,1,0:T(4,128)S(1)}, f32[4,4,256]{2,1,0:T(4,128)S(1)}, u32[]{:S(2)}, u32[]{:S(2)}) collective-permute-start(f32[4,4,256]{2,1,0:T(4,128)S(1)} %reduce_sum.205), channel_id=1, source_target_pairs={{0,12},{4,8},{8,4},{12,0},{1,13},{5,9},{9,5},{13,1},{2,14},{6,10},... | collective-permute-start | bytes 49160 | tf_op jit(solution)/shard_map/ppermute | solution.py:28
  32.5 2.1 %collective-permute-start.11 = (f32[4,4,256]{2,1,0:T(4,128)S(1)}, f32[4,4,256]{2,1,0:T(4,128)S(1)}, u32[]{:S(2)}, u32[]{:S(2)}) collective-permute-start(f32[4,4,256]{2,1,0:T(4,128)S(1)} %reduce_sum.205), channel_id=1, source_target_pairs={{0,4},{4,0},{8,12},{12,8},{1,5},{5,1},{9,13},{13,9},{2,6},{6,2},{1... | collective-permute-start | bytes 49160 | tf_op jit(solution)/shard_map/ppermute | solution.py:28
  34.6 1.1 %collective-permute-done.9 = f32[4,4,256]{2,1,0:T(4,128)S(1)} collective-permute-done((f32[4,4,256]{2,1,0:T(4,128)S(1)}, f32[4,4,256]{2,1,0:T(4,128)S(1)}, u32[]{:S(2)}, u32[]{:S(2)}) %collective-permute-start.9) | collective-permute-done | bytes 16416 | tf_op jit(solution)/shard_map/ppermute | solution.py:28
  35.7 1.4 %collective-permute-done.10 = f32[4,4,256]{2,1,0:T(4,128)S(1)} collective-permute-done((f32[4,4,256]{2,1,0:T(4,128)S(1)}, f32[4,4,256]{2,1,0:T(4,128)S(1)}, u32[]{:S(2)}, u32[]{:S(2)}) %collective-permute-start.10) | collective-permute-done | bytes 16416 | tf_op jit(solution)/shard_map/ppermute | solution.py:28
  37.4 0.4 fusion
  37.8 0.4 fusion.1
  38.2 0.6 %copy-done.2 = f32[6,512]{1,0:T(8,128)} copy-done((f32[6,512]{1,0:T(8,128)}, f32[6,512]{1,0:T(8,128)S(1)}, u32[]{:S(2)}) %copy-start.2) | copy-done | bytes 12312
  (73 shorter events, 1.5 us)
Async XLA Ops:
  0.6 1.8 %copy-start.4 = (bf16[256,24]{0,1:T(8,128)(2,1)S(1)}, bf16[256,24]{0,1:T(8,128)(2,1)}, u32[]{:S(2)}) copy-start(bf16[256,24]{0,1:T(8,128)(2,1)} %param.11) | copy-start | bytes 36868
  0.6 1.8 %copy-start.8 = (s32[256]{0:T(256)S(1)}, s32[256]{0:T(256)}, u32[]{:S(2)}) copy-start(s32[256]{0:T(256)} %param.12) | copy-start | bytes 3076
  0.7 1.8 %copy-start.7 = (s32[256]{0:T(256)S(1)}, s32[256]{0:T(256)}, u32[]{:S(2)}) copy-start(s32[256]{0:T(256)} %param.13) | copy-start | bytes 3076
  2.4 5.9 %copy-start.5 = (bf16[6,512]{1,0:T(8,128)(2,1)S(1)}, bf16[6,512]{1,0:T(8,128)(2,1)}, u32[]{:S(2)}) copy-start(bf16[6,512]{1,0:T(8,128)(2,1)} %param.9) | copy-start | bytes 18436
  2.4 5.9 %copy-start.1 = (bf16[6,64,512]{2,1,0:T(8,128)(2,1)S(1)}, bf16[6,64,512]{2,1,0:T(8,128)(2,1)}, u32[]{:S(2)}) copy-start(bf16[6,64,512]{2,1,0:T(8,128)(2,1)} %param.8) | copy-start | bytes 1179652
  2.6 8.5 %collective-permute-start.2 = (bf16[266,256]{1,0:T(8,128)(2,1)S(1)}, bf16[266,256]{1,0:T(8,128)(2,1)S(1)}, u32[]{:S(2)}, u32[]{:S(2)}) collective-permute-start(bf16[266,256]{1,0:T(8,128)(2,1)S(1)} %get-tuple-element.22), channel_id=1, source_target_pairs={{0,4},{4,0},{8,12},{12,8},{1,5},{5,1},{9,13},{13,9},{2,6},{6,2},{1... | collective-permute-start | bytes 408584 | tf_op jit(solution)/shard_map/ppermute | solution.py:118
  5.7 13.5 %collective-permute-start.1 = (bf16[266,256]{1,0:T(8,128)(2,1)S(1)}, bf16[266,256]{1,0:T(8,128)(2,1)S(1)}, u32[]{:S(2)}, u32[]{:S(2)}) collective-permute-start(bf16[266,256]{1,0:T(8,128)(2,1)S(1)} %get-tuple-element.21), channel_id=1, source_target_pairs={{0,8},{4,12},{8,0},{12,4},{1,9},{5,13},{9,1},{13,5},{2,10},{6,14},... | collective-permute-start | bytes 408584 | tf_op jit(solution)/shard_map/ppermute | solution.py:118
  8.3 12.5 %collective-permute-start = (bf16[266,256]{1,0:T(8,128)(2,1)S(1)}, bf16[266,256]{1,0:T(8,128)(2,1)S(1)}, u32[]{:S(2)}, u32[]{:S(2)}) collective-permute-start(bf16[266,256]{1,0:T(8,128)(2,1)S(1)} %get-tuple-element.20), channel_id=1, source_target_pairs={{0,12},{4,8},{8,4},{12,0},{1,13},{5,9},{9,5},{13,1},{2,14},{6,10},... | collective-permute-start | bytes 408584 | tf_op jit(solution)/shard_map/ppermute | solution.py:118
  8.3 1.0 %copy-start = (bf16[256,512]{1,0:T(8,128)(2,1)S(1)}, bf16[256,512]{1,0:T(8,128)(2,1)}, u32[]{:S(2)}) copy-start(bf16[256,512]{1,0:T(8,128)(2,1)} %param.10) | copy-start | bytes 786436
  9.8 0.7 %copy-start.6 = (f32[256,4]{0,1:T(4,128)S(1)}, f32[256,4]{0,1:T(4,128)}, u32[]{:S(2)}) copy-start(f32[256,4]{0,1:T(4,128)} %param.15) | copy-start | bytes 12292
  11.1 11.2 %collective-permute-start.5 = (bf16[256,256]{1,0:T(8,128)(2,1)S(1)}, bf16[256,256]{1,0:T(8,128)(2,1)S(1)}, u32[]{:S(2)}, u32[]{:S(2)}) collective-permute-start(bf16[256,256]{1,0:T(8,128)(2,1)S(1)} %slice.53), channel_id=1, source_target_pairs={{0,2},{2,0},{1,3},{3,1},{4,6},{6,4},{5,7},{7,5},{8,10},{10,8},{9,1... | collective-permute-start | bytes 393224 | tf_op jit(solution)/shard_map/ppermute | solution.py:122
  19.2 5.0 %collective-permute-start.4 = (bf16[256,256]{1,0:T(8,128)(2,1)S(1)}, bf16[256,256]{1,0:T(8,128)(2,1)S(1)}, u32[]{:S(2)}, u32[]{:S(2)}) collective-permute-start(bf16[256,256]{1,0:T(8,128)(2,1)S(1)} %slice.52), channel_id=1, source_target_pairs={{0,2},{2,0},{1,3},{3,1},{4,6},{6,4},{5,7},{7,5},{8,10},{10,8},{9,1... | collective-permute-start | bytes 393224 | tf_op jit(solution)/shard_map/ppermute | solution.py:122
  20.7 5.0 %collective-permute-start.3 = (bf16[256,256]{1,0:T(8,128)(2,1)S(1)}, bf16[256,256]{1,0:T(8,128)(2,1)S(1)}, u32[]{:S(2)}, u32[]{:S(2)}) collective-permute-start(bf16[256,256]{1,0:T(8,128)(2,1)S(1)} %slice.51), channel_id=1, source_target_pairs={{0,2},{2,0},{1,3},{3,1},{4,6},{6,4},{5,7},{7,5},{8,10},{10,8},{9,1... | collective-permute-start | bytes 393224 | tf_op jit(solution)/shard_map/ppermute | solution.py:122
  26.2 3.3 %collective-permute-start.6 = (f32[4,4,256]{2,1,0:T(4,128)S(1)}, f32[4,4,256]{2,1,0:T(4,128)S(1)}, u32[]{:S(2)}, u32[]{:S(2)}) collective-permute-start(f32[4,4,256]{2,1,0:T(4,128)S(1)} %constant_dynamic-update-slice_fusion.2), channel_id=1, source_target_pairs={{0,3},{1,2},{2,1},{3,0},{4,7},{5,6},{6,5},{7,4},{8,11},{9,10},{10,... | collective-permute-start | bytes 49160 | tf_op jit(solution)/shard_map/ppermute | solution.py:28
  26.3 3.8 %collective-permute-start.7 = (f32[4,4,256]{2,1,0:T(4,128)S(1)}, f32[4,4,256]{2,1,0:T(4,128)S(1)}, u32[]{:S(2)}, u32[]{:S(2)}) collective-permute-start(f32[4,4,256]{2,1,0:T(4,128)S(1)} %constant_dynamic-update-slice_fusion.2), channel_id=1, source_target_pairs={{0,2},{1,3},{2,0},{3,1},{4,6},{5,7},{6,4},{7,5},{8,10},{9,11},{10,... | collective-permute-start | bytes 49160 | tf_op jit(solution)/shard_map/ppermute | solution.py:28
  27.7 2.4 %collective-permute-start.8 = (f32[4,4,256]{2,1,0:T(4,128)S(1)}, f32[4,4,256]{2,1,0:T(4,128)S(1)}, u32[]{:S(2)}, u32[]{:S(2)}) collective-permute-start(f32[4,4,256]{2,1,0:T(4,128)S(1)} %constant_dynamic-update-slice_fusion.2), channel_id=1, source_target_pairs={{0,1},{1,0},{2,3},{3,2},{4,5},{5,4},{6,7},{7,6},{8,9},{9,8},{10,11... | collective-permute-start | bytes 49160 | tf_op jit(solution)/shard_map/ppermute | solution.py:28
  30.1 5.6 %collective-permute-start.9 = (f32[4,4,256]{2,1,0:T(4,128)S(1)}, f32[4,4,256]{2,1,0:T(4,128)S(1)}, u32[]{:S(2)}, u32[]{:S(2)}) collective-permute-start(f32[4,4,256]{2,1,0:T(4,128)S(1)} %reduce_sum.205), channel_id=1, source_target_pairs={{0,12},{4,8},{8,4},{12,0},{1,13},{5,9},{9,5},{13,1},{2,14},{6,10},... | collective-permute-start | bytes 49160 | tf_op jit(solution)/shard_map/ppermute | solution.py:28
  32.5 4.6 %collective-permute-start.10 = (f32[4,4,256]{2,1,0:T(4,128)S(1)}, f32[4,4,256]{2,1,0:T(4,128)S(1)}, u32[]{:S(2)}, u32[]{:S(2)}) collective-permute-start(f32[4,4,256]{2,1,0:T(4,128)S(1)} %reduce_sum.205), channel_id=1, source_target_pairs={{0,8},{4,12},{8,0},{12,4},{1,9},{5,13},{9,1},{13,5},{2,10},{6,14},... | collective-permute-start | bytes 49160 | tf_op jit(solution)/shard_map/ppermute | solution.py:28
  32.5 4.6 %collective-permute-start.11 = (f32[4,4,256]{2,1,0:T(4,128)S(1)}, f32[4,4,256]{2,1,0:T(4,128)S(1)}, u32[]{:S(2)}, u32[]{:S(2)}) collective-permute-start(f32[4,4,256]{2,1,0:T(4,128)S(1)} %reduce_sum.205), channel_id=1, source_target_pairs={{0,4},{4,0},{8,12},{12,8},{1,5},{5,1},{9,13},{13,9},{2,6},{6,2},{1... | collective-permute-start | bytes 49160 | tf_op jit(solution)/shard_map/ppermute | solution.py:28
  37.2 0.6 %copy-start.3 = (f32[256,4]{0,1:T(4,128)}, f32[256,4]{0,1:T(4,128)S(1)}, u32[]{:S(2)}) copy-start(f32[256,4]{0,1:T(4,128)S(1)} %get-tuple-element.23) | copy-start | bytes 12292
  38.2 0.6 %copy-start.2 = (f32[6,512]{1,0:T(8,128)}, f32[6,512]{1,0:T(8,128)S(1)}, u32[]{:S(2)}) copy-start(f32[6,512]{1,0:T(8,128)S(1)} %constant_dynamic-update-slice_fusion) | copy-start | bytes 36868
